TPU v7x, 32 devices: a whole 2x2x4 slice. The times are simulated.
32 devices in a mesh: tok: 2 (over x), voc: 4 (over y, core), wid: 4 (over z).
Axes of the slice: x: 2, y: 2, z: 4, core: 2. Of those that a mesh axis runs over, the one named last changes fastest.
Arguments:
- hidden: bfloat16 [512, 8192], P('tok', 'wid'), may hold values from -1500 to 1500
- proj: bfloat16 [3584, 8192], P('voc', 'wid'), may hold values from -0.0625 to 0.0625
- table: bfloat16 [19456, 3584], P(('voc', 'wid'), 'tok'), may hold values from -10 to 10
- targets: int32 [512], P('tok'), may hold values from 0 to 19455
- valid: int32 [512], P('tok'), may hold values from 0 to 1, as said below
Outputs:
- grad_proj: float32 [3584, 8192], P('voc', 'wid')
- loss: float32 [], replicated
Inputs may be any that keep to these rules, and one draw needn't show every extreme that they name: `valid`: position 0 is always scored.
All inputs are finite; a program needn't handle non-finite values.
Results may differ from a plain program's by a relative error of at most 0.008.
Values may be sent and summed in bfloat16 or wider, within the bound.
No kernel may reach another device: no remote copies, remote signals or barrier semaphores. Data moves between devices by JAX's collectives and lax.ppermute only.
A program may use at most 128 MiB of HBM per device.

v0:
```python
import jax
import jax.numpy as jnp
from jax import lax
from jax.sharding import PartitionSpec as P


def on_device(hidden, proj, table, targets, valid):
    tok_rows = hidden.shape[0]
    block_rows = table.shape[0]
    partial_value = lax.dot_general(
        hidden, proj, (((1,), (1,)), ((), ())), preferred_element_type=jnp.float32
    )
    summed = lax.psum(partial_value, "wid")
    projected = lax.all_gather(summed.astype(jnp.bfloat16), "voc", axis=1, tiled=True)
    full_table = lax.all_gather(table, "tok", axis=1, tiled=True)
    logits = lax.dot_general(
        projected, full_table, (((1,), (1,)), ((), ())), preferred_element_type=jnp.float32
    )
    block_base = (lax.axis_index("voc") * lax.axis_size("wid") + lax.axis_index("wid")) * block_rows
    local_ids = targets - block_base
    is_target = local_ids[:, None] == lax.broadcasted_iota(jnp.int32, (tok_rows, block_rows), 1)
    picked_here = jnp.sum(jnp.where(is_target, logits, 0.0), axis=1)
    peak_here = jnp.max(logits, axis=1)
    row_peak = lax.pmax(peak_here, ("voc", "wid"))
    exp_here = jnp.sum(jnp.exp(logits - row_peak[:, None]), axis=1)
    row_total, picked = lax.psum((exp_here, picked_here), ("voc", "wid"))
    log_total = row_peak + jnp.log(row_total)
    weight = valid.astype(jnp.float32)
    dlogits = (
        weight[:, None] * (jnp.exp(logits - log_total[:, None]) - is_target.astype(jnp.float32))
    ).astype(jnp.bfloat16)
    reduced = lax.psum_scatter(
        lax.dot_general(
            full_table, dlogits, (((0,), (1,)), ((), ())), preferred_element_type=jnp.float32
        ),
        "voc",
        scatter_dimension=0,
        tiled=True,
    )
    grad_rows = lax.psum(reduced, "wid").astype(jnp.bfloat16)
    grad_part = jnp.dot(grad_rows, hidden, preferred_element_type=jnp.float32)
    loss_part = jnp.sum(weight * (log_total - picked))
    count_part = jnp.sum(weight)
    grad_proj, loss_sum, position_count = lax.psum((grad_part, loss_part, count_part), "tok")
    return (grad_proj, loss_sum / position_count)


def solution(mesh):
    return jax.shard_map(
        on_device,
        mesh=mesh,
        in_specs=(P("tok", "wid"), P("voc", "wid"), P(("voc", "wid"), "tok"), P("tok"), P("tok")),
        out_specs=(P("voc", "wid"), P()),
        check_vma=False,
    )
```

profile of v0, /device:TPU:0, one launch (start us, length us, event | category | flops | bytes accessed | tf_op | source)
XLA Modules:
  0.0 535.9 jit_solution(15466897181801371139)
XLA Ops:
  7.2 0.0 all-gather.3.cloned.1.call-start
  7.2 1.2 copy-done
  8.4 3.3 fusion.6
  11.7 41.0 %all-reduce.7 = bf16[256,896]{1,0:T(8,128)(2,1)} all-reduce(f32[256,896]{1,0:T(8,128)S(1)} %fusion.6), channel_id=1, replica_groups=mesh['tok'=2,'voc'=4,'wid'=4] {'wid'}, use_global_device_ids=true, to_apply=%region_0.0 | all-reduce | flops 229376 | bytes 1376256 | tf_op jit(solution)/shard_map/psum | solution.py:13
  52.7 0.0 all-gather.3.cloned.1.call-update
  52.7 0.0 all-gather.5.cloned.1.call-start
  52.8 0.7 all-gather.5.cloned.1.call-update
  53.5 0.0 reduce-scatter.2.cloned.1.call-start
  53.6 19.9 %all-gather.3.cloned.1.call-done = bf16[256,3584]{1,0:T(8,128)(2,1)} async-done(((bf16[256,896]{1,0:T(8,128)(2,1)}), bf16[256,3584]{1,0:T(8,128)(2,1)}) %all-gather.3.cloned.1.call-update) | async-done | bytes 1835024 | tf_op jit(solution)/shard_map/all_gather | solution.py:14
  73.5 111.7 %all-gather.5.cloned.1.call-done = bf16[1216,3584]{1,0:T(8,128)(2,1)} async-done(((bf16[1216,1792]{1,0:T(8,128)(2,1)}), bf16[1216,3584]{1,0:T(8,128)(2,1)}) %all-gather.5.cloned.1.call-update) | async-done | bytes 8716304 | tf_op jit(solution)/shard_map/all_gather | solution.py:15
  185.1 6.5 %fusion.5 = (f32[256]{0:T(256)S(1)}, f32[256,1216]{0,1:T(8,128)S(1)}) fusion(bf16[256,3584]{1,0:T(8,128)(2,1)} %all-gather.3.cloned.1.call-done, bf16[1216,3584]{1,0:T(8,128)(2,1)} %all-gather.5.cloned.1.call-done), kind=kOutput, calls=%fused_computation.14 | convolution fusion | flops 2231680768 | bytes 11797504 | tf_op jit(solution)/shard_map/dot_general | solution.py:16
  191.6 33.4 %pmax.7 = f32[256]{0:T(256)S(1)} all-reduce(f32[256]{0:T(256)S(1)} %get-tuple-element.11), channel_id=1, replica_groups=mesh['tok'=2,'voc'=4,'wid'=4] {'voc','wid'}, use_global_device_ids=true, to_apply=%region_2.3 | all-reduce | flops 256 | bytes 2048 | tf_op jit(solution)/shard_map/pmax | solution.py:24
  225.0 0.3 select_reduce_fusion
  225.4 29.7 %all-reduce = (f32[256]{0:T(256)S(1)}, f32[256]{0:T(256)S(1)}) all-reduce(f32[256]{0:T(256)S(1)} %get-tuple-element.3, f32[256]{0:T(256)S(1)} %get-tuple-element.2), channel_id=1, replica_groups=mesh['tok'=2,'voc'=4,'wid'=4] {'voc','wid'}, use_global_device_ids=true, to_apply=%region_4.5 | all-reduce | flops 512 | bytes 4096 | tf_op jit(solution)/shard_map/psum | solution.py:26
  255.0 0.6 convert_reduce_fusion
  255.7 7.9 %convolution_bitcast_fusion = f32[3584,256]{0,1:T(8,128)} fusion(bf16[1216,3584]{1,0:T(8,128)(2,1)} %all-gather.5.cloned.1.call-done, f32[256,1216]{0,1:T(8,128)S(1)} %get-tuple-element.12, s32[256]{0:T(256)S(1)} %broadcast_subtract_fusion, f32[256]{0:T(256)S(1)} %get-tuple-element.10, f32[256]{0:T(256)S(1)} %convert_element_type.15), kind=kOutput, calls=%fused_computation | convolution fusion | flops 2233237504 | bytes 13634560 | tf_op jit(solution)/shard_map/dot_general | solution.py:33
  263.6 0.0 reduce-scatter.2.cloned.1.call-update
  263.6 0.0 all-reduce.6.cloned.1.call-start
  263.7 39.4 %reduce-scatter.2.cloned.1.call-done = f32[896,256]{0,1:T(8,128)} async-done(((f32[3584,256]{0,1:T(8,128)}), f32[896,256]{0,1:T(8,128)}) %reduce-scatter.2.cloned.1.call-update) | async-done | bytes 917520 | tf_op jit(solution)/shard_map/reduce_scatter | solution.py:32
  303.1 39.8 %all-reduce.8 = bf16[896,256]{0,1:T(8,128)(2,1)S(1)} all-reduce(f32[896,256]{0,1:T(8,128)} %reduce-scatter.2.cloned.1.call-done), channel_id=1, replica_groups=mesh['tok'=2,'voc'=4,'wid'=4] {'wid'}, use_global_device_ids=true, to_apply=%region_6.7 | all-reduce | flops 229376 | bytes 1376256 | tf_op jit(solution)/shard_map/psum | solution.py:40
  342.9 4.2 fusion.7
  347.1 5.7 %all-reduce.1 = (f32[]{:T(128)}, f32[]{:T(128)}) all-reduce(f32[]{:T(128)} %get-tuple-element.5, f32[]{:T(128)} %get-tuple-element.4), channel_id=1, replica_groups=mesh['tok'=2,'voc'=4,'wid'=4] {'tok'}, use_global_device_ids=true, to_apply=%region_11.12 | all-reduce | flops 2 | bytes 16 | tf_op jit(solution)/shard_map/psum | solution.py:44
  354.2 167.0 %all-reduce.6.cloned.1.call-done = f32[896,2048]{1,0:T(8,128)} async-done(((f32[896,2048]{1,0:T(8,128)}), f32[896,2048]{1,0:T(8,128)}) %all-reduce.6.cloned.1.call-update) | async-done | bytes 7340048 | tf_op jit(solution)/shard_map/psum | solution.py:44
  521.2 7.1 %copy.12 = f32[896,2048]{1,0:T(8,128)} copy(f32[896,2048]{1,0:T(8,128)} %all-reduce.6.cloned.1.call-done) | data formatting | bytes 14680064
  (8 shorter events, 0.0 us)
Async XLA Ops:
  7.2 1.2 copy-start
  7.2 66.3 %all-gather.3.cloned.1.call-start = ((), (), s32[]{:S(2)}) async-start(), calls=%async_computation.1 | async-start | bytes 2293760 | tf_op jit(solution)/shard_map/all_gather | solution.py:14
  52.7 0.8 copy-start.1
  52.7 0.8 copy-start.2
  52.7 132.4 %all-gather.5.cloned.1.call-start = ((), (), s32[]{:S(2)}) async-start(), calls=%async_computation.2 | async-start | bytes 13074432 | tf_op jit(solution)/shard_map/all_gather | solution.py:15
  53.5 249.6 %reduce-scatter.2.cloned.1.call-start = ((), (), s32[]{:S(2)}) async-start(), calls=%async_computation.3 | async-start | bytes 4587520 | tf_op jit(solution)/shard_map/reduce_scatter | solution.py:32
  263.6 257.6 %all-reduce.6.cloned.1.call-start = ((), (), s32[]{:S(2)}) async-start(), calls=%async_computation.4 | async-start | bytes 14680064 | tf_op jit(solution)/shard_map/psum | solution.py:44
Sparse Core Ops, SparseCore 0:
  52.8 20.5 all-gather.2
  75.0 110.0 all-gather.4
  263.7 39.2 reduce-scatter.1
  347.3 173.8 all-reduce.5
where the time goes:
time: 536 us
  waiting for transfers between devices  339 us (63%)
  blocking collectives  150 us (28%)
  matrix products  21.9 us (4%)
  between operations  16.4 us (3%)
  local copies, waits for them, and re-layouts  8.27 us (2%)
    psum x1, waiting for transfers between devices, on_device(): lax.psum((grad_part, loss_part, count_part), 'tok')  167 us
    all_gather x1, waiting for transfers between devices, on_device(): full_table = lax.all_gather(table, 'tok', axis=1, tiled=True)  112 us
    psum x1, blocking collectives, on_device(): summed = lax.psum(partial_value, 'wid')  41 us
    psum x1, blocking collectives, on_device(): grad_rows = lax.psum(reduced, 'wid').astype(jnp.bfloat16)  39.8 us
    reduce_scatter x1, waiting for transfers between devices, on_device(): lax.psum_scatter(lax.dot_general(full_table, dlogits, (((0,), (1,)), ((),...  39.4 us
    pmax x1, blocking collectives, on_device(): row_peak = lax.pmax(peak_here, ('voc', 'wid'))  33.4 us
    psum x1, blocking collectives, on_device(): row_total, picked = lax.psum((exp_here, picked_here), ('voc', 'wid'))  29.7 us
    all_gather x1, waiting for transfers between devices, on_device(): lax.all_gather(summed.astype(jnp.bfloat16), 'voc', axis=1, tiled=True)  19.9 us
  transfers between devices with their start and end apart: 4, of which 4 were waited for; matrix products, arithmetic and copies ran while one was open for 0% of the time, Pallas kernels for 0%

commit v1 on v0

v1 whole, which is shorter than its diff:
```python
import jax
import jax.numpy as jnp
from jax import lax
from jax.sharding import PartitionSpec as P


def tok_pieces(x, n_tok):
    pieces = [x]
    for k in range(1, n_tok):
        perm = [(i, (i + k) % n_tok) for i in range(n_tok)]
        pieces.append(lax.ppermute(x, "tok", perm))
    return pieces


def on_device(hidden, proj, table, targets, valid):
    tok_rows = hidden.shape[0]
    block_rows = table.shape[0]
    n_tok = lax.axis_size("tok")
    t = lax.axis_index("tok")
    d_cols = table.shape[1]

    table_pieces = tok_pieces(table, n_tok)
    if n_tok == 2:
        hidden_other = lax.ppermute(hidden, "tok", [(0, 1), (1, 0)])

    partial_value = lax.dot_general(
        hidden, proj, (((1,), (1,)), ((), ())), preferred_element_type=jnp.float32
    )
    summed = lax.psum(partial_value, "wid")
    projected = lax.all_gather(summed.astype(jnp.bfloat16), "voc", axis=1, tiled=True)

    logits = None
    for k, piece in enumerate(table_pieces):
        cols = lax.dynamic_slice_in_dim(projected, ((t - k) % n_tok) * d_cols, d_cols, axis=1)
        part = lax.dot_general(
            cols, piece, (((1,), (1,)), ((), ())), preferred_element_type=jnp.float32
        )
        logits = part if logits is None else logits + part

    block_base = (lax.axis_index("voc") * lax.axis_size("wid") + lax.axis_index("wid")) * block_rows
    local_ids = targets - block_base
    is_target = local_ids[:, None] == lax.broadcasted_iota(jnp.int32, (tok_rows, block_rows), 1)
    picked_here = jnp.sum(jnp.where(is_target, logits, 0.0), axis=1)
    peak_here = jnp.max(logits, axis=1)
    exp_here = jnp.sum(jnp.exp(logits - peak_here[:, None]), axis=1)
    weight = valid.astype(jnp.float32)

    stats = jnp.stack([peak_here, exp_here, picked_here, weight])
    gathered = lax.all_gather(stats, ("tok", "voc", "wid"))
    gathered = gathered.reshape(n_tok, -1, 4, tok_rows)
    peaks = gathered[:, :, 0]
    row_peak_all = jnp.max(peaks, axis=1)
    row_total_all = jnp.sum(gathered[:, :, 1] * jnp.exp(peaks - row_peak_all[:, None]), axis=1)
    log_total_all = row_peak_all + jnp.log(row_total_all)
    picked_all = jnp.sum(gathered[:, :, 2], axis=1)
    weight_all = gathered[:, 0, 3]
    loss = jnp.sum(weight_all * (log_total_all - picked_all)) / jnp.sum(weight_all)
    log_total = lax.dynamic_index_in_dim(log_total_all, t, axis=0, keepdims=False)

    dlogits = (
        weight[:, None] * (jnp.exp(logits - log_total[:, None]) - is_target.astype(jnp.float32))
    ).astype(jnp.bfloat16)

    full_rows = jnp.zeros((d_cols * n_tok, tok_rows), jnp.float32)
    for k, piece in enumerate(table_pieces):
        part = lax.dot_general(
            piece, dlogits, (((0,), (1,)), ((), ())), preferred_element_type=jnp.float32
        )
        full_rows = lax.dynamic_update_slice_in_dim(full_rows, part, ((t - k) % n_tok) * d_cols, axis=0)
    reduced = lax.psum_scatter(full_rows, "voc", scatter_dimension=0, tiled=True)
    grad_rows_t = lax.psum(reduced, "wid").astype(jnp.bfloat16)

    if n_tok == 2:
        grad_other = lax.ppermute(grad_rows_t, "tok", [(0, 1), (1, 0)])
        first = t == 0
        grad_all = jnp.where(
            first,
            jnp.concatenate([grad_rows_t, grad_other], axis=1),
            jnp.concatenate([grad_other, grad_rows_t], axis=1),
        )
        hidden_all = jnp.where(
            first,
            jnp.concatenate([hidden, hidden_other], axis=0),
            jnp.concatenate([hidden_other, hidden], axis=0),
        )
        grad_proj = jnp.dot(grad_all, hidden_all, preferred_element_type=jnp.float32)
    else:
        grad_all = lax.all_gather(grad_rows_t, "tok", axis=1, tiled=True)
        hidden_all = lax.all_gather(hidden, "tok", axis=0, tiled=True)
        grad_proj = jnp.dot(grad_all, hidden_all, preferred_element_type=jnp.float32)
    return (grad_proj, loss)


def solution(mesh):
    return jax.shard_map(
        on_device,
        mesh=mesh,
        in_specs=(P("tok", "wid"), P("voc", "wid"), P(("voc", "wid"), "tok"), P("tok"), P("tok")),
        out_specs=(P("voc", "wid"), P()),
        check_vma=False,
    )
```

time: 536 us -> 289 us (0.54)
  waiting for transfers between devices: 339 us -> 90 us
    psum x1 -> x0, waiting for transfers between devices: 167 us -> none  [on_device(): lax.psum((grad_part, loss_part, count_part), 'tok')]
    all_gather x1 -> x0, waiting for transfers between devices: 112 us -> none  [on_device(): full_table = lax.all_gather(table, 'tok', axis=1, tiled=True)]
    all_gather x0 -> x1, blocking collectives: none -> 68.6 us  [on_device(): gathered = lax.all_gather(stats, ('tok', 'voc', 'wid'))]
    psum x3 -> x1, blocking collectives: 75.2 us -> 39.8 us  [on_device(): grad_rows_t = lax.psum(reduced, 'wid').astype(jnp.bfloat16)]
    ppermute x0 -> x3, waiting for transfers between devices: none -> 34.8 us  [the longest x1 27.7 us: tok_pieces(): pieces.append(lax.ppermute(x, 'tok', perm))]
    pmax x1 -> x0, blocking collectives: 33.4 us -> none  [on_device(): row_peak = lax.pmax(peak_here, ('voc', 'wid'))]
    unnamed x7 -> x12, local copies, waits for them, and re-layouts: 8.27 us -> 1.23 us
    dot_general x3 -> x5, matrix products: 18.6 us -> 20.4 us  [the longest x2 7.65 us: on_device(): lax.dot_general(cols, piece, (((1,), (1,)), ((), ())), preferred_element_...]
  transfers between devices with their start and end apart: 4 -> 5, of which waited for: 4 -> 4; matrix products, arithmetic and copies ran while one was open for 0% -> 3% of each run, Pallas kernels for 0% -> 0%
where the time goes in v1:
time: 289 us
  blocking collectives  148 us (51%)
  waiting for transfers between devices  90 us (31%)
  matrix products  24 us (8%)
  between operations  16.6 us (6%)
  starting transfers between devices  5.11 us (2%)
  local copies, waits for them, and re-layouts  3.5 us (1%)
    all_gather x1, blocking collectives, on_device(): gathered = lax.all_gather(stats, ('tok', 'voc', 'wid'))  68.6 us
    psum x1, blocking collectives, on_device(): grad_rows_t = lax.psum(reduced, 'wid').astype(jnp.bfloat16)  39.8 us
    psum x1, blocking collectives, on_device(): summed = lax.psum(partial_value, 'wid')  39.6 us
    reduce_scatter x1, waiting for transfers between devices, on_device(): lax.psum_scatter(full_rows, 'voc', scatter_dimension=0, tiled=True)  36 us
    ppermute x1, waiting for transfers between devices, tok_pieces(): pieces.append(lax.ppermute(x, 'tok', perm))  27.7 us
    all_gather x1, waiting for transfers between devices, on_device(): lax.all_gather(summed.astype(jnp.bfloat16), 'voc', axis=1, tiled=True)  19.2 us
    dot_general x2, matrix products, on_device(): lax.dot_general(cols, piece, (((1,), (1,)), ((), ())), preferred_element_...  7.65 us
    dot_general x2, matrix products, on_device(): lax.dot_general(piece, dlogits, (((0,), (1,)), ((), ())), preferred_eleme...  7.56 us
  transfers between devices with their start and end apart: 5, of which 4 were waited for; matrix products, arithmetic and copies ran while one was open for 3% of the time, Pallas kernels for 0%

profile of v1, /device:TPU:0, one launch (start us, length us, event | category | flops | bytes accessed | tf_op | source)
XLA Modules:
  0.0 289.0 jit_solution(2506522054853496714)
XLA Ops:
  7.2 0.0 all-gather.4.cloned.1.call-start
  7.2 3.0 %collective-permute-start = (bf16[1216,1792]{1,0:T(8,128)(2,1)}, bf16[1216,1792]{1,0:T(8,128)(2,1)}, u32[]{:S(2)}, u32[]{:S(2)}) collective-permute-start(bf16[1216,1792]{1,0:T(8,128)(2,1)} %param.7), channel_id=1, source_target_pairs={{0,16},{16,0},{1,17},{17,1},{2,18},{18,2},{3,19},{19,3},{4,20},{20... | collective-permute-start | bytes 13074440 | tf_op jit(solution)/shard_map/ppermute | solution.py:11
  10.2 3.6 %fusion.27 = f32[256,896]{1,0:T(8,128)S(1)} fusion(bf16[256,2048]{1,0:T(8,128)(2,1)} %param.5, bf16[896,2048]{1,0:T(8,128)(2,1)} %param.6), kind=kOutput, calls=%fused_computation.45 | convolution fusion | flops 939524096 | bytes 5636096 | tf_op jit(solution)/shard_map/dot_general | solution.py:26
  13.9 39.6 %all-reduce.2 = bf16[256,896]{1,0:T(8,128)(2,1)} all-reduce(f32[256,896]{1,0:T(8,128)S(1)} %fusion.27), channel_id=1, replica_groups=mesh['tok'=2,'voc'=4,'wid'=4] {'wid'}, use_global_device_ids=true, to_apply=%region_0.0 | all-reduce | flops 229376 | bytes 1376256 | tf_op jit(solution)/shard_map/psum | solution.py:29
  53.5 0.0 reduce-scatter.2.cloned.1.call-start
  53.6 19.2 %all-gather.4.cloned.1.call-done = bf16[256,3584]{1,0:T(8,128)(2,1)} async-done(((bf16[256,896]{1,0:T(8,128)(2,1)}), bf16[256,3584]{1,0:T(8,128)(2,1)}) %all-gather.4.cloned.1.call-update) | async-done | bytes 1835024 | tf_op jit(solution)/shard_map/all_gather | solution.py:30
  72.8 4.0 %fusion.15 = f32[256,1216]{0,1:T(8,128)S(1)} fusion(bf16[1216,1792]{1,0:T(8,128)(2,1)} %param.7, bf16[256,3584]{1,0:T(8,128)(2,1)} %all-gather.4.cloned.1.call-done, s32[]{:T(128)S(6)} %select_n.49), kind=kOutput, calls=%fused_computation.24 | convolution fusion | flops 1115684864 | bytes 6520836 | tf_op jit(solution)/shard_map/dot_general | solution.py:35
  76.9 27.7 %collective-permute-done = bf16[1216,1792]{1,0:T(8,128)(2,1)} collective-permute-done((bf16[1216,1792]{1,0:T(8,128)(2,1)}, bf16[1216,1792]{1,0:T(8,128)(2,1)}, u32[]{:S(2)}, u32[]{:S(2)}) %collective-permute-start) | collective-permute-done | bytes 4358176 | tf_op jit(solution)/shard_map/ppermute | solution.py:11
  104.6 3.6 %fusion.26 = (f32[256]{0:T(256)S(1)}, f32[256,1216]{0,1:T(8,128)S(1)}) fusion(f32[256,1216]{0,1:T(8,128)S(1)} %fusion.15, bf16[1216,1792]{1,0:T(8,128)(2,1)} %collective-permute-done, bf16[256,3584]{1,0:T(8,128)(2,1)S(1)} %copy-done.2, s32[]{:T(128)S(6)} %select_n.51), kind=kOutput, calls=%fused_computation.44 | convolution fusion | flops 1116307200 | bytes 7767044 | tf_op jit(solution)/shard_map/dot_general | solution.py:35
  108.3 0.3 exponential_reduce_fusion
  108.6 68.6 %all-gather.1 = f32[32,4,256]{2,1,0:T(4,128)S(1)} all-gather(f32[1,4,256]{2,1,0:T(4,128)S(1)} %maximum_bitcast_fusion), channel_id=2, replica_groups=mesh['tok'=2,'voc'=4,'wid'=4] {'tok','voc','wid'}, dimensions={0}, use_global_device_ids=true | all-gather | bytes 135168 | tf_op jit(solution)/shard_map/all_gather | solution.py:49
  177.3 0.1 slice_reduce_fusion
  177.4 0.6 slice_reduce_fusion.1
  178.0 0.6 fusion.22
  178.6 2.3 broadcast_in_dim.6
  180.9 2.7 fusion.1
  183.5 4.9 %fusion = f32[3584,256]{0,1:T(8,128)} fusion(f32[3584,256]{0,1:T(8,128)} %fusion.1, s32[]{:T(128)S(6)} %select_n.51, bf16[1216,1792]{1,0:T(8,128)(2,1)} %collective-permute-done, f32[256,1216]{0,1:T(8,128)S(1)} %get-tuple-element.13, f32[256]{0:T(256)S(1)} %bitcast.44, s32[256]{0:T(256)S(1)} %broadcast_subtract_fusion, f32[256]{0:T(256)S(1)} %convert_element_type.15), kind=kOutput, calls=%fused_computation.2 | convolution fusion | flops 1117552640 | bytes 7441412 | tf_op jit(solution)/shard_map/dot_general | solution.py:66
  188.5 1.2 copy-done.3
  189.7 0.5 collective-permute-start.2
  190.2 36.0 %reduce-scatter.2.cloned.1.call-done = f32[896,256]{0,1:T(8,128)} async-done(((f32[3584,256]{0,1:T(8,128)}), f32[896,256]{0,1:T(8,128)}) %reduce-scatter.2.cloned.1.call-update) | async-done | bytes 917520 | tf_op jit(solution)/shard_map/reduce_scatter | solution.py:70
  226.2 39.8 %all-reduce.3 = bf16[896,256]{0,1:T(8,128)(2,1)S(1)} all-reduce(f32[896,256]{0,1:T(8,128)} %reduce-scatter.2.cloned.1.call-done), channel_id=1, replica_groups=mesh['tok'=2,'voc'=4,'wid'=4] {'wid'}, use_global_device_ids=true, to_apply=%region_7.8 | all-reduce | flops 229376 | bytes 1376256 | tf_op jit(solution)/shard_map/psum | solution.py:71
  266.0 1.5 collective-permute-start.1
  268.8 7.1 %collective-permute-done.1 = bf16[896,256]{0,1:T(8,128)(2,1)S(1)} collective-permute-done((bf16[896,256]{0,1:T(8,128)(2,1)S(1)}, bf16[896,256]{0,1:T(8,128)(2,1)S(1)}, u32[]{:S(2)}, u32[]{:S(2)}) %collective-permute-start.1) | collective-permute-done | bytes 458784 | tf_op jit(solution)/shard_map/ppermute | solution.py:74
  275.8 5.2 %fusion.2 = f32[896,2048]{1,0:T(8,128)} fusion(bf16[256,2048]{1,0:T(8,128)(2,1)S(1)} %collective-permute-done.2, bf16[256,2048]{1,0:T(8,128)(2,1)S(1)} %copy-done.3, pred[]{:T(512)S(6)} %eq.16, bf16[896,256]{0,1:T(8,128)(2,1)S(1)} %collective-permute-done.1, bf16[896,256]{0,1:T(8,128)(2,1)S(1)} %all-reduce.3), kind=kOutput, calls=%fused_computation.6 | convolution fusion | flops 1892614144 | bytes 10354689 | tf_op jit(solution)/shard_map/dot_general | solution.py:86
  (20 shorter events, 0.1 us)
Async XLA Ops:
  7.2 65.7 %all-gather.4.cloned.1.call-start = ((), (), s32[]{:S(2)}) async-start(), calls=%async_computation.1 | async-start | bytes 2293760 | tf_op jit(solution)/shard_map/all_gather | solution.py:30
  7.2 97.4 %collective-permute-start = (bf16[1216,1792]{1,0:T(8,128)(2,1)}, bf16[1216,1792]{1,0:T(8,128)(2,1)}, u32[]{:S(2)}, u32[]{:S(2)}) collective-permute-start(bf16[1216,1792]{1,0:T(8,128)(2,1)} %param.7), channel_id=1, source_target_pairs={{0,16},{16,0},{1,17},{17,1},{2,18},{18,2},{3,19},{19,3},{4,20},{20... | collective-permute-start | bytes 13074440 | tf_op jit(solution)/shard_map/ppermute | solution.py:11
  13.9 39.7 %copy-start = (s32[256]{0:T(256)S(1)}, s32[256]{0:T(256)}, u32[]{:S(2)}) copy-start(s32[256]{0:T(256)} %param.9) | copy-start | bytes 3076
  13.9 39.8 %copy-start.1 = (s32[256]{0:T(256)S(1)}, s32[256]{0:T(256)}, u32[]{:S(2)}) copy-start(s32[256]{0:T(256)} %param.8) | copy-start | bytes 3076
  53.5 172.7 %reduce-scatter.2.cloned.1.call-start = ((), (), s32[]{:S(2)}) async-start(), calls=%async_computation.2 | async-start | bytes 4587520 | tf_op jit(solution)/shard_map/reduce_scatter | solution.py:70
  72.8 31.8 %copy-start.2 = (bf16[256,3584]{1,0:T(8,128)(2,1)S(1)}, bf16[256,3584]{1,0:T(8,128)(2,1)}, u32[]{:S(2)}) copy-start(bf16[256,3584]{1,0:T(8,128)(2,1)} %all-gather.4.cloned.1.call-done) | copy-start | bytes 5505028
  72.8 108.0 %slice-start = ((s8[4358144]{0:T(1024)(128)(4,1)}), s8[4194304]{0:T(1024)(128)(4,1)S(1)}, s32[]{:S(2)}) async-start(s8[4358144]{0:T(1024)(128)(4,1)} %bitcast.38), calls=%async_computation.3 | async-start | bytes 8388608
  76.9 104.0 %slice-start.1 = ((s8[4358144]{0:T(1024)(128)(4,1)}), s8[163840]{0:T(1024)(128)(4,1)S(1)}, s32[]{:S(2)}) async-start(s8[4358144]{0:T(1024)(128)(4,1)} %bitcast.38), calls=%async_computation.4 | async-start | bytes 327680
  188.4 1.2 copy-start.3
  189.7 79.1 %collective-permute-start.2 = (bf16[256,2048]{1,0:T(8,128)(2,1)S(1)}, bf16[256,2048]{1,0:T(8,128)(2,1)S(1)}, u32[]{:S(2)}, u32[]{:S(2)}) collective-permute-start(bf16[256,2048]{1,0:T(8,128)(2,1)S(1)} %copy-done.3), channel_id=1, source_target_pairs={{0,16},{16,0},{1,17},{17,1},{2,18},{18,2},{3,19},{19,3},{4,20},{20... | collective-permute-start | bytes 3145736 | tf_op jit(solution)/shard_map/ppermute | solution.py:24
  266.0 9.8 %collective-permute-start.1 = (bf16[896,256]{0,1:T(8,128)(2,1)S(1)}, bf16[896,256]{0,1:T(8,128)(2,1)S(1)}, u32[]{:S(2)}, u32[]{:S(2)}) collective-permute-start(bf16[896,256]{0,1:T(8,128)(2,1)S(1)} %all-reduce.3), channel_id=1, source_target_pairs={{0,16},{16,0},{1,17},{17,1},{2,18},{18,2},{3,19},{19,3},{4,20},{20... | collective-permute-start | bytes 1376264 | tf_op jit(solution)/shard_map/ppermute | solution.py:74
Sparse Core Ops, SparseCore 0:
  53.6 19.1 all-gather.3
  188.6 37.5 reduce-scatter.1

commit v2 on v1

--- a/solution.py
+++ b/solution.py
@@ -10,6 +10,41 @@
         perm = [(i, (i + k) % n_tok) for i in range(n_tok)]
         pieces.append(lax.ppermute(x, "tok", perm))
     return pieces
+
+
+def combine(a, b):
+    peak = jnp.maximum(a[0], b[0])
+    total = a[1] * jnp.exp(a[0] - peak) + b[1] * jnp.exp(b[0] - peak)
+    return jnp.stack([peak, total, a[2] + b[2]])
+
+
+def butterfly(stats, axes):
+    for ax in axes:
+        n = lax.axis_size(ax)
+        if n & (n - 1):
+            gathered = lax.all_gather(stats, ax)
+            out = gathered[0]
+            for i in range(1, n):
+                out = combine(out, gathered[i])
+            stats = out
+            continue
+        b = 1
+        while b < n:
+            other = lax.ppermute(stats, ax, [(i, i ^ b) for i in range(n)])
+            stats = combine(stats, other)
+            b *= 2
+    return stats
+
+
+def tree_sum(x, ax):
+    n = lax.axis_size(ax)
+    if n & (n - 1):
+        return lax.psum(x, ax)
+    b = 1
+    while b < n:
+        x = x + lax.ppermute(x, ax, [(i, i ^ b) for i in range(n)])
+        b *= 2
+    return x
 
 
 def on_device(hidden, proj, table, targets, valid):
@@ -45,17 +80,13 @@
     exp_here = jnp.sum(jnp.exp(logits - peak_here[:, None]), axis=1)
     weight = valid.astype(jnp.float32)
 
-    stats = jnp.stack([peak_here, exp_here, picked_here, weight])
-    gathered = lax.all_gather(stats, ("tok", "voc", "wid"))
-    gathered = gathered.reshape(n_tok, -1, 4, tok_rows)
-    peaks = gathered[:, :, 0]
-    row_peak_all = jnp.max(peaks, axis=1)
-    row_total_all = jnp.sum(gathered[:, :, 1] * jnp.exp(peaks - row_peak_all[:, None]), axis=1)
-    log_total_all = row_peak_all + jnp.log(row_total_all)
-    picked_all = jnp.sum(gathered[:, :, 2], axis=1)
-    weight_all = gathered[:, 0, 3]
-    loss = jnp.sum(weight_all * (log_total_all - picked_all)) / jnp.sum(weight_all)
-    log_total = lax.dynamic_index_in_dim(log_total_all, t, axis=0, keepdims=False)
+    stats = jnp.stack([peak_here, exp_here, picked_here])
+    stats = butterfly(stats, ("voc", "wid"))
+    log_total = stats[0] + jnp.log(stats[1])
+    picked = stats[2]
+    sums = jnp.stack([jnp.sum(weight * (log_total - picked)), jnp.sum(weight)])
+    sums = tree_sum(sums, "tok")
+    loss = sums[0] / sums[1]
 
     dlogits = (
         weight[:, None] * (jnp.exp(logits - log_total[:, None]) - is_target.astype(jnp.float32))

time: 289 us -> 242 us (0.84)
  blocking collectives: 148 us -> 79.4 us
  waiting for transfers between devices: 90 us -> 99.8 us
  starting transfers between devices: 5.11 us -> 13.6 us
    all_gather x1 -> x0, blocking collectives: 68.6 us -> none  [on_device(): gathered = lax.all_gather(stats, ('tok', 'voc', 'wid'))]
    ppermute x0 -> x5, waiting for transfers between devices: none -> 12.8 us  [the longest x4 6.44 us: butterfly(): other = lax.ppermute(stats, ax, [(i, i ^ b) for i in range(n)])]
    ppermute x0 -> x5, starting transfers between devices: none -> 7.21 us  [the longest x4 6.7 us: butterfly(): other = lax.ppermute(stats, ax, [(i, i ^ b) for i in range(n)])]
    ppermute x1, waiting for transfers between devices: 7.09 us -> 0.01 us  [on_device(): grad_other = lax.ppermute(grad_rows_t, 'tok', [(0, 1), (1, 0)])]
    reduce_scatter x1, waiting for transfers between devices: 36 us -> 40 us  [on_device(): lax.psum_scatter(full_rows, 'voc', scatter_dimension=0, tiled=True)]
  transfers between devices with their start and end apart: 5 -> 10, of which waited for: 4 -> 8; matrix products, arithmetic and copies ran while one was open for 3% -> 5% of each run, Pallas kernels for 0% -> 0%
where the time goes in v2:
time: 242 us
  waiting for transfers between devices  99.8 us (41%)
  blocking collectives  79.4 us (33%)
  matrix products  24 us (10%)
  between operations  16.7 us (7%)
  starting transfers between devices  13.6 us (6%)
  local copies, waits for them, and re-layouts  4.08 us (2%)
  other arithmetic  3.96 us (2%)
    reduce_scatter x1, waiting for transfers between devices, on_device(): lax.psum_scatter(full_rows, 'voc', scatter_dimension=0, tiled=True)  40 us
    psum x1, blocking collectives, on_device(): grad_rows_t = lax.psum(reduced, 'wid').astype(jnp.bfloat16)  39.8 us
    psum x1, blocking collectives, on_device(): summed = lax.psum(partial_value, 'wid')  39.6 us
    ppermute x1, waiting for transfers between devices, tok_pieces(): pieces.append(lax.ppermute(x, 'tok', perm))  27.8 us
    all_gather x1, waiting for transfers between devices, on_device(): lax.all_gather(summed.astype(jnp.bfloat16), 'voc', axis=1, tiled=True)  19.2 us
    dot_general x2, matrix products, on_device(): lax.dot_general(cols, piece, (((1,), (1,)), ((), ())), preferred_element_...  7.6 us
    dot_general x2, matrix products, on_device(): lax.dot_general(piece, dlogits, (((0,), (1,)), ((), ())), preferred_eleme...  7.57 us
    ppermute x4, starting transfers between devices, butterfly(): other = lax.ppermute(stats, ax, [(i, i ^ b) for i in range(n)])  6.7 us
  transfers between devices with their start and end apart: 10, of which 8 were waited for; matrix products, arithmetic and copies ran while one was open for 5% of the time, Pallas kernels for 0%

profile of v2, /device:TPU:0, one launch (start us, length us, event | category | flops | bytes accessed | tf_op | source)
XLA Modules:
  0.0 241.6 jit_solution(15965750216695365797)
XLA Ops:
  7.2 3.0 %collective-permute-start = (bf16[1216,1792]{1,0:T(8,128)(2,1)}, bf16[1216,1792]{1,0:T(8,128)(2,1)}, u32[]{:S(2)}, u32[]{:S(2)}) collective-permute-start(bf16[1216,1792]{1,0:T(8,128)(2,1)} %param.7), channel_id=1, source_target_pairs={{0,16},{16,0},{1,17},{17,1},{2,18},{18,2},{3,19},{19,3},{4,20},{20... | collective-permute-start | bytes 13074440 | tf_op jit(solution)/shard_map/ppermute | solution.py:11
  10.2 3.6 %fusion.32 = f32[256,896]{1,0:T(8,128)S(1)} fusion(bf16[256,2048]{1,0:T(8,128)(2,1)} %param.5, bf16[896,2048]{1,0:T(8,128)(2,1)} %param.6), kind=kOutput, calls=%fused_computation.63 | convolution fusion | flops 939524096 | bytes 5636096 | tf_op jit(solution)/shard_map/dot_general | solution.py:61
  13.9 39.6 %all-reduce.2 = bf16[256,896]{1,0:T(8,128)(2,1)} all-reduce(f32[256,896]{1,0:T(8,128)S(1)} %fusion.32), channel_id=1, replica_groups=mesh['tok'=2,'voc'=4,'wid'=4] {'wid'}, use_global_device_ids=true, to_apply=%region_0.0 | all-reduce | flops 229376 | bytes 1376256 | tf_op jit(solution)/shard_map/psum | solution.py:64
  53.6 19.2 %all-gather.2.cloned.1.call-done = bf16[256,3584]{1,0:T(8,128)(2,1)} async-done(((bf16[256,896]{1,0:T(8,128)(2,1)}), bf16[256,3584]{1,0:T(8,128)(2,1)}) %all-gather.2.cloned.1.call-update) | async-done | bytes 1835024 | tf_op jit(solution)/shard_map/all_gather | solution.py:65
  72.8 4.0 %fusion.15 = f32[256,1216]{0,1:T(8,128)S(1)} fusion(bf16[1216,1792]{1,0:T(8,128)(2,1)} %param.7, bf16[256,3584]{1,0:T(8,128)(2,1)} %all-gather.2.cloned.1.call-done, s32[]{:T(128)S(6)} %select_n.45), kind=kOutput, calls=%fused_computation.24 | convolution fusion | flops 1115684864 | bytes 6520836 | tf_op jit(solution)/shard_map/dot_general | solution.py:70
  76.8 27.8 %collective-permute-done = bf16[1216,1792]{1,0:T(8,128)(2,1)} collective-permute-done((bf16[1216,1792]{1,0:T(8,128)(2,1)}, bf16[1216,1792]{1,0:T(8,128)(2,1)}, u32[]{:S(2)}, u32[]{:S(2)}) %collective-permute-start) | collective-permute-done | bytes 4358176 | tf_op jit(solution)/shard_map/ppermute | solution.py:11
  104.6 3.6 %fusion.31 = (f32[256]{0:T(256)S(1)}, f32[256,1216]{0,1:T(8,128)S(1)}) fusion(f32[256,1216]{0,1:T(8,128)S(1)} %fusion.15, bf16[1216,1792]{1,0:T(8,128)(2,1)} %collective-permute-done, bf16[256,3584]{1,0:T(8,128)(2,1)S(1)} %copy-done.2, s32[]{:T(128)S(6)} %select_n.47), kind=kOutput, calls=%fused_computation.62 | convolution fusion | flops 1116307200 | bytes 7767044 | tf_op jit(solution)/shard_map/dot_general | solution.py:70
  109.9 1.8 collective-permute-start.2
  111.7 1.8 collective-permute-done.2
  113.6 1.9 collective-permute-start.3
  115.4 1.8 collective-permute-done.3
  117.3 2.9 %collective-permute-start.4 = (f32[3,256]{1,0:T(4,128)S(1)}, f32[3,256]{1,0:T(4,128)S(1)}, u32[]{:S(2)}, u32[]{:S(2)}) collective-permute-start(f32[3,256]{1,0:T(4,128)S(1)} %pad_maximum_fusion.3), channel_id=1, source_target_pairs={{0,2},{1,3},{2,0},{3,1},{4,6},{5,7},{6,4},{7,5},{8,10},{9,11},{10,... | collective-permute-start | bytes 9224 | tf_op jit(solution)/shard_map/ppermute | solution.py:33
  120.2 1.7 collective-permute-done.4
  122.6 2.3 broadcast_in_dim.6
  124.8 2.7 %fusion.1 = f32[3584,256]{0,1:T(8,128)} fusion(f32[3584,256]{0,1:T(8,128)} %broadcast_in_dim.6, s32[]{:T(128)S(6)} %select_n.45, bf16[1216,1792]{1,0:T(8,128)(2,1)S(1)} %bitcast.33, f32[256,1216]{0,1:T(8,128)S(1)} %get-tuple-element.31, f32[256]{0:T(256)S(1)} %get-tuple-element.6, s32[256]{0:T(256)S(1)} %broadcast_subtract_fusion, ...), kind=kOutput, calls=%fused_computation.4 | convolution fusion | flops 1117552640 | bytes 7441412 | tf_op jit(solution)/shard_map/dot_general | solution.py:97
  127.5 4.9 %fusion = f32[3584,256]{0,1:T(8,128)} fusion(f32[3584,256]{0,1:T(8,128)} %fusion.1, s32[]{:T(128)S(6)} %select_n.47, bf16[1216,1792]{1,0:T(8,128)(2,1)} %collective-permute-done, f32[256,1216]{0,1:T(8,128)S(1)} %get-tuple-element.31, f32[256]{0:T(256)S(1)} %get-tuple-element.6, s32[256]{0:T(256)S(1)} %broadcast_subtract_fusion, f32[256]{0:T(256)S(1)} %convert_element_type.15), kind=kOutput, calls=%fused_computation.2 | convolution fusion | flops 1117552640 | bytes 7441412 | tf_op jit(solution)/shard_map/dot_general | solution.py:97
  133.6 1.7 collective-permute-start.6
  135.4 40.0 %reduce-scatter.2.cloned.1.call-done = f32[896,256]{0,1:T(8,128)} async-done(((f32[3584,256]{0,1:T(8,128)}), f32[896,256]{0,1:T(8,128)}) %reduce-scatter.2.cloned.1.call-update) | async-done | bytes 917520 | tf_op jit(solution)/shard_map/reduce_scatter | solution.py:101
  175.4 39.8 %all-reduce.3 = bf16[896,256]{0,1:T(8,128)(2,1)S(1)} all-reduce(f32[896,256]{0,1:T(8,128)} %reduce-scatter.2.cloned.1.call-done), channel_id=1, replica_groups=mesh['tok'=2,'voc'=4,'wid'=4] {'wid'}, use_global_device_ids=true, to_apply=%region_5.6 | all-reduce | flops 229376 | bytes 1376256 | tf_op jit(solution)/shard_map/psum | solution.py:102
  215.1 1.6 collective-permute-start.5
  216.7 1.4 pad_maximum_fusion.4
  218.7 6.4 %collective-permute-done.7 = f32[2]{0:T(128)S(1)} collective-permute-done((f32[2]{0:T(128)S(1)}, f32[2]{0:T(128)S(1)}, u32[]{:S(2)}, u32[]{:S(2)}) %collective-permute-start.7) | collective-permute-done | bytes 40 | tf_op jit(solution)/shard_map/ppermute | solution.py:45
  225.0 1.4 fusion.39
  228.4 5.2 %fusion.2 = f32[896,2048]{1,0:T(8,128)} fusion(bf16[256,2048]{1,0:T(8,128)(2,1)S(1)} %collective-permute-done.6, bf16[256,2048]{1,0:T(8,128)(2,1)S(1)} %copy-done.3, pred[]{:T(512)S(6)} %eq.16, bf16[896,256]{0,1:T(8,128)(2,1)S(1)} %collective-permute-done.5, bf16[896,256]{0,1:T(8,128)(2,1)S(1)} %all-reduce.3), kind=kOutput, calls=%fused_computation.6 | convolution fusion | flops 1892614144 | bytes 10354689 | tf_op jit(solution)/shard_map/dot_general | solution.py:117
  (35 shorter events, 4.8 us)
Async XLA Ops:
  7.2 65.7 %all-gather.2.cloned.1.call-start = ((), (), s32[]{:S(2)}) async-start(), calls=%async_computation.1 | async-start | bytes 2293760 | tf_op jit(solution)/shard_map/all_gather | solution.py:65
  7.2 97.4 %collective-permute-start = (bf16[1216,1792]{1,0:T(8,128)(2,1)}, bf16[1216,1792]{1,0:T(8,128)(2,1)}, u32[]{:S(2)}, u32[]{:S(2)}) collective-permute-start(bf16[1216,1792]{1,0:T(8,128)(2,1)} %param.7), channel_id=1, source_target_pairs={{0,16},{16,0},{1,17},{17,1},{2,18},{18,2},{3,19},{19,3},{4,20},{20... | collective-permute-start | bytes 13074440 | tf_op jit(solution)/shard_map/ppermute | solution.py:11
  13.9 39.7 %copy-start.1 = (s32[256]{0:T(256)S(1)}, s32[256]{0:T(256)}, u32[]{:S(2)}) copy-start(s32[256]{0:T(256)} %param.8) | copy-start | bytes 3076
  53.5 121.9 %reduce-scatter.2.cloned.1.call-start = ((), (), s32[]{:S(2)}) async-start(), calls=%async_computation.2 | async-start | bytes 4587520 | tf_op jit(solution)/shard_map/reduce_scatter | solution.py:101
  72.8 31.8 %copy-start.2 = (bf16[256,3584]{1,0:T(8,128)(2,1)S(1)}, bf16[256,3584]{1,0:T(8,128)(2,1)}, u32[]{:S(2)}) copy-start(bf16[256,3584]{1,0:T(8,128)(2,1)} %all-gather.2.cloned.1.call-done) | copy-start | bytes 5505028
  72.8 52.0 %slice-start = ((s8[4358144]{0:T(1024)(128)(4,1)}), s8[4194304]{0:T(1024)(128)(4,1)S(1)}, s32[]{:S(2)}) async-start(s8[4358144]{0:T(1024)(128)(4,1)} %bitcast.32), calls=%async_computation.3 | async-start | bytes 8388608
  76.8 43.3 %copy-start = (s32[256]{0:T(256)S(1)}, s32[256]{0:T(256)}, u32[]{:S(2)}) copy-start(s32[256]{0:T(256)} %param.9) | copy-start | bytes 3076
  76.8 48.0 %slice-start.1 = ((s8[4358144]{0:T(1024)(128)(4,1)}), s8[163840]{0:T(1024)(128)(4,1)S(1)}, s32[]{:S(2)}) async-start(s8[4358144]{0:T(1024)(128)(4,1)} %bitcast.32), calls=%async_computation.4 | async-start | bytes 327680
  108.6 1.2 collective-permute-start.1
  109.9 3.7 %collective-permute-start.2 = (f32[3,256]{1,0:T(4,128)S(1)}, f32[3,256]{1,0:T(4,128)S(1)}, u32[]{:S(2)}, u32[]{:S(2)}) collective-permute-start(f32[3,256]{1,0:T(4,128)S(1)} %pad_maximum_fusion.1), channel_id=1, source_target_pairs={{0,8},{4,12},{8,0},{12,4},{1,9},{5,13},{9,1},{13,5},{2,10},{6,14},... | collective-permute-start | bytes 9224 | tf_op jit(solution)/shard_map/ppermute | solution.py:33
  113.6 3.7 %collective-permute-start.3 = (f32[3,256]{1,0:T(4,128)S(1)}, f32[3,256]{1,0:T(4,128)S(1)}, u32[]{:S(2)}, u32[]{:S(2)}) collective-permute-start(f32[3,256]{1,0:T(4,128)S(1)} %pad_maximum_fusion.2), channel_id=1, source_target_pairs={{0,1},{1,0},{2,3},{3,2},{4,5},{5,4},{6,7},{7,6},{8,9},{9,8},{10,11... | collective-permute-start | bytes 9224 | tf_op jit(solution)/shard_map/ppermute | solution.py:33
  117.3 4.6 %collective-permute-start.4 = (f32[3,256]{1,0:T(4,128)S(1)}, f32[3,256]{1,0:T(4,128)S(1)}, u32[]{:S(2)}, u32[]{:S(2)}) collective-permute-start(f32[3,256]{1,0:T(4,128)S(1)} %pad_maximum_fusion.3), channel_id=1, source_target_pairs={{0,2},{1,3},{2,0},{3,1},{4,6},{5,7},{6,4},{7,5},{8,10},{9,11},{10,... | collective-permute-start | bytes 9224 | tf_op jit(solution)/shard_map/ppermute | solution.py:33
  132.4 1.2 copy-start.3
  133.6 94.7 %collective-permute-start.6 = (bf16[256,2048]{1,0:T(8,128)(2,1)S(1)}, bf16[256,2048]{1,0:T(8,128)(2,1)S(1)}, u32[]{:S(2)}, u32[]{:S(2)}) collective-permute-start(bf16[256,2048]{1,0:T(8,128)(2,1)S(1)} %copy-done.3), channel_id=1, source_target_pairs={{0,16},{16,0},{1,17},{17,1},{2,18},{18,2},{3,19},{19,3},{4,20},{20... | collective-permute-start | bytes 3145736 | tf_op jit(solution)/shard_map/ppermute | solution.py:59
  215.1 13.2 %collective-permute-start.5 = (bf16[896,256]{0,1:T(8,128)(2,1)S(1)}, bf16[896,256]{0,1:T(8,128)(2,1)S(1)}, u32[]{:S(2)}, u32[]{:S(2)}) collective-permute-start(bf16[896,256]{0,1:T(8,128)(2,1)S(1)} %all-reduce.3), channel_id=1, source_target_pairs={{0,16},{16,0},{1,17},{17,1},{2,18},{18,2},{3,19},{19,3},{4,20},{20... | collective-permute-start | bytes 1376264 | tf_op jit(solution)/shard_map/ppermute | solution.py:105
  218.1 6.9 %collective-permute-start.7 = (f32[2]{0:T(128)S(1)}, f32[2]{0:T(128)S(1)}, u32[]{:S(2)}, u32[]{:S(2)}) collective-permute-start(f32[2]{0:T(128)S(1)} %pad_maximum_fusion.4), channel_id=1, source_target_pairs={{0,16},{16,0},{1,17},{17,1},{2,18},{18,2},{3,19},{19,3},{4,20},{20... | collective-permute-start | bytes 32 | tf_op jit(solution)/shard_map/ppermute | solution.py:45
Sparse Core Ops, SparseCore 0:
  53.6 19.1 all-gather.1
  132.5 42.7 reduce-scatter.1

commit v3 on v2

--- a/solution.py
+++ b/solution.py
@@ -45,6 +45,41 @@
         x = x + lax.ppermute(x, ax, [(i, i ^ b) for i in range(n)])
         b *= 2
     return x
+
+
+def is_pow2(n):
+    return n & (n - 1) == 0
+
+
+def halving_scatter(x, axes):
+    for ax in axes:
+        n = lax.axis_size(ax)
+        i = lax.axis_index(ax)
+        b = 1
+        while b < n:
+            m = x.shape[0]
+            x = x.reshape((m // 2, 2) + x.shape[1:])
+            bit = (i // b) % 2
+            keep = lax.dynamic_index_in_dim(x, bit, axis=1, keepdims=False)
+            send = lax.dynamic_index_in_dim(x, 1 - bit, axis=1, keepdims=False)
+            x = keep + lax.ppermute(send, ax, [(k, k ^ b) for k in range(n)])
+            b *= 2
+        x = x[0]
+    return x
+
+
+def doubling_gather(x, ax):
+    n = lax.axis_size(ax)
+    i = lax.axis_index(ax)
+    b = n // 2
+    lead = 0
+    while b >= 1:
+        other = lax.ppermute(x, ax, [(k, k ^ b) for k in range(n)])
+        bit = (i // b) % 2
+        x = jnp.where(bit == 0, jnp.stack([x, other], axis=lead), jnp.stack([other, x], axis=lead))
+        lead += 1
+        b //= 2
+    return x.reshape((n,) + x.shape[lead:])
 
 
 def on_device(hidden, proj, table, targets, valid):
@@ -98,8 +133,15 @@
             piece, dlogits, (((0,), (1,)), ((), ())), preferred_element_type=jnp.float32
         )
         full_rows = lax.dynamic_update_slice_in_dim(full_rows, part, ((t - k) % n_tok) * d_cols, axis=0)
-    reduced = lax.psum_scatter(full_rows, "voc", scatter_dimension=0, tiled=True)
-    grad_rows_t = lax.psum(reduced, "wid").astype(jnp.bfloat16)
+    if all(is_pow2(lax.axis_size(ax)) for ax in ("voc", "wid")):
+        n_voc, n_wid = lax.axis_size("voc"), lax.axis_size("wid")
+        blocks = full_rows.reshape((n_voc, n_wid, -1, tok_rows))
+        mine = halving_scatter(blocks, ("voc", "wid")).astype(jnp.bfloat16)
+        grad_rows_t = doubling_gather(mine, "wid")
+        grad_rows_t = grad_rows_t.reshape((-1, tok_rows))
+    else:
+        reduced = lax.psum_scatter(full_rows, "voc", scatter_dimension=0, tiled=True)
+        grad_rows_t = lax.psum(reduced, "wid").astype(jnp.bfloat16)
 
     if n_tok == 2:
         grad_other = lax.ppermute(grad_rows_t, "tok", [(0, 1), (1, 0)])

time: 242 us -> 237 us (0.979)
  blocking collectives: 79.4 us -> 39.6 us
  waiting for transfers between devices: 99.8 us -> 116 us
  starting transfers between devices: 13.6 us -> 20 us
  local copies, waits for them, and re-layouts: 4.08 us -> 8.95 us
  matrix products: 24 us -> 27.8 us
  other arithmetic: 3.96 us -> 7.44 us
    ppermute x0 -> x6, waiting for transfers between devices: none -> 56.3 us  [the longest x4 42.2 us: halving_scatter(): x = keep + lax.ppermute(send, ax, [(k, k ^ b) for k in range(n)])]
    reduce_scatter x1 -> x0, waiting for transfers between devices: 40 us -> none  [on_device(): lax.psum_scatter(full_rows, 'voc', scatter_dimension=0, tiled=True)]
    psum x1 -> x0, blocking collectives: 39.8 us -> none  [on_device(): grad_rows_t = lax.psum(reduced, 'wid').astype(jnp.bfloat16)]
    ppermute x0 -> x6, starting transfers between devices: none -> 6.65 us  [the longest x4 6.5 us: halving_scatter(): x = keep + lax.ppermute(send, ax, [(k, k ^ b) for k in range(n)])]
    dot_general x0 -> x2, local copies, waits for them, and re-layouts: none -> 4.6 us  [on_device(): lax.dot_general(piece, dlogits, (((0,), (1,)), ((), ())), preferred_eleme...]
    add x0 -> x3, other arithmetic: none -> 3.7 us  [halving_scatter(): x = keep + lax.ppermute(send, ax, [(k, k ^ b) for k in range(n)])]
  transfers between devices with their start and end apart: 10 -> 15, of which waited for: 8 -> 13; matrix products, arithmetic and copies ran while one was open for 5% -> 5% of each run, Pallas kernels for 0% -> 0%
where the time goes in v3:
time: 237 us
  waiting for transfers between devices  116 us (49%)
  blocking collectives  39.6 us (17%)
  matrix products  27.8 us (12%)
  starting transfers between devices  20 us (8%)
  between operations  16.8 us (7%)
  local copies, waits for them, and re-layouts  8.95 us (4%)
  other arithmetic  7.44 us (3%)
    ppermute x4, waiting for transfers between devices, halving_scatter(): x = keep + lax.ppermute(send, ax, [(k, k ^ b) for k in range(n)])  42.2 us
    psum x1, blocking collectives, on_device(): summed = lax.psum(partial_value, 'wid')  39.6 us
    ppermute x1, waiting for transfers between devices, tok_pieces(): pieces.append(lax.ppermute(x, 'tok', perm))  27.8 us
    all_gather x1, waiting for transfers between devices, on_device(): lax.all_gather(summed.astype(jnp.bfloat16), 'voc', axis=1, tiled=True)  19.3 us
    ppermute x2, waiting for transfers between devices, doubling_gather(): other = lax.ppermute(x, ax, [(k, k ^ b) for k in range(n)])  14 us
    dot_general x2, matrix products, on_device(): lax.dot_general(piece, dlogits, (((0,), (1,)), ((), ())), preferred_eleme...  9.81 us
    dot_general x2, matrix products, on_device(): lax.dot_general(cols, piece, (((1,), (1,)), ((), ())), preferred_element_...  7.63 us
    dot_general x1, matrix products, on_device(): jnp.dot(grad_all, hidden_all, preferred_element_type=jnp.float32)  6.72 us
  transfers between devices with their start and end apart: 15, of which 13 were waited for; matrix products, arithmetic and copies ran while one was open for 5% of the time, Pallas kernels for 0%

profile of v3, /device:TPU:0, one launch (start us, length us, event | category | flops | bytes accessed | tf_op | source)
XLA Modules:
  0.0 236.6 jit_solution(8381243741419759421)
XLA Ops:
  7.2 3.0 %collective-permute-start = (bf16[1216,1792]{1,0:T(8,128)(2,1)}, bf16[1216,1792]{1,0:T(8,128)(2,1)}, u32[]{:S(2)}, u32[]{:S(2)}) collective-permute-start(bf16[1216,1792]{1,0:T(8,128)(2,1)} %param.7), channel_id=1, source_target_pairs={{0,16},{16,0},{1,17},{17,1},{2,18},{18,2},{3,19},{19,3},{4,20},{20... | collective-permute-start | bytes 13074440 | tf_op jit(solution)/shard_map/ppermute | solution.py:11
  10.2 3.6 %fusion.30 = f32[256,896]{1,0:T(8,128)S(1)} fusion(bf16[256,2048]{1,0:T(8,128)(2,1)} %param.5, bf16[896,2048]{1,0:T(8,128)(2,1)} %param.6), kind=kOutput, calls=%fused_computation.74 | convolution fusion | flops 939524096 | bytes 5636096 | tf_op jit(solution)/shard_map/dot_general | solution.py:96
  13.9 39.6 %all-reduce.1 = bf16[256,896]{1,0:T(8,128)(2,1)} all-reduce(f32[256,896]{1,0:T(8,128)S(1)} %fusion.30), channel_id=1, replica_groups=mesh['tok'=2,'voc'=4,'wid'=4] {'wid'}, use_global_device_ids=true, to_apply=%region_0.0 | all-reduce | flops 229376 | bytes 1376256 | tf_op jit(solution)/shard_map/psum | solution.py:99
  53.5 19.3 %all-gather.2.cloned.1.call-done = bf16[256,3584]{1,0:T(8,128)(2,1)} async-done(((bf16[256,896]{1,0:T(8,128)(2,1)}), bf16[256,3584]{1,0:T(8,128)(2,1)}) %all-gather.2.cloned.1.call-update) | async-done | bytes 1835024 | tf_op jit(solution)/shard_map/all_gather | solution.py:100
  72.8 4.0 %fusion.13 = f32[256,1216]{0,1:T(8,128)S(1)} fusion(bf16[1216,1792]{1,0:T(8,128)(2,1)} %param.7, bf16[256,3584]{1,0:T(8,128)(2,1)} %all-gather.2.cloned.1.call-done, s32[]{:T(128)S(6)} %select_n.140), kind=kOutput, calls=%fused_computation.25 | convolution fusion | flops 1115684864 | bytes 6520836 | tf_op jit(solution)/shard_map/dot_general | solution.py:105
  76.8 27.8 %collective-permute-done = bf16[1216,1792]{1,0:T(8,128)(2,1)} collective-permute-done((bf16[1216,1792]{1,0:T(8,128)(2,1)}, bf16[1216,1792]{1,0:T(8,128)(2,1)}, u32[]{:S(2)}, u32[]{:S(2)}) %collective-permute-start) | collective-permute-done | bytes 4358176 | tf_op jit(solution)/shard_map/ppermute | solution.py:11
  104.6 3.6 %fusion.29 = (f32[256]{0:T(256)S(1)}, f32[256,1216]{0,1:T(8,128)S(1)}) fusion(f32[256,1216]{0,1:T(8,128)S(1)} %fusion.13, bf16[1216,1792]{1,0:T(8,128)(2,1)} %collective-permute-done, bf16[256,3584]{1,0:T(8,128)(2,1)S(1)} %copy-done.4, s32[]{:T(128)S(6)} %select_n.142), kind=kOutput, calls=%fused_computation.73 | convolution fusion | flops 1116307200 | bytes 7767044 | tf_op jit(solution)/shard_map/dot_general | solution.py:105
  113.6 1.9 collective-permute-start.3
  117.3 2.9 %collective-permute-start.4 = (f32[3,256]{1,0:T(4,128)S(1)}, f32[3,256]{1,0:T(4,128)S(1)}, u32[]{:S(2)}, u32[]{:S(2)}) collective-permute-start(f32[3,256]{1,0:T(4,128)S(1)} %pad_maximum_fusion.3), channel_id=1, source_target_pairs={{0,2},{1,3},{2,0},{3,1},{4,6},{5,7},{6,4},{7,5},{8,10},{9,11},{10,... | collective-permute-start | bytes 9224 | tf_op jit(solution)/shard_map/ppermute | solution.py:33
  122.5 4.9 %convolution_bitcast_fusion.1 = f32[1792,256]{0,1:T(8,128)} fusion(bf16[1216,1792]{1,0:T(8,128)(2,1)} %param.7, f32[256,1216]{0,1:T(8,128)S(1)} %get-tuple-element.31, f32[256]{0:T(256)S(1)} %get-tuple-element.6, s32[256]{0:T(256)S(1)} %broadcast_subtract_fusion, f32[256]{0:T(256)S(1)} %convert_element_type.19), kind=kOutput, calls=%fused_computation.2 | convolution fusion | flops 1117552640 | bytes 7441408 | tf_op jit(solution)/shard_map/dot_general | solution.py:132
  127.4 4.9 %convolution_bitcast_fusion = f32[1792,256]{0,1:T(8,128)} fusion(bf16[1216,1792]{1,0:T(8,128)(2,1)} %collective-permute-done, f32[256,1216]{0,1:T(8,128)S(1)} %get-tuple-element.31, f32[256]{0:T(256)S(1)} %get-tuple-element.6, s32[256]{0:T(256)S(1)} %broadcast_subtract_fusion, f32[256]{0:T(256)S(1)} %convert_element_type.19), kind=kOutput, calls=%fused_computation.1 | convolution fusion | flops 1117552640 | bytes 7441408 | tf_op jit(solution)/shard_map/dot_general | solution.py:132
  134.1 2.8 %copy.10 = f32[1792,256]{1,0:T(8,128)} copy(f32[1792,256]{0,1:T(8,128)} %convolution_bitcast_fusion.1) | data formatting | bytes 3670016 | tf_op jit(solution)/shard_map/dot_general | solution.py:132
  140.5 3.9 %collective-permute-done.5 = f32[2,4,224,256]{3,2,1,0:T(8,128)} collective-permute-done((f32[2,4,224,256]{3,2,1,0:T(8,128)S(1)}, f32[2,4,224,256]{3,2,1,0:T(8,128)}, u32[]{:S(2)}, u32[]{:S(2)}) %collective-permute-start.5) | collective-permute-done | bytes 1835040 | tf_op jit(solution)/shard_map/ppermute | solution.py:65
  144.4 2.3 bitcast_add_fusion
  146.9 1.8 collective-permute-start.6
  148.7 20.8 %collective-permute-done.6 = f32[1,4,224,256]{3,2,1,0:T(8,128)} collective-permute-done((f32[1,4,224,256]{3,2,1,0:T(8,128)S(1)}, f32[1,4,224,256]{3,2,1,0:T(8,128)}, u32[]{:S(2)}, u32[]{:S(2)}) %collective-permute-start.6) | collective-permute-done | bytes 917536 | tf_op jit(solution)/shard_map/ppermute | solution.py:65
  170.8 1.8 collective-permute-start.7
  172.7 10.0 %collective-permute-done.7 = f32[2,224,256]{2,1,0:T(8,128)S(1)} collective-permute-done((f32[2,224,256]{2,1,0:T(8,128)S(1)}, f32[2,224,256]{2,1,0:T(8,128)S(1)}, u32[]{:S(2)}, u32[]{:S(2)}) %collective-permute-start.7) | collective-permute-done | bytes 458784 | tf_op jit(solution)/shard_map/ppermute | solution.py:65
  182.8 2.8 %collective-permute-start.8 = (f32[1,224,256]{2,1,0:T(8,128)S(1)}, f32[1,224,256]{2,1,0:T(8,128)S(1)}, u32[]{:S(2)}, u32[]{:S(2)}) collective-permute-start(f32[1,224,256]{2,1,0:T(8,128)S(1)} %constant_dynamic-slice_fusion), channel_id=1, source_target_pairs={{0,2},{1,3},{2,0},{3,1},{4,6},{5,7},{6,4},{7,5},{8,10},{9,11},{10,... | collective-permute-start | bytes 688136 | tf_op jit(solution)/shard_map/ppermute | solution.py:65
  187.1 7.6 %collective-permute-done.8 = f32[1,224,256]{2,1,0:T(8,128)S(1)} collective-permute-done((f32[1,224,256]{2,1,0:T(8,128)S(1)}, f32[1,224,256]{2,1,0:T(8,128)S(1)}, u32[]{:S(2)}, u32[]{:S(2)}) %collective-permute-start.8) | collective-permute-done | bytes 229408 | tf_op jit(solution)/shard_map/ppermute | solution.py:65
  194.8 8.1 %collective-permute-done.9 = bf16[224,256]{1,0:T(8,128)(2,1)S(1)} collective-permute-done((bf16[224,256]{1,0:T(8,128)(2,1)S(1)}, bf16[224,256]{1,0:T(8,128)(2,1)S(1)}, u32[]{:S(2)}, u32[]{:S(2)}) %collective-permute-start.9) | collective-permute-done | bytes 114720 | tf_op jit(solution)/shard_map/ppermute | solution.py:77
  203.0 6.0 %collective-permute-done.10 = bf16[2,224,256]{2,1,0:T(8,128)(2,1)S(1)} collective-permute-done((bf16[2,224,256]{2,1,0:T(8,128)(2,1)S(1)}, bf16[2,224,256]{2,1,0:T(8,128)(2,1)S(1)}, u32[]{:S(2)}, u32[]{:S(2)}) %collective-permute-start.10) | collective-permute-done | bytes 229408 | tf_op jit(solution)/shard_map/ppermute | solution.py:77
  212.4 6.2 %collective-permute-done.13 = f32[2]{0:T(128)S(1)} collective-permute-done((f32[2]{0:T(128)S(1)}, f32[2]{0:T(128)S(1)}, u32[]{:S(2)}, u32[]{:S(2)}) %collective-permute-start.13) | collective-permute-done | bytes 40 | tf_op jit(solution)/shard_map/ppermute | solution.py:45
  221.9 6.7 %fusion = f32[896,2048]{1,0:T(8,128)} fusion(bf16[256,2048]{1,0:T(8,128)(2,1)} %collective-permute-done.12, bf16[256,2048]{1,0:T(8,128)(2,1)S(1)} %copy-done.5, pred[]{:T(512)S(6)} %eq.28, bf16[896,256]{1,0:T(8,128)(2,1)S(1)} %collective-permute-done.11, bf16[896,256]{1,0:T(8,128)(2,1)S(1)} %bitcast.57), kind=kOutput, calls=%fused_computation.4 | convolution fusion | flops 1892614144 | bytes 10354689 | tf_op jit(solution)/shard_map/dot_general | solution.py:159
  (58 shorter events, 23.4 us)
Async XLA Ops:
  7.2 65.7 %all-gather.2.cloned.1.call-start = ((), (), s32[]{:S(2)}) async-start(), calls=%async_computation | async-start | bytes 2293760 | tf_op jit(solution)/shard_map/all_gather | solution.py:100
  7.2 97.4 %collective-permute-start = (bf16[1216,1792]{1,0:T(8,128)(2,1)}, bf16[1216,1792]{1,0:T(8,128)(2,1)}, u32[]{:S(2)}, u32[]{:S(2)}) collective-permute-start(bf16[1216,1792]{1,0:T(8,128)(2,1)} %param.7), channel_id=1, source_target_pairs={{0,16},{16,0},{1,17},{17,1},{2,18},{18,2},{3,19},{19,3},{4,20},{20... | collective-permute-start | bytes 13074440 | tf_op jit(solution)/shard_map/ppermute | solution.py:11
  13.9 39.7 %copy-start.3 = (s32[256]{0:T(256)S(1)}, s32[256]{0:T(256)}, u32[]{:S(2)}) copy-start(s32[256]{0:T(256)} %param.8) | copy-start | bytes 3076
  72.8 31.8 %copy-start.4 = (bf16[256,3584]{1,0:T(8,128)(2,1)S(1)}, bf16[256,3584]{1,0:T(8,128)(2,1)}, u32[]{:S(2)}) copy-start(bf16[256,3584]{1,0:T(8,128)(2,1)} %all-gather.2.cloned.1.call-done) | copy-start | bytes 5505028
  76.8 43.4 %copy-start.2 = (s32[256]{0:T(256)S(1)}, s32[256]{0:T(256)}, u32[]{:S(2)}) copy-start(s32[256]{0:T(256)} %param.9) | copy-start | bytes 3076
  108.6 1.2 collective-permute-start.1
  109.9 3.7 %collective-permute-start.2 = (f32[3,256]{1,0:T(4,128)S(1)}, f32[3,256]{1,0:T(4,128)S(1)}, u32[]{:S(2)}, u32[]{:S(2)}) collective-permute-start(f32[3,256]{1,0:T(4,128)S(1)} %pad_maximum_fusion.1), channel_id=1, source_target_pairs={{0,8},{4,12},{8,0},{12,4},{1,9},{5,13},{9,1},{13,5},{2,10},{6,14},... | collective-permute-start | bytes 9224 | tf_op jit(solution)/shard_map/ppermute | solution.py:33
  113.6 3.7 %collective-permute-start.3 = (f32[3,256]{1,0:T(4,128)S(1)}, f32[3,256]{1,0:T(4,128)S(1)}, u32[]{:S(2)}, u32[]{:S(2)}) collective-permute-start(f32[3,256]{1,0:T(4,128)S(1)} %pad_maximum_fusion.2), channel_id=1, source_target_pairs={{0,1},{1,0},{2,3},{3,2},{4,5},{5,4},{6,7},{7,6},{8,9},{9,8},{10,11... | collective-permute-start | bytes 9224 | tf_op jit(solution)/shard_map/ppermute | solution.py:33
  117.3 4.6 %collective-permute-start.4 = (f32[3,256]{1,0:T(4,128)S(1)}, f32[3,256]{1,0:T(4,128)S(1)}, u32[]{:S(2)}, u32[]{:S(2)}) collective-permute-start(f32[3,256]{1,0:T(4,128)S(1)} %pad_maximum_fusion.3), channel_id=1, source_target_pairs={{0,2},{1,3},{2,0},{3,1},{4,6},{5,7},{6,4},{7,5},{8,10},{9,11},{10,... | collective-permute-start | bytes 9224 | tf_op jit(solution)/shard_map/ppermute | solution.py:33
  136.9 1.5 copy-start.1
  138.7 1.8 copy-start
  140.5 3.9 %collective-permute-start.5 = (f32[2,4,224,256]{3,2,1,0:T(8,128)S(1)}, f32[2,4,224,256]{3,2,1,0:T(8,128)}, u32[]{:S(2)}, u32[]{:S(2)}) collective-permute-start(f32[2,4,224,256]{3,2,1,0:T(8,128)S(1)} %dynamic-slice_bitcast_fusion), channel_id=1, source_target_pairs={{0,4},{4,0},{8,12},{12,8},{1,5},{5,1},{9,13},{13,9},{2,6},{6,2},{1... | collective-permute-start | bytes 5505032 | tf_op jit(solution)/shard_map/ppermute | solution.py:65
  146.9 22.6 %collective-permute-start.6 = (f32[1,4,224,256]{3,2,1,0:T(8,128)S(1)}, f32[1,4,224,256]{3,2,1,0:T(8,128)}, u32[]{:S(2)}, u32[]{:S(2)}) collective-permute-start(f32[1,4,224,256]{3,2,1,0:T(8,128)S(1)} %constant_dynamic-slice_fusion.1), channel_id=1, source_target_pairs={{0,8},{4,12},{8,0},{12,4},{1,9},{5,13},{9,1},{13,5},{2,10},{6,14},... | collective-permute-start | bytes 2752520 | tf_op jit(solution)/shard_map/ppermute | solution.py:65
  170.8 14.8 %copy-start.5 = (bf16[256,2048]{1,0:T(8,128)(2,1)S(1)}, bf16[256,2048]{1,0:T(8,128)(2,1)}, u32[]{:S(2)}) copy-start(bf16[256,2048]{1,0:T(8,128)(2,1)} %param.5) | copy-start | bytes 3145732
  170.8 11.8 %collective-permute-start.7 = (f32[2,224,256]{2,1,0:T(8,128)S(1)}, f32[2,224,256]{2,1,0:T(8,128)S(1)}, u32[]{:S(2)}, u32[]{:S(2)}) collective-permute-start(f32[2,224,256]{2,1,0:T(8,128)S(1)} %dynamic-slice_bitcast_fusion.1), channel_id=1, source_target_pairs={{0,1},{1,0},{2,3},{3,2},{4,5},{5,4},{6,7},{7,6},{8,9},{9,8},{10,11... | collective-permute-start | bytes 1376264 | tf_op jit(solution)/shard_map/ppermute | solution.py:65
  182.8 11.9 %collective-permute-start.8 = (f32[1,224,256]{2,1,0:T(8,128)S(1)}, f32[1,224,256]{2,1,0:T(8,128)S(1)}, u32[]{:S(2)}, u32[]{:S(2)}) collective-permute-start(f32[1,224,256]{2,1,0:T(8,128)S(1)} %constant_dynamic-slice_fusion), channel_id=1, source_target_pairs={{0,2},{1,3},{2,0},{3,1},{4,6},{5,7},{6,4},{7,5},{8,10},{9,11},{10,... | collective-permute-start | bytes 688136 | tf_op jit(solution)/shard_map/ppermute | solution.py:65
  185.6 36.3 %collective-permute-start.12 = (bf16[256,2048]{1,0:T(8,128)(2,1)S(1)}, bf16[256,2048]{1,0:T(8,128)(2,1)}, u32[]{:S(2)}, u32[]{:S(2)}) collective-permute-start(bf16[256,2048]{1,0:T(8,128)(2,1)S(1)} %copy-done.5), channel_id=1, source_target_pairs={{0,16},{16,0},{1,17},{17,1},{2,18},{18,2},{3,19},{19,3},{4,20},{20... | collective-permute-start | bytes 3145736 | tf_op jit(solution)/shard_map/ppermute | solution.py:94
  194.7 8.2 %collective-permute-start.9 = (bf16[224,256]{1,0:T(8,128)(2,1)S(1)}, bf16[224,256]{1,0:T(8,128)(2,1)S(1)}, u32[]{:S(2)}, u32[]{:S(2)}) collective-permute-start(bf16[224,256]{1,0:T(8,128)(2,1)S(1)} %bitcast.54), channel_id=1, source_target_pairs={{0,2},{1,3},{2,0},{3,1},{4,6},{5,7},{6,4},{7,5},{8,10},{9,11},{10,... | collective-permute-start | bytes 344072 | tf_op jit(solution)/shard_map/ppermute | solution.py:77
  202.9 6.1 %collective-permute-start.10 = (bf16[2,224,256]{2,1,0:T(8,128)(2,1)S(1)}, bf16[2,224,256]{2,1,0:T(8,128)(2,1)S(1)}, u32[]{:S(2)}, u32[]{:S(2)}) collective-permute-start(bf16[2,224,256]{2,1,0:T(8,128)(2,1)S(1)} %maximum_select_fusion.6), channel_id=1, source_target_pairs={{0,1},{1,0},{2,3},{3,2},{4,5},{5,4},{6,7},{7,6},{8,9},{9,8},{10,11... | collective-permute-start | bytes 688136 | tf_op jit(solution)/shard_map/ppermute | solution.py:77
  209.0 12.8 %collective-permute-start.11 = (bf16[896,256]{1,0:T(8,128)(2,1)S(1)}, bf16[896,256]{1,0:T(8,128)(2,1)S(1)}, u32[]{:S(2)}, u32[]{:S(2)}) collective-permute-start(bf16[896,256]{1,0:T(8,128)(2,1)S(1)} %bitcast.56), channel_id=1, source_target_pairs={{0,16},{16,0},{1,17},{17,1},{2,18},{18,2},{3,19},{19,3},{4,20},{20... | collective-permute-start | bytes 1376264 | tf_op jit(solution)/shard_map/ppermute | solution.py:147
  211.9 6.8 %collective-permute-start.13 = (f32[2]{0:T(128)S(1)}, f32[2]{0:T(128)S(1)}, u32[]{:S(2)}, u32[]{:S(2)}) collective-permute-start(f32[2]{0:T(128)S(1)} %pad_maximum_fusion.4), channel_id=1, source_target_pairs={{0,16},{16,0},{1,17},{17,1},{2,18},{18,2},{3,19},{19,3},{4,20},{20... | collective-permute-start | bytes 32 | tf_op jit(solution)/shard_map/ppermute | solution.py:45
Sparse Core Ops, SparseCore 0:
  53.6 19.1 all-gather.1

commit v4 on v3

--- a/solution.py
+++ b/solution.py
@@ -51,20 +51,25 @@
     return n & (n - 1) == 0
 
 
-def halving_scatter(x, axes):
-    for ax in axes:
+def bit_list(ax, n):
+    out = []
+    b = 1
+    while b < n:
+        out.append((ax, b))
+        b *= 2
+    return out
+
+
+def halving_steps(x, dims, order):
+    dims = list(dims)
+    for ax, b in order:
+        pos = dims.index((ax, b))
         n = lax.axis_size(ax)
-        i = lax.axis_index(ax)
-        b = 1
-        while b < n:
-            m = x.shape[0]
-            x = x.reshape((m // 2, 2) + x.shape[1:])
-            bit = (i // b) % 2
-            keep = lax.dynamic_index_in_dim(x, bit, axis=1, keepdims=False)
-            send = lax.dynamic_index_in_dim(x, 1 - bit, axis=1, keepdims=False)
-            x = keep + lax.ppermute(send, ax, [(k, k ^ b) for k in range(n)])
-            b *= 2
-        x = x[0]
+        bit = (lax.axis_index(ax) // b) % 2
+        keep = lax.dynamic_index_in_dim(x, bit, axis=pos, keepdims=False)
+        send = lax.dynamic_index_in_dim(x, 1 - bit, axis=pos, keepdims=False)
+        x = keep + lax.ppermute(send, ax, [(k, k ^ b) for k in range(n)])
+        dims.pop(pos)
     return x
 
 
@@ -127,18 +132,35 @@
         weight[:, None] * (jnp.exp(logits - log_total[:, None]) - is_target.astype(jnp.float32))
     ).astype(jnp.bfloat16)
 
-    full_rows = jnp.zeros((d_cols * n_tok, tok_rows), jnp.float32)
+    parts = []
     for k, piece in enumerate(table_pieces):
-        part = lax.dot_general(
-            piece, dlogits, (((0,), (1,)), ((), ())), preferred_element_type=jnp.float32
+        parts.append(
+            lax.dot_general(piece, dlogits, (((0,), (1,)), ((), ())), preferred_element_type=jnp.float32)
         )
-        full_rows = lax.dynamic_update_slice_in_dim(full_rows, part, ((t - k) % n_tok) * d_cols, axis=0)
-    if all(is_pow2(lax.axis_size(ax)) for ax in ("voc", "wid")):
-        n_voc, n_wid = lax.axis_size("voc"), lax.axis_size("wid")
-        blocks = full_rows.reshape((n_voc, n_wid, -1, tok_rows))
-        mine = halving_scatter(blocks, ("voc", "wid")).astype(jnp.bfloat16)
-        grad_rows_t = doubling_gather(mine, "wid")
-        grad_rows_t = grad_rows_t.reshape((-1, tok_rows))
+    if n_tok == 2:
+        full_rows = jnp.where(
+            t == 0, jnp.concatenate(parts, axis=0), jnp.concatenate(parts[::-1], axis=0)
+        )
+    else:
+        full_rows = jnp.zeros((d_cols * n_tok, tok_rows), jnp.float32)
+        for k, part in enumerate(parts):
+            full_rows = lax.dynamic_update_slice_in_dim(
+                full_rows, part, ((t - k) % n_tok) * d_cols, axis=0
+            )
+    n_voc, n_wid = lax.axis_size("voc"), lax.axis_size("wid")
+    if is_pow2(n_voc) and is_pow2(n_wid) and n_voc > 1 and tok_rows % 2 == 0:
+        voc_bits = bit_list("voc", n_voc)
+        wid_bits = bit_list("wid", n_wid)
+        dims = voc_bits[::-1] + wid_bits[::-1]
+        blocks = full_rows.reshape(tuple(2 for _ in dims) + (-1, tok_rows))
+        first = voc_bits[0]
+        blocks = halving_steps(blocks, dims, [first])
+        dims = [d for d in dims if d != first]
+        half = tok_rows // 2
+        part_a = halving_steps(blocks[..., :half], dims, voc_bits[1:] + wid_bits)
+        part_b = halving_steps(blocks[..., half:], dims, wid_bits + voc_bits[1:])
+        mine = jnp.concatenate([part_a, part_b], axis=-1).astype(jnp.bfloat16)
+        grad_rows_t = doubling_gather(mine, "wid").reshape((-1, tok_rows))
     else:
         reduced = lax.psum_scatter(full_rows, "voc", scatter_dimension=0, tiled=True)
         grad_rows_t = lax.psum(reduced, "wid").astype(jnp.bfloat16)

time: 237 us -> 223 us (0.941)
  waiting for transfers between devices: 116 us -> 98.1 us
  starting transfers between devices: 20 us -> 23.4 us
  matrix products: 27.8 us -> 25.3 us
    ppermute x4 -> x7, waiting for transfers between devices: 42.2 us -> 27.5 us  [halving_steps(): x = keep + lax.ppermute(send, ax, [(k, k ^ b) for k in range(n)])]
    select_n x0 -> x1, local copies, waits for them, and re-layouts: none -> 5.11 us  [on_device(): jnp.where(t == 0, jnp.concatenate(parts, axis=0), jnp.concatenate(parts[:...]
    dot_general x2 -> x0, local copies, waits for them, and re-layouts: 4.6 us -> none  [on_device(): lax.dot_general(piece, dlogits, (((0,), (1,)), ((), ())), preferred_eleme...]
    ppermute x4 -> x7, starting transfers between devices: 6.5 us -> 9.91 us  [halving_steps(): x = keep + lax.ppermute(send, ax, [(k, k ^ b) for k in range(n)])]
    unnamed x12 -> x8, local copies, waits for them, and re-layouts: 2.97 us -> 0.02 us
    squeeze x4 -> x7, local copies, waits for them, and re-layouts: 0.27 us -> 3.01 us  [halving_steps(): send = lax.dynamic_index_in_dim(x, 1 - bit, axis=pos, keepdims=False)]
    dot_general x2, matrix products: 9.81 us -> 7.32 us  [on_device(): lax.dot_general(piece, dlogits, (((0,), (1,)), ((), ())), preferred_eleme...]
  transfers between devices with their start and end apart: 15 -> 18, of which waited for: 13 -> 14; matrix products, arithmetic and copies ran while one was open for 5% -> 6% of each run, Pallas kernels for 0% -> 0%
where the time goes in v4:
time: 223 us; the launch traced here: 221 us
  waiting for transfers between devices  98.1 us (44%)
  blocking collectives  39.6 us (18%)
  matrix products  25.3 us (11%)
  starting transfers between devices  23.4 us (10%)
  between operations  16.8 us (8%)
  other arithmetic  9.15 us (4%)
  local copies, waits for them, and re-layouts  8.95 us (4%)
    psum x1, blocking collectives, on_device(): summed = lax.psum(partial_value, 'wid')  39.6 us
    ppermute x1, waiting for transfers between devices, tok_pieces(): pieces.append(lax.ppermute(x, 'tok', perm))  27.8 us
    ppermute x7, waiting for transfers between devices, halving_steps(): x = keep + lax.ppermute(send, ax, [(k, k ^ b) for k in range(n)])  27.5 us
    all_gather x1, waiting for transfers between devices, on_device(): lax.all_gather(summed.astype(jnp.bfloat16), 'voc', axis=1, tiled=True)  19.3 us
    ppermute x2, waiting for transfers between devices, doubling_gather(): other = lax.ppermute(x, ax, [(k, k ^ b) for k in range(n)])  11.9 us
    ppermute x7, starting transfers between devices, halving_steps(): x = keep + lax.ppermute(send, ax, [(k, k ^ b) for k in range(n)])  9.91 us
    dot_general x2, matrix products, on_device(): lax.dot_general(cols, piece, (((1,), (1,)), ((), ())), preferred_element_...  7.63 us
    dot_general x2, matrix products, on_device(): lax.dot_general(piece, dlogits, (((0,), (1,)), ((), ())), preferred_eleme...  7.32 us
  transfers between devices with their start and end apart: 18, of which 14 were waited for; matrix products, arithmetic and copies ran while one was open for 6% of the time, Pallas kernels for 0%

profile of v4, /device:TPU:0, one launch (start us, length us, event | category | flops | bytes accessed | tf_op | source)
XLA Modules:
  0.0 221.3 jit_solution(14037778649733307210)
XLA Ops:
  7.2 3.0 %collective-permute-start = (bf16[1216,1792]{1,0:T(8,128)(2,1)}, bf16[1216,1792]{1,0:T(8,128)(2,1)}, u32[]{:S(2)}, u32[]{:S(2)}) collective-permute-start(bf16[1216,1792]{1,0:T(8,128)(2,1)} %param.7), channel_id=1, source_target_pairs={{0,16},{16,0},{1,17},{17,1},{2,18},{18,2},{3,19},{19,3},{4,20},{20... | collective-permute-start | bytes 13074440 | tf_op jit(solution)/shard_map/ppermute | solution.py:11
  10.2 3.6 %fusion.33 = f32[256,896]{1,0:T(8,128)S(1)} fusion(bf16[256,2048]{1,0:T(8,128)(2,1)} %param.5, bf16[896,2048]{1,0:T(8,128)(2,1)} %param.6), kind=kOutput, calls=%fused_computation.84 | convolution fusion | flops 939524096 | bytes 5636096 | tf_op jit(solution)/shard_map/dot_general | solution.py:101
  13.9 39.6 %all-reduce.1 = bf16[256,896]{1,0:T(8,128)(2,1)} all-reduce(f32[256,896]{1,0:T(8,128)S(1)} %fusion.33), channel_id=1, replica_groups=mesh['tok'=2,'voc'=4,'wid'=4] {'wid'}, use_global_device_ids=true, to_apply=%region_0.0 | all-reduce | flops 229376 | bytes 1376256 | tf_op jit(solution)/shard_map/psum | solution.py:104
  53.5 19.3 %all-gather.2.cloned.1.call-done = bf16[256,3584]{1,0:T(8,128)(2,1)} async-done(((bf16[256,896]{1,0:T(8,128)(2,1)}), bf16[256,3584]{1,0:T(8,128)(2,1)}) %all-gather.2.cloned.1.call-update) | async-done | bytes 1835024 | tf_op jit(solution)/shard_map/all_gather | solution.py:105
  72.8 4.0 %fusion.13 = f32[256,1216]{0,1:T(8,128)S(1)} fusion(bf16[1216,1792]{1,0:T(8,128)(2,1)} %param.7, bf16[256,3584]{1,0:T(8,128)(2,1)} %all-gather.2.cloned.1.call-done, s32[]{:T(128)S(6)} %select_n.163), kind=kOutput, calls=%fused_computation.25 | convolution fusion | flops 1115684864 | bytes 6520836 | tf_op jit(solution)/shard_map/dot_general | solution.py:110
  76.8 27.8 %collective-permute-done = bf16[1216,1792]{1,0:T(8,128)(2,1)} collective-permute-done((bf16[1216,1792]{1,0:T(8,128)(2,1)}, bf16[1216,1792]{1,0:T(8,128)(2,1)}, u32[]{:S(2)}, u32[]{:S(2)}) %collective-permute-start) | collective-permute-done | bytes 4358176 | tf_op jit(solution)/shard_map/ppermute | solution.py:11
  104.6 3.6 %fusion.32 = (f32[256]{0:T(256)S(1)}, f32[256,1216]{0,1:T(8,128)S(1)}) fusion(f32[256,1216]{0,1:T(8,128)S(1)} %fusion.13, bf16[1216,1792]{1,0:T(8,128)(2,1)} %collective-permute-done, bf16[256,3584]{1,0:T(8,128)(2,1)S(1)} %copy-done.2, s32[]{:T(128)S(6)} %select_n.165), kind=kOutput, calls=%fused_computation.83 | convolution fusion | flops 1116307200 | bytes 7767044 | tf_op jit(solution)/shard_map/dot_general | solution.py:110
  117.3 2.9 %collective-permute-start.4 = (f32[3,256]{1,0:T(4,128)S(1)}, f32[3,256]{1,0:T(4,128)S(1)}, u32[]{:S(2)}, u32[]{:S(2)}) collective-permute-start(f32[3,256]{1,0:T(4,128)S(1)} %pad_maximum_fusion.4), channel_id=1, source_target_pairs={{0,2},{1,3},{2,0},{3,1},{4,6},{5,7},{6,4},{7,5},{8,10},{9,11},{10,... | collective-permute-start | bytes 9224 | tf_op jit(solution)/shard_map/ppermute | solution.py:33
  122.5 3.7 %convolution_bitcast_fusion.1 = f32[1792,256]{0,1:T(8,128)S(1)} fusion(bf16[1216,1792]{1,0:T(8,128)(2,1)} %param.7, f32[256,1216]{0,1:T(8,128)S(1)} %get-tuple-element.33, f32[256]{0:T(256)S(1)} %get-tuple-element.6, s32[256]{0:T(256)S(1)} %broadcast_subtract_fusion, f32[256]{0:T(256)S(1)} %convert_element_type.29), kind=kOutput, calls=%fused_computation.3 | convolution fusion | flops 1117552640 | bytes 7441408 | tf_op jit(solution)/shard_map/dot_general | solution.py:138
  126.2 3.7 %convolution_bitcast_fusion = f32[1792,256]{0,1:T(8,128)S(1)} fusion(bf16[1216,1792]{1,0:T(8,128)(2,1)} %collective-permute-done, f32[256,1216]{0,1:T(8,128)S(1)} %get-tuple-element.33, f32[256]{0:T(256)S(1)} %get-tuple-element.6, s32[256]{0:T(256)S(1)} %broadcast_subtract_fusion, f32[256]{0:T(256)S(1)} %convert_element_type.29), kind=kOutput, calls=%fused_computation.2 | convolution fusion | flops 1117552640 | bytes 7441408 | tf_op jit(solution)/shard_map/dot_general | solution.py:138
  129.8 2.3 %maximum_select_fusion = f32[3584,256]{0,1:T(8,128)} fusion(f32[1792,256]{0,1:T(8,128)S(1)} %convolution_bitcast_fusion, f32[1792,256]{0,1:T(8,128)S(1)} %convolution_bitcast_fusion.1, pred[]{:T(512)S(6)} %eq.30), kind=kLoop, calls=%fused_computation | loop fusion | flops 2752512 | bytes 7340033 | tf_op jit(solution)/shard_map/jit(_where)/select_n | solution.py:141
  132.1 5.1 %copy.11 = f32[3584,256]{1,0:T(8,128)} copy(f32[3584,256]{0,1:T(8,128)} %maximum_select_fusion) | data formatting | bytes 7340032 | tf_op jit(solution)/shard_map/jit(_where)/select_n | solution.py:141
  137.2 2.9 %dynamic-slice_bitcast_fusion = f32[2,2,2,224,256]{4,3,2,1,0:T(8,128)} fusion(f32[2,2,2,2,224,256]{5,4,3,2,1,0:T(8,128)} %bitcast.69, s32[]{:T(128)S(6)} %select_n.171), kind=kLoop, calls=%fused_computation.13 | loop fusion | bytes 3670020 | tf_op jit(solution)/shard_map/jit(dynamic_index_in_dim)/squeeze | solution.py:70
  140.1 4.0 %collective-permute-done.5 = f32[2,2,2,224,256]{4,3,2,1,0:T(8,128)S(1)} collective-permute-done((f32[2,2,2,224,256]{4,3,2,1,0:T(8,128)}, f32[2,2,2,224,256]{4,3,2,1,0:T(8,128)S(1)}, u32[]{:S(2)}, u32[]{:S(2)}) %collective-permute-start.5) | collective-permute-done | bytes 1835040 | tf_op jit(solution)/shard_map/ppermute | solution.py:71
  146.1 1.9 collective-permute-start.9
  151.1 7.7 %collective-permute-done.9 = f32[2,2,224,128]{3,2,1,0:T(8,128)S(1)} collective-permute-done((f32[2,2,224,128]{3,2,1,0:T(8,128)S(1)}, f32[2,2,224,128]{3,2,1,0:T(8,128)S(1)}, u32[]{:S(2)}, u32[]{:S(2)}) %collective-permute-start.9) | collective-permute-done | bytes 458784 | tf_op jit(solution)/shard_map/ppermute | solution.py:71
  158.9 2.8 %collective-permute-start.10 = (f32[2,224,128]{2,1,0:T(8,128)S(1)}, f32[2,224,128]{2,1,0:T(8,128)S(1)}, u32[]{:S(2)}, u32[]{:S(2)}) collective-permute-start(f32[2,224,128]{2,1,0:T(8,128)S(1)} %dynamic-slice_bitcast_fusion.3), channel_id=1, source_target_pairs={{0,2},{1,3},{2,0},{3,1},{4,6},{5,7},{6,4},{7,5},{8,10},{9,11},{10,... | collective-permute-start | bytes 688136 | tf_op jit(solution)/shard_map/ppermute | solution.py:71
  164.4 7.5 %collective-permute-done.10 = f32[2,224,128]{2,1,0:T(8,128)S(1)} collective-permute-done((f32[2,224,128]{2,1,0:T(8,128)S(1)}, f32[2,224,128]{2,1,0:T(8,128)S(1)}, u32[]{:S(2)}, u32[]{:S(2)}) %collective-permute-start.10) | collective-permute-done | bytes 229408 | tf_op jit(solution)/shard_map/ppermute | solution.py:71
  174.0 2.8 %collective-permute-done.11 = f32[224,128]{1,0:T(8,128)S(1)} collective-permute-done((f32[224,128]{1,0:T(8,128)S(1)}, f32[224,128]{1,0:T(8,128)S(1)}, u32[]{:S(2)}, u32[]{:S(2)}) %collective-permute-start.11) | collective-permute-done | bytes 114720 | tf_op jit(solution)/shard_map/ppermute | solution.py:71
  176.8 5.5 %collective-permute-done.8 = f32[224,128]{1,0:T(8,128)S(1)} collective-permute-done((f32[224,128]{1,0:T(8,128)S(1)}, f32[224,128]{1,0:T(8,128)S(1)}, u32[]{:S(2)}, u32[]{:S(2)}) %collective-permute-start.8) | collective-permute-done | bytes 114720 | tf_op jit(solution)/shard_map/ppermute | solution.py:71
  182.5 6.0 %collective-permute-done.12 = bf16[224,256]{1,0:T(8,128)(2,1)S(1)} collective-permute-done((bf16[224,256]{1,0:T(8,128)(2,1)S(1)}, bf16[224,256]{1,0:T(8,128)(2,1)S(1)}, u32[]{:S(2)}, u32[]{:S(2)}) %collective-permute-start.12) | collective-permute-done | bytes 114720 | tf_op jit(solution)/shard_map/ppermute | solution.py:82
  188.7 6.0 %collective-permute-done.13 = bf16[2,224,256]{2,1,0:T(8,128)(2,1)S(1)} collective-permute-done((bf16[2,224,256]{2,1,0:T(8,128)(2,1)S(1)}, bf16[2,224,256]{2,1,0:T(8,128)(2,1)S(1)}, u32[]{:S(2)}, u32[]{:S(2)}) %collective-permute-start.13) | collective-permute-done | bytes 229408 | tf_op jit(solution)/shard_map/ppermute | solution.py:82
  198.2 5.2 %collective-permute-done.16 = f32[2]{0:T(128)S(1)} collective-permute-done((f32[2]{0:T(128)S(1)}, f32[2]{0:T(128)S(1)}, u32[]{:S(2)}, u32[]{:S(2)}) %collective-permute-start.16) | collective-permute-done | bytes 40 | tf_op jit(solution)/shard_map/ppermute | solution.py:45
  206.6 6.7 %fusion = f32[896,2048]{1,0:T(8,128)} fusion(bf16[256,2048]{1,0:T(8,128)(2,1)} %collective-permute-done.15, bf16[256,2048]{1,0:T(8,128)(2,1)S(1)} %copy-done.3, pred[]{:T(512)S(6)} %eq.30, bf16[896,256]{1,0:T(8,128)(2,1)S(1)} %collective-permute-done.14, bf16[896,256]{1,0:T(8,128)(2,1)S(1)} %bitcast.76), kind=kOutput, calls=%fused_computation.5 | convolution fusion | flops 1892614144 | bytes 10354689 | tf_op jit(solution)/shard_map/dot_general | solution.py:181
  (66 shorter events, 27.1 us)
Async XLA Ops:
  7.2 65.7 %all-gather.2.cloned.1.call-start = ((), (), s32[]{:S(2)}) async-start(), calls=%async_computation | async-start | bytes 2293760 | tf_op jit(solution)/shard_map/all_gather | solution.py:105
  7.2 97.4 %collective-permute-start = (bf16[1216,1792]{1,0:T(8,128)(2,1)}, bf16[1216,1792]{1,0:T(8,128)(2,1)}, u32[]{:S(2)}, u32[]{:S(2)}) collective-permute-start(bf16[1216,1792]{1,0:T(8,128)(2,1)} %param.7), channel_id=1, source_target_pairs={{0,16},{16,0},{1,17},{17,1},{2,18},{18,2},{3,19},{19,3},{4,20},{20... | collective-permute-start | bytes 13074440 | tf_op jit(solution)/shard_map/ppermute | solution.py:11
  13.9 39.7 %copy-start.1 = (s32[256]{0:T(256)S(1)}, s32[256]{0:T(256)}, u32[]{:S(2)}) copy-start(s32[256]{0:T(256)} %param.8) | copy-start | bytes 3076
  72.8 31.8 %copy-start.2 = (bf16[256,3584]{1,0:T(8,128)(2,1)S(1)}, bf16[256,3584]{1,0:T(8,128)(2,1)}, u32[]{:S(2)}) copy-start(bf16[256,3584]{1,0:T(8,128)(2,1)} %all-gather.2.cloned.1.call-done) | copy-start | bytes 5505028
  76.8 43.4 %copy-start = (s32[256]{0:T(256)S(1)}, s32[256]{0:T(256)}, u32[]{:S(2)}) copy-start(s32[256]{0:T(256)} %param.9) | copy-start | bytes 3076
  108.6 1.2 collective-permute-start.1
  109.9 3.7 %collective-permute-start.2 = (f32[3,256]{1,0:T(4,128)S(1)}, f32[3,256]{1,0:T(4,128)S(1)}, u32[]{:S(2)}, u32[]{:S(2)}) collective-permute-start(f32[3,256]{1,0:T(4,128)S(1)} %pad_maximum_fusion.2), channel_id=1, source_target_pairs={{0,8},{4,12},{8,0},{12,4},{1,9},{5,13},{9,1},{13,5},{2,10},{6,14},... | collective-permute-start | bytes 9224 | tf_op jit(solution)/shard_map/ppermute | solution.py:33
  113.6 3.7 %collective-permute-start.3 = (f32[3,256]{1,0:T(4,128)S(1)}, f32[3,256]{1,0:T(4,128)S(1)}, u32[]{:S(2)}, u32[]{:S(2)}) collective-permute-start(f32[3,256]{1,0:T(4,128)S(1)} %pad_maximum_fusion.3), channel_id=1, source_target_pairs={{0,1},{1,0},{2,3},{3,2},{4,5},{5,4},{6,7},{7,6},{8,9},{9,8},{10,11... | collective-permute-start | bytes 9224 | tf_op jit(solution)/shard_map/ppermute | solution.py:33
  117.3 4.6 %collective-permute-start.4 = (f32[3,256]{1,0:T(4,128)S(1)}, f32[3,256]{1,0:T(4,128)S(1)}, u32[]{:S(2)}, u32[]{:S(2)}) collective-permute-start(f32[3,256]{1,0:T(4,128)S(1)} %pad_maximum_fusion.4), channel_id=1, source_target_pairs={{0,2},{1,3},{2,0},{3,1},{4,6},{5,7},{6,4},{7,5},{8,10},{9,11},{10,... | collective-permute-start | bytes 9224 | tf_op jit(solution)/shard_map/ppermute | solution.py:33
  140.1 4.0 %collective-permute-start.5 = (f32[2,2,2,224,256]{4,3,2,1,0:T(8,128)}, f32[2,2,2,224,256]{4,3,2,1,0:T(8,128)S(1)}, u32[]{:S(2)}, u32[]{:S(2)}) collective-permute-start(f32[2,2,2,224,256]{4,3,2,1,0:T(8,128)} %dynamic-slice_bitcast_fusion), channel_id=1, source_target_pairs={{0,4},{4,0},{8,12},{12,8},{1,5},{5,1},{9,13},{13,9},{2,6},{6,2},{1... | collective-permute-start | bytes 5505032 | tf_op jit(solution)/shard_map/ppermute | solution.py:71
  146.1 12.7 %collective-permute-start.9 = (f32[2,2,224,128]{3,2,1,0:T(8,128)S(1)}, f32[2,2,224,128]{3,2,1,0:T(8,128)S(1)}, u32[]{:S(2)}, u32[]{:S(2)}) collective-permute-start(f32[2,2,224,128]{3,2,1,0:T(8,128)S(1)} %dynamic-slice_bitcast_fusion.1), channel_id=1, source_target_pairs={{0,1},{1,0},{2,3},{3,2},{4,5},{5,4},{6,7},{7,6},{8,9},{9,8},{10,11... | collective-permute-start | bytes 1376264 | tf_op jit(solution)/shard_map/ppermute | solution.py:71
  148.0 13.7 %collective-permute-start.6 = (f32[2,2,224,128]{3,2,1,0:T(8,128)S(1)}, f32[2,2,224,128]{3,2,1,0:T(8,128)}, u32[]{:S(2)}, u32[]{:S(2)}) collective-permute-start(f32[2,2,224,128]{3,2,1,0:T(8,128)S(1)} %dynamic-slice_bitcast_fusion.2), channel_id=1, source_target_pairs={{0,8},{4,12},{8,0},{12,4},{1,9},{5,13},{9,1},{13,5},{2,10},{6,14},... | collective-permute-start | bytes 1376264 | tf_op jit(solution)/shard_map/ppermute | solution.py:71
  149.6 57.0 %collective-permute-start.15 = (bf16[256,2048]{1,0:T(8,128)(2,1)}, bf16[256,2048]{1,0:T(8,128)(2,1)}, u32[]{:S(2)}, u32[]{:S(2)}) collective-permute-start(bf16[256,2048]{1,0:T(8,128)(2,1)} %param.5), channel_id=1, source_target_pairs={{0,16},{16,0},{1,17},{17,1},{2,18},{18,2},{3,19},{19,3},{4,20},{20... | collective-permute-start | bytes 3145736 | tf_op jit(solution)/shard_map/ppermute | solution.py:99
  158.9 13.0 %collective-permute-start.10 = (f32[2,224,128]{2,1,0:T(8,128)S(1)}, f32[2,224,128]{2,1,0:T(8,128)S(1)}, u32[]{:S(2)}, u32[]{:S(2)}) collective-permute-start(f32[2,224,128]{2,1,0:T(8,128)S(1)} %dynamic-slice_bitcast_fusion.3), channel_id=1, source_target_pairs={{0,2},{1,3},{2,0},{3,1},{4,6},{5,7},{6,4},{7,5},{8,10},{9,11},{10,... | collective-permute-start | bytes 688136 | tf_op jit(solution)/shard_map/ppermute | solution.py:71
  162.8 10.8 %collective-permute-start.7 = (f32[2,224,128]{2,1,0:T(8,128)S(1)}, f32[2,224,128]{2,1,0:T(8,128)S(1)}, u32[]{:S(2)}, u32[]{:S(2)}) collective-permute-start(f32[2,224,128]{2,1,0:T(8,128)S(1)} %dynamic-slice_bitcast_fusion.4), channel_id=1, source_target_pairs={{0,1},{1,0},{2,3},{3,2},{4,5},{5,4},{6,7},{7,6},{8,9},{9,8},{10,11... | collective-permute-start | bytes 688136 | tf_op jit(solution)/shard_map/ppermute | solution.py:71
  171.9 4.9 %collective-permute-start.11 = (f32[224,128]{1,0:T(8,128)S(1)}, f32[224,128]{1,0:T(8,128)S(1)}, u32[]{:S(2)}, u32[]{:S(2)}) collective-permute-start(f32[224,128]{1,0:T(8,128)S(1)} %dynamic-slice_bitcast_fusion.5), channel_id=1, source_target_pairs={{0,8},{4,12},{8,0},{12,4},{1,9},{5,13},{9,1},{13,5},{2,10},{6,14},... | collective-permute-start | bytes 344072 | tf_op jit(solution)/shard_map/ppermute | solution.py:71
  173.6 8.7 %collective-permute-start.8 = (f32[224,128]{1,0:T(8,128)S(1)}, f32[224,128]{1,0:T(8,128)S(1)}, u32[]{:S(2)}, u32[]{:S(2)}) collective-permute-start(f32[224,128]{1,0:T(8,128)S(1)} %dynamic-slice_bitcast_fusion.6), channel_id=1, source_target_pairs={{0,2},{1,3},{2,0},{3,1},{4,6},{5,7},{6,4},{7,5},{8,10},{9,11},{10,... | collective-permute-start | bytes 344072 | tf_op jit(solution)/shard_map/ppermute | solution.py:71
  176.8 29.8 %copy-start.3 = (bf16[256,2048]{1,0:T(8,128)(2,1)S(1)}, bf16[256,2048]{1,0:T(8,128)(2,1)}, u32[]{:S(2)}) copy-start(bf16[256,2048]{1,0:T(8,128)(2,1)} %param.5) | copy-start | bytes 3145732
  182.4 6.1 %collective-permute-start.12 = (bf16[224,256]{1,0:T(8,128)(2,1)S(1)}, bf16[224,256]{1,0:T(8,128)(2,1)S(1)}, u32[]{:S(2)}, u32[]{:S(2)}) collective-permute-start(bf16[224,256]{1,0:T(8,128)(2,1)S(1)} %pad_maximum_fusion), channel_id=1, source_target_pairs={{0,2},{1,3},{2,0},{3,1},{4,6},{5,7},{6,4},{7,5},{8,10},{9,11},{10,... | collective-permute-start | bytes 344072 | tf_op jit(solution)/shard_map/ppermute | solution.py:82
  188.5 6.1 %collective-permute-start.13 = (bf16[2,224,256]{2,1,0:T(8,128)(2,1)S(1)}, bf16[2,224,256]{2,1,0:T(8,128)(2,1)S(1)}, u32[]{:S(2)}, u32[]{:S(2)}) collective-permute-start(bf16[2,224,256]{2,1,0:T(8,128)(2,1)S(1)} %maximum_select_fusion.7), channel_id=1, source_target_pairs={{0,1},{1,0},{2,3},{3,2},{4,5},{5,4},{6,7},{7,6},{8,9},{9,8},{10,11... | collective-permute-start | bytes 688136 | tf_op jit(solution)/shard_map/ppermute | solution.py:82
  194.7 11.9 %collective-permute-start.14 = (bf16[896,256]{1,0:T(8,128)(2,1)S(1)}, bf16[896,256]{1,0:T(8,128)(2,1)S(1)}, u32[]{:S(2)}, u32[]{:S(2)}) collective-permute-start(bf16[896,256]{1,0:T(8,128)(2,1)S(1)} %bitcast.75), channel_id=1, source_target_pairs={{0,16},{16,0},{1,17},{17,1},{2,18},{18,2},{3,19},{19,3},{4,20},{20... | collective-permute-start | bytes 1376264 | tf_op jit(solution)/shard_map/ppermute | solution.py:169
  197.6 5.7 %collective-permute-start.16 = (f32[2]{0:T(128)S(1)}, f32[2]{0:T(128)S(1)}, u32[]{:S(2)}, u32[]{:S(2)}) collective-permute-start(f32[2]{0:T(128)S(1)} %pad_maximum_fusion.5), channel_id=1, source_target_pairs={{0,16},{16,0},{1,17},{17,1},{2,18},{18,2},{3,19},{19,3},{4,20},{20... | collective-permute-start | bytes 32 | tf_op jit(solution)/shard_map/ppermute | solution.py:45
Sparse Core Ops, SparseCore 0:
  53.6 19.1 all-gather.1

commit v5 on v4

--- a/solution.py
+++ b/solution.py
@@ -60,12 +60,12 @@
     return out
 
 
-def halving_steps(x, dims, order):
+def halving_steps(x, dims, order, bits=None):
     dims = list(dims)
     for ax, b in order:
         pos = dims.index((ax, b))
         n = lax.axis_size(ax)
-        bit = (lax.axis_index(ax) // b) % 2
+        bit = (lax.axis_index(ax) // b) % 2 if bits is None else bits[(ax, b)]
         keep = lax.dynamic_index_in_dim(x, bit, axis=pos, keepdims=False)
         send = lax.dynamic_index_in_dim(x, 1 - bit, axis=pos, keepdims=False)
         x = keep + lax.ppermute(send, ax, [(k, k ^ b) for k in range(n)])
@@ -132,40 +132,78 @@
         weight[:, None] * (jnp.exp(logits - log_total[:, None]) - is_target.astype(jnp.float32))
     ).astype(jnp.bfloat16)
 
-    parts = []
-    for k, piece in enumerate(table_pieces):
-        parts.append(
-            lax.dot_general(piece, dlogits, (((0,), (1,)), ((), ())), preferred_element_type=jnp.float32)
-        )
-    if n_tok == 2:
-        full_rows = jnp.where(
-            t == 0, jnp.concatenate(parts, axis=0), jnp.concatenate(parts[::-1], axis=0)
-        )
+    n_voc, n_wid = lax.axis_size("voc"), lax.axis_size("wid")
+    grad_rows_pos = None
+    if (
+        n_tok == 2
+        and n_voc >= 2
+        and is_pow2(n_voc)
+        and is_pow2(n_wid)
+        and tok_rows % (2 * n_wid) == 0
+        and d_cols % (n_voc // 2) == 0
+    ):
+        per_piece = n_voc // 2
+        q_cols = d_cols // per_piece
+        stacked = jnp.stack(
+            [
+                jnp.stack(
+                    [
+                        jnp.dot(dlogits, piece[:, i * q_cols : (i + 1) * q_cols], preferred_element_type=jnp.float32)
+                        for i in range(per_piece)
+                    ]
+                )
+                for piece in table_pieces
+            ]
+        )
+        voc_bits = bit_list("voc", n_voc)
+        wid_bits = bit_list("wid", n_wid)
+        v = lax.axis_index("voc")
+        bits = {key: (v // key[1]) % 2 for key in voc_bits}
+        bits[voc_bits[-1]] = ((v // per_piece) % 2) ^ t
+        for key in wid_bits:
+            bits[key] = (lax.axis_index("wid") // key[1]) % 2
+        dims = [voc_bits[-1]] + voc_bits[:-1][::-1] + wid_bits[::-1]
+        blocks = stacked.reshape(tuple(2 for _ in dims) + (tok_rows // n_wid, q_cols))
+        first = voc_bits[0]
+        blocks = halving_steps(blocks, dims, [first], bits)
+        dims = [d for d in dims if d != first]
+        half = tok_rows // n_wid // 2
+        rest_voc = voc_bits[1:]
+        part_a = halving_steps(blocks[..., :half, :], dims, rest_voc + wid_bits, bits)
+        part_b = halving_steps(blocks[..., half:, :], dims, wid_bits + rest_voc, bits)
+        mine = jnp.concatenate([part_a, part_b], axis=0).astype(jnp.bfloat16)
+        grad_rows_pos = doubling_gather(mine, "wid").reshape((tok_rows, q_cols))
     else:
+        parts = []
+        for k, piece in enumerate(table_pieces):
+            parts.append(
+                lax.dot_general(piece, dlogits, (((0,), (1,)), ((), ())), preferred_element_type=jnp.float32)
+            )
         full_rows = jnp.zeros((d_cols * n_tok, tok_rows), jnp.float32)
         for k, part in enumerate(parts):
             full_rows = lax.dynamic_update_slice_in_dim(
                 full_rows, part, ((t - k) % n_tok) * d_cols, axis=0
             )
-    n_voc, n_wid = lax.axis_size("voc"), lax.axis_size("wid")
-    if is_pow2(n_voc) and is_pow2(n_wid) and n_voc > 1 and tok_rows % 2 == 0:
-        voc_bits = bit_list("voc", n_voc)
-        wid_bits = bit_list("wid", n_wid)
-        dims = voc_bits[::-1] + wid_bits[::-1]
-        blocks = full_rows.reshape(tuple(2 for _ in dims) + (-1, tok_rows))
-        first = voc_bits[0]
-        blocks = halving_steps(blocks, dims, [first])
-        dims = [d for d in dims if d != first]
-        half = tok_rows // 2
-        part_a = halving_steps(blocks[..., :half], dims, voc_bits[1:] + wid_bits)
-        part_b = halving_steps(blocks[..., half:], dims, wid_bits + voc_bits[1:])
-        mine = jnp.concatenate([part_a, part_b], axis=-1).astype(jnp.bfloat16)
-        grad_rows_t = doubling_gather(mine, "wid").reshape((-1, tok_rows))
-    else:
         reduced = lax.psum_scatter(full_rows, "voc", scatter_dimension=0, tiled=True)
         grad_rows_t = lax.psum(reduced, "wid").astype(jnp.bfloat16)
 
-    if n_tok == 2:
+    if grad_rows_pos is not None:
+        grad_other = lax.ppermute(grad_rows_pos, "tok", [(0, 1), (1, 0)])
+        first = t == 0
+        grad_all = jnp.where(
+            first,
+            jnp.concatenate([grad_rows_pos, grad_other], axis=0),
+            jnp.concatenate([grad_other, grad_rows_pos], axis=0),
+        )
+        hidden_all = jnp.where(
+            first,
+            jnp.concatenate([hidden, hidden_other], axis=0),
+            jnp.concatenate([hidden_other, hidden], axis=0),
+        )
+        grad_proj = lax.dot_general(
+            grad_all, hidden_all, (((0,), (0,)), ((), ())), preferred_element_type=jnp.float32
+        )
+    elif n_tok == 2:
         grad_other = lax.ppermute(grad_rows_t, "tok", [(0, 1), (1, 0)])
         first = t == 0
         grad_all = jnp.where(

time: 223 us -> 219 us (0.982)
  local copies, waits for them, and re-layouts: 8.95 us -> 4.12 us
  matrix products: 25.3 us -> 28 us
    select_n x2 -> x0, local copies, waits for them, and re-layouts: 5.14 us -> none  [the longest x1 5.11 us: on_device(): jnp.where(t == 0, jnp.concatenate(parts, axis=0), jnp.concatenate(parts[:...]
    dot_general x3 -> x5, matrix products: 14 us -> 16.8 us  [the longest x4 9.95 us: on_device(): jnp.dot(dlogits, piece[:, i * q_cols:(i + 1) * q_cols], preferred_element...]
    select_n x1 -> x0, other arithmetic: 2.29 us -> none  [on_device(): jnp.where(t == 0, jnp.concatenate(parts, axis=0), jnp.concatenate(parts[:...]
where the time goes in v5:
time: 219 us; the launch traced here: 218 us
  waiting for transfers between devices  98.1 us (45%)
  blocking collectives  39.6 us (18%)
  matrix products  28 us (13%)
  starting transfers between devices  23.3 us (11%)
  between operations  16.9 us (8%)
  other arithmetic  7.57 us (3%)
  local copies, waits for them, and re-layouts  4.12 us (2%)
    psum x1, blocking collectives, on_device(): summed = lax.psum(partial_value, 'wid')  39.6 us
    ppermute x1, waiting for transfers between devices, tok_pieces(): pieces.append(lax.ppermute(x, 'tok', perm))  27.8 us
    ppermute x7, waiting for transfers between devices, halving_steps(): x = keep + lax.ppermute(send, ax, [(k, k ^ b) for k in range(n)])  27.6 us
    all_gather x1, waiting for transfers between devices, on_device(): lax.all_gather(summed.astype(jnp.bfloat16), 'voc', axis=1, tiled=True)  19.3 us
    ppermute x2, waiting for transfers between devices, doubling_gather(): other = lax.ppermute(x, ax, [(k, k ^ b) for k in range(n)])  11.9 us
    dot_general x4, matrix products, on_device(): jnp.dot(dlogits, piece[:, i * q_cols:(i + 1) * q_cols], preferred_element...  9.95 us
    ppermute x7, starting transfers between devices, halving_steps(): x = keep + lax.ppermute(send, ax, [(k, k ^ b) for k in range(n)])  9.87 us
    dot_general x2, matrix products, on_device(): lax.dot_general(cols, piece, (((1,), (1,)), ((), ())), preferred_element_...  7.64 us
  transfers between devices with their start and end apart: 18, of which 14 were waited for; matrix products, arithmetic and copies ran while one was open for 6% of the time, Pallas kernels for 0%

profile of v5, /device:TPU:0, one launch (start us, length us, event | category | flops | bytes accessed | tf_op | source)
XLA Modules:
  0.0 217.7 jit_solution(6896587793180092605)
XLA Ops:
  7.2 3.0 %collective-permute-start = (bf16[1216,1792]{1,0:T(8,128)(2,1)}, bf16[1216,1792]{1,0:T(8,128)(2,1)}, u32[]{:S(2)}, u32[]{:S(2)}) collective-permute-start(bf16[1216,1792]{1,0:T(8,128)(2,1)} %param.7), channel_id=1, source_target_pairs={{0,16},{16,0},{1,17},{17,1},{2,18},{18,2},{3,19},{19,3},{4,20},{20... | collective-permute-start | bytes 13074440 | tf_op jit(solution)/shard_map/ppermute | solution.py:11
  10.2 3.6 %fusion.41 = f32[256,896]{1,0:T(8,128)S(1)} fusion(bf16[256,2048]{1,0:T(8,128)(2,1)} %param.5, bf16[896,2048]{1,0:T(8,128)(2,1)} %param.6), kind=kOutput, calls=%fused_computation.90 | convolution fusion | flops 939524096 | bytes 5636096 | tf_op jit(solution)/shard_map/dot_general | solution.py:101
  13.9 39.6 %all-reduce.1 = bf16[256,896]{1,0:T(8,128)(2,1)} all-reduce(f32[256,896]{1,0:T(8,128)S(1)} %fusion.41), channel_id=1, replica_groups=mesh['tok'=2,'voc'=4,'wid'=4] {'wid'}, use_global_device_ids=true, to_apply=%region_0.0 | all-reduce | flops 229376 | bytes 1376256 | tf_op jit(solution)/shard_map/psum | solution.py:104
  53.5 19.3 %all-gather.2.cloned.1.call-done = bf16[256,3584]{1,0:T(8,128)(2,1)} async-done(((bf16[256,896]{1,0:T(8,128)(2,1)}), bf16[256,3584]{1,0:T(8,128)(2,1)}) %all-gather.2.cloned.1.call-update) | async-done | bytes 1835024 | tf_op jit(solution)/shard_map/all_gather | solution.py:105
  72.8 4.0 %fusion.21 = f32[256,1216]{0,1:T(8,128)S(1)} fusion(bf16[1216,1792]{1,0:T(8,128)(2,1)} %param.7, bf16[256,3584]{1,0:T(8,128)(2,1)} %all-gather.2.cloned.1.call-done, s32[]{:T(128)S(6)} %select_n.141), kind=kOutput, calls=%fused_computation.31 | convolution fusion | flops 1115684864 | bytes 6520836 | tf_op jit(solution)/shard_map/dot_general | solution.py:110
  76.8 27.8 %collective-permute-done = bf16[1216,1792]{1,0:T(8,128)(2,1)} collective-permute-done((bf16[1216,1792]{1,0:T(8,128)(2,1)}, bf16[1216,1792]{1,0:T(8,128)(2,1)}, u32[]{:S(2)}, u32[]{:S(2)}) %collective-permute-start) | collective-permute-done | bytes 4358176 | tf_op jit(solution)/shard_map/ppermute | solution.py:11
  104.6 3.6 %fusion.40 = (f32[256]{0:T(256)S(1)}, f32[256,1216]{0,1:T(8,128)S(1)}) fusion(f32[256,1216]{0,1:T(8,128)S(1)} %fusion.21, bf16[1216,1792]{1,0:T(8,128)(2,1)} %collective-permute-done, bf16[256,3584]{1,0:T(8,128)(2,1)S(1)} %copy-done.3, s32[]{:T(128)S(6)} %select_n.143), kind=kOutput, calls=%fused_computation.89 | convolution fusion | flops 1116307200 | bytes 7767044 | tf_op jit(solution)/shard_map/dot_general | solution.py:110
  113.6 1.9 collective-permute-start.3
  117.3 2.9 %collective-permute-start.4 = (f32[3,256]{1,0:T(4,128)S(1)}, f32[3,256]{1,0:T(4,128)S(1)}, u32[]{:S(2)}, u32[]{:S(2)}) collective-permute-start(f32[3,256]{1,0:T(4,128)S(1)} %pad_maximum_fusion.4), channel_id=1, source_target_pairs={{0,2},{1,3},{2,0},{3,1},{4,6},{5,7},{6,4},{7,5},{8,10},{9,11},{10,... | collective-permute-start | bytes 9224 | tf_op jit(solution)/shard_map/ppermute | solution.py:33
  122.9 2.5 %fusion.4 = f32[256,896]{1,0:T(8,128)S(1)} fusion(bf16[256,1216]{0,1:T(8,128)(2,1)S(1)} %multiply_convert_fusion, bf16[1216,1792]{1,0:T(8,128)(2,1)} %param.7), kind=kOutput, calls=%fused_computation.6 | convolution fusion | flops 557842432 | bytes 3719168 | tf_op jit(solution)/shard_map/dot_general | solution.py:151
  125.4 2.5 %fusion.6 = f32[256,896]{1,0:T(8,128)S(1)} fusion(bf16[256,1216]{0,1:T(8,128)(2,1)S(1)} %multiply_convert_fusion, bf16[1216,1792]{1,0:T(8,128)(2,1)} %param.7), kind=kOutput, calls=%fused_computation.8 | convolution fusion | flops 557842432 | bytes 3719168 | tf_op jit(solution)/shard_map/dot_general | solution.py:151
  127.9 2.5 %fusion = f32[256,896]{1,0:T(8,128)S(1)} fusion(bf16[256,1216]{0,1:T(8,128)(2,1)S(1)} %multiply_convert_fusion, bf16[1216,1792]{1,0:T(8,128)(2,1)} %collective-permute-done), kind=kOutput, calls=%fused_computation.2 | convolution fusion | flops 557842432 | bytes 3719168 | tf_op jit(solution)/shard_map/dot_general | solution.py:151
  130.4 2.5 %fusion.2 = f32[256,896]{1,0:T(8,128)S(1)} fusion(bf16[256,1216]{0,1:T(8,128)(2,1)S(1)} %multiply_convert_fusion, bf16[1216,1792]{1,0:T(8,128)(2,1)} %collective-permute-done), kind=kOutput, calls=%fused_computation.4 | convolution fusion | flops 557842432 | bytes 3719168 | tf_op jit(solution)/shard_map/dot_general | solution.py:151
  136.5 4.0 %collective-permute-done.5 = f32[2,2,2,64,896]{4,3,2,1,0:T(8,128)S(1)} collective-permute-done((f32[2,2,2,64,896]{4,3,2,1,0:T(8,128)}, f32[2,2,2,64,896]{4,3,2,1,0:T(8,128)S(1)}, u32[]{:S(2)}, u32[]{:S(2)}) %collective-permute-start.5) | collective-permute-done | bytes 1835040 | tf_op jit(solution)/shard_map/ppermute | solution.py:71
  142.4 1.9 collective-permute-start.9
  147.4 7.7 %collective-permute-done.9 = f32[2,2,32,896]{3,2,1,0:T(8,128)S(1)} collective-permute-done((f32[2,2,32,896]{3,2,1,0:T(8,128)S(1)}, f32[2,2,32,896]{3,2,1,0:T(8,128)S(1)}, u32[]{:S(2)}, u32[]{:S(2)}) %collective-permute-start.9) | collective-permute-done | bytes 458784 | tf_op jit(solution)/shard_map/ppermute | solution.py:71
  155.2 2.8 %collective-permute-start.10 = (f32[2,32,896]{2,1,0:T(8,128)S(1)}, f32[2,32,896]{2,1,0:T(8,128)S(1)}, u32[]{:S(2)}, u32[]{:S(2)}) collective-permute-start(f32[2,32,896]{2,1,0:T(8,128)S(1)} %dynamic-slice_bitcast_fusion.3), channel_id=1, source_target_pairs={{0,2},{1,3},{2,0},{3,1},{4,6},{5,7},{6,4},{7,5},{8,10},{9,11},{10,... | collective-permute-start | bytes 688136 | tf_op jit(solution)/shard_map/ppermute | solution.py:71
  160.7 7.5 %collective-permute-done.10 = f32[2,32,896]{2,1,0:T(8,128)S(1)} collective-permute-done((f32[2,32,896]{2,1,0:T(8,128)S(1)}, f32[2,32,896]{2,1,0:T(8,128)S(1)}, u32[]{:S(2)}, u32[]{:S(2)}) %collective-permute-start.10) | collective-permute-done | bytes 229408 | tf_op jit(solution)/shard_map/ppermute | solution.py:71
  170.3 2.8 %collective-permute-done.11 = f32[32,896]{1,0:T(8,128)S(1)} collective-permute-done((f32[32,896]{1,0:T(8,128)S(1)}, f32[32,896]{1,0:T(8,128)S(1)}, u32[]{:S(2)}, u32[]{:S(2)}) %collective-permute-start.11) | collective-permute-done | bytes 114720 | tf_op jit(solution)/shard_map/ppermute | solution.py:71
  173.1 5.6 %collective-permute-done.8 = f32[32,896]{1,0:T(8,128)S(1)} collective-permute-done((f32[32,896]{1,0:T(8,128)S(1)}, f32[32,896]{1,0:T(8,128)S(1)}, u32[]{:S(2)}, u32[]{:S(2)}) %collective-permute-start.8) | collective-permute-done | bytes 114720 | tf_op jit(solution)/shard_map/ppermute | solution.py:71
  178.8 5.9 %collective-permute-done.12 = bf16[64,896]{1,0:T(8,128)(2,1)S(1)} collective-permute-done((bf16[64,896]{1,0:T(8,128)(2,1)S(1)}, bf16[64,896]{1,0:T(8,128)(2,1)S(1)}, u32[]{:S(2)}, u32[]{:S(2)}) %collective-permute-start.12) | collective-permute-done | bytes 114720 | tf_op jit(solution)/shard_map/ppermute | solution.py:82
  184.9 5.9 %collective-permute-done.13 = bf16[2,64,896]{2,1,0:T(8,128)(2,1)S(1)} collective-permute-done((bf16[2,64,896]{2,1,0:T(8,128)(2,1)S(1)}, bf16[2,64,896]{2,1,0:T(8,128)(2,1)S(1)}, u32[]{:S(2)}, u32[]{:S(2)}) %collective-permute-start.13) | collective-permute-done | bytes 229408 | tf_op jit(solution)/shard_map/ppermute | solution.py:82
  194.4 5.2 %collective-permute-done.16 = f32[2]{0:T(128)S(1)} collective-permute-done((f32[2]{0:T(128)S(1)}, f32[2]{0:T(128)S(1)}, u32[]{:S(2)}, u32[]{:S(2)}) %collective-permute-start.16) | collective-permute-done | bytes 40 | tf_op jit(solution)/shard_map/ppermute | solution.py:45
  202.9 6.8 %fusion.8 = f32[896,2048]{1,0:T(8,128)} fusion(bf16[256,2048]{1,0:T(8,128)(2,1)} %collective-permute-done.15, bf16[256,2048]{1,0:T(8,128)(2,1)S(1)} %copy-done.4, pred[]{:T(512)S(6)} %eq.26, bf16[256,896]{1,0:T(8,128)(2,1)S(1)} %collective-permute-done.14, bf16[256,896]{1,0:T(8,128)(2,1)S(1)} %bitcast.79), kind=kOutput, calls=%fused_computation.11 | convolution fusion | flops 1892614144 | bytes 10354689 | tf_op jit(solution)/shard_map/dot_general | solution.py:203
  (69 shorter events, 29.0 us)
Async XLA Ops:
  7.2 46.4 %copy-start.2 = (s32[256]{0:T(256)S(1)}, s32[256]{0:T(256)}, u32[]{:S(2)}) copy-start(s32[256]{0:T(256)} %param.8) | copy-start | bytes 3076
  7.2 65.6 %all-gather.2.cloned.1.call-start = ((), (), s32[]{:S(2)}) async-start(), calls=%async_computation | async-start | bytes 2293760 | tf_op jit(solution)/shard_map/all_gather | solution.py:105
  7.2 97.4 %collective-permute-start = (bf16[1216,1792]{1,0:T(8,128)(2,1)}, bf16[1216,1792]{1,0:T(8,128)(2,1)}, u32[]{:S(2)}, u32[]{:S(2)}) collective-permute-start(bf16[1216,1792]{1,0:T(8,128)(2,1)} %param.7), channel_id=1, source_target_pairs={{0,16},{16,0},{1,17},{17,1},{2,18},{18,2},{3,19},{19,3},{4,20},{20... | collective-permute-start | bytes 13074440 | tf_op jit(solution)/shard_map/ppermute | solution.py:11
  72.8 31.8 %copy-start.3 = (bf16[256,3584]{1,0:T(8,128)(2,1)S(1)}, bf16[256,3584]{1,0:T(8,128)(2,1)}, u32[]{:S(2)}) copy-start(bf16[256,3584]{1,0:T(8,128)(2,1)} %all-gather.2.cloned.1.call-done) | copy-start | bytes 5505028
  76.8 43.4 %copy-start.1 = (s32[256]{0:T(256)S(1)}, s32[256]{0:T(256)}, u32[]{:S(2)}) copy-start(s32[256]{0:T(256)} %param.9) | copy-start | bytes 3076
  108.6 1.2 collective-permute-start.1
  109.9 3.7 %collective-permute-start.2 = (f32[3,256]{1,0:T(4,128)S(1)}, f32[3,256]{1,0:T(4,128)S(1)}, u32[]{:S(2)}, u32[]{:S(2)}) collective-permute-start(f32[3,256]{1,0:T(4,128)S(1)} %pad_maximum_fusion.2), channel_id=1, source_target_pairs={{0,8},{4,12},{8,0},{12,4},{1,9},{5,13},{9,1},{13,5},{2,10},{6,14},... | collective-permute-start | bytes 9224 | tf_op jit(solution)/shard_map/ppermute | solution.py:33
  113.6 3.7 %collective-permute-start.3 = (f32[3,256]{1,0:T(4,128)S(1)}, f32[3,256]{1,0:T(4,128)S(1)}, u32[]{:S(2)}, u32[]{:S(2)}) collective-permute-start(f32[3,256]{1,0:T(4,128)S(1)} %pad_maximum_fusion.3), channel_id=1, source_target_pairs={{0,1},{1,0},{2,3},{3,2},{4,5},{5,4},{6,7},{7,6},{8,9},{9,8},{10,11... | collective-permute-start | bytes 9224 | tf_op jit(solution)/shard_map/ppermute | solution.py:33
  117.3 4.6 %collective-permute-start.4 = (f32[3,256]{1,0:T(4,128)S(1)}, f32[3,256]{1,0:T(4,128)S(1)}, u32[]{:S(2)}, u32[]{:S(2)}) collective-permute-start(f32[3,256]{1,0:T(4,128)S(1)} %pad_maximum_fusion.4), channel_id=1, source_target_pairs={{0,2},{1,3},{2,0},{3,1},{4,6},{5,7},{6,4},{7,5},{8,10},{9,11},{10,... | collective-permute-start | bytes 9224 | tf_op jit(solution)/shard_map/ppermute | solution.py:33
  133.3 1.8 copy-start
  136.5 4.0 %collective-permute-start.5 = (f32[2,2,2,64,896]{4,3,2,1,0:T(8,128)}, f32[2,2,2,64,896]{4,3,2,1,0:T(8,128)S(1)}, u32[]{:S(2)}, u32[]{:S(2)}) collective-permute-start(f32[2,2,2,64,896]{4,3,2,1,0:T(8,128)} %dynamic-slice_bitcast_fusion), channel_id=1, source_target_pairs={{0,4},{4,0},{8,12},{12,8},{1,5},{5,1},{9,13},{13,9},{2,6},{6,2},{1... | collective-permute-start | bytes 5505032 | tf_op jit(solution)/shard_map/ppermute | solution.py:71
  142.4 12.7 %collective-permute-start.9 = (f32[2,2,32,896]{3,2,1,0:T(8,128)S(1)}, f32[2,2,32,896]{3,2,1,0:T(8,128)S(1)}, u32[]{:S(2)}, u32[]{:S(2)}) collective-permute-start(f32[2,2,32,896]{3,2,1,0:T(8,128)S(1)} %dynamic-slice_bitcast_fusion.1), channel_id=1, source_target_pairs={{0,1},{1,0},{2,3},{3,2},{4,5},{5,4},{6,7},{7,6},{8,9},{9,8},{10,11... | collective-permute-start | bytes 1376264 | tf_op jit(solution)/shard_map/ppermute | solution.py:71
  144.3 13.7 %collective-permute-start.6 = (f32[2,2,32,896]{3,2,1,0:T(8,128)S(1)}, f32[2,2,32,896]{3,2,1,0:T(8,128)}, u32[]{:S(2)}, u32[]{:S(2)}) collective-permute-start(f32[2,2,32,896]{3,2,1,0:T(8,128)S(1)} %dynamic-slice_bitcast_fusion.2), channel_id=1, source_target_pairs={{0,8},{4,12},{8,0},{12,4},{1,9},{5,13},{9,1},{13,5},{2,10},{6,14},... | collective-permute-start | bytes 1376264 | tf_op jit(solution)/shard_map/ppermute | solution.py:71
  145.9 57.0 %collective-permute-start.15 = (bf16[256,2048]{1,0:T(8,128)(2,1)}, bf16[256,2048]{1,0:T(8,128)(2,1)}, u32[]{:S(2)}, u32[]{:S(2)}) collective-permute-start(bf16[256,2048]{1,0:T(8,128)(2,1)} %param.5), channel_id=1, source_target_pairs={{0,16},{16,0},{1,17},{17,1},{2,18},{18,2},{3,19},{19,3},{4,20},{20... | collective-permute-start | bytes 3145736 | tf_op jit(solution)/shard_map/ppermute | solution.py:99
  155.2 13.0 %collective-permute-start.10 = (f32[2,32,896]{2,1,0:T(8,128)S(1)}, f32[2,32,896]{2,1,0:T(8,128)S(1)}, u32[]{:S(2)}, u32[]{:S(2)}) collective-permute-start(f32[2,32,896]{2,1,0:T(8,128)S(1)} %dynamic-slice_bitcast_fusion.3), channel_id=1, source_target_pairs={{0,2},{1,3},{2,0},{3,1},{4,6},{5,7},{6,4},{7,5},{8,10},{9,11},{10,... | collective-permute-start | bytes 688136 | tf_op jit(solution)/shard_map/ppermute | solution.py:71
  159.1 10.8 %collective-permute-start.7 = (f32[2,32,896]{2,1,0:T(8,128)S(1)}, f32[2,32,896]{2,1,0:T(8,128)S(1)}, u32[]{:S(2)}, u32[]{:S(2)}) collective-permute-start(f32[2,32,896]{2,1,0:T(8,128)S(1)} %dynamic-slice_bitcast_fusion.4), channel_id=1, source_target_pairs={{0,1},{1,0},{2,3},{3,2},{4,5},{5,4},{6,7},{7,6},{8,9},{9,8},{10,11... | collective-permute-start | bytes 688136 | tf_op jit(solution)/shard_map/ppermute | solution.py:71
  168.2 34.6 %copy-start.4 = (bf16[256,2048]{1,0:T(8,128)(2,1)S(1)}, bf16[256,2048]{1,0:T(8,128)(2,1)}, u32[]{:S(2)}) copy-start(bf16[256,2048]{1,0:T(8,128)(2,1)} %param.5) | copy-start | bytes 3145732
  168.2 4.9 %collective-permute-start.11 = (f32[32,896]{1,0:T(8,128)S(1)}, f32[32,896]{1,0:T(8,128)S(1)}, u32[]{:S(2)}, u32[]{:S(2)}) collective-permute-start(f32[32,896]{1,0:T(8,128)S(1)} %dynamic-slice_bitcast_fusion.5), channel_id=1, source_target_pairs={{0,8},{4,12},{8,0},{12,4},{1,9},{5,13},{9,1},{13,5},{2,10},{6,14},... | collective-permute-start | bytes 344072 | tf_op jit(solution)/shard_map/ppermute | solution.py:71
  169.9 8.7 %collective-permute-start.8 = (f32[32,896]{1,0:T(8,128)S(1)}, f32[32,896]{1,0:T(8,128)S(1)}, u32[]{:S(2)}, u32[]{:S(2)}) collective-permute-start(f32[32,896]{1,0:T(8,128)S(1)} %dynamic-slice_bitcast_fusion.6), channel_id=1, source_target_pairs={{0,2},{1,3},{2,0},{3,1},{4,6},{5,7},{6,4},{7,5},{8,10},{9,11},{10,... | collective-permute-start | bytes 344072 | tf_op jit(solution)/shard_map/ppermute | solution.py:71
  178.7 6.0 %collective-permute-start.12 = (bf16[64,896]{1,0:T(8,128)(2,1)S(1)}, bf16[64,896]{1,0:T(8,128)(2,1)S(1)}, u32[]{:S(2)}, u32[]{:S(2)}) collective-permute-start(bf16[64,896]{1,0:T(8,128)(2,1)S(1)} %pad_maximum_fusion), channel_id=1, source_target_pairs={{0,2},{1,3},{2,0},{3,1},{4,6},{5,7},{6,4},{7,5},{8,10},{9,11},{10,... | collective-permute-start | bytes 344072 | tf_op jit(solution)/shard_map/ppermute | solution.py:82
  184.8 6.1 %collective-permute-start.13 = (bf16[2,64,896]{2,1,0:T(8,128)(2,1)S(1)}, bf16[2,64,896]{2,1,0:T(8,128)(2,1)S(1)}, u32[]{:S(2)}, u32[]{:S(2)}) collective-permute-start(bf16[2,64,896]{2,1,0:T(8,128)(2,1)S(1)} %maximum_select_fusion.6), channel_id=1, source_target_pairs={{0,1},{1,0},{2,3},{3,2},{4,5},{5,4},{6,7},{7,6},{8,9},{9,8},{10,11... | collective-permute-start | bytes 688136 | tf_op jit(solution)/shard_map/ppermute | solution.py:82
  190.9 11.9 %collective-permute-start.14 = (bf16[256,896]{1,0:T(8,128)(2,1)S(1)}, bf16[256,896]{1,0:T(8,128)(2,1)S(1)}, u32[]{:S(2)}, u32[]{:S(2)}) collective-permute-start(bf16[256,896]{1,0:T(8,128)(2,1)S(1)} %bitcast.78), channel_id=1, source_target_pairs={{0,16},{16,0},{1,17},{17,1},{2,18},{18,2},{3,19},{19,3},{4,20},{20... | collective-permute-start | bytes 1376264 | tf_op jit(solution)/shard_map/ppermute | solution.py:191
  193.9 5.7 %collective-permute-start.16 = (f32[2]{0:T(128)S(1)}, f32[2]{0:T(128)S(1)}, u32[]{:S(2)}, u32[]{:S(2)}) collective-permute-start(f32[2]{0:T(128)S(1)} %pad_maximum_fusion.5), channel_id=1, source_target_pairs={{0,16},{16,0},{1,17},{17,1},{2,18},{18,2},{3,19},{19,3},{4,20},{20... | collective-permute-start | bytes 32 | tf_op jit(solution)/shard_map/ppermute | solution.py:45
Sparse Core Ops, SparseCore 0:
  53.6 19.1 all-gather.1

commit v6 on v5

--- a/solution.py
+++ b/solution.py
@@ -134,16 +134,51 @@
 
     n_voc, n_wid = lax.axis_size("voc"), lax.axis_size("wid")
     grad_rows_pos = None
-    if (
+    grad_path = (
         n_tok == 2
         and n_voc >= 2
         and is_pow2(n_voc)
         and is_pow2(n_wid)
         and tok_rows % (2 * n_wid) == 0
         and d_cols % (n_voc // 2) == 0
-    ):
+    )
+    per_piece = 0
+    if grad_path:
         per_piece = n_voc // 2
         q_cols = d_cols // per_piece
+    if grad_path and per_piece == 2:
+        c = lax.axis_index("voc") % 2
+
+        def quarter_dots(sel):
+            return jnp.stack(
+                [
+                    jnp.dot(
+                        dlogits,
+                        lax.dynamic_slice_in_dim(piece, sel * q_cols, q_cols, axis=1),
+                        preferred_element_type=jnp.float32,
+                    )
+                    for piece in table_pieces
+                ]
+            )
+
+        sent = quarter_dots(1 - c)
+        received = lax.ppermute(sent, "voc", [(k, k ^ 1) for k in range(n_voc)])
+        blocks = quarter_dots(c) + received
+        voc_bits = bit_list("voc", n_voc)
+        wid_bits = bit_list("wid", n_wid)
+        v = lax.axis_index("voc")
+        bits = {voc_bits[-1]: ((v // per_piece) % 2) ^ t}
+        for key in wid_bits:
+            bits[key] = (lax.axis_index("wid") // key[1]) % 2
+        dims = [voc_bits[-1]] + wid_bits[::-1]
+        blocks = blocks.reshape(tuple(2 for _ in dims) + (tok_rows // n_wid, q_cols))
+        half = tok_rows // n_wid // 2
+        rest_voc = voc_bits[1:]
+        part_a = halving_steps(blocks[..., :half, :], dims, rest_voc + wid_bits, bits)
+        part_b = halving_steps(blocks[..., half:, :], dims, wid_bits + rest_voc, bits)
+        mine = jnp.concatenate([part_a, part_b], axis=0).astype(jnp.bfloat16)
+        grad_rows_pos = doubling_gather(mine, "wid").reshape((tok_rows, q_cols))
+    elif grad_path:
         stacked = jnp.stack(
             [
                 jnp.stack(

time: 219 us -> 212 us (0.968)
  waiting for transfers between devices: 98.1 us -> 94.8 us
  local copies, waits for them, and re-layouts: 4.12 us -> 0.89 us
    ppermute x7 -> x6, waiting for transfers between devices: 27.6 us -> 24.2 us  [halving_steps(): x = keep + lax.ppermute(send, ax, [(k, k ^ b) for k in range(n)])]
    ppermute x7 -> x6, starting transfers between devices: 9.87 us -> 9.89 us  [halving_steps(): x = keep + lax.ppermute(send, ax, [(k, k ^ b) for k in range(n)])]
  transfers between devices with their start and end apart: 18 -> 18, of which waited for: 14 -> 13; matrix products, arithmetic and copies ran while one was open for 6% -> 8% of each run, Pallas kernels for 0% -> 0%
where the time goes in v6:
time: 212 us; the launch traced here: 211 us
  waiting for transfers between devices  94.8 us (45%)
  blocking collectives  39.6 us (19%)
  matrix products  27.9 us (13%)
  starting transfers between devices  23.4 us (11%)
  between operations  16.9 us (8%)
  other arithmetic  7.42 us (4%)
    psum x1, blocking collectives, on_device(): summed = lax.psum(partial_value, 'wid')  39.6 us
    ppermute x1, waiting for transfers between devices, tok_pieces(): pieces.append(lax.ppermute(x, 'tok', perm))  27.8 us
    ppermute x6, waiting for transfers between devices, halving_steps(): x = keep + lax.ppermute(send, ax, [(k, k ^ b) for k in range(n)])  24.2 us
    all_gather x1, waiting for transfers between devices, on_device(): lax.all_gather(summed.astype(jnp.bfloat16), 'voc', axis=1, tiled=True)  19.3 us
    ppermute x2, waiting for transfers between devices, doubling_gather(): other = lax.ppermute(x, ax, [(k, k ^ b) for k in range(n)])  11.9 us
    dot_general x4, matrix products, quarter_dots(): jnp.dot(dlogits, lax.dynamic_slice_in_dim(piece, sel * q_cols, q_cols, ax...  9.96 us
    ppermute x6, starting transfers between devices, halving_steps(): x = keep + lax.ppermute(send, ax, [(k, k ^ b) for k in range(n)])  9.89 us
    dot_general x2, matrix products, on_device(): lax.dot_general(cols, piece, (((1,), (1,)), ((), ())), preferred_element_...  7.62 us
  transfers between devices with their start and end apart: 18, of which 13 were waited for; matrix products, arithmetic and copies ran while one was open for 8% of the time, Pallas kernels for 0%

profile of v6, /device:TPU:0, one launch (start us, length us, event | category | flops | bytes accessed | tf_op | source)
XLA Modules:
  0.0 210.9 jit_solution(8015810751743900668)
XLA Ops:
  7.2 3.0 %collective-permute-start = (bf16[1216,1792]{1,0:T(8,128)(2,1)}, bf16[1216,1792]{1,0:T(8,128)(2,1)}, u32[]{:S(2)}, u32[]{:S(2)}) collective-permute-start(bf16[1216,1792]{1,0:T(8,128)(2,1)} %param.7), channel_id=1, source_target_pairs={{0,16},{16,0},{1,17},{17,1},{2,18},{18,2},{3,19},{19,3},{4,20},{20... | collective-permute-start | bytes 13074440 | tf_op jit(solution)/shard_map/ppermute | solution.py:11
  10.2 3.6 %fusion.57 = f32[256,896]{1,0:T(8,128)S(1)} fusion(bf16[256,2048]{1,0:T(8,128)(2,1)} %param.5, bf16[896,2048]{1,0:T(8,128)(2,1)} %param.6), kind=kOutput, calls=%fused_computation.97 | convolution fusion | flops 939524096 | bytes 5636096 | tf_op jit(solution)/shard_map/dot_general | solution.py:101
  13.9 39.6 %all-reduce.1 = bf16[256,896]{1,0:T(8,128)(2,1)} all-reduce(f32[256,896]{1,0:T(8,128)S(1)} %fusion.57), channel_id=1, replica_groups=mesh['tok'=2,'voc'=4,'wid'=4] {'wid'}, use_global_device_ids=true, to_apply=%region_0.0 | all-reduce | flops 229376 | bytes 1376256 | tf_op jit(solution)/shard_map/psum | solution.py:104
  53.5 19.3 %all-gather.2.cloned.1.call-done = bf16[256,3584]{1,0:T(8,128)(2,1)} async-done(((bf16[256,896]{1,0:T(8,128)(2,1)}), bf16[256,3584]{1,0:T(8,128)(2,1)}) %all-gather.2.cloned.1.call-update) | async-done | bytes 1835024 | tf_op jit(solution)/shard_map/all_gather | solution.py:105
  72.8 4.0 %fusion.33 = f32[256,1216]{0,1:T(8,128)S(1)} fusion(bf16[1216,1792]{1,0:T(8,128)(2,1)} %param.7, bf16[256,3584]{1,0:T(8,128)(2,1)} %all-gather.2.cloned.1.call-done, s32[]{:T(128)S(6)} %select_n.141), kind=kOutput, calls=%fused_computation.34 | convolution fusion | flops 1115684864 | bytes 6520836 | tf_op jit(solution)/shard_map/dot_general | solution.py:110
  76.8 27.8 %collective-permute-done = bf16[1216,1792]{1,0:T(8,128)(2,1)} collective-permute-done((bf16[1216,1792]{1,0:T(8,128)(2,1)}, bf16[1216,1792]{1,0:T(8,128)(2,1)}, u32[]{:S(2)}, u32[]{:S(2)}) %collective-permute-start) | collective-permute-done | bytes 4358176 | tf_op jit(solution)/shard_map/ppermute | solution.py:11
  104.6 3.6 %fusion.56 = (f32[256]{0:T(256)S(1)}, f32[256,1216]{0,1:T(8,128)S(1)}) fusion(f32[256,1216]{0,1:T(8,128)S(1)} %fusion.33, bf16[1216,1792]{1,0:T(8,128)(2,1)} %collective-permute-done, bf16[256,3584]{1,0:T(8,128)(2,1)S(1)} %copy-done.2, s32[]{:T(128)S(6)} %select_n.143), kind=kOutput, calls=%fused_computation.96 | convolution fusion | flops 1116307200 | bytes 7767044 | tf_op jit(solution)/shard_map/dot_general | solution.py:110
  109.9 1.8 collective-permute-start.2
  113.6 1.9 collective-permute-start.3
  117.3 2.9 %collective-permute-start.4 = (f32[3,256]{1,0:T(4,128)S(1)}, f32[3,256]{1,0:T(4,128)S(1)}, u32[]{:S(2)}, u32[]{:S(2)}) collective-permute-start(f32[3,256]{1,0:T(4,128)S(1)} %pad_maximum_fusion.5), channel_id=1, source_target_pairs={{0,2},{1,3},{2,0},{3,1},{4,6},{5,7},{6,4},{7,5},{8,10},{9,11},{10,... | collective-permute-start | bytes 9224 | tf_op jit(solution)/shard_map/ppermute | solution.py:33
  122.8 2.5 %fusion.21 = f32[1,256,896]{2,1,0:T(8,128)S(1)} fusion(bf16[256,1216]{0,1:T(8,128)(2,1)S(1)} %multiply_convert_fusion, bf16[1216,1792]{1,0:T(8,128)(2,1)} %param.7, s32[]{:T(128)S(6)} %select_n.147), kind=kOutput, calls=%fused_computation.21 | convolution fusion | flops 557842432 | bytes 3719172 | tf_op jit(solution)/shard_map/dot_general | solution.py:155
  125.3 2.5 %fusion.24 = f32[1,256,896]{2,1,0:T(8,128)S(1)} fusion(bf16[256,1216]{0,1:T(8,128)(2,1)S(1)} %multiply_convert_fusion, bf16[1216,1792]{1,0:T(8,128)(2,1)} %collective-permute-done, s32[]{:T(128)S(6)} %select_n.147), kind=kOutput, calls=%fused_computation.22 | convolution fusion | flops 557842432 | bytes 3719172 | tf_op jit(solution)/shard_map/dot_general | solution.py:155
  128.1 2.5 %fusion.15 = f32[1,256,896]{2,1,0:T(8,128)S(1)} fusion(bf16[256,1216]{0,1:T(8,128)(2,1)S(1)} %multiply_convert_fusion, bf16[1216,1792]{1,0:T(8,128)(2,1)} %param.7, s32[]{:T(128)S(6)} %select_n.146), kind=kOutput, calls=%fused_computation.19 | convolution fusion | flops 557842432 | bytes 3719172 | tf_op jit(solution)/shard_map/dot_general | solution.py:155
  130.6 2.5 %fusion.18 = f32[1,256,896]{2,1,0:T(8,128)S(1)} fusion(bf16[256,1216]{0,1:T(8,128)(2,1)S(1)} %multiply_convert_fusion, bf16[1216,1792]{1,0:T(8,128)(2,1)} %collective-permute-done, s32[]{:T(128)S(6)} %select_n.146), kind=kOutput, calls=%fused_computation.20 | convolution fusion | flops 557842432 | bytes 3719172 | tf_op jit(solution)/shard_map/dot_general | solution.py:155
  135.0 1.9 collective-permute-start.9
  140.0 8.0 %collective-permute-done.9 = f32[2,2,32,896]{3,2,1,0:T(8,128)S(1)} collective-permute-done((f32[2,2,32,896]{3,2,1,0:T(8,128)S(1)}, f32[2,2,32,896]{3,2,1,0:T(8,128)S(1)}, u32[]{:S(2)}, u32[]{:S(2)}) %collective-permute-start.9) | collective-permute-done | bytes 458784 | tf_op jit(solution)/shard_map/ppermute | solution.py:71
  148.1 2.8 %collective-permute-start.10 = (f32[2,32,896]{2,1,0:T(8,128)S(1)}, f32[2,32,896]{2,1,0:T(8,128)S(1)}, u32[]{:S(2)}, u32[]{:S(2)}) collective-permute-start(f32[2,32,896]{2,1,0:T(8,128)S(1)} %dynamic-slice_bitcast_fusion.2), channel_id=1, source_target_pairs={{0,2},{1,3},{2,0},{3,1},{4,6},{5,7},{6,4},{7,5},{8,10},{9,11},{10,... | collective-permute-start | bytes 688136 | tf_op jit(solution)/shard_map/ppermute | solution.py:71
  153.7 7.8 %collective-permute-done.10 = f32[2,32,896]{2,1,0:T(8,128)S(1)} collective-permute-done((f32[2,32,896]{2,1,0:T(8,128)S(1)}, f32[2,32,896]{2,1,0:T(8,128)S(1)}, u32[]{:S(2)}, u32[]{:S(2)}) %collective-permute-start.10) | collective-permute-done | bytes 229408 | tf_op jit(solution)/shard_map/ppermute | solution.py:71
  163.6 2.8 %collective-permute-done.11 = f32[32,896]{1,0:T(8,128)S(1)} collective-permute-done((f32[32,896]{1,0:T(8,128)S(1)}, f32[32,896]{1,0:T(8,128)S(1)}, u32[]{:S(2)}, u32[]{:S(2)}) %collective-permute-start.11) | collective-permute-done | bytes 114720 | tf_op jit(solution)/shard_map/ppermute | solution.py:71
  166.5 5.5 %collective-permute-done.8 = f32[32,896]{1,0:T(8,128)S(1)} collective-permute-done((f32[32,896]{1,0:T(8,128)S(1)}, f32[32,896]{1,0:T(8,128)S(1)}, u32[]{:S(2)}, u32[]{:S(2)}) %collective-permute-start.8) | collective-permute-done | bytes 114720 | tf_op jit(solution)/shard_map/ppermute | solution.py:71
  172.1 6.0 %collective-permute-done.12 = bf16[64,896]{1,0:T(8,128)(2,1)S(1)} collective-permute-done((bf16[64,896]{1,0:T(8,128)(2,1)S(1)}, bf16[64,896]{1,0:T(8,128)(2,1)S(1)}, u32[]{:S(2)}, u32[]{:S(2)}) %collective-permute-start.12) | collective-permute-done | bytes 114720 | tf_op jit(solution)/shard_map/ppermute | solution.py:82
  178.3 5.9 %collective-permute-done.13 = bf16[2,64,896]{2,1,0:T(8,128)(2,1)S(1)} collective-permute-done((bf16[2,64,896]{2,1,0:T(8,128)(2,1)S(1)}, bf16[2,64,896]{2,1,0:T(8,128)(2,1)S(1)}, u32[]{:S(2)}, u32[]{:S(2)}) %collective-permute-start.13) | collective-permute-done | bytes 229408 | tf_op jit(solution)/shard_map/ppermute | solution.py:82
  187.8 5.1 %collective-permute-done.16 = f32[2]{0:T(128)S(1)} collective-permute-done((f32[2]{0:T(128)S(1)}, f32[2]{0:T(128)S(1)}, u32[]{:S(2)}, u32[]{:S(2)}) %collective-permute-start.16) | collective-permute-done | bytes 40 | tf_op jit(solution)/shard_map/ppermute | solution.py:45
  196.2 6.7 %fusion.8 = f32[896,2048]{1,0:T(8,128)} fusion(bf16[256,2048]{1,0:T(8,128)(2,1)} %collective-permute-done.15, bf16[256,2048]{1,0:T(8,128)(2,1)S(1)} %copy-done.3, pred[]{:T(512)S(6)} %eq.26, bf16[256,896]{1,0:T(8,128)(2,1)S(1)} %collective-permute-done.14, bf16[256,896]{1,0:T(8,128)(2,1)S(1)} %bitcast.77), kind=kOutput, calls=%fused_computation.10 | convolution fusion | flops 1892614144 | bytes 10354689 | tf_op jit(solution)/shard_map/dot_general | solution.py:238
  (66 shorter events, 23.9 us)
Async XLA Ops:
  7.2 65.7 %all-gather.2.cloned.1.call-start = ((), (), s32[]{:S(2)}) async-start(), calls=%async_computation | async-start | bytes 2293760 | tf_op jit(solution)/shard_map/all_gather | solution.py:105
  7.2 97.4 %collective-permute-start = (bf16[1216,1792]{1,0:T(8,128)(2,1)}, bf16[1216,1792]{1,0:T(8,128)(2,1)}, u32[]{:S(2)}, u32[]{:S(2)}) collective-permute-start(bf16[1216,1792]{1,0:T(8,128)(2,1)} %param.7), channel_id=1, source_target_pairs={{0,16},{16,0},{1,17},{17,1},{2,18},{18,2},{3,19},{19,3},{4,20},{20... | collective-permute-start | bytes 13074440 | tf_op jit(solution)/shard_map/ppermute | solution.py:11
  13.9 39.7 %copy-start.1 = (s32[256]{0:T(256)S(1)}, s32[256]{0:T(256)}, u32[]{:S(2)}) copy-start(s32[256]{0:T(256)} %param.8) | copy-start | bytes 3076
  72.8 31.8 %copy-start.2 = (bf16[256,3584]{1,0:T(8,128)(2,1)S(1)}, bf16[256,3584]{1,0:T(8,128)(2,1)}, u32[]{:S(2)}) copy-start(bf16[256,3584]{1,0:T(8,128)(2,1)} %all-gather.2.cloned.1.call-done) | copy-start | bytes 5505028
  76.8 43.4 %copy-start = (s32[256]{0:T(256)S(1)}, s32[256]{0:T(256)}, u32[]{:S(2)}) copy-start(s32[256]{0:T(256)} %param.9) | copy-start | bytes 3076
  108.6 1.2 collective-permute-start.1
  109.9 3.7 %collective-permute-start.2 = (f32[3,256]{1,0:T(4,128)S(1)}, f32[3,256]{1,0:T(4,128)S(1)}, u32[]{:S(2)}, u32[]{:S(2)}) collective-permute-start(f32[3,256]{1,0:T(4,128)S(1)} %pad_maximum_fusion.3), channel_id=1, source_target_pairs={{0,8},{4,12},{8,0},{12,4},{1,9},{5,13},{9,1},{13,5},{2,10},{6,14},... | collective-permute-start | bytes 9224 | tf_op jit(solution)/shard_map/ppermute | solution.py:33
  113.6 3.7 %collective-permute-start.3 = (f32[3,256]{1,0:T(4,128)S(1)}, f32[3,256]{1,0:T(4,128)S(1)}, u32[]{:S(2)}, u32[]{:S(2)}) collective-permute-start(f32[3,256]{1,0:T(4,128)S(1)} %pad_maximum_fusion.4), channel_id=1, source_target_pairs={{0,1},{1,0},{2,3},{3,2},{4,5},{5,4},{6,7},{7,6},{8,9},{9,8},{10,11... | collective-permute-start | bytes 9224 | tf_op jit(solution)/shard_map/ppermute | solution.py:33
  117.3 4.6 %collective-permute-start.4 = (f32[3,256]{1,0:T(4,128)S(1)}, f32[3,256]{1,0:T(4,128)S(1)}, u32[]{:S(2)}, u32[]{:S(2)}) collective-permute-start(f32[3,256]{1,0:T(4,128)S(1)} %pad_maximum_fusion.5), channel_id=1, source_target_pairs={{0,2},{1,3},{2,0},{3,1},{4,6},{5,7},{6,4},{7,5},{8,10},{9,11},{10,... | collective-permute-start | bytes 9224 | tf_op jit(solution)/shard_map/ppermute | solution.py:33
  127.9 5.1 %collective-permute-start.5 = (f32[2,256,896]{2,1,0:T(8,128)S(1)}, f32[2,256,896]{2,1,0:T(8,128)}, u32[]{:S(2)}, u32[]{:S(2)}) collective-permute-start(f32[2,256,896]{2,1,0:T(8,128)S(1)} %pad_maximum_fusion), channel_id=1, source_target_pairs={{0,4},{4,0},{8,12},{12,8},{1,5},{5,1},{9,13},{13,9},{2,6},{6,2},{1... | collective-permute-start | bytes 5505032 | tf_op jit(solution)/shard_map/ppermute | solution.py:165
  135.0 13.0 %collective-permute-start.9 = (f32[2,2,32,896]{3,2,1,0:T(8,128)S(1)}, f32[2,2,32,896]{3,2,1,0:T(8,128)S(1)}, u32[]{:S(2)}, u32[]{:S(2)}) collective-permute-start(f32[2,2,32,896]{3,2,1,0:T(8,128)S(1)} %dynamic-slice_bitcast_fusion), channel_id=1, source_target_pairs={{0,1},{1,0},{2,3},{3,2},{4,5},{5,4},{6,7},{7,6},{8,9},{9,8},{10,11... | collective-permute-start | bytes 1376264 | tf_op jit(solution)/shard_map/ppermute | solution.py:71
  136.9 14.0 %collective-permute-start.6 = (f32[2,2,32,896]{3,2,1,0:T(8,128)S(1)}, f32[2,2,32,896]{3,2,1,0:T(8,128)}, u32[]{:S(2)}, u32[]{:S(2)}) collective-permute-start(f32[2,2,32,896]{3,2,1,0:T(8,128)S(1)} %dynamic-slice_bitcast_fusion.1), channel_id=1, source_target_pairs={{0,8},{4,12},{8,0},{12,4},{1,9},{5,13},{9,1},{13,5},{2,10},{6,14},... | collective-permute-start | bytes 1376264 | tf_op jit(solution)/shard_map/ppermute | solution.py:71
  138.5 57.7 %collective-permute-start.15 = (bf16[256,2048]{1,0:T(8,128)(2,1)}, bf16[256,2048]{1,0:T(8,128)(2,1)}, u32[]{:S(2)}, u32[]{:S(2)}) collective-permute-start(bf16[256,2048]{1,0:T(8,128)(2,1)} %param.5), channel_id=1, source_target_pairs={{0,16},{16,0},{1,17},{17,1},{2,18},{18,2},{3,19},{19,3},{4,20},{20... | collective-permute-start | bytes 3145736 | tf_op jit(solution)/shard_map/ppermute | solution.py:99
  148.1 13.4 %collective-permute-start.10 = (f32[2,32,896]{2,1,0:T(8,128)S(1)}, f32[2,32,896]{2,1,0:T(8,128)S(1)}, u32[]{:S(2)}, u32[]{:S(2)}) collective-permute-start(f32[2,32,896]{2,1,0:T(8,128)S(1)} %dynamic-slice_bitcast_fusion.2), channel_id=1, source_target_pairs={{0,2},{1,3},{2,0},{3,1},{4,6},{5,7},{6,4},{7,5},{8,10},{9,11},{10,... | collective-permute-start | bytes 688136 | tf_op jit(solution)/shard_map/ppermute | solution.py:71
  152.1 11.2 %collective-permute-start.7 = (f32[2,32,896]{2,1,0:T(8,128)S(1)}, f32[2,32,896]{2,1,0:T(8,128)S(1)}, u32[]{:S(2)}, u32[]{:S(2)}) collective-permute-start(f32[2,32,896]{2,1,0:T(8,128)S(1)} %dynamic-slice_bitcast_fusion.3), channel_id=1, source_target_pairs={{0,1},{1,0},{2,3},{3,2},{4,5},{5,4},{6,7},{7,6},{8,9},{9,8},{10,11... | collective-permute-start | bytes 688136 | tf_op jit(solution)/shard_map/ppermute | solution.py:71
  161.6 34.6 %copy-start.3 = (bf16[256,2048]{1,0:T(8,128)(2,1)S(1)}, bf16[256,2048]{1,0:T(8,128)(2,1)}, u32[]{:S(2)}) copy-start(bf16[256,2048]{1,0:T(8,128)(2,1)} %param.5) | copy-start | bytes 3145732
  161.6 4.9 %collective-permute-start.11 = (f32[32,896]{1,0:T(8,128)S(1)}, f32[32,896]{1,0:T(8,128)S(1)}, u32[]{:S(2)}, u32[]{:S(2)}) collective-permute-start(f32[32,896]{1,0:T(8,128)S(1)} %dynamic-slice_bitcast_fusion.4), channel_id=1, source_target_pairs={{0,8},{4,12},{8,0},{12,4},{1,9},{5,13},{9,1},{13,5},{2,10},{6,14},... | collective-permute-start | bytes 344072 | tf_op jit(solution)/shard_map/ppermute | solution.py:71
  163.3 8.7 %collective-permute-start.8 = (f32[32,896]{1,0:T(8,128)S(1)}, f32[32,896]{1,0:T(8,128)S(1)}, u32[]{:S(2)}, u32[]{:S(2)}) collective-permute-start(f32[32,896]{1,0:T(8,128)S(1)} %dynamic-slice_bitcast_fusion.5), channel_id=1, source_target_pairs={{0,2},{1,3},{2,0},{3,1},{4,6},{5,7},{6,4},{7,5},{8,10},{9,11},{10,... | collective-permute-start | bytes 344072 | tf_op jit(solution)/shard_map/ppermute | solution.py:71
  172.0 6.1 %collective-permute-start.12 = (bf16[64,896]{1,0:T(8,128)(2,1)S(1)}, bf16[64,896]{1,0:T(8,128)(2,1)S(1)}, u32[]{:S(2)}, u32[]{:S(2)}) collective-permute-start(bf16[64,896]{1,0:T(8,128)(2,1)S(1)} %pad_maximum_fusion.1), channel_id=1, source_target_pairs={{0,2},{1,3},{2,0},{3,1},{4,6},{5,7},{6,4},{7,5},{8,10},{9,11},{10,... | collective-permute-start | bytes 344072 | tf_op jit(solution)/shard_map/ppermute | solution.py:82
  178.2 6.1 %collective-permute-start.13 = (bf16[2,64,896]{2,1,0:T(8,128)(2,1)S(1)}, bf16[2,64,896]{2,1,0:T(8,128)(2,1)S(1)}, u32[]{:S(2)}, u32[]{:S(2)}) collective-permute-start(bf16[2,64,896]{2,1,0:T(8,128)(2,1)S(1)} %maximum_select_fusion.6), channel_id=1, source_target_pairs={{0,1},{1,0},{2,3},{3,2},{4,5},{5,4},{6,7},{7,6},{8,9},{9,8},{10,11... | collective-permute-start | bytes 688136 | tf_op jit(solution)/shard_map/ppermute | solution.py:82
  184.3 11.9 %collective-permute-start.14 = (bf16[256,896]{1,0:T(8,128)(2,1)S(1)}, bf16[256,896]{1,0:T(8,128)(2,1)S(1)}, u32[]{:S(2)}, u32[]{:S(2)}) collective-permute-start(bf16[256,896]{1,0:T(8,128)(2,1)S(1)} %bitcast.76), channel_id=1, source_target_pairs={{0,16},{16,0},{1,17},{17,1},{2,18},{18,2},{3,19},{19,3},{4,20},{20... | collective-permute-start | bytes 1376264 | tf_op jit(solution)/shard_map/ppermute | solution.py:226
  187.2 5.7 %collective-permute-start.16 = (f32[2]{0:T(128)S(1)}, f32[2]{0:T(128)S(1)}, u32[]{:S(2)}, u32[]{:S(2)}) collective-permute-start(f32[2]{0:T(128)S(1)} %pad_maximum_fusion.6), channel_id=1, source_target_pairs={{0,16},{16,0},{1,17},{17,1},{2,18},{18,2},{3,19},{19,3},{4,20},{20... | collective-permute-start | bytes 32 | tf_op jit(solution)/shard_map/ppermute | solution.py:45
Sparse Core Ops, SparseCore 0:
  53.6 19.1 all-gather.1

commit v7 on v6

--- a/solution.py
+++ b/solution.py
@@ -102,7 +102,11 @@
         hidden, proj, (((1,), (1,)), ((), ())), preferred_element_type=jnp.float32
     )
     summed = lax.psum(partial_value, "wid")
-    projected = lax.all_gather(summed.astype(jnp.bfloat16), "voc", axis=1, tiled=True)
+    if is_pow2(lax.axis_size("voc")):
+        quarters = doubling_gather(summed.astype(jnp.bfloat16), "voc")
+        projected = quarters.transpose(1, 0, 2).reshape((tok_rows, -1))
+    else:
+        projected = lax.all_gather(summed.astype(jnp.bfloat16), "voc", axis=1, tiled=True)
 
     logits = None
     for k, piece in enumerate(table_pieces):

time: 212 us -> 198 us (0.934)
  between operations: 16.9 us -> 3.54 us
  waiting for transfers between devices: 94.8 us -> 90.4 us
  local copies, waits for them, and re-layouts: 0.89 us -> 3.44 us
    all_gather x1 -> x0, waiting for transfers between devices: 19.3 us -> none  [on_device(): lax.all_gather(summed.astype(jnp.bfloat16), 'voc', axis=1, tiled=True)]
    ppermute x2 -> x4, waiting for transfers between devices: 11.9 us -> 22.1 us  [doubling_gather(): other = lax.ppermute(x, ax, [(k, k ^ b) for k in range(n)])]
    ppermute x1, waiting for transfers between devices: 27.8 us -> 32.5 us  [tok_pieces(): pieces.append(lax.ppermute(x, 'tok', perm))]
    transpose x0 -> x1, local copies, waits for them, and re-layouts: none -> 2.4 us  [on_device(): projected = quarters.transpose(1, 0, 2).reshape((tok_rows, -1))]
  transfers between devices with their start and end apart: 18 -> 19, of which waited for: 13 -> 14; matrix products, arithmetic and copies ran while one was open for 8% -> 10% of each run, Pallas kernels for 0% -> 0%
where the time goes in v7:
time: 198 us
  waiting for transfers between devices  90.4 us (46%)
  blocking collectives  39.1 us (20%)
  matrix products  28 us (14%)
  starting transfers between devices  25 us (13%)
  other arithmetic  8.1 us (4%)
  between operations  3.54 us (2%)
  local copies, waits for them, and re-layouts  3.44 us (2%)
    psum x1, blocking collectives, on_device(): summed = lax.psum(partial_value, 'wid')  39.1 us
    ppermute x1, waiting for transfers between devices, tok_pieces(): pieces.append(lax.ppermute(x, 'tok', perm))  32.5 us
    ppermute x6, waiting for transfers between devices, halving_steps(): x = keep + lax.ppermute(send, ax, [(k, k ^ b) for k in range(n)])  24.2 us
    ppermute x4, waiting for transfers between devices, doubling_gather(): other = lax.ppermute(x, ax, [(k, k ^ b) for k in range(n)])  22.1 us
    dot_general x4, matrix products, quarter_dots(): jnp.dot(dlogits, lax.dynamic_slice_in_dim(piece, sel * q_cols, q_cols, ax...  10 us
    ppermute x6, starting transfers between devices, halving_steps(): x = keep + lax.ppermute(send, ax, [(k, k ^ b) for k in range(n)])  9.89 us
    dot_general x2, matrix products, on_device(): lax.dot_general(cols, piece, (((1,), (1,)), ((), ())), preferred_element_...  7.57 us
    dot_general x1, matrix products, on_device(): lax.dot_general(grad_all, hidden_all, (((0,), (0,)), ((), ())), preferred...  6.78 us
  transfers between devices with their start and end apart: 19, of which 14 were waited for; matrix products, arithmetic and copies ran while one was open for 10% of the time, Pallas kernels for 0%

profile of v7, /device:TPU:0, one launch (start us, length us, event | category | flops | bytes accessed | tf_op | source)
XLA Modules:
  0.0 197.6 jit_solution(13892461878227462424)
XLA Ops:
  0.6 3.0 %collective-permute-start.2 = (bf16[1216,1792]{1,0:T(8,128)(2,1)}, bf16[1216,1792]{1,0:T(8,128)(2,1)}, u32[]{:S(2)}, u32[]{:S(2)}) collective-permute-start(bf16[1216,1792]{1,0:T(8,128)(2,1)} %param.7), channel_id=1, source_target_pairs={{0,16},{16,0},{1,17},{17,1},{2,18},{18,2},{3,19},{19,3},{4,20},{20... | collective-permute-start | bytes 13074440 | tf_op jit(solution)/shard_map/ppermute | solution.py:11
  3.6 3.6 %fusion.57 = f32[256,896]{1,0:T(8,128)S(1)} fusion(bf16[256,2048]{1,0:T(8,128)(2,1)} %param.5, bf16[896,2048]{1,0:T(8,128)(2,1)} %param.6), kind=kOutput, calls=%fused_computation.100 | convolution fusion | flops 939524096 | bytes 5636096 | tf_op jit(solution)/shard_map/dot_general | solution.py:101
  7.3 39.1 %all-reduce.1 = bf16[256,896]{1,0:T(8,128)(2,1)S(1)} all-reduce(f32[256,896]{1,0:T(8,128)S(1)} %fusion.57), channel_id=1, replica_groups=mesh['tok'=2,'voc'=4,'wid'=4] {'wid'}, use_global_device_ids=true, to_apply=%region_0.0 | all-reduce | flops 229376 | bytes 1376256 | tf_op jit(solution)/shard_map/psum | solution.py:104
  48.0 7.9 %collective-permute-done = bf16[256,896]{1,0:T(8,128)(2,1)S(1)} collective-permute-done((bf16[256,896]{1,0:T(8,128)(2,1)S(1)}, bf16[256,896]{1,0:T(8,128)(2,1)S(1)}, u32[]{:S(2)}, u32[]{:S(2)}) %collective-permute-start) | collective-permute-done | bytes 458784 | tf_op jit(solution)/shard_map/ppermute | solution.py:82
  56.4 2.2 %collective-permute-done.1 = bf16[2,256,896]{2,1,0:T(8,128)(2,1)S(1)} collective-permute-done((bf16[2,256,896]{2,1,0:T(8,128)(2,1)S(1)}, bf16[2,256,896]{2,1,0:T(8,128)(2,1)S(1)}, u32[]{:S(2)}, u32[]{:S(2)}) %collective-permute-start.1) | collective-permute-done | bytes 917536 | tf_op jit(solution)/shard_map/ppermute | solution.py:82
  59.1 2.4 %copy.8 = bf16[256,4,896]{0,2,1:T(8,128)(2,1)} copy(bf16[256,4,896]{2,0,1:T(8,128)(2,1)S(1)} %bitcast.80) | data formatting | bytes 3670016 | tf_op jit(solution)/shard_map/transpose | solution.py:107
  61.5 4.0 %fusion.33 = f32[256,1216]{0,1:T(8,128)S(1)} fusion(bf16[1216,1792]{1,0:T(8,128)(2,1)} %param.7, bf16[256,3584]{0,1:T(8,128)(2,1)} %bitcast.84, s32[]{:T(128)S(6)} %select_n.188), kind=kOutput, calls=%fused_computation.37 | convolution fusion | flops 1115684864 | bytes 6520836 | tf_op jit(solution)/shard_map/dot_general | solution.py:114
  65.5 32.5 %collective-permute-done.2 = bf16[1216,1792]{1,0:T(8,128)(2,1)} collective-permute-done((bf16[1216,1792]{1,0:T(8,128)(2,1)}, bf16[1216,1792]{1,0:T(8,128)(2,1)}, u32[]{:S(2)}, u32[]{:S(2)}) %collective-permute-start.2) | collective-permute-done | bytes 4358176 | tf_op jit(solution)/shard_map/ppermute | solution.py:11
  98.0 3.6 %fusion.56 = (f32[256]{0:T(256)S(1)}, f32[256,1216]{0,1:T(8,128)S(1)}) fusion(f32[256,1216]{0,1:T(8,128)S(1)} %fusion.33, bf16[1216,1792]{1,0:T(8,128)(2,1)} %collective-permute-done.2, bf16[256,3584]{0,1:T(8,128)(2,1)S(1)} %bitcast.85, s32[]{:T(128)S(6)} %select_n.190), kind=kOutput, calls=%fused_computation.99 | convolution fusion | flops 1116307200 | bytes 7767044 | tf_op jit(solution)/shard_map/dot_general | solution.py:114
  107.0 1.9 collective-permute-start.5
  110.7 2.9 %collective-permute-start.6 = (f32[3,256]{1,0:T(4,128)S(1)}, f32[3,256]{1,0:T(4,128)S(1)}, u32[]{:S(2)}, u32[]{:S(2)}) collective-permute-start(f32[3,256]{1,0:T(4,128)S(1)} %pad_maximum_fusion.5), channel_id=1, source_target_pairs={{0,2},{1,3},{2,0},{3,1},{4,6},{5,7},{6,4},{7,5},{8,10},{9,11},{10,... | collective-permute-start | bytes 9224 | tf_op jit(solution)/shard_map/ppermute | solution.py:33
  116.2 2.5 %fusion.21 = f32[1,256,896]{2,1,0:T(8,128)S(1)} fusion(bf16[256,1216]{0,1:T(8,128)(2,1)S(1)} %multiply_convert_fusion, bf16[1216,1792]{1,0:T(8,128)(2,1)} %param.7, s32[]{:T(128)S(6)} %select_n.193), kind=kOutput, calls=%fused_computation.22 | convolution fusion | flops 557842432 | bytes 3719172 | tf_op jit(solution)/shard_map/dot_general | solution.py:159
  118.7 2.5 %fusion.24 = f32[1,256,896]{2,1,0:T(8,128)S(1)} fusion(bf16[256,1216]{0,1:T(8,128)(2,1)S(1)} %multiply_convert_fusion, bf16[1216,1792]{1,0:T(8,128)(2,1)} %collective-permute-done.2, s32[]{:T(128)S(6)} %select_n.193), kind=kOutput, calls=%fused_computation.23 | convolution fusion | flops 557842432 | bytes 3719172 | tf_op jit(solution)/shard_map/dot_general | solution.py:159
  121.5 2.5 %fusion.15 = f32[1,256,896]{2,1,0:T(8,128)S(1)} fusion(bf16[256,1216]{0,1:T(8,128)(2,1)S(1)} %multiply_convert_fusion, bf16[1216,1792]{1,0:T(8,128)(2,1)} %param.7, s32[]{:T(128)S(6)} %select_n.192), kind=kOutput, calls=%fused_computation.20 | convolution fusion | flops 557842432 | bytes 3719172 | tf_op jit(solution)/shard_map/dot_general | solution.py:159
  124.0 2.5 %fusion.18 = f32[1,256,896]{2,1,0:T(8,128)S(1)} fusion(bf16[256,1216]{0,1:T(8,128)(2,1)S(1)} %multiply_convert_fusion, bf16[1216,1792]{1,0:T(8,128)(2,1)} %collective-permute-done.2, s32[]{:T(128)S(6)} %select_n.192), kind=kOutput, calls=%fused_computation.21 | convolution fusion | flops 557842432 | bytes 3719172 | tf_op jit(solution)/shard_map/dot_general | solution.py:159
  133.5 8.0 %collective-permute-done.11 = f32[2,2,32,896]{3,2,1,0:T(8,128)S(1)} collective-permute-done((f32[2,2,32,896]{3,2,1,0:T(8,128)S(1)}, f32[2,2,32,896]{3,2,1,0:T(8,128)S(1)}, u32[]{:S(2)}, u32[]{:S(2)}) %collective-permute-start.11) | collective-permute-done | bytes 458784 | tf_op jit(solution)/shard_map/ppermute | solution.py:71
  141.6 2.8 %collective-permute-start.12 = (f32[2,32,896]{2,1,0:T(8,128)S(1)}, f32[2,32,896]{2,1,0:T(8,128)S(1)}, u32[]{:S(2)}, u32[]{:S(2)}) collective-permute-start(f32[2,32,896]{2,1,0:T(8,128)S(1)} %dynamic-slice_bitcast_fusion.2), channel_id=1, source_target_pairs={{0,2},{1,3},{2,0},{3,1},{4,6},{5,7},{6,4},{7,5},{8,10},{9,11},{10,... | collective-permute-start | bytes 688136 | tf_op jit(solution)/shard_map/ppermute | solution.py:71
  147.2 7.8 %collective-permute-done.12 = f32[2,32,896]{2,1,0:T(8,128)S(1)} collective-permute-done((f32[2,32,896]{2,1,0:T(8,128)S(1)}, f32[2,32,896]{2,1,0:T(8,128)S(1)}, u32[]{:S(2)}, u32[]{:S(2)}) %collective-permute-start.12) | collective-permute-done | bytes 229408 | tf_op jit(solution)/shard_map/ppermute | solution.py:71
  157.1 2.8 %collective-permute-done.13 = f32[32,896]{1,0:T(8,128)S(1)} collective-permute-done((f32[32,896]{1,0:T(8,128)S(1)}, f32[32,896]{1,0:T(8,128)S(1)}, u32[]{:S(2)}, u32[]{:S(2)}) %collective-permute-start.13) | collective-permute-done | bytes 114720 | tf_op jit(solution)/shard_map/ppermute | solution.py:71
  159.9 5.5 %collective-permute-done.10 = f32[32,896]{1,0:T(8,128)S(1)} collective-permute-done((f32[32,896]{1,0:T(8,128)S(1)}, f32[32,896]{1,0:T(8,128)S(1)}, u32[]{:S(2)}, u32[]{:S(2)}) %collective-permute-start.10) | collective-permute-done | bytes 114720 | tf_op jit(solution)/shard_map/ppermute | solution.py:71
  165.6 6.0 %collective-permute-done.14 = bf16[64,896]{1,0:T(8,128)(2,1)S(1)} collective-permute-done((bf16[64,896]{1,0:T(8,128)(2,1)S(1)}, bf16[64,896]{1,0:T(8,128)(2,1)S(1)}, u32[]{:S(2)}, u32[]{:S(2)}) %collective-permute-start.14) | collective-permute-done | bytes 114720 | tf_op jit(solution)/shard_map/ppermute | solution.py:82
  171.7 5.9 %collective-permute-done.15 = bf16[2,64,896]{2,1,0:T(8,128)(2,1)S(1)} collective-permute-done((bf16[2,64,896]{2,1,0:T(8,128)(2,1)S(1)}, bf16[2,64,896]{2,1,0:T(8,128)(2,1)S(1)}, u32[]{:S(2)}, u32[]{:S(2)}) %collective-permute-start.15) | collective-permute-done | bytes 229408 | tf_op jit(solution)/shard_map/ppermute | solution.py:82
  181.2 5.1 %collective-permute-done.18 = f32[2]{0:T(128)S(1)} collective-permute-done((f32[2]{0:T(128)S(1)}, f32[2]{0:T(128)S(1)}, u32[]{:S(2)}, u32[]{:S(2)}) %collective-permute-start.18) | collective-permute-done | bytes 40 | tf_op jit(solution)/shard_map/ppermute | solution.py:45
  189.7 6.8 %fusion.8 = f32[896,2048]{1,0:T(8,128)} fusion(bf16[256,2048]{1,0:T(8,128)(2,1)} %collective-permute-done.17, bf16[256,2048]{1,0:T(8,128)(2,1)S(1)} %copy-done.3, pred[]{:T(512)S(6)} %eq.34, bf16[256,896]{1,0:T(8,128)(2,1)S(1)} %collective-permute-done.16, bf16[256,896]{1,0:T(8,128)(2,1)S(1)} %bitcast.94), kind=kOutput, calls=%fused_computation.10 | convolution fusion | flops 1892614144 | bytes 10354689 | tf_op jit(solution)/shard_map/dot_general | solution.py:242
  (72 shorter events, 30.0 us)
Async XLA Ops:
  0.6 97.4 %collective-permute-start.2 = (bf16[1216,1792]{1,0:T(8,128)(2,1)}, bf16[1216,1792]{1,0:T(8,128)(2,1)}, u32[]{:S(2)}, u32[]{:S(2)}) collective-permute-start(bf16[1216,1792]{1,0:T(8,128)(2,1)} %param.7), channel_id=1, source_target_pairs={{0,16},{16,0},{1,17},{17,1},{2,18},{18,2},{3,19},{19,3},{4,20},{20... | collective-permute-start | bytes 13074440 | tf_op jit(solution)/shard_map/ppermute | solution.py:11
  7.3 48.9 %copy-start.2 = (s32[256]{0:T(256)S(1)}, s32[256]{0:T(256)}, u32[]{:S(2)}) copy-start(s32[256]{0:T(256)} %param.8) | copy-start | bytes 3076
  46.4 9.5 %collective-permute-start = (bf16[256,896]{1,0:T(8,128)(2,1)S(1)}, bf16[256,896]{1,0:T(8,128)(2,1)S(1)}, u32[]{:S(2)}, u32[]{:S(2)}) collective-permute-start(bf16[256,896]{1,0:T(8,128)(2,1)S(1)} %all-reduce.1), channel_id=1, source_target_pairs={{0,8},{4,12},{8,0},{12,4},{1,9},{5,13},{9,1},{13,5},{2,10},{6,14},... | collective-permute-start | bytes 1376264 | tf_op jit(solution)/shard_map/ppermute | solution.py:82
  56.1 2.5 %collective-permute-start.1 = (bf16[2,256,896]{2,1,0:T(8,128)(2,1)S(1)}, bf16[2,256,896]{2,1,0:T(8,128)(2,1)S(1)}, u32[]{:S(2)}, u32[]{:S(2)}) collective-permute-start(bf16[2,256,896]{2,1,0:T(8,128)(2,1)S(1)} %maximum_select_fusion.4), channel_id=1, source_target_pairs={{0,4},{4,0},{8,12},{12,8},{1,5},{5,1},{9,13},{13,9},{2,6},{6,2},{1... | collective-permute-start | bytes 2752520 | tf_op jit(solution)/shard_map/ppermute | solution.py:82
  61.5 36.5 %copy-start = (bf16[256,4,896]{0,2,1:T(8,128)(2,1)S(1)}, bf16[256,4,896]{0,2,1:T(8,128)(2,1)}, u32[]{:S(2)}) copy-start(bf16[256,4,896]{0,2,1:T(8,128)(2,1)} %copy.8) | copy-start | bytes 5505028
  65.5 48.1 %copy-start.1 = (s32[256]{0:T(256)S(1)}, s32[256]{0:T(256)}, u32[]{:S(2)}) copy-start(s32[256]{0:T(256)} %param.9) | copy-start | bytes 3076
  102.0 1.2 collective-permute-start.3
  103.3 3.7 %collective-permute-start.4 = (f32[3,256]{1,0:T(4,128)S(1)}, f32[3,256]{1,0:T(4,128)S(1)}, u32[]{:S(2)}, u32[]{:S(2)}) collective-permute-start(f32[3,256]{1,0:T(4,128)S(1)} %pad_maximum_fusion.3), channel_id=1, source_target_pairs={{0,8},{4,12},{8,0},{12,4},{1,9},{5,13},{9,1},{13,5},{2,10},{6,14},... | collective-permute-start | bytes 9224 | tf_op jit(solution)/shard_map/ppermute | solution.py:33
  107.0 3.7 %collective-permute-start.5 = (f32[3,256]{1,0:T(4,128)S(1)}, f32[3,256]{1,0:T(4,128)S(1)}, u32[]{:S(2)}, u32[]{:S(2)}) collective-permute-start(f32[3,256]{1,0:T(4,128)S(1)} %pad_maximum_fusion.4), channel_id=1, source_target_pairs={{0,1},{1,0},{2,3},{3,2},{4,5},{5,4},{6,7},{7,6},{8,9},{9,8},{10,11... | collective-permute-start | bytes 9224 | tf_op jit(solution)/shard_map/ppermute | solution.py:33
  110.7 4.6 %collective-permute-start.6 = (f32[3,256]{1,0:T(4,128)S(1)}, f32[3,256]{1,0:T(4,128)S(1)}, u32[]{:S(2)}, u32[]{:S(2)}) collective-permute-start(f32[3,256]{1,0:T(4,128)S(1)} %pad_maximum_fusion.5), channel_id=1, source_target_pairs={{0,2},{1,3},{2,0},{3,1},{4,6},{5,7},{6,4},{7,5},{8,10},{9,11},{10,... | collective-permute-start | bytes 9224 | tf_op jit(solution)/shard_map/ppermute | solution.py:33
  121.4 5.1 %collective-permute-start.7 = (f32[2,256,896]{2,1,0:T(8,128)S(1)}, f32[2,256,896]{2,1,0:T(8,128)}, u32[]{:S(2)}, u32[]{:S(2)}) collective-permute-start(f32[2,256,896]{2,1,0:T(8,128)S(1)} %pad_maximum_fusion), channel_id=1, source_target_pairs={{0,4},{4,0},{8,12},{12,8},{1,5},{5,1},{9,13},{13,9},{2,6},{6,2},{1... | collective-permute-start | bytes 5505032 | tf_op jit(solution)/shard_map/ppermute | solution.py:169
  128.5 13.0 %collective-permute-start.11 = (f32[2,2,32,896]{3,2,1,0:T(8,128)S(1)}, f32[2,2,32,896]{3,2,1,0:T(8,128)S(1)}, u32[]{:S(2)}, u32[]{:S(2)}) collective-permute-start(f32[2,2,32,896]{3,2,1,0:T(8,128)S(1)} %dynamic-slice_bitcast_fusion), channel_id=1, source_target_pairs={{0,1},{1,0},{2,3},{3,2},{4,5},{5,4},{6,7},{7,6},{8,9},{9,8},{10,11... | collective-permute-start | bytes 1376264 | tf_op jit(solution)/shard_map/ppermute | solution.py:71
  130.4 14.0 %collective-permute-start.8 = (f32[2,2,32,896]{3,2,1,0:T(8,128)S(1)}, f32[2,2,32,896]{3,2,1,0:T(8,128)}, u32[]{:S(2)}, u32[]{:S(2)}) collective-permute-start(f32[2,2,32,896]{3,2,1,0:T(8,128)S(1)} %dynamic-slice_bitcast_fusion.1), channel_id=1, source_target_pairs={{0,8},{4,12},{8,0},{12,4},{1,9},{5,13},{9,1},{13,5},{2,10},{6,14},... | collective-permute-start | bytes 1376264 | tf_op jit(solution)/shard_map/ppermute | solution.py:71
  132.0 57.7 %collective-permute-start.17 = (bf16[256,2048]{1,0:T(8,128)(2,1)}, bf16[256,2048]{1,0:T(8,128)(2,1)}, u32[]{:S(2)}, u32[]{:S(2)}) collective-permute-start(bf16[256,2048]{1,0:T(8,128)(2,1)} %param.5), channel_id=1, source_target_pairs={{0,16},{16,0},{1,17},{17,1},{2,18},{18,2},{3,19},{19,3},{4,20},{20... | collective-permute-start | bytes 3145736 | tf_op jit(solution)/shard_map/ppermute | solution.py:99
  141.6 13.4 %collective-permute-start.12 = (f32[2,32,896]{2,1,0:T(8,128)S(1)}, f32[2,32,896]{2,1,0:T(8,128)S(1)}, u32[]{:S(2)}, u32[]{:S(2)}) collective-permute-start(f32[2,32,896]{2,1,0:T(8,128)S(1)} %dynamic-slice_bitcast_fusion.2), channel_id=1, source_target_pairs={{0,2},{1,3},{2,0},{3,1},{4,6},{5,7},{6,4},{7,5},{8,10},{9,11},{10,... | collective-permute-start | bytes 688136 | tf_op jit(solution)/shard_map/ppermute | solution.py:71
  145.5 11.2 %collective-permute-start.9 = (f32[2,32,896]{2,1,0:T(8,128)S(1)}, f32[2,32,896]{2,1,0:T(8,128)S(1)}, u32[]{:S(2)}, u32[]{:S(2)}) collective-permute-start(f32[2,32,896]{2,1,0:T(8,128)S(1)} %dynamic-slice_bitcast_fusion.3), channel_id=1, source_target_pairs={{0,1},{1,0},{2,3},{3,2},{4,5},{5,4},{6,7},{7,6},{8,9},{9,8},{10,11... | collective-permute-start | bytes 688136 | tf_op jit(solution)/shard_map/ppermute | solution.py:71
  155.0 34.6 %copy-start.3 = (bf16[256,2048]{1,0:T(8,128)(2,1)S(1)}, bf16[256,2048]{1,0:T(8,128)(2,1)}, u32[]{:S(2)}) copy-start(bf16[256,2048]{1,0:T(8,128)(2,1)} %param.5) | copy-start | bytes 3145732
  155.1 4.9 %collective-permute-start.13 = (f32[32,896]{1,0:T(8,128)S(1)}, f32[32,896]{1,0:T(8,128)S(1)}, u32[]{:S(2)}, u32[]{:S(2)}) collective-permute-start(f32[32,896]{1,0:T(8,128)S(1)} %dynamic-slice_bitcast_fusion.4), channel_id=1, source_target_pairs={{0,8},{4,12},{8,0},{12,4},{1,9},{5,13},{9,1},{13,5},{2,10},{6,14},... | collective-permute-start | bytes 344072 | tf_op jit(solution)/shard_map/ppermute | solution.py:71
  156.8 8.7 %collective-permute-start.10 = (f32[32,896]{1,0:T(8,128)S(1)}, f32[32,896]{1,0:T(8,128)S(1)}, u32[]{:S(2)}, u32[]{:S(2)}) collective-permute-start(f32[32,896]{1,0:T(8,128)S(1)} %dynamic-slice_bitcast_fusion.5), channel_id=1, source_target_pairs={{0,2},{1,3},{2,0},{3,1},{4,6},{5,7},{6,4},{7,5},{8,10},{9,11},{10,... | collective-permute-start | bytes 344072 | tf_op jit(solution)/shard_map/ppermute | solution.py:71
  165.5 6.1 %collective-permute-start.14 = (bf16[64,896]{1,0:T(8,128)(2,1)S(1)}, bf16[64,896]{1,0:T(8,128)(2,1)S(1)}, u32[]{:S(2)}, u32[]{:S(2)}) collective-permute-start(bf16[64,896]{1,0:T(8,128)(2,1)S(1)} %pad_maximum_fusion.1), channel_id=1, source_target_pairs={{0,2},{1,3},{2,0},{3,1},{4,6},{5,7},{6,4},{7,5},{8,10},{9,11},{10,... | collective-permute-start | bytes 344072 | tf_op jit(solution)/shard_map/ppermute | solution.py:82
  171.6 6.1 %collective-permute-start.15 = (bf16[2,64,896]{2,1,0:T(8,128)(2,1)S(1)}, bf16[2,64,896]{2,1,0:T(8,128)(2,1)S(1)}, u32[]{:S(2)}, u32[]{:S(2)}) collective-permute-start(bf16[2,64,896]{2,1,0:T(8,128)(2,1)S(1)} %maximum_select_fusion.9), channel_id=1, source_target_pairs={{0,1},{1,0},{2,3},{3,2},{4,5},{5,4},{6,7},{7,6},{8,9},{9,8},{10,11... | collective-permute-start | bytes 688136 | tf_op jit(solution)/shard_map/ppermute | solution.py:82
  177.8 11.9 %collective-permute-start.16 = (bf16[256,896]{1,0:T(8,128)(2,1)S(1)}, bf16[256,896]{1,0:T(8,128)(2,1)S(1)}, u32[]{:S(2)}, u32[]{:S(2)}) collective-permute-start(bf16[256,896]{1,0:T(8,128)(2,1)S(1)} %bitcast.93), channel_id=1, source_target_pairs={{0,16},{16,0},{1,17},{17,1},{2,18},{18,2},{3,19},{19,3},{4,20},{20... | collective-permute-start | bytes 1376264 | tf_op jit(solution)/shard_map/ppermute | solution.py:230
  180.7 5.7 %collective-permute-start.18 = (f32[2]{0:T(128)S(1)}, f32[2]{0:T(128)S(1)}, u32[]{:S(2)}, u32[]{:S(2)}) collective-permute-start(f32[2]{0:T(128)S(1)} %pad_maximum_fusion.6), channel_id=1, source_target_pairs={{0,16},{16,0},{1,17},{17,1},{2,18},{18,2},{3,19},{19,3},{4,20},{20... | collective-permute-start | bytes 32 | tf_op jit(solution)/shard_map/ppermute | solution.py:45

commit v8 on v7

--- a/solution.py
+++ b/solution.py
@@ -130,7 +130,6 @@
     picked = stats[2]
     sums = jnp.stack([jnp.sum(weight * (log_total - picked)), jnp.sum(weight)])
     sums = tree_sum(sums, "tok")
-    loss = sums[0] / sums[1]
 
     dlogits = (
         weight[:, None] * (jnp.exp(logits - log_total[:, None]) - is_target.astype(jnp.float32))
@@ -181,6 +180,7 @@
         part_a = halving_steps(blocks[..., :half, :], dims, rest_voc + wid_bits, bits)
         part_b = halving_steps(blocks[..., half:, :], dims, wid_bits + rest_voc, bits)
         mine = jnp.concatenate([part_a, part_b], axis=0).astype(jnp.bfloat16)
+        sums, mine = lax.optimization_barrier((sums, mine))
         grad_rows_pos = doubling_gather(mine, "wid").reshape((tok_rows, q_cols))
     elif grad_path:
         stacked = jnp.stack(
@@ -228,20 +228,10 @@
 
     if grad_rows_pos is not None:
         grad_other = lax.ppermute(grad_rows_pos, "tok", [(0, 1), (1, 0)])
-        first = t == 0
-        grad_all = jnp.where(
-            first,
-            jnp.concatenate([grad_rows_pos, grad_other], axis=0),
-            jnp.concatenate([grad_other, grad_rows_pos], axis=0),
-        )
-        hidden_all = jnp.where(
-            first,
-            jnp.concatenate([hidden, hidden_other], axis=0),
-            jnp.concatenate([hidden_other, hidden], axis=0),
-        )
+        by_pos = (((0,), (0,)), ((), ()))
         grad_proj = lax.dot_general(
-            grad_all, hidden_all, (((0,), (0,)), ((), ())), preferred_element_type=jnp.float32
-        )
+            grad_rows_pos, hidden, by_pos, preferred_element_type=jnp.float32
+        ) + lax.dot_general(grad_other, hidden_other, by_pos, preferred_element_type=jnp.float32)
     elif n_tok == 2:
         grad_other = lax.ppermute(grad_rows_t, "tok", [(0, 1), (1, 0)])
         first = t == 0
@@ -260,6 +250,7 @@
         grad_all = lax.all_gather(grad_rows_t, "tok", axis=1, tiled=True)
         hidden_all = lax.all_gather(hidden, "tok", axis=0, tiled=True)
         grad_proj = jnp.dot(grad_all, hidden_all, preferred_element_type=jnp.float32)
+    loss = sums[0] / sums[1]
     return (grad_proj, loss)
 
 

time: 198 us -> 204 us (1.030)
  waiting for transfers between devices: 90.4 us -> 101 us
  starting transfers between devices: 25 us -> 22.3 us
    ppermute x1, waiting for transfers between devices: 0.01 us -> 9.49 us  [on_device(): hidden_other = lax.ppermute(hidden, 'tok', [(0, 1), (1, 0)])]
    ppermute x1, waiting for transfers between devices: 0.01 us -> 4.92 us  [on_device(): grad_other = lax.ppermute(grad_rows_pos, 'tok', [(0, 1), (1, 0)])]
    ppermute x1, waiting for transfers between devices: 5.14 us -> 0.37 us  [tree_sum(): x = x + lax.ppermute(x, ax, [(i, i ^ b) for i in range(n)])]
    dot_general x1 -> x2, matrix products: 6.78 us -> 5.37 us  [the longest x1 4.22 us: on_device(): lax.dot_general(grad_other, hidden_other, by_pos, preferred_element_type=...]
  transfers between devices with their start and end apart: 19 -> 19, of which waited for: 14 -> 18; matrix products, arithmetic and copies ran while one was open for 10% -> 10% of each run, Pallas kernels for 0% -> 0%
where the time goes in v8:
time: 204 us; the launch traced here: 203 us
  waiting for transfers between devices  101 us (50%)
  blocking collectives  39.1 us (19%)
  matrix products  26.5 us (13%)
  starting transfers between devices  22.3 us (11%)
  other arithmetic  7.09 us (3%)
  between operations  3.58 us (2%)
  local copies, waits for them, and re-layouts  3.43 us (2%)
    psum x1, blocking collectives, on_device(): summed = lax.psum(partial_value, 'wid')  39.1 us
    ppermute x1, waiting for transfers between devices, tok_pieces(): pieces.append(lax.ppermute(x, 'tok', perm))  32.5 us
    ppermute x6, waiting for transfers between devices, halving_steps(): x = keep + lax.ppermute(send, ax, [(k, k ^ b) for k in range(n)])  25.5 us
    ppermute x4, waiting for transfers between devices, doubling_gather(): other = lax.ppermute(x, ax, [(k, k ^ b) for k in range(n)])  21.8 us
    dot_general x4, matrix products, quarter_dots(): jnp.dot(dlogits, lax.dynamic_slice_in_dim(piece, sel * q_cols, q_cols, ax...  9.96 us
    ppermute x1, waiting for transfers between devices, on_device(): hidden_other = lax.ppermute(hidden, 'tok', [(0, 1), (1, 0)])  9.49 us
    ppermute x6, starting transfers between devices, halving_steps(): x = keep + lax.ppermute(send, ax, [(k, k ^ b) for k in range(n)])  8.2 us
    dot_general x2, matrix products, on_device(): lax.dot_general(cols, piece, (((1,), (1,)), ((), ())), preferred_element_...  7.57 us
  transfers between devices with their start and end apart: 19, of which 18 were waited for; matrix products, arithmetic and copies ran while one was open for 10% of the time, Pallas kernels for 0%

profile of v8, /device:TPU:0, one launch (start us, length us, event | category | flops | bytes accessed | tf_op | source)
XLA Modules:
  0.0 203.1 jit_solution(5887904071657516729)
XLA Ops:
  0.6 3.0 %collective-permute-start.2 = (bf16[1216,1792]{1,0:T(8,128)(2,1)}, bf16[1216,1792]{1,0:T(8,128)(2,1)}, u32[]{:S(2)}, u32[]{:S(2)}) collective-permute-start(bf16[1216,1792]{1,0:T(8,128)(2,1)} %param.7), channel_id=1, source_target_pairs={{0,16},{16,0},{1,17},{17,1},{2,18},{18,2},{3,19},{19,3},{4,20},{20... | collective-permute-start | bytes 13074440 | tf_op jit(solution)/shard_map/ppermute | solution.py:11
  3.6 3.6 %fusion.43 = f32[256,896]{1,0:T(8,128)S(1)} fusion(bf16[256,2048]{1,0:T(8,128)(2,1)} %param.5, bf16[896,2048]{1,0:T(8,128)(2,1)} %param.6), kind=kOutput, calls=%fused_computation.84 | convolution fusion | flops 939524096 | bytes 5636096 | tf_op jit(solution)/shard_map/dot_general | solution.py:101
  7.3 39.1 %all-reduce.1 = bf16[256,896]{1,0:T(8,128)(2,1)S(1)} all-reduce(f32[256,896]{1,0:T(8,128)S(1)} %fusion.43), channel_id=1, replica_groups=mesh['tok'=2,'voc'=4,'wid'=4] {'wid'}, use_global_device_ids=true, to_apply=%region_0.0 | all-reduce | flops 229376 | bytes 1376256 | tf_op jit(solution)/shard_map/psum | solution.py:104
  48.0 7.9 %collective-permute-done = bf16[256,896]{1,0:T(8,128)(2,1)S(1)} collective-permute-done((bf16[256,896]{1,0:T(8,128)(2,1)S(1)}, bf16[256,896]{1,0:T(8,128)(2,1)S(1)}, u32[]{:S(2)}, u32[]{:S(2)}) %collective-permute-start) | collective-permute-done | bytes 458784 | tf_op jit(solution)/shard_map/ppermute | solution.py:82
  59.1 2.4 %copy.8 = bf16[256,4,896]{0,2,1:T(8,128)(2,1)} copy(bf16[256,4,896]{2,0,1:T(8,128)(2,1)S(1)} %bitcast.82) | data formatting | bytes 3670016 | tf_op jit(solution)/shard_map/transpose | solution.py:107
  61.5 4.0 %fusion.21 = f32[256,1216]{0,1:T(8,128)S(1)} fusion(bf16[1216,1792]{1,0:T(8,128)(2,1)} %param.7, bf16[256,3584]{0,1:T(8,128)(2,1)} %bitcast.88, s32[]{:T(128)S(6)} %select_n.171), kind=kOutput, calls=%fused_computation.24 | convolution fusion | flops 1115684864 | bytes 6520836 | tf_op jit(solution)/shard_map/dot_general | solution.py:114
  65.5 32.5 %collective-permute-done.2 = bf16[1216,1792]{1,0:T(8,128)(2,1)} collective-permute-done((bf16[1216,1792]{1,0:T(8,128)(2,1)}, bf16[1216,1792]{1,0:T(8,128)(2,1)}, u32[]{:S(2)}, u32[]{:S(2)}) %collective-permute-start.2) | collective-permute-done | bytes 4358176 | tf_op jit(solution)/shard_map/ppermute | solution.py:11
  98.0 3.6 %fusion.42 = (f32[256]{0:T(256)S(1)}, f32[256,1216]{0,1:T(8,128)S(1)}) fusion(f32[256,1216]{0,1:T(8,128)S(1)} %fusion.21, bf16[1216,1792]{1,0:T(8,128)(2,1)} %collective-permute-done.2, bf16[256,3584]{0,1:T(8,128)(2,1)S(1)} %bitcast.89, s32[]{:T(128)S(6)} %select_n.173), kind=kOutput, calls=%fused_computation.83 | convolution fusion | flops 1116307200 | bytes 7767044 | tf_op jit(solution)/shard_map/dot_general | solution.py:114
  110.7 2.9 %collective-permute-start.6 = (f32[3,256]{1,0:T(4,128)S(1)}, f32[3,256]{1,0:T(4,128)S(1)}, u32[]{:S(2)}, u32[]{:S(2)}) collective-permute-start(f32[3,256]{1,0:T(4,128)S(1)} %pad_maximum_fusion.5), channel_id=1, source_target_pairs={{0,2},{1,3},{2,0},{3,1},{4,6},{5,7},{6,4},{7,5},{8,10},{9,11},{10,... | collective-permute-start | bytes 9224 | tf_op jit(solution)/shard_map/ppermute | solution.py:33
  116.2 2.5 %fusion.14 = f32[1,256,896]{2,1,0:T(8,128)S(1)} fusion(bf16[256,1216]{0,1:T(8,128)(2,1)S(1)} %multiply_convert_fusion, bf16[1216,1792]{1,0:T(8,128)(2,1)} %param.7, s32[]{:T(128)S(6)} %select_n.176), kind=kOutput, calls=%fused_computation.15 | convolution fusion | flops 557842432 | bytes 3719172 | tf_op jit(solution)/shard_map/dot_general | solution.py:158
  118.7 2.5 %fusion.17 = f32[1,256,896]{2,1,0:T(8,128)S(1)} fusion(bf16[256,1216]{0,1:T(8,128)(2,1)S(1)} %multiply_convert_fusion, bf16[1216,1792]{1,0:T(8,128)(2,1)} %collective-permute-done.2, s32[]{:T(128)S(6)} %select_n.176), kind=kOutput, calls=%fused_computation.16 | convolution fusion | flops 557842432 | bytes 3719172 | tf_op jit(solution)/shard_map/dot_general | solution.py:158
  121.5 2.5 %fusion.8 = f32[1,256,896]{2,1,0:T(8,128)S(1)} fusion(bf16[256,1216]{0,1:T(8,128)(2,1)S(1)} %multiply_convert_fusion, bf16[1216,1792]{1,0:T(8,128)(2,1)} %param.7, s32[]{:T(128)S(6)} %select_n.175), kind=kOutput, calls=%fused_computation.13 | convolution fusion | flops 557842432 | bytes 3719172 | tf_op jit(solution)/shard_map/dot_general | solution.py:158
  124.0 2.5 %fusion.11 = f32[1,256,896]{2,1,0:T(8,128)S(1)} fusion(bf16[256,1216]{0,1:T(8,128)(2,1)S(1)} %multiply_convert_fusion, bf16[1216,1792]{1,0:T(8,128)(2,1)} %collective-permute-done.2, s32[]{:T(128)S(6)} %select_n.175), kind=kOutput, calls=%fused_computation.14 | convolution fusion | flops 557842432 | bytes 3719172 | tf_op jit(solution)/shard_map/dot_general | solution.py:158
  136.6 4.8 %collective-permute-done.9 = f32[2,2,32,896]{3,2,1,0:T(8,128)S(1)} collective-permute-done((f32[2,2,32,896]{3,2,1,0:T(8,128)S(1)}, f32[2,2,32,896]{3,2,1,0:T(8,128)S(1)}, u32[]{:S(2)}, u32[]{:S(2)}) %collective-permute-start.9) | collective-permute-done | bytes 458784 | tf_op jit(solution)/shard_map/ppermute | solution.py:71
  143.4 3.3 %collective-permute-done.12 = f32[2,2,32,896]{3,2,1,0:T(8,128)S(1)} collective-permute-done((f32[2,2,32,896]{3,2,1,0:T(8,128)S(1)}, f32[2,2,32,896]{3,2,1,0:T(8,128)S(1)}, u32[]{:S(2)}, u32[]{:S(2)}) %collective-permute-start.12) | collective-permute-done | bytes 458784 | tf_op jit(solution)/shard_map/ppermute | solution.py:71
  146.8 2.7 %collective-permute-start.13 = (f32[2,32,896]{2,1,0:T(8,128)S(1)}, f32[2,32,896]{2,1,0:T(8,128)S(1)}, u32[]{:S(2)}, u32[]{:S(2)}) collective-permute-start(f32[2,32,896]{2,1,0:T(8,128)S(1)} %dynamic-slice_bitcast_fusion.2), channel_id=1, source_target_pairs={{0,2},{1,3},{2,0},{3,1},{4,6},{5,7},{6,4},{7,5},{8,10},{9,11},{10,... | collective-permute-start | bytes 688136 | tf_op jit(solution)/shard_map/ppermute | solution.py:71
  149.5 4.8 %collective-permute-done.10 = f32[2,32,896]{2,1,0:T(8,128)S(1)} collective-permute-done((f32[2,32,896]{2,1,0:T(8,128)S(1)}, f32[2,32,896]{2,1,0:T(8,128)S(1)}, u32[]{:S(2)}, u32[]{:S(2)}) %collective-permute-start.10) | collective-permute-done | bytes 229408 | tf_op jit(solution)/shard_map/ppermute | solution.py:71
  154.4 7.8 %collective-permute-done.13 = f32[2,32,896]{2,1,0:T(8,128)S(1)} collective-permute-done((f32[2,32,896]{2,1,0:T(8,128)S(1)}, f32[2,32,896]{2,1,0:T(8,128)S(1)}, u32[]{:S(2)}, u32[]{:S(2)}) %collective-permute-start.13) | collective-permute-done | bytes 229408 | tf_op jit(solution)/shard_map/ppermute | solution.py:71
  163.6 3.5 %collective-permute-done.14 = f32[32,896]{1,0:T(8,128)S(1)} collective-permute-done((f32[32,896]{1,0:T(8,128)S(1)}, f32[32,896]{1,0:T(8,128)S(1)}, u32[]{:S(2)}, u32[]{:S(2)}) %collective-permute-start.14) | collective-permute-done | bytes 114720 | tf_op jit(solution)/shard_map/ppermute | solution.py:71
  167.4 6.6 %collective-permute-done.15 = bf16[64,896]{1,0:T(8,128)(2,1)S(1)} collective-permute-done((bf16[64,896]{1,0:T(8,128)(2,1)S(1)}, bf16[64,896]{1,0:T(8,128)(2,1)S(1)}, u32[]{:S(2)}, u32[]{:S(2)}) %collective-permute-start.15) | collective-permute-done | bytes 114720 | tf_op jit(solution)/shard_map/ppermute | solution.py:82
  175.1 5.0 %collective-permute-done.16 = bf16[2,64,896]{2,1,0:T(8,128)(2,1)S(1)} collective-permute-done((bf16[2,64,896]{2,1,0:T(8,128)(2,1)S(1)}, bf16[2,64,896]{2,1,0:T(8,128)(2,1)S(1)}, u32[]{:S(2)}, u32[]{:S(2)}) %collective-permute-start.16) | collective-permute-done | bytes 229408 | tf_op jit(solution)/shard_map/ppermute | solution.py:82
  183.3 9.5 %collective-permute-done.18 = bf16[256,2048]{1,0:T(8,128)(2,1)S(1)} collective-permute-done((bf16[256,2048]{1,0:T(8,128)(2,1)S(1)}, bf16[256,2048]{1,0:T(8,128)(2,1)S(1)}, u32[]{:S(2)}, u32[]{:S(2)}) %collective-permute-start.18) | collective-permute-done | bytes 1048608 | tf_op jit(solution)/shard_map/ppermute | solution.py:99
  192.8 4.9 %collective-permute-done.17 = bf16[256,896]{1,0:T(8,128)(2,1)S(1)} collective-permute-done((bf16[256,896]{1,0:T(8,128)(2,1)S(1)}, bf16[256,896]{1,0:T(8,128)(2,1)S(1)}, u32[]{:S(2)}, u32[]{:S(2)}) %collective-permute-start.17) | collective-permute-done | bytes 458784 | tf_op jit(solution)/shard_map/ppermute | solution.py:230
  197.8 4.2 %convolution_add_fusion = f32[896,2048]{1,0:T(8,128)} fusion(f32[896,2048]{1,0:T(8,128)S(1)} %fusion.44, bf16[256,896]{1,0:T(8,128)(2,1)S(1)} %collective-permute-done.17, bf16[256,2048]{1,0:T(8,128)(2,1)S(1)} %collective-permute-done.18), kind=kOutput, calls=%fused_computation | convolution fusion | flops 941359104 | bytes 16187392 | tf_op jit(solution)/shard_map/dot_general | solution.py:234
  (72 shorter events, 33.3 us)
Async XLA Ops:
  0.6 97.4 %collective-permute-start.2 = (bf16[1216,1792]{1,0:T(8,128)(2,1)}, bf16[1216,1792]{1,0:T(8,128)(2,1)}, u32[]{:S(2)}, u32[]{:S(2)}) collective-permute-start(bf16[1216,1792]{1,0:T(8,128)(2,1)} %param.7), channel_id=1, source_target_pairs={{0,16},{16,0},{1,17},{17,1},{2,18},{18,2},{3,19},{19,3},{4,20},{20... | collective-permute-start | bytes 13074440 | tf_op jit(solution)/shard_map/ppermute | solution.py:11
  7.3 48.9 %copy-start.3 = (s32[256]{0:T(256)S(1)}, s32[256]{0:T(256)}, u32[]{:S(2)}) copy-start(s32[256]{0:T(256)} %param.8) | copy-start | bytes 3076
  46.4 9.5 %collective-permute-start = (bf16[256,896]{1,0:T(8,128)(2,1)S(1)}, bf16[256,896]{1,0:T(8,128)(2,1)S(1)}, u32[]{:S(2)}, u32[]{:S(2)}) collective-permute-start(bf16[256,896]{1,0:T(8,128)(2,1)S(1)} %all-reduce.1), channel_id=1, source_target_pairs={{0,8},{4,12},{8,0},{12,4},{1,9},{5,13},{9,1},{13,5},{2,10},{6,14},... | collective-permute-start | bytes 1376264 | tf_op jit(solution)/shard_map/ppermute | solution.py:82
  56.1 2.5 %collective-permute-start.1 = (bf16[2,256,896]{2,1,0:T(8,128)(2,1)S(1)}, bf16[2,256,896]{2,1,0:T(8,128)(2,1)S(1)}, u32[]{:S(2)}, u32[]{:S(2)}) collective-permute-start(bf16[2,256,896]{2,1,0:T(8,128)(2,1)S(1)} %maximum_select_fusion.2), channel_id=1, source_target_pairs={{0,4},{4,0},{8,12},{12,8},{1,5},{5,1},{9,13},{13,9},{2,6},{6,2},{1... | collective-permute-start | bytes 2752520 | tf_op jit(solution)/shard_map/ppermute | solution.py:82
  61.5 36.5 %copy-start = (bf16[256,4,896]{0,2,1:T(8,128)(2,1)S(1)}, bf16[256,4,896]{0,2,1:T(8,128)(2,1)}, u32[]{:S(2)}) copy-start(bf16[256,4,896]{0,2,1:T(8,128)(2,1)} %copy.8) | copy-start | bytes 5505028
  65.5 48.1 %copy-start.2 = (s32[256]{0:T(256)S(1)}, s32[256]{0:T(256)}, u32[]{:S(2)}) copy-start(s32[256]{0:T(256)} %param.9) | copy-start | bytes 3076
  102.0 1.2 collective-permute-start.3
  103.3 3.7 %collective-permute-start.4 = (f32[3,256]{1,0:T(4,128)S(1)}, f32[3,256]{1,0:T(4,128)S(1)}, u32[]{:S(2)}, u32[]{:S(2)}) collective-permute-start(f32[3,256]{1,0:T(4,128)S(1)} %pad_maximum_fusion.3), channel_id=1, source_target_pairs={{0,8},{4,12},{8,0},{12,4},{1,9},{5,13},{9,1},{13,5},{2,10},{6,14},... | collective-permute-start | bytes 9224 | tf_op jit(solution)/shard_map/ppermute | solution.py:33
  107.0 3.7 %collective-permute-start.5 = (f32[3,256]{1,0:T(4,128)S(1)}, f32[3,256]{1,0:T(4,128)S(1)}, u32[]{:S(2)}, u32[]{:S(2)}) collective-permute-start(f32[3,256]{1,0:T(4,128)S(1)} %pad_maximum_fusion.4), channel_id=1, source_target_pairs={{0,1},{1,0},{2,3},{3,2},{4,5},{5,4},{6,7},{7,6},{8,9},{9,8},{10,11... | collective-permute-start | bytes 9224 | tf_op jit(solution)/shard_map/ppermute | solution.py:33
  110.7 4.6 %collective-permute-start.6 = (f32[3,256]{1,0:T(4,128)S(1)}, f32[3,256]{1,0:T(4,128)S(1)}, u32[]{:S(2)}, u32[]{:S(2)}) collective-permute-start(f32[3,256]{1,0:T(4,128)S(1)} %pad_maximum_fusion.5), channel_id=1, source_target_pairs={{0,2},{1,3},{2,0},{3,1},{4,6},{5,7},{6,4},{7,5},{8,10},{9,11},{10,... | collective-permute-start | bytes 9224 | tf_op jit(solution)/shard_map/ppermute | solution.py:33
  121.4 5.2 %collective-permute-start.8 = (f32[2,256,896]{2,1,0:T(8,128)S(1)}, f32[2,256,896]{2,1,0:T(8,128)}, u32[]{:S(2)}, u32[]{:S(2)}) collective-permute-start(f32[2,256,896]{2,1,0:T(8,128)S(1)} %pad_maximum_fusion), channel_id=1, source_target_pairs={{0,4},{4,0},{8,12},{12,8},{1,5},{5,1},{9,13},{13,9},{2,6},{6,2},{1... | collective-permute-start | bytes 5505032 | tf_op jit(solution)/shard_map/ppermute | solution.py:168
  128.5 12.9 %collective-permute-start.9 = (f32[2,2,32,896]{3,2,1,0:T(8,128)S(1)}, f32[2,2,32,896]{3,2,1,0:T(8,128)S(1)}, u32[]{:S(2)}, u32[]{:S(2)}) collective-permute-start(f32[2,2,32,896]{3,2,1,0:T(8,128)S(1)} %dynamic-slice_bitcast_fusion.1), channel_id=1, source_target_pairs={{0,8},{4,12},{8,0},{12,4},{1,9},{5,13},{9,1},{13,5},{2,10},{6,14},... | collective-permute-start | bytes 1376264 | tf_op jit(solution)/shard_map/ppermute | solution.py:71
  131.7 3.5 %collective-permute-start.7 = (f32[2]{0:T(128)S(1)}, f32[2]{0:T(128)S(1)}, u32[]{:S(2)}, u32[]{:S(2)}) collective-permute-start(f32[2]{0:T(128)S(1)} %pad_maximum_fusion.6), channel_id=1, source_target_pairs={{0,16},{16,0},{1,17},{17,1},{2,18},{18,2},{3,19},{19,3},{4,20},{20... | collective-permute-start | bytes 32 | tf_op jit(solution)/shard_map/ppermute | solution.py:45
  133.2 13.5 %collective-permute-start.12 = (f32[2,2,32,896]{3,2,1,0:T(8,128)S(1)}, f32[2,2,32,896]{3,2,1,0:T(8,128)S(1)}, u32[]{:S(2)}, u32[]{:S(2)}) collective-permute-start(f32[2,2,32,896]{3,2,1,0:T(8,128)S(1)} %dynamic-slice_bitcast_fusion), channel_id=1, source_target_pairs={{0,1},{1,0},{2,3},{3,2},{4,5},{5,4},{6,7},{7,6},{8,9},{9,8},{10,11... | collective-permute-start | bytes 1376264 | tf_op jit(solution)/shard_map/ppermute | solution.py:71
  141.5 12.7 %collective-permute-start.10 = (f32[2,32,896]{2,1,0:T(8,128)S(1)}, f32[2,32,896]{2,1,0:T(8,128)S(1)}, u32[]{:S(2)}, u32[]{:S(2)}) collective-permute-start(f32[2,32,896]{2,1,0:T(8,128)S(1)} %dynamic-slice_bitcast_fusion.3), channel_id=1, source_target_pairs={{0,1},{1,0},{2,3},{3,2},{4,5},{5,4},{6,7},{7,6},{8,9},{9,8},{10,11... | collective-permute-start | bytes 688136 | tf_op jit(solution)/shard_map/ppermute | solution.py:71
  146.8 20.5 %copy-start.1 = (bf16[256,2048]{1,0:T(8,128)(2,1)S(1)}, bf16[256,2048]{1,0:T(8,128)(2,1)}, u32[]{:S(2)}) copy-start(bf16[256,2048]{1,0:T(8,128)(2,1)} %param.5) | copy-start | bytes 3145732
  146.8 15.5 %collective-permute-start.13 = (f32[2,32,896]{2,1,0:T(8,128)S(1)}, f32[2,32,896]{2,1,0:T(8,128)S(1)}, u32[]{:S(2)}, u32[]{:S(2)}) collective-permute-start(f32[2,32,896]{2,1,0:T(8,128)S(1)} %dynamic-slice_bitcast_fusion.2), channel_id=1, source_target_pairs={{0,2},{1,3},{2,0},{3,1},{4,6},{5,7},{6,4},{7,5},{8,10},{9,11},{10,... | collective-permute-start | bytes 688136 | tf_op jit(solution)/shard_map/ppermute | solution.py:71
  154.3 9.3 %collective-permute-start.11 = (f32[32,896]{1,0:T(8,128)S(1)}, f32[32,896]{1,0:T(8,128)S(1)}, u32[]{:S(2)}, u32[]{:S(2)}) collective-permute-start(f32[32,896]{1,0:T(8,128)S(1)} %dynamic-slice_bitcast_fusion.5), channel_id=1, source_target_pairs={{0,2},{1,3},{2,0},{3,1},{4,6},{5,7},{6,4},{7,5},{8,10},{9,11},{10,... | collective-permute-start | bytes 344072 | tf_op jit(solution)/shard_map/ppermute | solution.py:71
  162.3 4.9 %collective-permute-start.14 = (f32[32,896]{1,0:T(8,128)S(1)}, f32[32,896]{1,0:T(8,128)S(1)}, u32[]{:S(2)}, u32[]{:S(2)}) collective-permute-start(f32[32,896]{1,0:T(8,128)S(1)} %dynamic-slice_bitcast_fusion.4), channel_id=1, source_target_pairs={{0,8},{4,12},{8,0},{12,4},{1,9},{5,13},{9,1},{13,5},{2,10},{6,14},... | collective-permute-start | bytes 344072 | tf_op jit(solution)/shard_map/ppermute | solution.py:71
  167.2 6.8 %collective-permute-start.15 = (bf16[64,896]{1,0:T(8,128)(2,1)S(1)}, bf16[64,896]{1,0:T(8,128)(2,1)S(1)}, u32[]{:S(2)}, u32[]{:S(2)}) collective-permute-start(bf16[64,896]{1,0:T(8,128)(2,1)S(1)} %pad_maximum_fusion.1), channel_id=1, source_target_pairs={{0,2},{1,3},{2,0},{3,1},{4,6},{5,7},{6,4},{7,5},{8,10},{9,11},{10,... | collective-permute-start | bytes 344072 | tf_op jit(solution)/shard_map/ppermute | solution.py:82
  167.3 25.5 %collective-permute-start.18 = (bf16[256,2048]{1,0:T(8,128)(2,1)S(1)}, bf16[256,2048]{1,0:T(8,128)(2,1)S(1)}, u32[]{:S(2)}, u32[]{:S(2)}) collective-permute-start(bf16[256,2048]{1,0:T(8,128)(2,1)S(1)} %copy-done.1), channel_id=1, source_target_pairs={{0,16},{16,0},{1,17},{17,1},{2,18},{18,2},{3,19},{19,3},{4,20},{20... | collective-permute-start | bytes 3145736 | tf_op jit(solution)/shard_map/ppermute | solution.py:99
  174.0 6.1 %collective-permute-start.16 = (bf16[2,64,896]{2,1,0:T(8,128)(2,1)S(1)}, bf16[2,64,896]{2,1,0:T(8,128)(2,1)S(1)}, u32[]{:S(2)}, u32[]{:S(2)}) collective-permute-start(bf16[2,64,896]{2,1,0:T(8,128)(2,1)S(1)} %maximum_select_fusion.5), channel_id=1, source_target_pairs={{0,1},{1,0},{2,3},{3,2},{4,5},{5,4},{6,7},{7,6},{8,9},{9,8},{10,11... | collective-permute-start | bytes 688136 | tf_op jit(solution)/shard_map/ppermute | solution.py:82
  180.2 17.6 %collective-permute-start.17 = (bf16[256,896]{1,0:T(8,128)(2,1)S(1)}, bf16[256,896]{1,0:T(8,128)(2,1)S(1)}, u32[]{:S(2)}, u32[]{:S(2)}) collective-permute-start(bf16[256,896]{1,0:T(8,128)(2,1)S(1)} %bitcast.86), channel_id=1, source_target_pairs={{0,16},{16,0},{1,17},{17,1},{2,18},{18,2},{3,19},{19,3},{4,20},{20... | collective-permute-start | bytes 1376264 | tf_op jit(solution)/shard_map/ppermute | solution.py:230

commit v9 on v8

--- a/solution.py
+++ b/solution.py
@@ -180,7 +180,6 @@
         part_a = halving_steps(blocks[..., :half, :], dims, rest_voc + wid_bits, bits)
         part_b = halving_steps(blocks[..., half:, :], dims, wid_bits + rest_voc, bits)
         mine = jnp.concatenate([part_a, part_b], axis=0).astype(jnp.bfloat16)
-        sums, mine = lax.optimization_barrier((sums, mine))
         grad_rows_pos = doubling_gather(mine, "wid").reshape((tok_rows, q_cols))
     elif grad_path:
         stacked = jnp.stack(

time: 204 us -> 193 us (0.946)
  waiting for transfers between devices: 101 us -> 84.8 us
  starting transfers between devices: 22.3 us -> 26.3 us
    ppermute x1, waiting for transfers between devices: 9.49 us -> 0.01 us  [on_device(): hidden_other = lax.ppermute(hidden, 'tok', [(0, 1), (1, 0)])]
    ppermute x6, waiting for transfers between devices: 25.5 us -> 22 us  [halving_steps(): x = keep + lax.ppermute(send, ax, [(k, k ^ b) for k in range(n)])]
    ppermute x4, waiting for transfers between devices: 21.8 us -> 18.4 us  [doubling_gather(): other = lax.ppermute(x, ax, [(k, k ^ b) for k in range(n)])]
  transfers between devices with their start and end apart: 19 -> 19, of which waited for: 18 -> 15; matrix products, arithmetic and copies ran while one was open for 10% -> 11% of each run, Pallas kernels for 0% -> 0%
where the time goes in v9:
time: 193 us
  waiting for transfers between devices  84.8 us (44%)
  blocking collectives  39.1 us (20%)
  matrix products  27.8 us (14%)
  starting transfers between devices  26.3 us (14%)
  other arithmetic  8.11 us (4%)
  between operations  3.51 us (2%)
  local copies, waits for them, and re-layouts  3.44 us (2%)
    psum x1, blocking collectives, on_device(): summed = lax.psum(partial_value, 'wid')  39.1 us
    ppermute x1, waiting for transfers between devices, tok_pieces(): pieces.append(lax.ppermute(x, 'tok', perm))  32.5 us
    ppermute x6, waiting for transfers between devices, halving_steps(): x = keep + lax.ppermute(send, ax, [(k, k ^ b) for k in range(n)])  22 us
    ppermute x4, waiting for transfers between devices, doubling_gather(): other = lax.ppermute(x, ax, [(k, k ^ b) for k in range(n)])  18.4 us
    dot_general x4, matrix products, quarter_dots(): jnp.dot(dlogits, lax.dynamic_slice_in_dim(piece, sel * q_cols, q_cols, ax...  10 us
    ppermute x6, starting transfers between devices, halving_steps(): x = keep + lax.ppermute(send, ax, [(k, k ^ b) for k in range(n)])  9.81 us
    dot_general x2, matrix products, on_device(): lax.dot_general(cols, piece, (((1,), (1,)), ((), ())), preferred_element_...  7.57 us
    ppermute x4, starting transfers between devices, butterfly(): other = lax.ppermute(stats, ax, [(i, i ^ b) for i in range(n)])  6.69 us
  transfers between devices with their start and end apart: 19, of which 15 were waited for; matrix products, arithmetic and copies ran while one was open for 11% of the time, Pallas kernels for 0%

profile of v9, /device:TPU:0, one launch (start us, length us, event | category | flops | bytes accessed | tf_op | source)
XLA Modules:
  0.0 193.0 jit_solution(17181969509838601987)
XLA Ops:
  0.6 3.0 %collective-permute-start.2 = (bf16[1216,1792]{1,0:T(8,128)(2,1)}, bf16[1216,1792]{1,0:T(8,128)(2,1)}, u32[]{:S(2)}, u32[]{:S(2)}) collective-permute-start(bf16[1216,1792]{1,0:T(8,128)(2,1)} %param.7), channel_id=1, source_target_pairs={{0,16},{16,0},{1,17},{17,1},{2,18},{18,2},{3,19},{19,3},{4,20},{20... | collective-permute-start | bytes 13074440 | tf_op jit(solution)/shard_map/ppermute | solution.py:11
  3.6 3.6 %fusion.43 = f32[256,896]{1,0:T(8,128)S(1)} fusion(bf16[256,2048]{1,0:T(8,128)(2,1)} %param.5, bf16[896,2048]{1,0:T(8,128)(2,1)} %param.6), kind=kOutput, calls=%fused_computation.85 | convolution fusion | flops 939524096 | bytes 5636096 | tf_op jit(solution)/shard_map/dot_general | solution.py:101
  7.3 39.1 %all-reduce.1 = bf16[256,896]{1,0:T(8,128)(2,1)S(1)} all-reduce(f32[256,896]{1,0:T(8,128)S(1)} %fusion.43), channel_id=1, replica_groups=mesh['tok'=2,'voc'=4,'wid'=4] {'wid'}, use_global_device_ids=true, to_apply=%region_0.0 | all-reduce | flops 229376 | bytes 1376256 | tf_op jit(solution)/shard_map/psum | solution.py:104
  48.0 7.9 %collective-permute-done = bf16[256,896]{1,0:T(8,128)(2,1)S(1)} collective-permute-done((bf16[256,896]{1,0:T(8,128)(2,1)S(1)}, bf16[256,896]{1,0:T(8,128)(2,1)S(1)}, u32[]{:S(2)}, u32[]{:S(2)}) %collective-permute-start) | collective-permute-done | bytes 458784 | tf_op jit(solution)/shard_map/ppermute | solution.py:82
  56.4 2.2 %collective-permute-done.1 = bf16[2,256,896]{2,1,0:T(8,128)(2,1)S(1)} collective-permute-done((bf16[2,256,896]{2,1,0:T(8,128)(2,1)S(1)}, bf16[2,256,896]{2,1,0:T(8,128)(2,1)S(1)}, u32[]{:S(2)}, u32[]{:S(2)}) %collective-permute-start.1) | collective-permute-done | bytes 917536 | tf_op jit(solution)/shard_map/ppermute | solution.py:82
  59.1 2.4 %copy.8 = bf16[256,4,896]{0,2,1:T(8,128)(2,1)} copy(bf16[256,4,896]{2,0,1:T(8,128)(2,1)S(1)} %bitcast.84) | data formatting | bytes 3670016 | tf_op jit(solution)/shard_map/transpose | solution.py:107
  61.5 4.0 %fusion.21 = f32[256,1216]{0,1:T(8,128)S(1)} fusion(bf16[1216,1792]{1,0:T(8,128)(2,1)} %param.7, bf16[256,3584]{0,1:T(8,128)(2,1)} %bitcast.90, s32[]{:T(128)S(6)} %select_n.171), kind=kOutput, calls=%fused_computation.24 | convolution fusion | flops 1115684864 | bytes 6520836 | tf_op jit(solution)/shard_map/dot_general | solution.py:114
  65.5 32.5 %collective-permute-done.2 = bf16[1216,1792]{1,0:T(8,128)(2,1)} collective-permute-done((bf16[1216,1792]{1,0:T(8,128)(2,1)}, bf16[1216,1792]{1,0:T(8,128)(2,1)}, u32[]{:S(2)}, u32[]{:S(2)}) %collective-permute-start.2) | collective-permute-done | bytes 4358176 | tf_op jit(solution)/shard_map/ppermute | solution.py:11
  98.0 3.6 %fusion.42 = (f32[256]{0:T(256)S(1)}, f32[256,1216]{0,1:T(8,128)S(1)}) fusion(f32[256,1216]{0,1:T(8,128)S(1)} %fusion.21, bf16[1216,1792]{1,0:T(8,128)(2,1)} %collective-permute-done.2, bf16[256,3584]{0,1:T(8,128)(2,1)S(1)} %bitcast.91, s32[]{:T(128)S(6)} %select_n.173), kind=kOutput, calls=%fused_computation.84 | convolution fusion | flops 1116307200 | bytes 7767044 | tf_op jit(solution)/shard_map/dot_general | solution.py:114
  110.7 2.9 %collective-permute-start.6 = (f32[3,256]{1,0:T(4,128)S(1)}, f32[3,256]{1,0:T(4,128)S(1)}, u32[]{:S(2)}, u32[]{:S(2)}) collective-permute-start(f32[3,256]{1,0:T(4,128)S(1)} %pad_maximum_fusion.5), channel_id=1, source_target_pairs={{0,2},{1,3},{2,0},{3,1},{4,6},{5,7},{6,4},{7,5},{8,10},{9,11},{10,... | collective-permute-start | bytes 9224 | tf_op jit(solution)/shard_map/ppermute | solution.py:33
  116.2 2.5 %fusion.14 = f32[1,256,896]{2,1,0:T(8,128)S(1)} fusion(bf16[256,1216]{0,1:T(8,128)(2,1)S(1)} %multiply_convert_fusion, bf16[1216,1792]{1,0:T(8,128)(2,1)} %param.7, s32[]{:T(128)S(6)} %select_n.176), kind=kOutput, calls=%fused_computation.15 | convolution fusion | flops 557842432 | bytes 3719172 | tf_op jit(solution)/shard_map/dot_general | solution.py:158
  118.7 2.5 %fusion.17 = f32[1,256,896]{2,1,0:T(8,128)S(1)} fusion(bf16[256,1216]{0,1:T(8,128)(2,1)S(1)} %multiply_convert_fusion, bf16[1216,1792]{1,0:T(8,128)(2,1)} %collective-permute-done.2, s32[]{:T(128)S(6)} %select_n.176), kind=kOutput, calls=%fused_computation.16 | convolution fusion | flops 557842432 | bytes 3719172 | tf_op jit(solution)/shard_map/dot_general | solution.py:158
  121.5 2.5 %fusion.8 = f32[1,256,896]{2,1,0:T(8,128)S(1)} fusion(bf16[256,1216]{0,1:T(8,128)(2,1)S(1)} %multiply_convert_fusion, bf16[1216,1792]{1,0:T(8,128)(2,1)} %param.7, s32[]{:T(128)S(6)} %select_n.175), kind=kOutput, calls=%fused_computation.13 | convolution fusion | flops 557842432 | bytes 3719172 | tf_op jit(solution)/shard_map/dot_general | solution.py:158
  124.0 2.5 %fusion.11 = f32[1,256,896]{2,1,0:T(8,128)S(1)} fusion(bf16[256,1216]{0,1:T(8,128)(2,1)S(1)} %multiply_convert_fusion, bf16[1216,1792]{1,0:T(8,128)(2,1)} %collective-permute-done.2, s32[]{:T(128)S(6)} %select_n.175), kind=kOutput, calls=%fused_computation.14 | convolution fusion | flops 557842432 | bytes 3719172 | tf_op jit(solution)/shard_map/dot_general | solution.py:158
  135.4 6.2 %collective-permute-done.8 = f32[2,2,32,896]{3,2,1,0:T(8,128)} collective-permute-done((f32[2,2,32,896]{3,2,1,0:T(8,128)S(1)}, f32[2,2,32,896]{3,2,1,0:T(8,128)}, u32[]{:S(2)}, u32[]{:S(2)}) %collective-permute-start.8) | collective-permute-done | bytes 458784 | tf_op jit(solution)/shard_map/ppermute | solution.py:71
  144.6 2.7 %collective-permute-start.12 = (f32[2,32,896]{2,1,0:T(8,128)S(1)}, f32[2,32,896]{2,1,0:T(8,128)S(1)}, u32[]{:S(2)}, u32[]{:S(2)}) collective-permute-start(f32[2,32,896]{2,1,0:T(8,128)S(1)} %dynamic-slice_bitcast_fusion.2), channel_id=1, source_target_pairs={{0,2},{1,3},{2,0},{3,1},{4,6},{5,7},{6,4},{7,5},{8,10},{9,11},{10,... | collective-permute-start | bytes 688136 | tf_op jit(solution)/shard_map/ppermute | solution.py:71
  147.3 7.3 %collective-permute-done.9 = f32[2,32,896]{2,1,0:T(8,128)S(1)} collective-permute-done((f32[2,32,896]{2,1,0:T(8,128)S(1)}, f32[2,32,896]{2,1,0:T(8,128)S(1)}, u32[]{:S(2)}, u32[]{:S(2)}) %collective-permute-start.9) | collective-permute-done | bytes 229408 | tf_op jit(solution)/shard_map/ppermute | solution.py:71
  154.9 5.3 %collective-permute-done.12 = f32[2,32,896]{2,1,0:T(8,128)S(1)} collective-permute-done((f32[2,32,896]{2,1,0:T(8,128)S(1)}, f32[2,32,896]{2,1,0:T(8,128)S(1)}, u32[]{:S(2)}, u32[]{:S(2)}) %collective-permute-start.12) | collective-permute-done | bytes 229408 | tf_op jit(solution)/shard_map/ppermute | solution.py:71
  162.4 2.6 %collective-permute-done.13 = f32[32,896]{1,0:T(8,128)S(1)} collective-permute-done((f32[32,896]{1,0:T(8,128)S(1)}, f32[32,896]{1,0:T(8,128)S(1)}, u32[]{:S(2)}, u32[]{:S(2)}) %collective-permute-start.13) | collective-permute-done | bytes 114720 | tf_op jit(solution)/shard_map/ppermute | solution.py:71
  166.6 4.4 %collective-permute-done.14 = bf16[64,896]{1,0:T(8,128)(2,1)S(1)} collective-permute-done((bf16[64,896]{1,0:T(8,128)(2,1)S(1)}, bf16[64,896]{1,0:T(8,128)(2,1)S(1)}, u32[]{:S(2)}, u32[]{:S(2)}) %collective-permute-start.14) | collective-permute-done | bytes 114720 | tf_op jit(solution)/shard_map/ppermute | solution.py:82
  171.0 2.9 %collective-permute-start.15 = (bf16[2,64,896]{2,1,0:T(8,128)(2,1)S(1)}, bf16[2,64,896]{2,1,0:T(8,128)(2,1)S(1)}, u32[]{:S(2)}, u32[]{:S(2)}) collective-permute-start(bf16[2,64,896]{2,1,0:T(8,128)(2,1)S(1)} %maximum_select_fusion.5), channel_id=1, source_target_pairs={{0,1},{1,0},{2,3},{3,2},{4,5},{5,4},{6,7},{7,6},{8,9},{9,8},{10,11... | collective-permute-start | bytes 688136 | tf_op jit(solution)/shard_map/ppermute | solution.py:82
  173.9 3.9 %collective-permute-done.15 = bf16[2,64,896]{2,1,0:T(8,128)(2,1)S(1)} collective-permute-done((bf16[2,64,896]{2,1,0:T(8,128)(2,1)S(1)}, bf16[2,64,896]{2,1,0:T(8,128)(2,1)S(1)}, u32[]{:S(2)}, u32[]{:S(2)}) %collective-permute-start.15) | collective-permute-done | bytes 229408 | tf_op jit(solution)/shard_map/ppermute | solution.py:82
  181.1 5.4 %collective-permute-done.16 = bf16[256,896]{1,0:T(8,128)(2,1)S(1)} collective-permute-done((bf16[256,896]{1,0:T(8,128)(2,1)S(1)}, bf16[256,896]{1,0:T(8,128)(2,1)S(1)}, u32[]{:S(2)}, u32[]{:S(2)}) %collective-permute-start.16) | collective-permute-done | bytes 458784 | tf_op jit(solution)/shard_map/ppermute | solution.py:229
  186.4 5.4 %convolution_add_fusion = f32[896,2048]{1,0:T(8,128)} fusion(f32[896,2048]{1,0:T(8,128)S(1)} %fusion.44, bf16[256,896]{1,0:T(8,128)(2,1)S(1)} %collective-permute-done.16, bf16[256,2048]{1,0:T(8,128)(2,1)} %collective-permute-done.17), kind=kOutput, calls=%fused_computation | convolution fusion | flops 941359104 | bytes 16187392 | tf_op jit(solution)/shard_map/dot_general | solution.py:233
  (73 shorter events, 32.2 us)
Async XLA Ops:
  0.6 97.4 %collective-permute-start.2 = (bf16[1216,1792]{1,0:T(8,128)(2,1)}, bf16[1216,1792]{1,0:T(8,128)(2,1)}, u32[]{:S(2)}, u32[]{:S(2)}) collective-permute-start(bf16[1216,1792]{1,0:T(8,128)(2,1)} %param.7), channel_id=1, source_target_pairs={{0,16},{16,0},{1,17},{17,1},{2,18},{18,2},{3,19},{19,3},{4,20},{20... | collective-permute-start | bytes 13074440 | tf_op jit(solution)/shard_map/ppermute | solution.py:11
  7.3 48.9 %copy-start.3 = (s32[256]{0:T(256)S(1)}, s32[256]{0:T(256)}, u32[]{:S(2)}) copy-start(s32[256]{0:T(256)} %param.8) | copy-start | bytes 3076
  46.4 9.5 %collective-permute-start = (bf16[256,896]{1,0:T(8,128)(2,1)S(1)}, bf16[256,896]{1,0:T(8,128)(2,1)S(1)}, u32[]{:S(2)}, u32[]{:S(2)}) collective-permute-start(bf16[256,896]{1,0:T(8,128)(2,1)S(1)} %all-reduce.1), channel_id=1, source_target_pairs={{0,8},{4,12},{8,0},{12,4},{1,9},{5,13},{9,1},{13,5},{2,10},{6,14},... | collective-permute-start | bytes 1376264 | tf_op jit(solution)/shard_map/ppermute | solution.py:82
  56.1 2.5 %collective-permute-start.1 = (bf16[2,256,896]{2,1,0:T(8,128)(2,1)S(1)}, bf16[2,256,896]{2,1,0:T(8,128)(2,1)S(1)}, u32[]{:S(2)}, u32[]{:S(2)}) collective-permute-start(bf16[2,256,896]{2,1,0:T(8,128)(2,1)S(1)} %maximum_select_fusion.2), channel_id=1, source_target_pairs={{0,4},{4,0},{8,12},{12,8},{1,5},{5,1},{9,13},{13,9},{2,6},{6,2},{1... | collective-permute-start | bytes 2752520 | tf_op jit(solution)/shard_map/ppermute | solution.py:82
  61.5 36.5 %copy-start = (bf16[256,4,896]{0,2,1:T(8,128)(2,1)S(1)}, bf16[256,4,896]{0,2,1:T(8,128)(2,1)}, u32[]{:S(2)}) copy-start(bf16[256,4,896]{0,2,1:T(8,128)(2,1)} %copy.8) | copy-start | bytes 5505028
  65.5 48.1 %copy-start.2 = (s32[256]{0:T(256)S(1)}, s32[256]{0:T(256)}, u32[]{:S(2)}) copy-start(s32[256]{0:T(256)} %param.9) | copy-start | bytes 3076
  102.0 1.2 collective-permute-start.3
  103.3 3.7 %collective-permute-start.4 = (f32[3,256]{1,0:T(4,128)S(1)}, f32[3,256]{1,0:T(4,128)S(1)}, u32[]{:S(2)}, u32[]{:S(2)}) collective-permute-start(f32[3,256]{1,0:T(4,128)S(1)} %pad_maximum_fusion.3), channel_id=1, source_target_pairs={{0,8},{4,12},{8,0},{12,4},{1,9},{5,13},{9,1},{13,5},{2,10},{6,14},... | collective-permute-start | bytes 9224 | tf_op jit(solution)/shard_map/ppermute | solution.py:33
  107.0 3.7 %collective-permute-start.5 = (f32[3,256]{1,0:T(4,128)S(1)}, f32[3,256]{1,0:T(4,128)S(1)}, u32[]{:S(2)}, u32[]{:S(2)}) collective-permute-start(f32[3,256]{1,0:T(4,128)S(1)} %pad_maximum_fusion.4), channel_id=1, source_target_pairs={{0,1},{1,0},{2,3},{3,2},{4,5},{5,4},{6,7},{7,6},{8,9},{9,8},{10,11... | collective-permute-start | bytes 9224 | tf_op jit(solution)/shard_map/ppermute | solution.py:33
  110.7 4.6 %collective-permute-start.6 = (f32[3,256]{1,0:T(4,128)S(1)}, f32[3,256]{1,0:T(4,128)S(1)}, u32[]{:S(2)}, u32[]{:S(2)}) collective-permute-start(f32[3,256]{1,0:T(4,128)S(1)} %pad_maximum_fusion.5), channel_id=1, source_target_pairs={{0,2},{1,3},{2,0},{3,1},{4,6},{5,7},{6,4},{7,5},{8,10},{9,11},{10,... | collective-permute-start | bytes 9224 | tf_op jit(solution)/shard_map/ppermute | solution.py:33
  121.4 5.1 %collective-permute-start.7 = (f32[2,256,896]{2,1,0:T(8,128)S(1)}, f32[2,256,896]{2,1,0:T(8,128)}, u32[]{:S(2)}, u32[]{:S(2)}) collective-permute-start(f32[2,256,896]{2,1,0:T(8,128)S(1)} %pad_maximum_fusion), channel_id=1, source_target_pairs={{0,4},{4,0},{8,12},{12,8},{1,5},{5,1},{9,13},{13,9},{2,6},{6,2},{1... | collective-permute-start | bytes 5505032 | tf_op jit(solution)/shard_map/ppermute | solution.py:168
  128.3 2.0 %copy-start.1 = (bf16[256,2048]{1,0:T(8,128)(2,1)S(1)}, bf16[256,2048]{1,0:T(8,128)(2,1)}, u32[]{:S(2)}) copy-start(bf16[256,2048]{1,0:T(8,128)(2,1)} %param.5) | copy-start | bytes 3145732
  128.5 13.1 %collective-permute-start.8 = (f32[2,2,32,896]{3,2,1,0:T(8,128)S(1)}, f32[2,2,32,896]{3,2,1,0:T(8,128)}, u32[]{:S(2)}, u32[]{:S(2)}) collective-permute-start(f32[2,2,32,896]{3,2,1,0:T(8,128)S(1)} %dynamic-slice_bitcast_fusion.1), channel_id=1, source_target_pairs={{0,8},{4,12},{8,0},{12,4},{1,9},{5,13},{9,1},{13,5},{2,10},{6,14},... | collective-permute-start | bytes 1376264 | tf_op jit(solution)/shard_map/ppermute | solution.py:71
  130.3 50.7 %collective-permute-start.17 = (bf16[256,2048]{1,0:T(8,128)(2,1)S(1)}, bf16[256,2048]{1,0:T(8,128)(2,1)}, u32[]{:S(2)}, u32[]{:S(2)}) collective-permute-start(bf16[256,2048]{1,0:T(8,128)(2,1)S(1)} %copy-done.1), channel_id=1, source_target_pairs={{0,16},{16,0},{1,17},{17,1},{2,18},{18,2},{3,19},{19,3},{4,20},{20... | collective-permute-start | bytes 3145736 | tf_op jit(solution)/shard_map/ppermute | solution.py:99
  131.8 12.7 %collective-permute-start.11 = (f32[2,2,32,896]{3,2,1,0:T(8,128)S(1)}, f32[2,2,32,896]{3,2,1,0:T(8,128)S(1)}, u32[]{:S(2)}, u32[]{:S(2)}) collective-permute-start(f32[2,2,32,896]{3,2,1,0:T(8,128)S(1)} %dynamic-slice_bitcast_fusion), channel_id=1, source_target_pairs={{0,1},{1,0},{2,3},{3,2},{4,5},{5,4},{6,7},{7,6},{8,9},{9,8},{10,11... | collective-permute-start | bytes 1376264 | tf_op jit(solution)/shard_map/ppermute | solution.py:71
  134.9 30.3 %collective-permute-start.18 = (f32[2]{0:T(128)S(1)}, f32[2]{0:T(128)S(1)}, u32[]{:S(2)}, u32[]{:S(2)}) collective-permute-start(f32[2]{0:T(128)S(1)} %pad_maximum_fusion.6), channel_id=1, source_target_pairs={{0,16},{16,0},{1,17},{17,1},{2,18},{18,2},{3,19},{19,3},{4,20},{20... | collective-permute-start | bytes 32 | tf_op jit(solution)/shard_map/ppermute | solution.py:45
  142.7 11.9 %collective-permute-start.9 = (f32[2,32,896]{2,1,0:T(8,128)S(1)}, f32[2,32,896]{2,1,0:T(8,128)S(1)}, u32[]{:S(2)}, u32[]{:S(2)}) collective-permute-start(f32[2,32,896]{2,1,0:T(8,128)S(1)} %dynamic-slice_bitcast_fusion.3), channel_id=1, source_target_pairs={{0,1},{1,0},{2,3},{3,2},{4,5},{5,4},{6,7},{7,6},{8,9},{9,8},{10,11... | collective-permute-start | bytes 688136 | tf_op jit(solution)/shard_map/ppermute | solution.py:71
  144.6 15.5 %collective-permute-start.12 = (f32[2,32,896]{2,1,0:T(8,128)S(1)}, f32[2,32,896]{2,1,0:T(8,128)S(1)}, u32[]{:S(2)}, u32[]{:S(2)}) collective-permute-start(f32[2,32,896]{2,1,0:T(8,128)S(1)} %dynamic-slice_bitcast_fusion.2), channel_id=1, source_target_pairs={{0,2},{1,3},{2,0},{3,1},{4,6},{5,7},{6,4},{7,5},{8,10},{9,11},{10,... | collective-permute-start | bytes 688136 | tf_op jit(solution)/shard_map/ppermute | solution.py:71
  154.7 7.7 %collective-permute-start.10 = (f32[32,896]{1,0:T(8,128)S(1)}, f32[32,896]{1,0:T(8,128)S(1)}, u32[]{:S(2)}, u32[]{:S(2)}) collective-permute-start(f32[32,896]{1,0:T(8,128)S(1)} %dynamic-slice_bitcast_fusion.5), channel_id=1, source_target_pairs={{0,2},{1,3},{2,0},{3,1},{4,6},{5,7},{6,4},{7,5},{8,10},{9,11},{10,... | collective-permute-start | bytes 344072 | tf_op jit(solution)/shard_map/ppermute | solution.py:71
  160.2 4.9 %collective-permute-start.13 = (f32[32,896]{1,0:T(8,128)S(1)}, f32[32,896]{1,0:T(8,128)S(1)}, u32[]{:S(2)}, u32[]{:S(2)}) collective-permute-start(f32[32,896]{1,0:T(8,128)S(1)} %dynamic-slice_bitcast_fusion.4), channel_id=1, source_target_pairs={{0,8},{4,12},{8,0},{12,4},{1,9},{5,13},{9,1},{13,5},{2,10},{6,14},... | collective-permute-start | bytes 344072 | tf_op jit(solution)/shard_map/ppermute | solution.py:71
  165.1 5.8 %collective-permute-start.14 = (bf16[64,896]{1,0:T(8,128)(2,1)S(1)}, bf16[64,896]{1,0:T(8,128)(2,1)S(1)}, u32[]{:S(2)}, u32[]{:S(2)}) collective-permute-start(bf16[64,896]{1,0:T(8,128)(2,1)S(1)} %pad_maximum_fusion.1), channel_id=1, source_target_pairs={{0,2},{1,3},{2,0},{3,1},{4,6},{5,7},{6,4},{7,5},{8,10},{9,11},{10,... | collective-permute-start | bytes 344072 | tf_op jit(solution)/shard_map/ppermute | solution.py:82
  171.0 6.9 %collective-permute-start.15 = (bf16[2,64,896]{2,1,0:T(8,128)(2,1)S(1)}, bf16[2,64,896]{2,1,0:T(8,128)(2,1)S(1)}, u32[]{:S(2)}, u32[]{:S(2)}) collective-permute-start(bf16[2,64,896]{2,1,0:T(8,128)(2,1)S(1)} %maximum_select_fusion.5), channel_id=1, source_target_pairs={{0,1},{1,0},{2,3},{3,2},{4,5},{5,4},{6,7},{7,6},{8,9},{9,8},{10,11... | collective-permute-start | bytes 688136 | tf_op jit(solution)/shard_map/ppermute | solution.py:82
  177.9 8.5 %collective-permute-start.16 = (bf16[256,896]{1,0:T(8,128)(2,1)S(1)}, bf16[256,896]{1,0:T(8,128)(2,1)S(1)}, u32[]{:S(2)}, u32[]{:S(2)}) collective-permute-start(bf16[256,896]{1,0:T(8,128)(2,1)S(1)} %bitcast.88), channel_id=1, source_target_pairs={{0,16},{16,0},{1,17},{17,1},{2,18},{18,2},{3,19},{19,3},{4,20},{20... | collective-permute-start | bytes 1376264 | tf_op jit(solution)/shard_map/ppermute | solution.py:229

commit v10 on v9

--- a/solution.py
+++ b/solution.py
@@ -36,6 +36,30 @@
     return stats
 
 
+def shift_gather(x, axes):
+    sizes = [lax.axis_size(ax) for ax in axes]
+    n = 1
+    lin = 0
+    for ax, size in zip(axes, sizes):
+        n *= size
+        lin = lin * size + lax.axis_index(ax)
+    got = [x]
+    for sh in range(1, n):
+        got.append(lax.ppermute(x, tuple(axes), [(k, (k + sh) % n) for k in range(n)]))
+    rev = jnp.stack([got[(-j) % n] for j in range(n)])
+    return jnp.roll(rev, lin, axis=0)
+
+
+def gather_combine(stats, axes):
+    for ax in axes:
+        g = shift_gather(stats, (ax,))
+        out = g[0]
+        for k in range(1, g.shape[0]):
+            out = combine(out, g[k])
+        stats = out
+    return stats
+
+
 def tree_sum(x, ax):
     n = lax.axis_size(ax)
     if n & (n - 1):
@@ -125,7 +149,7 @@
     weight = valid.astype(jnp.float32)
 
     stats = jnp.stack([peak_here, exp_here, picked_here])
-    stats = butterfly(stats, ("voc", "wid"))
+    stats = gather_combine(stats, ("voc", "wid"))
     log_total = stats[0] + jnp.log(stats[1])
     picked = stats[2]
     sums = jnp.stack([jnp.sum(weight * (log_total - picked)), jnp.sum(weight)])
@@ -137,6 +161,7 @@
 
     n_voc, n_wid = lax.axis_size("voc"), lax.axis_size("wid")
     grad_rows_pos = None
+    grad_all = None
     grad_path = (
         n_tok == 2
         and n_voc >= 2
@@ -180,7 +205,7 @@
         part_a = halving_steps(blocks[..., :half, :], dims, rest_voc + wid_bits, bits)
         part_b = halving_steps(blocks[..., half:, :], dims, wid_bits + rest_voc, bits)
         mine = jnp.concatenate([part_a, part_b], axis=0).astype(jnp.bfloat16)
-        grad_rows_pos = doubling_gather(mine, "wid").reshape((tok_rows, q_cols))
+        grad_all = shift_gather(mine, ("tok", "wid")).reshape((n_tok * tok_rows, q_cols))
     elif grad_path:
         stacked = jnp.stack(
             [
@@ -225,7 +250,16 @@
         reduced = lax.psum_scatter(full_rows, "voc", scatter_dimension=0, tiled=True)
         grad_rows_t = lax.psum(reduced, "wid").astype(jnp.bfloat16)
 
-    if grad_rows_pos is not None:
+    if grad_all is not None:
+        hidden_all = jnp.where(
+            t == 0,
+            jnp.concatenate([hidden, hidden_other], axis=0),
+            jnp.concatenate([hidden_other, hidden], axis=0),
+        )
+        grad_proj = lax.dot_general(
+            grad_all, hidden_all, (((0,), (0,)), ((), ())), preferred_element_type=jnp.float32
+        )
+    elif grad_rows_pos is not None:
         grad_other = lax.ppermute(grad_rows_pos, "tok", [(0, 1), (1, 0)])
         by_pos = (((0,), (0,)), ((), ()))
         grad_proj = lax.dot_general(

time: 193 us -> 216 us (1.12)
  waiting for transfers between devices: 84.8 us -> 105 us
    ppermute x5 -> x13, waiting for transfers between devices: 11.8 us -> 28.8 us  [shift_gather(): lax.ppermute(x, tuple(axes), [(k, (k + sh) % n) for k in range(n)])]
    ppermute x1, waiting for transfers between devices: 0.01 us -> 14.2 us  [tree_sum(): x = x + lax.ppermute(x, ax, [(i, i ^ b) for i in range(n)])]
    ppermute x5 -> x13, starting transfers between devices: 6.76 us -> 18.4 us  [shift_gather(): lax.ppermute(x, tuple(axes), [(k, (k + sh) % n) for k in range(n)])]
    ppermute x4 -> x2, waiting for transfers between devices: 18.4 us -> 10.1 us  [doubling_gather(): other = lax.ppermute(x, ax, [(k, k ^ b) for k in range(n)])]
    ppermute x6, starting transfers between devices: 9.81 us -> 2.44 us  [halving_steps(): x = keep + lax.ppermute(send, ax, [(k, k ^ b) for k in range(n)])]
    ppermute x4 -> x2, starting transfers between devices: 4.58 us -> 1.65 us  [doubling_gather(): other = lax.ppermute(x, ax, [(k, k ^ b) for k in range(n)])]
    ppermute x6, waiting for transfers between devices: 22 us -> 19.4 us  [halving_steps(): x = keep + lax.ppermute(send, ax, [(k, k ^ b) for k in range(n)])]
    dot_general x2 -> x1, matrix products: 6.57 us -> 6.75 us  [on_device(): lax.dot_general(grad_all, hidden_all, (((0,), (0,)), ((), ())), preferred...]
  transfers between devices with their start and end apart: 19 -> 25, of which waited for: 15 -> 16; matrix products, arithmetic and copies ran while one was open for 11% -> 10% of each run, Pallas kernels for 0% -> 0%
where the time goes in v10:
time: 216 us; the launch traced here: 215 us
  waiting for transfers between devices  105 us (49%)
  blocking collectives  39.1 us (18%)
  matrix products  27.9 us (13%)
  starting transfers between devices  27.6 us (13%)
  other arithmetic  7.07 us (3%)
  local copies, waits for them, and re-layouts  4.76 us (2%)
  between operations  3.6 us (2%)
    psum x1, blocking collectives, on_device(): summed = lax.psum(partial_value, 'wid')  39.1 us
    ppermute x1, waiting for transfers between devices, tok_pieces(): pieces.append(lax.ppermute(x, 'tok', perm))  32.5 us
    ppermute x13, waiting for transfers between devices, shift_gather(): lax.ppermute(x, tuple(axes), [(k, (k + sh) % n) for k in range(n)])  28.8 us
    ppermute x6, waiting for transfers between devices, halving_steps(): x = keep + lax.ppermute(send, ax, [(k, k ^ b) for k in range(n)])  19.4 us
    ppermute x13, starting transfers between devices, shift_gather(): lax.ppermute(x, tuple(axes), [(k, (k + sh) % n) for k in range(n)])  18.4 us
    ppermute x1, waiting for transfers between devices, tree_sum(): x = x + lax.ppermute(x, ax, [(i, i ^ b) for i in range(n)])  14.2 us
    ppermute x2, waiting for transfers between devices, doubling_gather(): other = lax.ppermute(x, ax, [(k, k ^ b) for k in range(n)])  10.1 us
    dot_general x4, matrix products, quarter_dots(): jnp.dot(dlogits, lax.dynamic_slice_in_dim(piece, sel * q_cols, q_cols, ax...  9.95 us
  transfers between devices with their start and end apart: 25, of which 16 were waited for; matrix products, arithmetic and copies ran while one was open for 10% of the time, Pallas kernels for 0%

profile of v10, /device:TPU:0, one launch (start us, length us, event | category | flops | bytes accessed | tf_op | source)
XLA Modules:
  0.0 215.1 jit_solution(2150313114564372351)
XLA Ops:
  0.6 3.0 %collective-permute-start.2 = (bf16[1216,1792]{1,0:T(8,128)(2,1)}, bf16[1216,1792]{1,0:T(8,128)(2,1)}, u32[]{:S(2)}, u32[]{:S(2)}) collective-permute-start(bf16[1216,1792]{1,0:T(8,128)(2,1)} %param.9), channel_id=1, source_target_pairs={{0,16},{16,0},{1,17},{17,1},{2,18},{18,2},{3,19},{19,3},{4,20},{20... | collective-permute-start | bytes 13074440 | tf_op jit(solution)/shard_map/ppermute | solution.py:11
  3.6 3.6 %fusion.81 = f32[256,896]{1,0:T(8,128)S(1)} fusion(bf16[256,2048]{1,0:T(8,128)(2,1)} %param.7, bf16[896,2048]{1,0:T(8,128)(2,1)} %param.8), kind=kOutput, calls=%fused_computation.152 | convolution fusion | flops 939524096 | bytes 5636096 | tf_op jit(solution)/shard_map/dot_general | solution.py:125
  7.3 39.1 %all-reduce.1 = bf16[256,896]{1,0:T(8,128)(2,1)S(1)} all-reduce(f32[256,896]{1,0:T(8,128)S(1)} %fusion.81), channel_id=1, replica_groups=mesh['tok'=2,'voc'=4,'wid'=4] {'wid'}, use_global_device_ids=true, to_apply=%region_0.0 | all-reduce | flops 229376 | bytes 1376256 | tf_op jit(solution)/shard_map/psum | solution.py:128
  48.0 7.9 %collective-permute-done = bf16[256,896]{1,0:T(8,128)(2,1)S(1)} collective-permute-done((bf16[256,896]{1,0:T(8,128)(2,1)S(1)}, bf16[256,896]{1,0:T(8,128)(2,1)S(1)}, u32[]{:S(2)}, u32[]{:S(2)}) %collective-permute-start) | collective-permute-done | bytes 458784 | tf_op jit(solution)/shard_map/ppermute | solution.py:106
  61.5 4.0 %fusion.28 = f32[256,1216]{0,1:T(8,128)S(1)} fusion(bf16[1216,1792]{1,0:T(8,128)(2,1)} %param.9, bf16[256,3584]{0,1:T(8,128)(2,1)} %bitcast.182, s32[]{:T(128)S(6)} %select_n.156), kind=kOutput, calls=%fused_computation.31 | convolution fusion | flops 1115684864 | bytes 6520836 | tf_op jit(solution)/shard_map/dot_general | solution.py:138
  65.5 32.5 %collective-permute-done.2 = bf16[1216,1792]{1,0:T(8,128)(2,1)} collective-permute-done((bf16[1216,1792]{1,0:T(8,128)(2,1)}, bf16[1216,1792]{1,0:T(8,128)(2,1)}, u32[]{:S(2)}, u32[]{:S(2)}) %collective-permute-start.2) | collective-permute-done | bytes 4358176 | tf_op jit(solution)/shard_map/ppermute | solution.py:11
  98.0 3.6 %fusion.80 = (f32[256]{0:T(256)S(1)}, f32[256,1216]{0,1:T(8,128)S(1)}) fusion(f32[256,1216]{0,1:T(8,128)S(1)} %fusion.28, bf16[1216,1792]{1,0:T(8,128)(2,1)} %collective-permute-done.2, bf16[256,3584]{0,1:T(8,128)(2,1)S(1)} %bitcast.183, s32[]{:T(128)S(6)} %select_n.158), kind=kOutput, calls=%fused_computation.151 | convolution fusion | flops 1116307200 | bytes 7767044 | tf_op jit(solution)/shard_map/dot_general | solution.py:138
  107.0 2.7 %collective-permute-start.7 = (f32[3,256]{1,0:T(4,128)S(1)}, f32[3,256]{1,0:T(4,128)S(1)}, u32[]{:S(2)}, u32[]{:S(2)}) collective-permute-start(f32[3,256]{1,0:T(4,128)S(1)} %get-tuple-element.21), channel_id=1, source_target_pairs={{0,2},{1,3},{2,0},{3,1},{4,6},{5,7},{6,4},{7,5},{8,10},{9,11},{10,... | collective-permute-start | bytes 9224 | tf_op jit(solution)/shard_map/ppermute | solution.py:48
  113.2 3.1 %collective-permute-done.8 = f32[3,256]{1,0:T(4,128)S(1)} collective-permute-done((f32[3,256]{1,0:T(4,128)S(1)}, f32[3,256]{1,0:T(4,128)S(1)}, u32[]{:S(2)}, u32[]{:S(2)}) %collective-permute-start.8) | collective-permute-done | bytes 3104 | tf_op jit(solution)/shard_map/ppermute | solution.py:48
  117.4 2.5 %fusion.21 = f32[1,256,896]{2,1,0:T(8,128)S(1)} fusion(bf16[256,1216]{0,1:T(8,128)(2,1)S(1)} %multiply_convert_fusion, bf16[1216,1792]{1,0:T(8,128)(2,1)} %param.9, s32[]{:T(128)S(6)} %select_n.161), kind=kOutput, calls=%fused_computation.22 | convolution fusion | flops 557842432 | bytes 3719172 | tf_op jit(solution)/shard_map/dot_general | solution.py:183
  119.9 2.5 %fusion.24 = f32[1,256,896]{2,1,0:T(8,128)S(1)} fusion(bf16[256,1216]{0,1:T(8,128)(2,1)S(1)} %multiply_convert_fusion, bf16[1216,1792]{1,0:T(8,128)(2,1)} %collective-permute-done.2, s32[]{:T(128)S(6)} %select_n.161), kind=kOutput, calls=%fused_computation.23 | convolution fusion | flops 557842432 | bytes 3719172 | tf_op jit(solution)/shard_map/dot_general | solution.py:183
  129.5 2.5 %fusion.18 = f32[1,256,896]{2,1,0:T(8,128)S(1)} fusion(bf16[256,1216]{0,1:T(8,128)(2,1)S(1)} %multiply_convert_fusion, bf16[1216,1792]{1,0:T(8,128)(2,1)} %collective-permute-done.2, s32[]{:T(128)S(6)} %select_n.160), kind=kOutput, calls=%fused_computation.21 | convolution fusion | flops 557842432 | bytes 3719172 | tf_op jit(solution)/shard_map/dot_general | solution.py:183
  134.1 14.2 %collective-permute-done.24 = f32[2]{0:T(128)S(1)} collective-permute-done((f32[2]{0:T(128)S(1)}, f32[2]{0:T(128)S(1)}, u32[]{:S(2)}, u32[]{:S(2)}) %collective-permute-start.24) | collective-permute-done | bytes 40 | tf_op jit(solution)/shard_map/ppermute | solution.py:69
  152.5 8.3 %collective-permute-done.10 = f32[2,2,32,896]{3,2,1,0:T(8,128)S(1)} collective-permute-done((f32[2,2,32,896]{3,2,1,0:T(8,128)S(1)}, f32[2,2,32,896]{3,2,1,0:T(8,128)S(1)}, u32[]{:S(2)}, u32[]{:S(2)}) %collective-permute-start.10) | collective-permute-done | bytes 458784 | tf_op jit(solution)/shard_map/ppermute | solution.py:95
  164.1 3.3 %collective-permute-done.11 = f32[2,32,896]{2,1,0:T(8,128)S(1)} collective-permute-done((f32[2,32,896]{2,1,0:T(8,128)S(1)}, f32[2,32,896]{2,1,0:T(8,128)S(1)}, u32[]{:S(2)}, u32[]{:S(2)}) %collective-permute-start.11) | collective-permute-done | bytes 229408 | tf_op jit(solution)/shard_map/ppermute | solution.py:95
  167.5 6.3 %collective-permute-done.12 = f32[32,896]{1,0:T(8,128)S(1)} collective-permute-done((f32[32,896]{1,0:T(8,128)S(1)}, f32[32,896]{1,0:T(8,128)S(1)}, u32[]{:S(2)}, u32[]{:S(2)}) %collective-permute-start.12) | collective-permute-done | bytes 114720 | tf_op jit(solution)/shard_map/ppermute | solution.py:95
  173.9 2.9 %collective-permute-start.21 = (bf16[64,896]{1,0:T(8,128)(2,1)S(1)}, bf16[64,896]{1,0:T(8,128)(2,1)S(1)}, u32[]{:S(2)}, u32[]{:S(2)}) collective-permute-start(bf16[64,896]{1,0:T(8,128)(2,1)S(1)} %pad_maximum_fusion.1), channel_id=1, source_target_pairs={{0,2},{1,3},{2,16},{3,17},{16,18},{17,19},{18,0},{19,1},{4,6},{5,7... | collective-permute-start | bytes 344072 | tf_op jit(solution)/shard_map/ppermute | solution.py:48
  180.2 7.2 %collective-permute-done.16 = bf16[64,896]{1,0:T(8,128)(2,1)S(1)} collective-permute-done((bf16[64,896]{1,0:T(8,128)(2,1)S(1)}, bf16[64,896]{1,0:T(8,128)(2,1)S(1)}, u32[]{:S(2)}, u32[]{:S(2)}) %collective-permute-start.16) | collective-permute-done | bytes 114720 | tf_op jit(solution)/shard_map/ppermute | solution.py:48
  187.3 2.6 %collective-permute-start.17 = (bf16[64,896]{1,0:T(8,128)(2,1)S(1)}, bf16[64,896]{1,0:T(8,128)(2,1)S(1)}, u32[]{:S(2)}, u32[]{:S(2)}) collective-permute-start(bf16[64,896]{1,0:T(8,128)(2,1)S(1)} %pad_maximum_fusion.1), channel_id=1, source_target_pairs={{0,18},{1,19},{2,0},{3,1},{16,2},{17,3},{18,16},{19,17},{4,22},{5,... | collective-permute-start | bytes 344072 | tf_op jit(solution)/shard_map/ppermute | solution.py:48
  189.9 4.3 %collective-permute-done.17 = bf16[64,896]{1,0:T(8,128)(2,1)S(1)} collective-permute-done((bf16[64,896]{1,0:T(8,128)(2,1)S(1)}, bf16[64,896]{1,0:T(8,128)(2,1)S(1)}, u32[]{:S(2)}, u32[]{:S(2)}) %collective-permute-start.17) | collective-permute-done | bytes 114720 | tf_op jit(solution)/shard_map/ppermute | solution.py:48
  194.3 2.5 %collective-permute-start.18 = (bf16[64,896]{1,0:T(8,128)(2,1)S(1)}, bf16[64,896]{1,0:T(8,128)(2,1)S(1)}, u32[]{:S(2)}, u32[]{:S(2)}) collective-permute-start(bf16[64,896]{1,0:T(8,128)(2,1)S(1)} %pad_maximum_fusion.1), channel_id=1, source_target_pairs={{0,17},{1,18},{2,19},{3,0},{16,1},{17,2},{18,3},{19,16},{4,21},{5,... | collective-permute-start | bytes 344072 | tf_op jit(solution)/shard_map/ppermute | solution.py:48
  196.8 5.2 %collective-permute-done.18 = bf16[64,896]{1,0:T(8,128)(2,1)S(1)} collective-permute-done((bf16[64,896]{1,0:T(8,128)(2,1)S(1)}, bf16[64,896]{1,0:T(8,128)(2,1)S(1)}, u32[]{:S(2)}, u32[]{:S(2)}) %collective-permute-start.18) | collective-permute-done | bytes 114720 | tf_op jit(solution)/shard_map/ppermute | solution.py:48
  202.0 4.8 %collective-permute-done.19 = bf16[64,896]{1,0:T(8,128)(2,1)S(1)} collective-permute-done((bf16[64,896]{1,0:T(8,128)(2,1)S(1)}, bf16[64,896]{1,0:T(8,128)(2,1)S(1)}, u32[]{:S(2)}, u32[]{:S(2)}) %collective-permute-start.19) | collective-permute-done | bytes 114720 | tf_op jit(solution)/shard_map/ppermute | solution.py:48
  207.2 6.8 %fusion.8 = f32[896,2048]{1,0:T(8,128)} fusion(bf16[512,896]{1,0:T(8,128)(2,1)S(1)} %bitcast.190, bf16[256,2048]{1,0:T(8,128)(2,1)} %collective-permute-done.23, bf16[256,2048]{1,0:T(8,128)(2,1)S(1)} %copy-done.3, pred[]{:T(512)S(6)} %eq.34), kind=kOutput, calls=%fused_computation.10 | convolution fusion | flops 1888485376 | bytes 10354689 | tf_op jit(solution)/shard_map/dot_general | solution.py:259
  (96 shorter events, 36.2 us)
Async XLA Ops:
  0.6 97.4 %collective-permute-start.2 = (bf16[1216,1792]{1,0:T(8,128)(2,1)}, bf16[1216,1792]{1,0:T(8,128)(2,1)}, u32[]{:S(2)}, u32[]{:S(2)}) collective-permute-start(bf16[1216,1792]{1,0:T(8,128)(2,1)} %param.9), channel_id=1, source_target_pairs={{0,16},{16,0},{1,17},{17,1},{2,18},{18,2},{3,19},{19,3},{4,20},{20... | collective-permute-start | bytes 13074440 | tf_op jit(solution)/shard_map/ppermute | solution.py:11
  46.4 9.5 %collective-permute-start = (bf16[256,896]{1,0:T(8,128)(2,1)S(1)}, bf16[256,896]{1,0:T(8,128)(2,1)S(1)}, u32[]{:S(2)}, u32[]{:S(2)}) collective-permute-start(bf16[256,896]{1,0:T(8,128)(2,1)S(1)} %all-reduce.1), channel_id=1, source_target_pairs={{0,8},{4,12},{8,0},{12,4},{1,9},{5,13},{9,1},{13,5},{2,10},{6,14},... | collective-permute-start | bytes 1376264 | tf_op jit(solution)/shard_map/ppermute | solution.py:106
  56.1 2.5 %collective-permute-start.1 = (bf16[2,256,896]{2,1,0:T(8,128)(2,1)S(1)}, bf16[2,256,896]{2,1,0:T(8,128)(2,1)S(1)}, u32[]{:S(2)}, u32[]{:S(2)}) collective-permute-start(bf16[2,256,896]{2,1,0:T(8,128)(2,1)S(1)} %maximum_select_fusion.4), channel_id=1, source_target_pairs={{0,4},{4,0},{8,12},{12,8},{1,5},{5,1},{9,13},{13,9},{2,6},{6,2},{1... | collective-permute-start | bytes 2752520 | tf_op jit(solution)/shard_map/ppermute | solution.py:106
  102.0 3.7 %collective-permute-start.4 = (f32[3,256]{1,0:T(4,128)S(1)}, f32[3,256]{1,0:T(4,128)S(1)}, u32[]{:S(2)}, u32[]{:S(2)}) collective-permute-start(f32[3,256]{1,0:T(4,128)S(1)} %get-tuple-element.23), channel_id=1, source_target_pairs={{0,8},{4,12},{8,0},{12,4},{1,9},{5,13},{9,1},{13,5},{2,10},{6,14},... | collective-permute-start | bytes 9224 | tf_op jit(solution)/shard_map/ppermute | solution.py:48
  103.8 3.0 %collective-permute-start.5 = (f32[3,256]{1,0:T(4,128)S(1)}, f32[3,256]{1,0:T(4,128)S(1)}, u32[]{:S(2)}, u32[]{:S(2)}) collective-permute-start(f32[3,256]{1,0:T(4,128)S(1)} %get-tuple-element.23), channel_id=1, source_target_pairs={{0,4},{4,8},{8,12},{12,0},{1,5},{5,9},{9,13},{13,1},{2,6},{6,10},{... | collective-permute-start | bytes 9224 | tf_op jit(solution)/shard_map/ppermute | solution.py:48
  107.0 4.7 %collective-permute-start.7 = (f32[3,256]{1,0:T(4,128)S(1)}, f32[3,256]{1,0:T(4,128)S(1)}, u32[]{:S(2)}, u32[]{:S(2)}) collective-permute-start(f32[3,256]{1,0:T(4,128)S(1)} %get-tuple-element.21), channel_id=1, source_target_pairs={{0,2},{1,3},{2,0},{3,1},{4,6},{5,7},{6,4},{7,5},{8,10},{9,11},{10,... | collective-permute-start | bytes 9224 | tf_op jit(solution)/shard_map/ppermute | solution.py:48
  109.6 3.6 %collective-permute-start.6 = (f32[3,256]{1,0:T(4,128)S(1)}, f32[3,256]{1,0:T(4,128)S(1)}, u32[]{:S(2)}, u32[]{:S(2)}) collective-permute-start(f32[3,256]{1,0:T(4,128)S(1)} %get-tuple-element.21), channel_id=1, source_target_pairs={{0,3},{1,0},{2,1},{3,2},{4,7},{5,4},{6,5},{7,6},{8,11},{9,8},{10,9... | collective-permute-start | bytes 9224 | tf_op jit(solution)/shard_map/ppermute | solution.py:48
  111.0 5.4 %collective-permute-start.8 = (f32[3,256]{1,0:T(4,128)S(1)}, f32[3,256]{1,0:T(4,128)S(1)}, u32[]{:S(2)}, u32[]{:S(2)}) collective-permute-start(f32[3,256]{1,0:T(4,128)S(1)} %get-tuple-element.21), channel_id=1, source_target_pairs={{0,1},{1,2},{2,3},{3,0},{4,5},{5,6},{6,7},{7,4},{8,9},{9,10},{10,1... | collective-permute-start | bytes 9224 | tf_op jit(solution)/shard_map/ppermute | solution.py:48
  122.6 9.5 %collective-permute-start.9 = (f32[2,256,896]{2,1,0:T(8,128)S(1)}, f32[2,256,896]{2,1,0:T(8,128)}, u32[]{:S(2)}, u32[]{:S(2)}) collective-permute-start(f32[2,256,896]{2,1,0:T(8,128)S(1)} %pad_maximum_fusion), channel_id=1, source_target_pairs={{0,4},{4,0},{8,12},{12,8},{1,5},{5,1},{9,13},{13,9},{2,6},{6,2},{1... | collective-permute-start | bytes 5505032 | tf_op jit(solution)/shard_map/ppermute | solution.py:193
  123.7 83.6 %collective-permute-start.23 = (bf16[256,2048]{1,0:T(8,128)(2,1)S(1)}, bf16[256,2048]{1,0:T(8,128)(2,1)}, u32[]{:S(2)}, u32[]{:S(2)}) collective-permute-start(bf16[256,2048]{1,0:T(8,128)(2,1)S(1)} %copy-done.3), channel_id=1, source_target_pairs={{0,16},{16,0},{1,17},{17,1},{2,18},{18,2},{3,19},{19,3},{4,20},{20... | collective-permute-start | bytes 3145736 | tf_op jit(solution)/shard_map/ppermute | solution.py:123
  126.5 21.8 %collective-permute-start.24 = (f32[2]{0:T(128)S(1)}, f32[2]{0:T(128)S(1)}, u32[]{:S(2)}, u32[]{:S(2)}) collective-permute-start(f32[2]{0:T(128)S(1)} %pad_maximum_fusion.5), channel_id=1, source_target_pairs={{0,16},{16,0},{1,17},{17,1},{2,18},{18,2},{3,19},{19,3},{4,20},{20... | collective-permute-start | bytes 32 | tf_op jit(solution)/shard_map/ppermute | solution.py:69
  134.0 18.3 %collective-permute-start.13 = (f32[2,2,32,896]{3,2,1,0:T(8,128)S(1)}, f32[2,2,32,896]{3,2,1,0:T(8,128)S(1)}, u32[]{:S(2)}, u32[]{:S(2)}) collective-permute-start(f32[2,2,32,896]{3,2,1,0:T(8,128)S(1)} %dynamic-slice_bitcast_fusion), channel_id=1, source_target_pairs={{0,1},{1,0},{2,3},{3,2},{4,5},{5,4},{6,7},{7,6},{8,9},{9,8},{10,11... | collective-permute-start | bytes 1376264 | tf_op jit(solution)/shard_map/ppermute | solution.py:95
  149.7 11.1 %collective-permute-start.10 = (f32[2,2,32,896]{3,2,1,0:T(8,128)S(1)}, f32[2,2,32,896]{3,2,1,0:T(8,128)S(1)}, u32[]{:S(2)}, u32[]{:S(2)}) collective-permute-start(f32[2,2,32,896]{3,2,1,0:T(8,128)S(1)} %dynamic-slice_bitcast_fusion.1), channel_id=1, source_target_pairs={{0,8},{4,12},{8,0},{12,4},{1,9},{5,13},{9,1},{13,5},{2,10},{6,14},... | collective-permute-start | bytes 1376264 | tf_op jit(solution)/shard_map/ppermute | solution.py:95
  152.4 10.1 %collective-permute-start.14 = (f32[2,32,896]{2,1,0:T(8,128)S(1)}, f32[2,32,896]{2,1,0:T(8,128)S(1)}, u32[]{:S(2)}, u32[]{:S(2)}) collective-permute-start(f32[2,32,896]{2,1,0:T(8,128)S(1)} %dynamic-slice_bitcast_fusion.2), channel_id=1, source_target_pairs={{0,2},{1,3},{2,0},{3,1},{4,6},{5,7},{6,4},{7,5},{8,10},{9,11},{10,... | collective-permute-start | bytes 688136 | tf_op jit(solution)/shard_map/ppermute | solution.py:95
  160.9 6.4 %collective-permute-start.11 = (f32[2,32,896]{2,1,0:T(8,128)S(1)}, f32[2,32,896]{2,1,0:T(8,128)S(1)}, u32[]{:S(2)}, u32[]{:S(2)}) collective-permute-start(f32[2,32,896]{2,1,0:T(8,128)S(1)} %dynamic-slice_bitcast_fusion.3), channel_id=1, source_target_pairs={{0,1},{1,0},{2,3},{3,2},{4,5},{5,4},{6,7},{7,6},{8,9},{9,8},{10,11... | collective-permute-start | bytes 688136 | tf_op jit(solution)/shard_map/ppermute | solution.py:95
  162.6 4.9 %collective-permute-start.15 = (f32[32,896]{1,0:T(8,128)S(1)}, f32[32,896]{1,0:T(8,128)S(1)}, u32[]{:S(2)}, u32[]{:S(2)}) collective-permute-start(f32[32,896]{1,0:T(8,128)S(1)} %dynamic-slice_bitcast_fusion.4), channel_id=1, source_target_pairs={{0,8},{4,12},{8,0},{12,4},{1,9},{5,13},{9,1},{13,5},{2,10},{6,14},... | collective-permute-start | bytes 344072 | tf_op jit(solution)/shard_map/ppermute | solution.py:95
  167.4 6.4 %collective-permute-start.12 = (f32[32,896]{1,0:T(8,128)S(1)}, f32[32,896]{1,0:T(8,128)S(1)}, u32[]{:S(2)}, u32[]{:S(2)}) collective-permute-start(f32[32,896]{1,0:T(8,128)S(1)} %dynamic-slice_bitcast_fusion.5), channel_id=1, source_target_pairs={{0,2},{1,3},{2,0},{3,1},{4,6},{5,7},{6,4},{7,5},{8,10},{9,11},{10,... | collective-permute-start | bytes 344072 | tf_op jit(solution)/shard_map/ppermute | solution.py:95
  173.8 33.1 %collective-permute-start.22 = (bf16[64,896]{1,0:T(8,128)(2,1)S(1)}, bf16[64,896]{1,0:T(8,128)(2,1)S(1)}, u32[]{:S(2)}, u32[]{:S(2)}) collective-permute-start(bf16[64,896]{1,0:T(8,128)(2,1)S(1)} %pad_maximum_fusion.1), channel_id=1, source_target_pairs={{0,1},{1,2},{2,3},{3,16},{16,17},{17,18},{18,19},{19,0},{4,5},{5,6... | collective-permute-start | bytes 344072 | tf_op jit(solution)/shard_map/ppermute | solution.py:48
  173.9 33.0 %collective-permute-start.21 = (bf16[64,896]{1,0:T(8,128)(2,1)S(1)}, bf16[64,896]{1,0:T(8,128)(2,1)S(1)}, u32[]{:S(2)}, u32[]{:S(2)}) collective-permute-start(bf16[64,896]{1,0:T(8,128)(2,1)S(1)} %pad_maximum_fusion.1), channel_id=1, source_target_pairs={{0,2},{1,3},{2,16},{3,17},{16,18},{17,19},{18,0},{19,1},{4,6},{5,7... | collective-permute-start | bytes 344072 | tf_op jit(solution)/shard_map/ppermute | solution.py:48
  176.8 30.0 %collective-permute-start.20 = (bf16[64,896]{1,0:T(8,128)(2,1)S(1)}, bf16[64,896]{1,0:T(8,128)(2,1)S(1)}, u32[]{:S(2)}, u32[]{:S(2)}) collective-permute-start(bf16[64,896]{1,0:T(8,128)(2,1)S(1)} %pad_maximum_fusion.1), channel_id=1, source_target_pairs={{0,3},{1,16},{2,17},{3,18},{16,19},{17,0},{18,1},{19,2},{4,7},{5,2... | collective-permute-start | bytes 344072 | tf_op jit(solution)/shard_map/ppermute | solution.py:48
  178.6 8.7 %collective-permute-start.16 = (bf16[64,896]{1,0:T(8,128)(2,1)S(1)}, bf16[64,896]{1,0:T(8,128)(2,1)S(1)}, u32[]{:S(2)}, u32[]{:S(2)}) collective-permute-start(bf16[64,896]{1,0:T(8,128)(2,1)S(1)} %pad_maximum_fusion.1), channel_id=1, source_target_pairs={{0,19},{1,0},{2,1},{3,2},{16,3},{17,16},{18,17},{19,18},{4,23},{5,... | collective-permute-start | bytes 344072 | tf_op jit(solution)/shard_map/ppermute | solution.py:48
  187.3 6.9 %collective-permute-start.17 = (bf16[64,896]{1,0:T(8,128)(2,1)S(1)}, bf16[64,896]{1,0:T(8,128)(2,1)S(1)}, u32[]{:S(2)}, u32[]{:S(2)}) collective-permute-start(bf16[64,896]{1,0:T(8,128)(2,1)S(1)} %pad_maximum_fusion.1), channel_id=1, source_target_pairs={{0,18},{1,19},{2,0},{3,1},{16,2},{17,3},{18,16},{19,17},{4,22},{5,... | collective-permute-start | bytes 344072 | tf_op jit(solution)/shard_map/ppermute | solution.py:48
  194.3 7.8 %collective-permute-start.18 = (bf16[64,896]{1,0:T(8,128)(2,1)S(1)}, bf16[64,896]{1,0:T(8,128)(2,1)S(1)}, u32[]{:S(2)}, u32[]{:S(2)}) collective-permute-start(bf16[64,896]{1,0:T(8,128)(2,1)S(1)} %pad_maximum_fusion.1), channel_id=1, source_target_pairs={{0,17},{1,18},{2,19},{3,0},{16,1},{17,2},{18,3},{19,16},{4,21},{5,... | collective-permute-start | bytes 344072 | tf_op jit(solution)/shard_map/ppermute | solution.py:48
  202.0 4.8 %collective-permute-start.19 = (bf16[64,896]{1,0:T(8,128)(2,1)S(1)}, bf16[64,896]{1,0:T(8,128)(2,1)S(1)}, u32[]{:S(2)}, u32[]{:S(2)}) collective-permute-start(bf16[64,896]{1,0:T(8,128)(2,1)S(1)} %pad_maximum_fusion.1), channel_id=1, source_target_pairs={{0,16},{1,17},{2,18},{3,19},{16,0},{17,1},{18,2},{19,3},{4,20},{5,... | collective-permute-start | bytes 344072 | tf_op jit(solution)/shard_map/ppermute | solution.py:48
  (5 other events, 134.7 us)

commit v11 on v9

--- a/solution.py
+++ b/solution.py
@@ -178,7 +178,7 @@
         half = tok_rows // n_wid // 2
         rest_voc = voc_bits[1:]
         part_a = halving_steps(blocks[..., :half, :], dims, rest_voc + wid_bits, bits)
-        part_b = halving_steps(blocks[..., half:, :], dims, wid_bits + rest_voc, bits)
+        part_b = halving_steps(blocks[..., half:, :], dims, wid_bits[:1] + rest_voc + wid_bits[1:], bits)
         mine = jnp.concatenate([part_a, part_b], axis=0).astype(jnp.bfloat16)
         grad_rows_pos = doubling_gather(mine, "wid").reshape((tok_rows, q_cols))
     elif grad_path:

time: 193 us -> 193 us (level)
    ppermute x4, waiting for transfers between devices: 18.4 us -> 22.8 us  [doubling_gather(): other = lax.ppermute(x, ax, [(k, k ^ b) for k in range(n)])]
    ppermute x6, waiting for transfers between devices: 22 us -> 18 us  [halving_steps(): x = keep + lax.ppermute(send, ax, [(k, k ^ b) for k in range(n)])]
    ppermute x4, starting transfers between devices: 4.58 us -> 1.79 us  [doubling_gather(): other = lax.ppermute(x, ax, [(k, k ^ b) for k in range(n)])]
  transfers between devices with their start and end apart: 19 -> 19, of which waited for: 15 -> 14; matrix products, arithmetic and copies ran while one was open for 11% -> 11% of each run, Pallas kernels for 0% -> 0%
where the time goes in v11:
time: 193 us; the launch traced here: 192 us
  waiting for transfers between devices  83.7 us (43%)
  blocking collectives  39.1 us (20%)
  matrix products  27.8 us (14%)
  starting transfers between devices  26.3 us (14%)
  other arithmetic  8.11 us (4%)
  between operations  3.52 us (2%)
  local copies, waits for them, and re-layouts  3.43 us (2%)
    psum x1, blocking collectives, on_device(): summed = lax.psum(partial_value, 'wid')  39.1 us
    ppermute x1, waiting for transfers between devices, tok_pieces(): pieces.append(lax.ppermute(x, 'tok', perm))  32.5 us
    ppermute x4, waiting for transfers between devices, doubling_gather(): other = lax.ppermute(x, ax, [(k, k ^ b) for k in range(n)])  22.8 us
    ppermute x6, waiting for transfers between devices, halving_steps(): x = keep + lax.ppermute(send, ax, [(k, k ^ b) for k in range(n)])  18 us
    ppermute x6, starting transfers between devices, halving_steps(): x = keep + lax.ppermute(send, ax, [(k, k ^ b) for k in range(n)])  11.2 us
    dot_general x4, matrix products, quarter_dots(): jnp.dot(dlogits, lax.dynamic_slice_in_dim(piece, sel * q_cols, q_cols, ax...  10 us
    dot_general x2, matrix products, on_device(): lax.dot_general(cols, piece, (((1,), (1,)), ((), ())), preferred_element_...  7.57 us
    ppermute x4, starting transfers between devices, butterfly(): other = lax.ppermute(stats, ax, [(i, i ^ b) for i in range(n)])  6.69 us
  transfers between devices with their start and end apart: 19, of which 14 were waited for; matrix products, arithmetic and copies ran while one was open for 11% of the time, Pallas kernels for 0%

profile of v11, /device:TPU:0, one launch (start us, length us, event | category | flops | bytes accessed | tf_op | source)
XLA Modules:
  0.0 192.0 jit_solution(17848873315624167992)
XLA Ops:
  0.6 3.0 %collective-permute-start.2 = (bf16[1216,1792]{1,0:T(8,128)(2,1)}, bf16[1216,1792]{1,0:T(8,128)(2,1)}, u32[]{:S(2)}, u32[]{:S(2)}) collective-permute-start(bf16[1216,1792]{1,0:T(8,128)(2,1)} %param.7), channel_id=1, source_target_pairs={{0,16},{16,0},{1,17},{17,1},{2,18},{18,2},{3,19},{19,3},{4,20},{20... | collective-permute-start | bytes 13074440 | tf_op jit(solution)/shard_map/ppermute | solution.py:11
  3.6 3.6 %fusion.43 = f32[256,896]{1,0:T(8,128)S(1)} fusion(bf16[256,2048]{1,0:T(8,128)(2,1)} %param.5, bf16[896,2048]{1,0:T(8,128)(2,1)} %param.6), kind=kOutput, calls=%fused_computation.85 | convolution fusion | flops 939524096 | bytes 5636096 | tf_op jit(solution)/shard_map/dot_general | solution.py:101
  7.3 39.1 %all-reduce.1 = bf16[256,896]{1,0:T(8,128)(2,1)S(1)} all-reduce(f32[256,896]{1,0:T(8,128)S(1)} %fusion.43), channel_id=1, replica_groups=mesh['tok'=2,'voc'=4,'wid'=4] {'wid'}, use_global_device_ids=true, to_apply=%region_0.0 | all-reduce | flops 229376 | bytes 1376256 | tf_op jit(solution)/shard_map/psum | solution.py:104
  48.0 7.9 %collective-permute-done = bf16[256,896]{1,0:T(8,128)(2,1)S(1)} collective-permute-done((bf16[256,896]{1,0:T(8,128)(2,1)S(1)}, bf16[256,896]{1,0:T(8,128)(2,1)S(1)}, u32[]{:S(2)}, u32[]{:S(2)}) %collective-permute-start) | collective-permute-done | bytes 458784 | tf_op jit(solution)/shard_map/ppermute | solution.py:82
  56.4 2.2 %collective-permute-done.1 = bf16[2,256,896]{2,1,0:T(8,128)(2,1)S(1)} collective-permute-done((bf16[2,256,896]{2,1,0:T(8,128)(2,1)S(1)}, bf16[2,256,896]{2,1,0:T(8,128)(2,1)S(1)}, u32[]{:S(2)}, u32[]{:S(2)}) %collective-permute-start.1) | collective-permute-done | bytes 917536 | tf_op jit(solution)/shard_map/ppermute | solution.py:82
  59.1 2.4 %copy.8 = bf16[256,4,896]{0,2,1:T(8,128)(2,1)} copy(bf16[256,4,896]{2,0,1:T(8,128)(2,1)S(1)} %bitcast.84) | data formatting | bytes 3670016 | tf_op jit(solution)/shard_map/transpose | solution.py:107
  61.5 4.0 %fusion.21 = f32[256,1216]{0,1:T(8,128)S(1)} fusion(bf16[1216,1792]{1,0:T(8,128)(2,1)} %param.7, bf16[256,3584]{0,1:T(8,128)(2,1)} %bitcast.90, s32[]{:T(128)S(6)} %select_n.172), kind=kOutput, calls=%fused_computation.24 | convolution fusion | flops 1115684864 | bytes 6520836 | tf_op jit(solution)/shard_map/dot_general | solution.py:114
  65.5 32.5 %collective-permute-done.2 = bf16[1216,1792]{1,0:T(8,128)(2,1)} collective-permute-done((bf16[1216,1792]{1,0:T(8,128)(2,1)}, bf16[1216,1792]{1,0:T(8,128)(2,1)}, u32[]{:S(2)}, u32[]{:S(2)}) %collective-permute-start.2) | collective-permute-done | bytes 4358176 | tf_op jit(solution)/shard_map/ppermute | solution.py:11
  98.0 3.6 %fusion.42 = (f32[256]{0:T(256)S(1)}, f32[256,1216]{0,1:T(8,128)S(1)}) fusion(f32[256,1216]{0,1:T(8,128)S(1)} %fusion.21, bf16[1216,1792]{1,0:T(8,128)(2,1)} %collective-permute-done.2, bf16[256,3584]{0,1:T(8,128)(2,1)S(1)} %bitcast.91, s32[]{:T(128)S(6)} %select_n.174), kind=kOutput, calls=%fused_computation.84 | convolution fusion | flops 1116307200 | bytes 7767044 | tf_op jit(solution)/shard_map/dot_general | solution.py:114
  107.0 1.9 collective-permute-start.5
  110.7 2.9 %collective-permute-start.6 = (f32[3,256]{1,0:T(4,128)S(1)}, f32[3,256]{1,0:T(4,128)S(1)}, u32[]{:S(2)}, u32[]{:S(2)}) collective-permute-start(f32[3,256]{1,0:T(4,128)S(1)} %pad_maximum_fusion.5), channel_id=1, source_target_pairs={{0,2},{1,3},{2,0},{3,1},{4,6},{5,7},{6,4},{7,5},{8,10},{9,11},{10,... | collective-permute-start | bytes 9224 | tf_op jit(solution)/shard_map/ppermute | solution.py:33
  116.2 2.5 %fusion.14 = f32[1,256,896]{2,1,0:T(8,128)S(1)} fusion(bf16[256,1216]{0,1:T(8,128)(2,1)S(1)} %multiply_convert_fusion, bf16[1216,1792]{1,0:T(8,128)(2,1)} %param.7, s32[]{:T(128)S(6)} %select_n.177), kind=kOutput, calls=%fused_computation.15 | convolution fusion | flops 557842432 | bytes 3719172 | tf_op jit(solution)/shard_map/dot_general | solution.py:158
  118.7 2.5 %fusion.17 = f32[1,256,896]{2,1,0:T(8,128)S(1)} fusion(bf16[256,1216]{0,1:T(8,128)(2,1)S(1)} %multiply_convert_fusion, bf16[1216,1792]{1,0:T(8,128)(2,1)} %collective-permute-done.2, s32[]{:T(128)S(6)} %select_n.177), kind=kOutput, calls=%fused_computation.16 | convolution fusion | flops 557842432 | bytes 3719172 | tf_op jit(solution)/shard_map/dot_general | solution.py:158
  121.5 2.5 %fusion.8 = f32[1,256,896]{2,1,0:T(8,128)S(1)} fusion(bf16[256,1216]{0,1:T(8,128)(2,1)S(1)} %multiply_convert_fusion, bf16[1216,1792]{1,0:T(8,128)(2,1)} %param.7, s32[]{:T(128)S(6)} %select_n.176), kind=kOutput, calls=%fused_computation.13 | convolution fusion | flops 557842432 | bytes 3719172 | tf_op jit(solution)/shard_map/dot_general | solution.py:158
  124.0 2.5 %fusion.11 = f32[1,256,896]{2,1,0:T(8,128)S(1)} fusion(bf16[256,1216]{0,1:T(8,128)(2,1)S(1)} %multiply_convert_fusion, bf16[1216,1792]{1,0:T(8,128)(2,1)} %collective-permute-done.2, s32[]{:T(128)S(6)} %select_n.176), kind=kOutput, calls=%fused_computation.14 | convolution fusion | flops 557842432 | bytes 3719172 | tf_op jit(solution)/shard_map/dot_general | solution.py:158
  135.4 6.2 %collective-permute-done.8 = f32[2,2,32,896]{3,2,1,0:T(8,128)} collective-permute-done((f32[2,2,32,896]{3,2,1,0:T(8,128)S(1)}, f32[2,2,32,896]{3,2,1,0:T(8,128)}, u32[]{:S(2)}, u32[]{:S(2)}) %collective-permute-start.8) | collective-permute-done | bytes 458784 | tf_op jit(solution)/shard_map/ppermute | solution.py:71
  142.7 1.9 collective-permute-start.9
  146.2 3.8 %collective-permute-done.9 = f32[2,32,896]{2,1,0:T(8,128)S(1)} collective-permute-done((f32[2,32,896]{2,1,0:T(8,128)S(1)}, f32[2,32,896]{2,1,0:T(8,128)S(1)}, u32[]{:S(2)}, u32[]{:S(2)}) %collective-permute-start.9) | collective-permute-done | bytes 229408 | tf_op jit(solution)/shard_map/ppermute | solution.py:71
  150.0 2.8 %collective-permute-start.10 = (f32[32,896]{1,0:T(8,128)S(1)}, f32[32,896]{1,0:T(8,128)S(1)}, u32[]{:S(2)}, u32[]{:S(2)}) collective-permute-start(f32[32,896]{1,0:T(8,128)S(1)} %dynamic-slice_bitcast_fusion.5), channel_id=1, source_target_pairs={{0,2},{1,3},{2,0},{3,1},{4,6},{5,7},{6,4},{7,5},{8,10},{9,11},{10,... | collective-permute-start | bytes 344072 | tf_op jit(solution)/shard_map/ppermute | solution.py:71
  154.3 6.8 %collective-permute-done.10 = f32[32,896]{1,0:T(8,128)S(1)} collective-permute-done((f32[32,896]{1,0:T(8,128)S(1)}, f32[32,896]{1,0:T(8,128)S(1)}, u32[]{:S(2)}, u32[]{:S(2)}) %collective-permute-start.10) | collective-permute-done | bytes 114720 | tf_op jit(solution)/shard_map/ppermute | solution.py:71
  163.9 6.7 %collective-permute-done.14 = bf16[64,896]{1,0:T(8,128)(2,1)S(1)} collective-permute-done((bf16[64,896]{1,0:T(8,128)(2,1)S(1)}, bf16[64,896]{1,0:T(8,128)(2,1)S(1)}, u32[]{:S(2)}, u32[]{:S(2)}) %collective-permute-start.14) | collective-permute-done | bytes 114720 | tf_op jit(solution)/shard_map/ppermute | solution.py:82
  170.8 5.9 %collective-permute-done.15 = bf16[2,64,896]{2,1,0:T(8,128)(2,1)S(1)} collective-permute-done((bf16[2,64,896]{2,1,0:T(8,128)(2,1)S(1)}, bf16[2,64,896]{2,1,0:T(8,128)(2,1)S(1)}, u32[]{:S(2)}, u32[]{:S(2)}) %collective-permute-start.15) | collective-permute-done | bytes 229408 | tf_op jit(solution)/shard_map/ppermute | solution.py:82
  181.5 4.0 %collective-permute-done.16 = bf16[256,896]{1,0:T(8,128)(2,1)S(1)} collective-permute-done((bf16[256,896]{1,0:T(8,128)(2,1)S(1)}, bf16[256,896]{1,0:T(8,128)(2,1)S(1)}, u32[]{:S(2)}, u32[]{:S(2)}) %collective-permute-start.16) | collective-permute-done | bytes 458784 | tf_op jit(solution)/shard_map/ppermute | solution.py:229
  185.5 5.4 %convolution_add_fusion = f32[896,2048]{1,0:T(8,128)} fusion(f32[896,2048]{1,0:T(8,128)S(1)} %fusion.44, bf16[256,896]{1,0:T(8,128)(2,1)S(1)} %collective-permute-done.16, bf16[256,2048]{1,0:T(8,128)(2,1)} %collective-permute-done.17), kind=kOutput, calls=%fused_computation | convolution fusion | flops 941359104 | bytes 16187392 | tf_op jit(solution)/shard_map/dot_general | solution.py:233
  (73 shorter events, 31.8 us)
Async XLA Ops:
  0.6 97.4 %collective-permute-start.2 = (bf16[1216,1792]{1,0:T(8,128)(2,1)}, bf16[1216,1792]{1,0:T(8,128)(2,1)}, u32[]{:S(2)}, u32[]{:S(2)}) collective-permute-start(bf16[1216,1792]{1,0:T(8,128)(2,1)} %param.7), channel_id=1, source_target_pairs={{0,16},{16,0},{1,17},{17,1},{2,18},{18,2},{3,19},{19,3},{4,20},{20... | collective-permute-start | bytes 13074440 | tf_op jit(solution)/shard_map/ppermute | solution.py:11
  7.3 48.9 %copy-start.3 = (s32[256]{0:T(256)S(1)}, s32[256]{0:T(256)}, u32[]{:S(2)}) copy-start(s32[256]{0:T(256)} %param.8) | copy-start | bytes 3076
  46.4 9.5 %collective-permute-start = (bf16[256,896]{1,0:T(8,128)(2,1)S(1)}, bf16[256,896]{1,0:T(8,128)(2,1)S(1)}, u32[]{:S(2)}, u32[]{:S(2)}) collective-permute-start(bf16[256,896]{1,0:T(8,128)(2,1)S(1)} %all-reduce.1), channel_id=1, source_target_pairs={{0,8},{4,12},{8,0},{12,4},{1,9},{5,13},{9,1},{13,5},{2,10},{6,14},... | collective-permute-start | bytes 1376264 | tf_op jit(solution)/shard_map/ppermute | solution.py:82
  56.1 2.5 %collective-permute-start.1 = (bf16[2,256,896]{2,1,0:T(8,128)(2,1)S(1)}, bf16[2,256,896]{2,1,0:T(8,128)(2,1)S(1)}, u32[]{:S(2)}, u32[]{:S(2)}) collective-permute-start(bf16[2,256,896]{2,1,0:T(8,128)(2,1)S(1)} %maximum_select_fusion.2), channel_id=1, source_target_pairs={{0,4},{4,0},{8,12},{12,8},{1,5},{5,1},{9,13},{13,9},{2,6},{6,2},{1... | collective-permute-start | bytes 2752520 | tf_op jit(solution)/shard_map/ppermute | solution.py:82
  61.5 36.5 %copy-start = (bf16[256,4,896]{0,2,1:T(8,128)(2,1)S(1)}, bf16[256,4,896]{0,2,1:T(8,128)(2,1)}, u32[]{:S(2)}) copy-start(bf16[256,4,896]{0,2,1:T(8,128)(2,1)} %copy.8) | copy-start | bytes 5505028
  65.5 48.1 %copy-start.2 = (s32[256]{0:T(256)S(1)}, s32[256]{0:T(256)}, u32[]{:S(2)}) copy-start(s32[256]{0:T(256)} %param.9) | copy-start | bytes 3076
  102.0 1.2 collective-permute-start.3
  103.3 3.7 %collective-permute-start.4 = (f32[3,256]{1,0:T(4,128)S(1)}, f32[3,256]{1,0:T(4,128)S(1)}, u32[]{:S(2)}, u32[]{:S(2)}) collective-permute-start(f32[3,256]{1,0:T(4,128)S(1)} %pad_maximum_fusion.3), channel_id=1, source_target_pairs={{0,8},{4,12},{8,0},{12,4},{1,9},{5,13},{9,1},{13,5},{2,10},{6,14},... | collective-permute-start | bytes 9224 | tf_op jit(solution)/shard_map/ppermute | solution.py:33
  107.0 3.7 %collective-permute-start.5 = (f32[3,256]{1,0:T(4,128)S(1)}, f32[3,256]{1,0:T(4,128)S(1)}, u32[]{:S(2)}, u32[]{:S(2)}) collective-permute-start(f32[3,256]{1,0:T(4,128)S(1)} %pad_maximum_fusion.4), channel_id=1, source_target_pairs={{0,1},{1,0},{2,3},{3,2},{4,5},{5,4},{6,7},{7,6},{8,9},{9,8},{10,11... | collective-permute-start | bytes 9224 | tf_op jit(solution)/shard_map/ppermute | solution.py:33
  110.7 4.6 %collective-permute-start.6 = (f32[3,256]{1,0:T(4,128)S(1)}, f32[3,256]{1,0:T(4,128)S(1)}, u32[]{:S(2)}, u32[]{:S(2)}) collective-permute-start(f32[3,256]{1,0:T(4,128)S(1)} %pad_maximum_fusion.5), channel_id=1, source_target_pairs={{0,2},{1,3},{2,0},{3,1},{4,6},{5,7},{6,4},{7,5},{8,10},{9,11},{10,... | collective-permute-start | bytes 9224 | tf_op jit(solution)/shard_map/ppermute | solution.py:33
  121.4 5.1 %collective-permute-start.7 = (f32[2,256,896]{2,1,0:T(8,128)S(1)}, f32[2,256,896]{2,1,0:T(8,128)}, u32[]{:S(2)}, u32[]{:S(2)}) collective-permute-start(f32[2,256,896]{2,1,0:T(8,128)S(1)} %pad_maximum_fusion), channel_id=1, source_target_pairs={{0,4},{4,0},{8,12},{12,8},{1,5},{5,1},{9,13},{13,9},{2,6},{6,2},{1... | collective-permute-start | bytes 5505032 | tf_op jit(solution)/shard_map/ppermute | solution.py:168
  128.3 2.0 %copy-start.1 = (bf16[256,2048]{1,0:T(8,128)(2,1)S(1)}, bf16[256,2048]{1,0:T(8,128)(2,1)}, u32[]{:S(2)}) copy-start(bf16[256,2048]{1,0:T(8,128)(2,1)} %param.5) | copy-start | bytes 3145732
  128.5 13.1 %collective-permute-start.8 = (f32[2,2,32,896]{3,2,1,0:T(8,128)S(1)}, f32[2,2,32,896]{3,2,1,0:T(8,128)}, u32[]{:S(2)}, u32[]{:S(2)}) collective-permute-start(f32[2,2,32,896]{3,2,1,0:T(8,128)S(1)} %dynamic-slice_bitcast_fusion.1), channel_id=1, source_target_pairs={{0,8},{4,12},{8,0},{12,4},{1,9},{5,13},{9,1},{13,5},{2,10},{6,14},... | collective-permute-start | bytes 1376264 | tf_op jit(solution)/shard_map/ppermute | solution.py:71
  130.3 51.2 %collective-permute-start.17 = (bf16[256,2048]{1,0:T(8,128)(2,1)S(1)}, bf16[256,2048]{1,0:T(8,128)(2,1)}, u32[]{:S(2)}, u32[]{:S(2)}) collective-permute-start(bf16[256,2048]{1,0:T(8,128)(2,1)S(1)} %copy-done.1), channel_id=1, source_target_pairs={{0,16},{16,0},{1,17},{17,1},{2,18},{18,2},{3,19},{19,3},{4,20},{20... | collective-permute-start | bytes 3145736 | tf_op jit(solution)/shard_map/ppermute | solution.py:99
  131.8 12.7 %collective-permute-start.11 = (f32[2,2,32,896]{3,2,1,0:T(8,128)S(1)}, f32[2,2,32,896]{3,2,1,0:T(8,128)S(1)}, u32[]{:S(2)}, u32[]{:S(2)}) collective-permute-start(f32[2,2,32,896]{3,2,1,0:T(8,128)S(1)} %dynamic-slice_bitcast_fusion), channel_id=1, source_target_pairs={{0,1},{1,0},{2,3},{3,2},{4,5},{5,4},{6,7},{7,6},{8,9},{9,8},{10,11... | collective-permute-start | bytes 1376264 | tf_op jit(solution)/shard_map/ppermute | solution.py:71
  134.9 27.7 %collective-permute-start.18 = (f32[2]{0:T(128)S(1)}, f32[2]{0:T(128)S(1)}, u32[]{:S(2)}, u32[]{:S(2)}) collective-permute-start(f32[2]{0:T(128)S(1)} %pad_maximum_fusion.6), channel_id=1, source_target_pairs={{0,16},{16,0},{1,17},{17,1},{2,18},{18,2},{3,19},{19,3},{4,20},{20... | collective-permute-start | bytes 32 | tf_op jit(solution)/shard_map/ppermute | solution.py:45
  142.7 7.3 %collective-permute-start.9 = (f32[2,32,896]{2,1,0:T(8,128)S(1)}, f32[2,32,896]{2,1,0:T(8,128)S(1)}, u32[]{:S(2)}, u32[]{:S(2)}) collective-permute-start(f32[2,32,896]{2,1,0:T(8,128)S(1)} %dynamic-slice_bitcast_fusion.3), channel_id=1, source_target_pairs={{0,1},{1,0},{2,3},{3,2},{4,5},{5,4},{6,7},{7,6},{8,9},{9,8},{10,11... | collective-permute-start | bytes 688136 | tf_op jit(solution)/shard_map/ppermute | solution.py:71
  144.6 8.2 %collective-permute-start.12 = (f32[2,32,896]{2,1,0:T(8,128)S(1)}, f32[2,32,896]{2,1,0:T(8,128)S(1)}, u32[]{:S(2)}, u32[]{:S(2)}) collective-permute-start(f32[2,32,896]{2,1,0:T(8,128)S(1)} %dynamic-slice_bitcast_fusion.2), channel_id=1, source_target_pairs={{0,8},{4,12},{8,0},{12,4},{1,9},{5,13},{9,1},{13,5},{2,10},{6,14},... | collective-permute-start | bytes 688136 | tf_op jit(solution)/shard_map/ppermute | solution.py:71
  150.0 11.1 %collective-permute-start.10 = (f32[32,896]{1,0:T(8,128)S(1)}, f32[32,896]{1,0:T(8,128)S(1)}, u32[]{:S(2)}, u32[]{:S(2)}) collective-permute-start(f32[32,896]{1,0:T(8,128)S(1)} %dynamic-slice_bitcast_fusion.5), channel_id=1, source_target_pairs={{0,2},{1,3},{2,0},{3,1},{4,6},{5,7},{6,4},{7,5},{8,10},{9,11},{10,... | collective-permute-start | bytes 344072 | tf_op jit(solution)/shard_map/ppermute | solution.py:71
  152.9 9.5 %collective-permute-start.13 = (f32[32,896]{1,0:T(8,128)S(1)}, f32[32,896]{1,0:T(8,128)S(1)}, u32[]{:S(2)}, u32[]{:S(2)}) collective-permute-start(f32[32,896]{1,0:T(8,128)S(1)} %dynamic-slice_bitcast_fusion.4), channel_id=1, source_target_pairs={{0,2},{1,3},{2,0},{3,1},{4,6},{5,7},{6,4},{7,5},{8,10},{9,11},{10,... | collective-permute-start | bytes 344072 | tf_op jit(solution)/shard_map/ppermute | solution.py:71
  162.5 8.2 %collective-permute-start.14 = (bf16[64,896]{1,0:T(8,128)(2,1)S(1)}, bf16[64,896]{1,0:T(8,128)(2,1)S(1)}, u32[]{:S(2)}, u32[]{:S(2)}) collective-permute-start(bf16[64,896]{1,0:T(8,128)(2,1)S(1)} %pad_maximum_fusion.1), channel_id=1, source_target_pairs={{0,2},{1,3},{2,0},{3,1},{4,6},{5,7},{6,4},{7,5},{8,10},{9,11},{10,... | collective-permute-start | bytes 344072 | tf_op jit(solution)/shard_map/ppermute | solution.py:82
  170.7 6.1 %collective-permute-start.15 = (bf16[2,64,896]{2,1,0:T(8,128)(2,1)S(1)}, bf16[2,64,896]{2,1,0:T(8,128)(2,1)S(1)}, u32[]{:S(2)}, u32[]{:S(2)}) collective-permute-start(bf16[2,64,896]{2,1,0:T(8,128)(2,1)S(1)} %maximum_select_fusion.5), channel_id=1, source_target_pairs={{0,1},{1,0},{2,3},{3,2},{4,5},{5,4},{6,7},{7,6},{8,9},{9,8},{10,11... | collective-permute-start | bytes 688136 | tf_op jit(solution)/shard_map/ppermute | solution.py:82
  176.9 8.6 %collective-permute-start.16 = (bf16[256,896]{1,0:T(8,128)(2,1)S(1)}, bf16[256,896]{1,0:T(8,128)(2,1)S(1)}, u32[]{:S(2)}, u32[]{:S(2)}) collective-permute-start(bf16[256,896]{1,0:T(8,128)(2,1)S(1)} %bitcast.88), channel_id=1, source_target_pairs={{0,16},{16,0},{1,17},{17,1},{2,18},{18,2},{3,19},{19,3},{4,20},{20... | collective-permute-start | bytes 1376264 | tf_op jit(solution)/shard_map/ppermute | solution.py:229

commit v12 on v11

--- a/solution.py
+++ b/solution.py
@@ -129,7 +129,7 @@
     log_total = stats[0] + jnp.log(stats[1])
     picked = stats[2]
     sums = jnp.stack([jnp.sum(weight * (log_total - picked)), jnp.sum(weight)])
-    sums = tree_sum(sums, "tok")
+    sums = tree_sum(lax.optimization_barrier(sums), "tok")
 
     dlogits = (
         weight[:, None] * (jnp.exp(logits - log_total[:, None]) - is_target.astype(jnp.float32))

time: 193 us -> 209 us (1.083)
  waiting for transfers between devices: 83.7 us -> 97.9 us
  starting transfers between devices: 26.3 us -> 31.3 us
    ppermute x1, waiting for transfers between devices: 0.01 us -> 20.6 us  [tree_sum(): x = x + lax.ppermute(x, ax, [(i, i ^ b) for i in range(n)])]
    ppermute x4, waiting for transfers between devices: 22.8 us -> 14.1 us  [doubling_gather(): other = lax.ppermute(x, ax, [(k, k ^ b) for k in range(n)])]
    ppermute x4, starting transfers between devices: 1.79 us -> 5.73 us  [doubling_gather(): other = lax.ppermute(x, ax, [(k, k ^ b) for k in range(n)])]
  transfers between devices with their start and end apart: 19 -> 19, of which waited for: 14 -> 14; matrix products, arithmetic and copies ran while one was open for 11% -> 10% of each run, Pallas kernels for 0% -> 0%
where the time goes in v12:
time: 209 us
  waiting for transfers between devices  97.9 us (47%)
  blocking collectives  39.1 us (19%)
  starting transfers between devices  31.3 us (15%)
  matrix products  26.6 us (13%)
  other arithmetic  6.74 us (3%)
  between operations  3.5 us (2%)
  local copies, waits for them, and re-layouts  3.43 us (2%)
    psum x1, blocking collectives, on_device(): summed = lax.psum(partial_value, 'wid')  39.1 us
    ppermute x1, waiting for transfers between devices, tok_pieces(): pieces.append(lax.ppermute(x, 'tok', perm))  32.5 us
    ppermute x1, waiting for transfers between devices, tree_sum(): x = x + lax.ppermute(x, ax, [(i, i ^ b) for i in range(n)])  20.6 us
    ppermute x6, waiting for transfers between devices, halving_steps(): x = keep + lax.ppermute(send, ax, [(k, k ^ b) for k in range(n)])  19.4 us
    ppermute x4, waiting for transfers between devices, doubling_gather(): other = lax.ppermute(x, ax, [(k, k ^ b) for k in range(n)])  14.1 us
    ppermute x6, starting transfers between devices, halving_steps(): x = keep + lax.ppermute(send, ax, [(k, k ^ b) for k in range(n)])  12.2 us
    dot_general x4, matrix products, quarter_dots(): jnp.dot(dlogits, lax.dynamic_slice_in_dim(piece, sel * q_cols, q_cols, ax...  10 us
    dot_general x2, matrix products, on_device(): lax.dot_general(cols, piece, (((1,), (1,)), ((), ())), preferred_element_...  7.57 us
  transfers between devices with their start and end apart: 19, of which 14 were waited for; matrix products, arithmetic and copies ran while one was open for 10% of the time, Pallas kernels for 0%

profile of v12, /device:TPU:0, one launch (start us, length us, event | category | flops | bytes accessed | tf_op | source)
XLA Modules:
  0.0 208.6 jit_solution(11200787702785420418)
XLA Ops:
  0.6 3.0 %collective-permute-start.2 = (bf16[1216,1792]{1,0:T(8,128)(2,1)}, bf16[1216,1792]{1,0:T(8,128)(2,1)}, u32[]{:S(2)}, u32[]{:S(2)}) collective-permute-start(bf16[1216,1792]{1,0:T(8,128)(2,1)} %param.7), channel_id=1, source_target_pairs={{0,16},{16,0},{1,17},{17,1},{2,18},{18,2},{3,19},{19,3},{4,20},{20... | collective-permute-start | bytes 13074440 | tf_op jit(solution)/shard_map/ppermute | solution.py:11
  3.6 3.6 %fusion.43 = f32[256,896]{1,0:T(8,128)S(1)} fusion(bf16[256,2048]{1,0:T(8,128)(2,1)} %param.5, bf16[896,2048]{1,0:T(8,128)(2,1)} %param.6), kind=kOutput, calls=%fused_computation.85 | convolution fusion | flops 939524096 | bytes 5636096 | tf_op jit(solution)/shard_map/dot_general | solution.py:101
  7.3 39.1 %all-reduce.1 = bf16[256,896]{1,0:T(8,128)(2,1)S(1)} all-reduce(f32[256,896]{1,0:T(8,128)S(1)} %fusion.43), channel_id=1, replica_groups=mesh['tok'=2,'voc'=4,'wid'=4] {'wid'}, use_global_device_ids=true, to_apply=%region_0.0 | all-reduce | flops 229376 | bytes 1376256 | tf_op jit(solution)/shard_map/psum | solution.py:104
  48.0 7.9 %collective-permute-done = bf16[256,896]{1,0:T(8,128)(2,1)S(1)} collective-permute-done((bf16[256,896]{1,0:T(8,128)(2,1)S(1)}, bf16[256,896]{1,0:T(8,128)(2,1)S(1)}, u32[]{:S(2)}, u32[]{:S(2)}) %collective-permute-start) | collective-permute-done | bytes 458784 | tf_op jit(solution)/shard_map/ppermute | solution.py:82
  56.4 2.2 %collective-permute-done.1 = bf16[2,256,896]{2,1,0:T(8,128)(2,1)S(1)} collective-permute-done((bf16[2,256,896]{2,1,0:T(8,128)(2,1)S(1)}, bf16[2,256,896]{2,1,0:T(8,128)(2,1)S(1)}, u32[]{:S(2)}, u32[]{:S(2)}) %collective-permute-start.1) | collective-permute-done | bytes 917536 | tf_op jit(solution)/shard_map/ppermute | solution.py:82
  59.1 2.4 %copy.8 = bf16[256,4,896]{0,2,1:T(8,128)(2,1)} copy(bf16[256,4,896]{2,0,1:T(8,128)(2,1)S(1)} %bitcast.84) | data formatting | bytes 3670016 | tf_op jit(solution)/shard_map/transpose | solution.py:107
  61.5 4.0 %fusion.21 = f32[256,1216]{0,1:T(8,128)S(1)} fusion(bf16[1216,1792]{1,0:T(8,128)(2,1)} %param.7, bf16[256,3584]{0,1:T(8,128)(2,1)} %bitcast.90, s32[]{:T(128)S(6)} %select_n.172), kind=kOutput, calls=%fused_computation.24 | convolution fusion | flops 1115684864 | bytes 6520836 | tf_op jit(solution)/shard_map/dot_general | solution.py:114
  65.5 32.5 %collective-permute-done.2 = bf16[1216,1792]{1,0:T(8,128)(2,1)} collective-permute-done((bf16[1216,1792]{1,0:T(8,128)(2,1)}, bf16[1216,1792]{1,0:T(8,128)(2,1)}, u32[]{:S(2)}, u32[]{:S(2)}) %collective-permute-start.2) | collective-permute-done | bytes 4358176 | tf_op jit(solution)/shard_map/ppermute | solution.py:11
  98.0 3.6 %fusion.42 = (f32[256]{0:T(256)S(1)}, f32[256,1216]{0,1:T(8,128)S(1)}) fusion(f32[256,1216]{0,1:T(8,128)S(1)} %fusion.21, bf16[1216,1792]{1,0:T(8,128)(2,1)} %collective-permute-done.2, bf16[256,3584]{0,1:T(8,128)(2,1)S(1)} %bitcast.91, s32[]{:T(128)S(6)} %select_n.174), kind=kOutput, calls=%fused_computation.84 | convolution fusion | flops 1116307200 | bytes 7767044 | tf_op jit(solution)/shard_map/dot_general | solution.py:114
  110.7 2.9 %collective-permute-start.6 = (f32[3,256]{1,0:T(4,128)S(1)}, f32[3,256]{1,0:T(4,128)S(1)}, u32[]{:S(2)}, u32[]{:S(2)}) collective-permute-start(f32[3,256]{1,0:T(4,128)S(1)} %pad_maximum_fusion.5), channel_id=1, source_target_pairs={{0,2},{1,3},{2,0},{3,1},{4,6},{5,7},{6,4},{7,5},{8,10},{9,11},{10,... | collective-permute-start | bytes 9224 | tf_op jit(solution)/shard_map/ppermute | solution.py:33
  116.2 2.5 %fusion.14 = f32[1,256,896]{2,1,0:T(8,128)S(1)} fusion(bf16[256,1216]{0,1:T(8,128)(2,1)S(1)} %multiply_convert_fusion, bf16[1216,1792]{1,0:T(8,128)(2,1)} %param.7, s32[]{:T(128)S(6)} %select_n.177), kind=kOutput, calls=%fused_computation.15 | convolution fusion | flops 557842432 | bytes 3719172 | tf_op jit(solution)/shard_map/dot_general | solution.py:158
  118.7 2.5 %fusion.17 = f32[1,256,896]{2,1,0:T(8,128)S(1)} fusion(bf16[256,1216]{0,1:T(8,128)(2,1)S(1)} %multiply_convert_fusion, bf16[1216,1792]{1,0:T(8,128)(2,1)} %collective-permute-done.2, s32[]{:T(128)S(6)} %select_n.177), kind=kOutput, calls=%fused_computation.16 | convolution fusion | flops 557842432 | bytes 3719172 | tf_op jit(solution)/shard_map/dot_general | solution.py:158
  121.5 2.5 %fusion.8 = f32[1,256,896]{2,1,0:T(8,128)S(1)} fusion(bf16[256,1216]{0,1:T(8,128)(2,1)S(1)} %multiply_convert_fusion, bf16[1216,1792]{1,0:T(8,128)(2,1)} %param.7, s32[]{:T(128)S(6)} %select_n.176), kind=kOutput, calls=%fused_computation.13 | convolution fusion | flops 557842432 | bytes 3719172 | tf_op jit(solution)/shard_map/dot_general | solution.py:158
  124.0 2.5 %fusion.11 = f32[1,256,896]{2,1,0:T(8,128)S(1)} fusion(bf16[256,1216]{0,1:T(8,128)(2,1)S(1)} %multiply_convert_fusion, bf16[1216,1792]{1,0:T(8,128)(2,1)} %collective-permute-done.2, s32[]{:T(128)S(6)} %select_n.176), kind=kOutput, calls=%fused_computation.14 | convolution fusion | flops 557842432 | bytes 3719172 | tf_op jit(solution)/shard_map/dot_general | solution.py:158
  132.0 9.5 %collective-permute-done.8 = f32[2,2,32,896]{3,2,1,0:T(8,128)S(1)} collective-permute-done((f32[2,2,32,896]{3,2,1,0:T(8,128)S(1)}, f32[2,2,32,896]{3,2,1,0:T(8,128)S(1)}, u32[]{:S(2)}, u32[]{:S(2)}) %collective-permute-start.8) | collective-permute-done | bytes 458784 | tf_op jit(solution)/shard_map/ppermute | solution.py:71
  146.1 2.8 %collective-permute-done.9 = f32[2,32,896]{2,1,0:T(8,128)S(1)} collective-permute-done((f32[2,32,896]{2,1,0:T(8,128)S(1)}, f32[2,32,896]{2,1,0:T(8,128)S(1)}, u32[]{:S(2)}, u32[]{:S(2)}) %collective-permute-start.9) | collective-permute-done | bytes 229408 | tf_op jit(solution)/shard_map/ppermute | solution.py:71
  149.0 2.8 %collective-permute-start.10 = (f32[32,896]{1,0:T(8,128)S(1)}, f32[32,896]{1,0:T(8,128)S(1)}, u32[]{:S(2)}, u32[]{:S(2)}) collective-permute-start(f32[32,896]{1,0:T(8,128)S(1)} %dynamic-slice_bitcast_fusion.5), channel_id=1, source_target_pairs={{0,2},{1,3},{2,0},{3,1},{4,6},{5,7},{6,4},{7,5},{8,10},{9,11},{10,... | collective-permute-start | bytes 344072 | tf_op jit(solution)/shard_map/ppermute | solution.py:71
  151.9 2.4 %collective-permute-start.13 = (f32[32,896]{1,0:T(8,128)S(1)}, f32[32,896]{1,0:T(8,128)S(1)}, u32[]{:S(2)}, u32[]{:S(2)}) collective-permute-start(f32[32,896]{1,0:T(8,128)S(1)} %dynamic-slice_bitcast_fusion.4), channel_id=1, source_target_pairs={{0,2},{1,3},{2,0},{3,1},{4,6},{5,7},{6,4},{7,5},{8,10},{9,11},{10,... | collective-permute-start | bytes 344072 | tf_op jit(solution)/shard_map/ppermute | solution.py:71
  154.3 5.8 %collective-permute-done.10 = f32[32,896]{1,0:T(8,128)S(1)} collective-permute-done((f32[32,896]{1,0:T(8,128)S(1)}, f32[32,896]{1,0:T(8,128)S(1)}, u32[]{:S(2)}, u32[]{:S(2)}) %collective-permute-start.10) | collective-permute-done | bytes 114720 | tf_op jit(solution)/shard_map/ppermute | solution.py:71
  165.0 20.6 %collective-permute-done.18 = f32[2]{0:T(128)S(1)} collective-permute-done((f32[2]{0:T(128)S(1)}, f32[2]{0:T(128)S(1)}, u32[]{:S(2)}, u32[]{:S(2)}) %collective-permute-start.18) | collective-permute-done | bytes 40 | tf_op jit(solution)/shard_map/ppermute | solution.py:45
  185.7 4.0 %collective-permute-start.15 = (bf16[2,64,896]{2,1,0:T(8,128)(2,1)S(1)}, bf16[2,64,896]{2,1,0:T(8,128)(2,1)S(1)}, u32[]{:S(2)}, u32[]{:S(2)}) collective-permute-start(bf16[2,64,896]{2,1,0:T(8,128)(2,1)S(1)} %maximum_select_fusion.5), channel_id=1, source_target_pairs={{0,1},{1,0},{2,3},{3,2},{4,5},{5,4},{6,7},{7,6},{8,9},{9,8},{10,11... | collective-permute-start | bytes 688136 | tf_op jit(solution)/shard_map/ppermute | solution.py:82
  189.8 3.9 %collective-permute-done.15 = bf16[2,64,896]{2,1,0:T(8,128)(2,1)S(1)} collective-permute-done((bf16[2,64,896]{2,1,0:T(8,128)(2,1)S(1)}, bf16[2,64,896]{2,1,0:T(8,128)(2,1)S(1)}, u32[]{:S(2)}, u32[]{:S(2)}) %collective-permute-start.15) | collective-permute-done | bytes 229408 | tf_op jit(solution)/shard_map/ppermute | solution.py:82
  198.5 4.8 %collective-permute-done.16 = bf16[256,896]{1,0:T(8,128)(2,1)S(1)} collective-permute-done((bf16[256,896]{1,0:T(8,128)(2,1)S(1)}, bf16[256,896]{1,0:T(8,128)(2,1)S(1)}, u32[]{:S(2)}, u32[]{:S(2)}) %collective-permute-start.16) | collective-permute-done | bytes 458784 | tf_op jit(solution)/shard_map/ppermute | solution.py:229
  203.3 4.2 %convolution_add_fusion = f32[896,2048]{1,0:T(8,128)} fusion(f32[896,2048]{1,0:T(8,128)S(1)} %fusion.44, bf16[256,896]{1,0:T(8,128)(2,1)S(1)} %collective-permute-done.16, bf16[256,2048]{1,0:T(8,128)(2,1)S(1)} %collective-permute-done.17), kind=kOutput, calls=%fused_computation | convolution fusion | flops 941359104 | bytes 16187392 | tf_op jit(solution)/shard_map/dot_general | solution.py:233
  (73 shorter events, 32.8 us)
Async XLA Ops:
  0.6 97.4 %collective-permute-start.2 = (bf16[1216,1792]{1,0:T(8,128)(2,1)}, bf16[1216,1792]{1,0:T(8,128)(2,1)}, u32[]{:S(2)}, u32[]{:S(2)}) collective-permute-start(bf16[1216,1792]{1,0:T(8,128)(2,1)} %param.7), channel_id=1, source_target_pairs={{0,16},{16,0},{1,17},{17,1},{2,18},{18,2},{3,19},{19,3},{4,20},{20... | collective-permute-start | bytes 13074440 | tf_op jit(solution)/shard_map/ppermute | solution.py:11
  7.3 48.9 %copy-start.3 = (s32[256]{0:T(256)S(1)}, s32[256]{0:T(256)}, u32[]{:S(2)}) copy-start(s32[256]{0:T(256)} %param.8) | copy-start | bytes 3076
  46.4 9.5 %collective-permute-start = (bf16[256,896]{1,0:T(8,128)(2,1)S(1)}, bf16[256,896]{1,0:T(8,128)(2,1)S(1)}, u32[]{:S(2)}, u32[]{:S(2)}) collective-permute-start(bf16[256,896]{1,0:T(8,128)(2,1)S(1)} %all-reduce.1), channel_id=1, source_target_pairs={{0,8},{4,12},{8,0},{12,4},{1,9},{5,13},{9,1},{13,5},{2,10},{6,14},... | collective-permute-start | bytes 1376264 | tf_op jit(solution)/shard_map/ppermute | solution.py:82
  56.1 2.5 %collective-permute-start.1 = (bf16[2,256,896]{2,1,0:T(8,128)(2,1)S(1)}, bf16[2,256,896]{2,1,0:T(8,128)(2,1)S(1)}, u32[]{:S(2)}, u32[]{:S(2)}) collective-permute-start(bf16[2,256,896]{2,1,0:T(8,128)(2,1)S(1)} %maximum_select_fusion.2), channel_id=1, source_target_pairs={{0,4},{4,0},{8,12},{12,8},{1,5},{5,1},{9,13},{13,9},{2,6},{6,2},{1... | collective-permute-start | bytes 2752520 | tf_op jit(solution)/shard_map/ppermute | solution.py:82
  61.5 36.5 %copy-start = (bf16[256,4,896]{0,2,1:T(8,128)(2,1)S(1)}, bf16[256,4,896]{0,2,1:T(8,128)(2,1)}, u32[]{:S(2)}) copy-start(bf16[256,4,896]{0,2,1:T(8,128)(2,1)} %copy.8) | copy-start | bytes 5505028
  65.5 48.1 %copy-start.2 = (s32[256]{0:T(256)S(1)}, s32[256]{0:T(256)}, u32[]{:S(2)}) copy-start(s32[256]{0:T(256)} %param.9) | copy-start | bytes 3076
  102.0 1.2 collective-permute-start.3
  103.3 3.7 %collective-permute-start.4 = (f32[3,256]{1,0:T(4,128)S(1)}, f32[3,256]{1,0:T(4,128)S(1)}, u32[]{:S(2)}, u32[]{:S(2)}) collective-permute-start(f32[3,256]{1,0:T(4,128)S(1)} %pad_maximum_fusion.3), channel_id=1, source_target_pairs={{0,8},{4,12},{8,0},{12,4},{1,9},{5,13},{9,1},{13,5},{2,10},{6,14},... | collective-permute-start | bytes 9224 | tf_op jit(solution)/shard_map/ppermute | solution.py:33
  107.0 3.7 %collective-permute-start.5 = (f32[3,256]{1,0:T(4,128)S(1)}, f32[3,256]{1,0:T(4,128)S(1)}, u32[]{:S(2)}, u32[]{:S(2)}) collective-permute-start(f32[3,256]{1,0:T(4,128)S(1)} %pad_maximum_fusion.4), channel_id=1, source_target_pairs={{0,1},{1,0},{2,3},{3,2},{4,5},{5,4},{6,7},{7,6},{8,9},{9,8},{10,11... | collective-permute-start | bytes 9224 | tf_op jit(solution)/shard_map/ppermute | solution.py:33
  110.7 4.6 %collective-permute-start.6 = (f32[3,256]{1,0:T(4,128)S(1)}, f32[3,256]{1,0:T(4,128)S(1)}, u32[]{:S(2)}, u32[]{:S(2)}) collective-permute-start(f32[3,256]{1,0:T(4,128)S(1)} %pad_maximum_fusion.5), channel_id=1, source_target_pairs={{0,2},{1,3},{2,0},{3,1},{4,6},{5,7},{6,4},{7,5},{8,10},{9,11},{10,... | collective-permute-start | bytes 9224 | tf_op jit(solution)/shard_map/ppermute | solution.py:33
  121.4 5.1 %collective-permute-start.7 = (f32[2,256,896]{2,1,0:T(8,128)S(1)}, f32[2,256,896]{2,1,0:T(8,128)}, u32[]{:S(2)}, u32[]{:S(2)}) collective-permute-start(f32[2,256,896]{2,1,0:T(8,128)S(1)} %pad_maximum_fusion), channel_id=1, source_target_pairs={{0,4},{4,0},{8,12},{12,8},{1,5},{5,1},{9,13},{13,9},{2,6},{6,2},{1... | collective-permute-start | bytes 5505032 | tf_op jit(solution)/shard_map/ppermute | solution.py:168
  128.5 13.0 %collective-permute-start.8 = (f32[2,2,32,896]{3,2,1,0:T(8,128)S(1)}, f32[2,2,32,896]{3,2,1,0:T(8,128)S(1)}, u32[]{:S(2)}, u32[]{:S(2)}) collective-permute-start(f32[2,2,32,896]{3,2,1,0:T(8,128)S(1)} %dynamic-slice_bitcast_fusion.1), channel_id=1, source_target_pairs={{0,8},{4,12},{8,0},{12,4},{1,9},{5,13},{9,1},{13,5},{2,10},{6,14},... | collective-permute-start | bytes 1376264 | tf_op jit(solution)/shard_map/ppermute | solution.py:71
  130.3 13.1 %collective-permute-start.11 = (f32[2,2,32,896]{3,2,1,0:T(8,128)S(1)}, f32[2,2,32,896]{3,2,1,0:T(8,128)}, u32[]{:S(2)}, u32[]{:S(2)}) collective-permute-start(f32[2,2,32,896]{3,2,1,0:T(8,128)S(1)} %dynamic-slice_bitcast_fusion), channel_id=1, source_target_pairs={{0,1},{1,0},{2,3},{3,2},{4,5},{5,4},{6,7},{7,6},{8,9},{9,8},{10,11... | collective-permute-start | bytes 1376264 | tf_op jit(solution)/shard_map/ppermute | solution.py:71
  141.5 7.4 %collective-permute-start.9 = (f32[2,32,896]{2,1,0:T(8,128)S(1)}, f32[2,32,896]{2,1,0:T(8,128)S(1)}, u32[]{:S(2)}, u32[]{:S(2)}) collective-permute-start(f32[2,32,896]{2,1,0:T(8,128)S(1)} %dynamic-slice_bitcast_fusion.3), channel_id=1, source_target_pairs={{0,1},{1,0},{2,3},{3,2},{4,5},{5,4},{6,7},{7,6},{8,9},{9,8},{10,11... | collective-permute-start | bytes 688136 | tf_op jit(solution)/shard_map/ppermute | solution.py:71
  144.5 17.1 %copy-start.1 = (bf16[256,2048]{1,0:T(8,128)(2,1)S(1)}, bf16[256,2048]{1,0:T(8,128)(2,1)}, u32[]{:S(2)}) copy-start(bf16[256,2048]{1,0:T(8,128)(2,1)} %param.5) | copy-start | bytes 3145732
  144.5 7.3 %collective-permute-start.12 = (f32[2,32,896]{2,1,0:T(8,128)S(1)}, f32[2,32,896]{2,1,0:T(8,128)S(1)}, u32[]{:S(2)}, u32[]{:S(2)}) collective-permute-start(f32[2,32,896]{2,1,0:T(8,128)S(1)} %dynamic-slice_bitcast_fusion.2), channel_id=1, source_target_pairs={{0,8},{4,12},{8,0},{12,4},{1,9},{5,13},{9,1},{13,5},{2,10},{6,14},... | collective-permute-start | bytes 688136 | tf_op jit(solution)/shard_map/ppermute | solution.py:71
  149.0 11.2 %collective-permute-start.10 = (f32[32,896]{1,0:T(8,128)S(1)}, f32[32,896]{1,0:T(8,128)S(1)}, u32[]{:S(2)}, u32[]{:S(2)}) collective-permute-start(f32[32,896]{1,0:T(8,128)S(1)} %dynamic-slice_bitcast_fusion.5), channel_id=1, source_target_pairs={{0,2},{1,3},{2,0},{3,1},{4,6},{5,7},{6,4},{7,5},{8,10},{9,11},{10,... | collective-permute-start | bytes 344072 | tf_op jit(solution)/shard_map/ppermute | solution.py:71
  151.9 9.5 %collective-permute-start.13 = (f32[32,896]{1,0:T(8,128)S(1)}, f32[32,896]{1,0:T(8,128)S(1)}, u32[]{:S(2)}, u32[]{:S(2)}) collective-permute-start(f32[32,896]{1,0:T(8,128)S(1)} %dynamic-slice_bitcast_fusion.4), channel_id=1, source_target_pairs={{0,2},{1,3},{2,0},{3,1},{4,6},{5,7},{6,4},{7,5},{8,10},{9,11},{10,... | collective-permute-start | bytes 344072 | tf_op jit(solution)/shard_map/ppermute | solution.py:71
  161.5 24.2 %collective-permute-start.14 = (bf16[64,896]{1,0:T(8,128)(2,1)S(1)}, bf16[64,896]{1,0:T(8,128)(2,1)S(1)}, u32[]{:S(2)}, u32[]{:S(2)}) collective-permute-start(bf16[64,896]{1,0:T(8,128)(2,1)S(1)} %pad_maximum_fusion.1), channel_id=1, source_target_pairs={{0,2},{1,3},{2,0},{3,1},{4,6},{5,7},{6,4},{7,5},{8,10},{9,11},{10,... | collective-permute-start | bytes 344072 | tf_op jit(solution)/shard_map/ppermute | solution.py:82
  161.6 36.9 %collective-permute-start.17 = (bf16[256,2048]{1,0:T(8,128)(2,1)S(1)}, bf16[256,2048]{1,0:T(8,128)(2,1)S(1)}, u32[]{:S(2)}, u32[]{:S(2)}) collective-permute-start(bf16[256,2048]{1,0:T(8,128)(2,1)S(1)} %copy-done.1), channel_id=1, source_target_pairs={{0,16},{16,0},{1,17},{17,1},{2,18},{18,2},{3,19},{19,3},{4,20},{20... | collective-permute-start | bytes 3145736 | tf_op jit(solution)/shard_map/ppermute | solution.py:99
  164.5 21.1 %collective-permute-start.18 = (f32[2]{0:T(128)S(1)}, f32[2]{0:T(128)S(1)}, u32[]{:S(2)}, u32[]{:S(2)}) collective-permute-start(f32[2]{0:T(128)S(1)} %pad_maximum_fusion.6), channel_id=1, source_target_pairs={{0,16},{16,0},{1,17},{17,1},{2,18},{18,2},{3,19},{19,3},{4,20},{20... | collective-permute-start | bytes 32 | tf_op jit(solution)/shard_map/ppermute | solution.py:45
  185.7 8.0 %collective-permute-start.15 = (bf16[2,64,896]{2,1,0:T(8,128)(2,1)S(1)}, bf16[2,64,896]{2,1,0:T(8,128)(2,1)S(1)}, u32[]{:S(2)}, u32[]{:S(2)}) collective-permute-start(bf16[2,64,896]{2,1,0:T(8,128)(2,1)S(1)} %maximum_select_fusion.5), channel_id=1, source_target_pairs={{0,1},{1,0},{2,3},{3,2},{4,5},{5,4},{6,7},{7,6},{8,9},{9,8},{10,11... | collective-permute-start | bytes 688136 | tf_op jit(solution)/shard_map/ppermute | solution.py:82
  193.8 9.5 %collective-permute-start.16 = (bf16[256,896]{1,0:T(8,128)(2,1)S(1)}, bf16[256,896]{1,0:T(8,128)(2,1)S(1)}, u32[]{:S(2)}, u32[]{:S(2)}) collective-permute-start(bf16[256,896]{1,0:T(8,128)(2,1)S(1)} %bitcast.88), channel_id=1, source_target_pairs={{0,16},{16,0},{1,17},{17,1},{2,18},{18,2},{3,19},{19,3},{4,20},{20... | collective-permute-start | bytes 1376264 | tf_op jit(solution)/shard_map/ppermute | solution.py:229

commit v13 on v11

--- a/solution.py
+++ b/solution.py
@@ -226,11 +226,23 @@
         grad_rows_t = lax.psum(reduced, "wid").astype(jnp.bfloat16)
 
     if grad_rows_pos is not None:
-        grad_other = lax.ppermute(grad_rows_pos, "tok", [(0, 1), (1, 0)])
+        half_rows = tok_rows // 2
         by_pos = (((0,), (0,)), ((), ()))
-        grad_proj = lax.dot_general(
-            grad_rows_pos, hidden, by_pos, preferred_element_type=jnp.float32
-        ) + lax.dot_general(grad_other, hidden_other, by_pos, preferred_element_type=jnp.float32)
+        sums_of = []
+        for rows, hid in ((grad_rows_pos, hidden), (None, hidden_other)):
+            if rows is None:
+                rows = [
+                    lax.ppermute(grad_rows_pos[i * half_rows : (i + 1) * half_rows], "tok", [(0, 1), (1, 0)])
+                    for i in range(2)
+                ]
+            else:
+                rows = [rows[i * half_rows : (i + 1) * half_rows] for i in range(2)]
+            dots = [
+                lax.dot_general(rows[i], hid[i * half_rows : (i + 1) * half_rows], by_pos, preferred_element_type=jnp.float32)
+                for i in range(2)
+            ]
+            sums_of.append(dots[0] + dots[1])
+        grad_proj = sums_of[0] + sums_of[1]
     elif n_tok == 2:
         grad_other = lax.ppermute(grad_rows_t, "tok", [(0, 1), (1, 0)])
         first = t == 0

time: 193 us -> 191 us (0.990)
  waiting for transfers between devices: 83.7 us -> 79 us
  matrix products: 27.8 us -> 30.9 us
    dot_general x2 -> x4, matrix products: 6.58 us -> 9.77 us  [on_device(): lax.dot_general(rows[i], hid[i * half_rows:(i + 1) * half_rows], by_pos,...]
    ppermute x1 -> x2, waiting for transfers between devices: 3.95 us -> 1.06 us  [on_device(): lax.ppermute(grad_rows_pos[i * half_rows:(i + 1) * half_rows], 'tok', [(0...]
    ppermute x4, waiting for transfers between devices: 22.8 us -> 20.8 us  [doubling_gather(): other = lax.ppermute(x, ax, [(k, k ^ b) for k in range(n)])]
  transfers between devices with their start and end apart: 19 -> 20, of which waited for: 14 -> 14; matrix products, arithmetic and copies ran while one was open for 11% -> 14% of each run, Pallas kernels for 0% -> 0%
where the time goes in v13:
time: 191 us
  waiting for transfers between devices  79 us (41%)
  blocking collectives  39.1 us (20%)
  matrix products  30.9 us (16%)
  starting transfers between devices  26.6 us (14%)
  other arithmetic  8.14 us (4%)
  between operations  3.53 us (2%)
  local copies, waits for them, and re-layouts  3.47 us (2%)
    psum x1, blocking collectives, on_device(): summed = lax.psum(partial_value, 'wid')  39.1 us
    ppermute x1, waiting for transfers between devices, tok_pieces(): pieces.append(lax.ppermute(x, 'tok', perm))  32.5 us
    ppermute x4, waiting for transfers between devices, doubling_gather(): other = lax.ppermute(x, ax, [(k, k ^ b) for k in range(n)])  20.8 us
    ppermute x6, waiting for transfers between devices, halving_steps(): x = keep + lax.ppermute(send, ax, [(k, k ^ b) for k in range(n)])  18.2 us
    ppermute x6, starting transfers between devices, halving_steps(): x = keep + lax.ppermute(send, ax, [(k, k ^ b) for k in range(n)])  10.9 us
    dot_general x4, matrix products, quarter_dots(): jnp.dot(dlogits, lax.dynamic_slice_in_dim(piece, sel * q_cols, q_cols, ax...  9.96 us
    dot_general x4, matrix products, on_device(): lax.dot_general(rows[i], hid[i * half_rows:(i + 1) * half_rows], by_pos,...  9.77 us
    dot_general x2, matrix products, on_device(): lax.dot_general(cols, piece, (((1,), (1,)), ((), ())), preferred_element_...  7.53 us
  transfers between devices with their start and end apart: 20, of which 14 were waited for; matrix products, arithmetic and copies ran while one was open for 14% of the time, Pallas kernels for 0%

profile of v13, /device:TPU:0, one launch (start us, length us, event | category | flops | bytes accessed | tf_op | source)
XLA Modules:
  0.0 190.8 jit_solution(2983659393567202485)
XLA Ops:
  0.6 3.0 %collective-permute-start.2 = (bf16[1216,1792]{1,0:T(8,128)(2,1)}, bf16[1216,1792]{1,0:T(8,128)(2,1)}, u32[]{:S(2)}, u32[]{:S(2)}) collective-permute-start(bf16[1216,1792]{1,0:T(8,128)(2,1)} %param.7), channel_id=1, source_target_pairs={{0,16},{16,0},{1,17},{17,1},{2,18},{18,2},{3,19},{19,3},{4,20},{20... | collective-permute-start | bytes 13074440 | tf_op jit(solution)/shard_map/ppermute | solution.py:11
  3.6 3.6 %fusion.51 = f32[256,896]{1,0:T(8,128)S(1)} fusion(bf16[256,2048]{1,0:T(8,128)(2,1)} %param.5, bf16[896,2048]{1,0:T(8,128)(2,1)} %param.6), kind=kOutput, calls=%fused_computation.93 | convolution fusion | flops 939524096 | bytes 5636096 | tf_op jit(solution)/shard_map/dot_general | solution.py:101
  7.3 39.1 %all-reduce.1 = bf16[256,896]{1,0:T(8,128)(2,1)S(1)} all-reduce(f32[256,896]{1,0:T(8,128)S(1)} %fusion.51), channel_id=1, replica_groups=mesh['tok'=2,'voc'=4,'wid'=4] {'wid'}, use_global_device_ids=true, to_apply=%region_0.0 | all-reduce | flops 229376 | bytes 1376256 | tf_op jit(solution)/shard_map/psum | solution.py:104
  48.0 7.9 %collective-permute-done = bf16[256,896]{1,0:T(8,128)(2,1)S(1)} collective-permute-done((bf16[256,896]{1,0:T(8,128)(2,1)S(1)}, bf16[256,896]{1,0:T(8,128)(2,1)S(1)}, u32[]{:S(2)}, u32[]{:S(2)}) %collective-permute-start) | collective-permute-done | bytes 458784 | tf_op jit(solution)/shard_map/ppermute | solution.py:82
  56.4 2.2 %collective-permute-done.1 = bf16[2,256,896]{2,1,0:T(8,128)(2,1)S(1)} collective-permute-done((bf16[2,256,896]{2,1,0:T(8,128)(2,1)S(1)}, bf16[2,256,896]{2,1,0:T(8,128)(2,1)S(1)}, u32[]{:S(2)}, u32[]{:S(2)}) %collective-permute-start.1) | collective-permute-done | bytes 917536 | tf_op jit(solution)/shard_map/ppermute | solution.py:82
  59.1 2.4 %copy.8 = bf16[256,4,896]{0,2,1:T(8,128)(2,1)} copy(bf16[256,4,896]{2,0,1:T(8,128)(2,1)S(1)} %bitcast.85) | data formatting | bytes 3670016 | tf_op jit(solution)/shard_map/transpose | solution.py:107
  61.5 3.9 %fusion.21 = f32[256,1216]{0,1:T(8,128)S(1)} fusion(bf16[1216,1792]{1,0:T(8,128)(2,1)} %param.7, bf16[256,3584]{0,1:T(8,128)(2,1)} %bitcast.89, s32[]{:T(128)S(6)} %select_n.168), kind=kOutput, calls=%fused_computation.24 | convolution fusion | flops 1115684864 | bytes 6520836 | tf_op jit(solution)/shard_map/dot_general | solution.py:114
  65.5 32.5 %collective-permute-done.2 = bf16[1216,1792]{1,0:T(8,128)(2,1)} collective-permute-done((bf16[1216,1792]{1,0:T(8,128)(2,1)}, bf16[1216,1792]{1,0:T(8,128)(2,1)}, u32[]{:S(2)}, u32[]{:S(2)}) %collective-permute-start.2) | collective-permute-done | bytes 4358176 | tf_op jit(solution)/shard_map/ppermute | solution.py:11
  98.0 3.6 %fusion.50 = (f32[256]{0:T(256)S(1)}, f32[256,1216]{0,1:T(8,128)S(1)}) fusion(f32[256,1216]{0,1:T(8,128)S(1)} %fusion.21, bf16[1216,1792]{1,0:T(8,128)(2,1)} %collective-permute-done.2, bf16[256,3584]{0,1:T(8,128)(2,1)S(1)} %bitcast.90, s32[]{:T(128)S(6)} %select_n.170), kind=kOutput, calls=%fused_computation.92 | convolution fusion | flops 1116307200 | bytes 7767044 | tf_op jit(solution)/shard_map/dot_general | solution.py:114
  107.0 1.9 collective-permute-start.5
  110.7 2.9 %collective-permute-start.6 = (f32[3,256]{1,0:T(4,128)S(1)}, f32[3,256]{1,0:T(4,128)S(1)}, u32[]{:S(2)}, u32[]{:S(2)}) collective-permute-start(f32[3,256]{1,0:T(4,128)S(1)} %pad_maximum_fusion.5), channel_id=1, source_target_pairs={{0,2},{1,3},{2,0},{3,1},{4,6},{5,7},{6,4},{7,5},{8,10},{9,11},{10,... | collective-permute-start | bytes 9224 | tf_op jit(solution)/shard_map/ppermute | solution.py:33
  116.2 2.5 %fusion.14 = f32[1,256,896]{2,1,0:T(8,128)S(1)} fusion(bf16[256,1216]{0,1:T(8,128)(2,1)S(1)} %multiply_convert_fusion, bf16[1216,1792]{1,0:T(8,128)(2,1)} %param.7, s32[]{:T(128)S(6)} %select_n.173), kind=kOutput, calls=%fused_computation.15 | convolution fusion | flops 557842432 | bytes 3719172 | tf_op jit(solution)/shard_map/dot_general | solution.py:158
  118.7 2.5 %fusion.17 = f32[1,256,896]{2,1,0:T(8,128)S(1)} fusion(bf16[256,1216]{0,1:T(8,128)(2,1)S(1)} %multiply_convert_fusion, bf16[1216,1792]{1,0:T(8,128)(2,1)} %collective-permute-done.2, s32[]{:T(128)S(6)} %select_n.173), kind=kOutput, calls=%fused_computation.16 | convolution fusion | flops 557842432 | bytes 3719172 | tf_op jit(solution)/shard_map/dot_general | solution.py:158
  121.4 2.5 %fusion.8 = f32[1,256,896]{2,1,0:T(8,128)S(1)} fusion(bf16[256,1216]{0,1:T(8,128)(2,1)S(1)} %multiply_convert_fusion, bf16[1216,1792]{1,0:T(8,128)(2,1)} %param.7, s32[]{:T(128)S(6)} %select_n.172), kind=kOutput, calls=%fused_computation.13 | convolution fusion | flops 557842432 | bytes 3719172 | tf_op jit(solution)/shard_map/dot_general | solution.py:158
  123.9 2.5 %fusion.11 = f32[1,256,896]{2,1,0:T(8,128)S(1)} fusion(bf16[256,1216]{0,1:T(8,128)(2,1)S(1)} %multiply_convert_fusion, bf16[1216,1792]{1,0:T(8,128)(2,1)} %collective-permute-done.2, s32[]{:T(128)S(6)} %select_n.172), kind=kOutput, calls=%fused_computation.14 | convolution fusion | flops 557842432 | bytes 3719172 | tf_op jit(solution)/shard_map/dot_general | solution.py:158
  135.3 6.2 %collective-permute-done.11 = f32[2,2,32,896]{3,2,1,0:T(8,128)} collective-permute-done((f32[2,2,32,896]{3,2,1,0:T(8,128)S(1)}, f32[2,2,32,896]{3,2,1,0:T(8,128)}, u32[]{:S(2)}, u32[]{:S(2)}) %collective-permute-start.11) | collective-permute-done | bytes 458784 | tf_op jit(solution)/shard_map/ppermute | solution.py:71
  146.1 3.9 %collective-permute-done.12 = f32[2,32,896]{2,1,0:T(8,128)S(1)} collective-permute-done((f32[2,32,896]{2,1,0:T(8,128)S(1)}, f32[2,32,896]{2,1,0:T(8,128)S(1)}, u32[]{:S(2)}, u32[]{:S(2)}) %collective-permute-start.12) | collective-permute-done | bytes 229408 | tf_op jit(solution)/shard_map/ppermute | solution.py:71
  150.1 2.7 %collective-permute-start.13 = (f32[32,896]{1,0:T(8,128)S(1)}, f32[32,896]{1,0:T(8,128)S(1)}, u32[]{:S(2)}, u32[]{:S(2)}) collective-permute-start(f32[32,896]{1,0:T(8,128)S(1)} %dynamic-slice_bitcast_fusion.4), channel_id=1, source_target_pairs={{0,2},{1,3},{2,0},{3,1},{4,6},{5,7},{6,4},{7,5},{8,10},{9,11},{10,... | collective-permute-start | bytes 344072 | tf_op jit(solution)/shard_map/ppermute | solution.py:71
  154.2 6.8 %collective-permute-done.13 = f32[32,896]{1,0:T(8,128)S(1)} collective-permute-done((f32[32,896]{1,0:T(8,128)S(1)}, f32[32,896]{1,0:T(8,128)S(1)}, u32[]{:S(2)}, u32[]{:S(2)}) %collective-permute-start.13) | collective-permute-done | bytes 114720 | tf_op jit(solution)/shard_map/ppermute | solution.py:71
  165.8 4.7 %collective-permute-done.14 = bf16[64,896]{1,0:T(8,128)(2,1)S(1)} collective-permute-done((bf16[64,896]{1,0:T(8,128)(2,1)S(1)}, bf16[64,896]{1,0:T(8,128)(2,1)S(1)}, u32[]{:S(2)}, u32[]{:S(2)}) %collective-permute-start.14) | collective-permute-done | bytes 114720 | tf_op jit(solution)/shard_map/ppermute | solution.py:82
  170.6 5.9 %collective-permute-done.15 = bf16[2,64,896]{2,1,0:T(8,128)(2,1)S(1)} collective-permute-done((bf16[2,64,896]{2,1,0:T(8,128)(2,1)S(1)}, bf16[2,64,896]{2,1,0:T(8,128)(2,1)S(1)}, u32[]{:S(2)}, u32[]{:S(2)}) %collective-permute-start.15) | collective-permute-done | bytes 229408 | tf_op jit(solution)/shard_map/ppermute | solution.py:82
  178.8 2.2 %fusion.26 = f32[896,2048]{1,0:T(8,128)S(1)} fusion(bf16[128,896]{1,0:T(8,128)(2,1)S(1)} %bitcast.96, bf16[256,2048]{1,0:T(8,128)(2,1)} %param.5), kind=kOutput, calls=%fused_computation.29 | convolution fusion | flops 469762048 | bytes 8093696 | tf_op jit(solution)/shard_map/dot_general | solution.py:241
  181.0 2.2 %fusion.28 = f32[896,2048]{1,0:T(8,128)S(1)} fusion(bf16[128,896]{1,0:T(8,128)(2,1)S(1)} %bitcast.94, bf16[256,2048]{1,0:T(8,128)(2,1)} %param.5), kind=kOutput, calls=%fused_computation.31 | convolution fusion | flops 469762048 | bytes 8093696 | tf_op jit(solution)/shard_map/dot_general | solution.py:241
  185.4 4.3 %add_add_fusion = f32[896,2048]{1,0:T(8,128)} fusion(f32[896,2048]{1,0:T(8,128)S(1)} %fusion.23, f32[896,2048]{1,0:T(8,128)S(1)} %fusion.28, f32[896,2048]{1,0:T(8,128)S(1)} %fusion.26, bf16[128,896]{1,0:T(8,128)(2,1)S(1)} %collective-permute-done.16, bf16[256,2048]{1,0:T(8,128)(2,1)S(1)} %collective-permute-done.17), kind=kOutput, calls=%fused_computation | convolution fusion | flops 475267072 | bytes 30113792 | tf_op jit(solution)/shard_map/dot_general | solution.py:241
  (76 shorter events, 35.2 us)
Async XLA Ops:
  0.6 97.4 %collective-permute-start.2 = (bf16[1216,1792]{1,0:T(8,128)(2,1)}, bf16[1216,1792]{1,0:T(8,128)(2,1)}, u32[]{:S(2)}, u32[]{:S(2)}) collective-permute-start(bf16[1216,1792]{1,0:T(8,128)(2,1)} %param.7), channel_id=1, source_target_pairs={{0,16},{16,0},{1,17},{17,1},{2,18},{18,2},{3,19},{19,3},{4,20},{20... | collective-permute-start | bytes 13074440 | tf_op jit(solution)/shard_map/ppermute | solution.py:11
  7.3 48.9 %copy-start.2 = (s32[256]{0:T(256)S(1)}, s32[256]{0:T(256)}, u32[]{:S(2)}) copy-start(s32[256]{0:T(256)} %param.8) | copy-start | bytes 3076
  46.4 9.5 %collective-permute-start = (bf16[256,896]{1,0:T(8,128)(2,1)S(1)}, bf16[256,896]{1,0:T(8,128)(2,1)S(1)}, u32[]{:S(2)}, u32[]{:S(2)}) collective-permute-start(bf16[256,896]{1,0:T(8,128)(2,1)S(1)} %all-reduce.1), channel_id=1, source_target_pairs={{0,8},{4,12},{8,0},{12,4},{1,9},{5,13},{9,1},{13,5},{2,10},{6,14},... | collective-permute-start | bytes 1376264 | tf_op jit(solution)/shard_map/ppermute | solution.py:82
  56.1 2.5 %collective-permute-start.1 = (bf16[2,256,896]{2,1,0:T(8,128)(2,1)S(1)}, bf16[2,256,896]{2,1,0:T(8,128)(2,1)S(1)}, u32[]{:S(2)}, u32[]{:S(2)}) collective-permute-start(bf16[2,256,896]{2,1,0:T(8,128)(2,1)S(1)} %maximum_select_fusion.2), channel_id=1, source_target_pairs={{0,4},{4,0},{8,12},{12,8},{1,5},{5,1},{9,13},{13,9},{2,6},{6,2},{1... | collective-permute-start | bytes 2752520 | tf_op jit(solution)/shard_map/ppermute | solution.py:82
  61.5 36.5 %copy-start = (bf16[256,4,896]{0,2,1:T(8,128)(2,1)S(1)}, bf16[256,4,896]{0,2,1:T(8,128)(2,1)}, u32[]{:S(2)}) copy-start(bf16[256,4,896]{0,2,1:T(8,128)(2,1)} %copy.8) | copy-start | bytes 5505028
  65.5 48.1 %copy-start.1 = (s32[256]{0:T(256)S(1)}, s32[256]{0:T(256)}, u32[]{:S(2)}) copy-start(s32[256]{0:T(256)} %param.9) | copy-start | bytes 3076
  102.0 1.2 collective-permute-start.3
  103.3 3.7 %collective-permute-start.4 = (f32[3,256]{1,0:T(4,128)S(1)}, f32[3,256]{1,0:T(4,128)S(1)}, u32[]{:S(2)}, u32[]{:S(2)}) collective-permute-start(f32[3,256]{1,0:T(4,128)S(1)} %pad_maximum_fusion.3), channel_id=1, source_target_pairs={{0,8},{4,12},{8,0},{12,4},{1,9},{5,13},{9,1},{13,5},{2,10},{6,14},... | collective-permute-start | bytes 9224 | tf_op jit(solution)/shard_map/ppermute | solution.py:33
  107.0 3.7 %collective-permute-start.5 = (f32[3,256]{1,0:T(4,128)S(1)}, f32[3,256]{1,0:T(4,128)S(1)}, u32[]{:S(2)}, u32[]{:S(2)}) collective-permute-start(f32[3,256]{1,0:T(4,128)S(1)} %pad_maximum_fusion.4), channel_id=1, source_target_pairs={{0,1},{1,0},{2,3},{3,2},{4,5},{5,4},{6,7},{7,6},{8,9},{9,8},{10,11... | collective-permute-start | bytes 9224 | tf_op jit(solution)/shard_map/ppermute | solution.py:33
  110.7 4.6 %collective-permute-start.6 = (f32[3,256]{1,0:T(4,128)S(1)}, f32[3,256]{1,0:T(4,128)S(1)}, u32[]{:S(2)}, u32[]{:S(2)}) collective-permute-start(f32[3,256]{1,0:T(4,128)S(1)} %pad_maximum_fusion.5), channel_id=1, source_target_pairs={{0,2},{1,3},{2,0},{3,1},{4,6},{5,7},{6,4},{7,5},{8,10},{9,11},{10,... | collective-permute-start | bytes 9224 | tf_op jit(solution)/shard_map/ppermute | solution.py:33
  121.3 5.1 %collective-permute-start.7 = (f32[2,256,896]{2,1,0:T(8,128)S(1)}, f32[2,256,896]{2,1,0:T(8,128)}, u32[]{:S(2)}, u32[]{:S(2)}) collective-permute-start(f32[2,256,896]{2,1,0:T(8,128)S(1)} %pad_maximum_fusion), channel_id=1, source_target_pairs={{0,4},{4,0},{8,12},{12,8},{1,5},{5,1},{9,13},{13,9},{2,6},{6,2},{1... | collective-permute-start | bytes 5505032 | tf_op jit(solution)/shard_map/ppermute | solution.py:168
  128.4 13.1 %collective-permute-start.11 = (f32[2,2,32,896]{3,2,1,0:T(8,128)S(1)}, f32[2,2,32,896]{3,2,1,0:T(8,128)}, u32[]{:S(2)}, u32[]{:S(2)}) collective-permute-start(f32[2,2,32,896]{3,2,1,0:T(8,128)S(1)} %dynamic-slice_bitcast_fusion), channel_id=1, source_target_pairs={{0,1},{1,0},{2,3},{3,2},{4,5},{5,4},{6,7},{7,6},{8,9},{9,8},{10,11... | collective-permute-start | bytes 1376264 | tf_op jit(solution)/shard_map/ppermute | solution.py:71
  130.3 52.9 %collective-permute-start.17 = (bf16[256,2048]{1,0:T(8,128)(2,1)}, bf16[256,2048]{1,0:T(8,128)(2,1)S(1)}, u32[]{:S(2)}, u32[]{:S(2)}) collective-permute-start(bf16[256,2048]{1,0:T(8,128)(2,1)} %param.5), channel_id=1, source_target_pairs={{0,16},{16,0},{1,17},{17,1},{2,18},{18,2},{3,19},{19,3},{4,20},{20... | collective-permute-start | bytes 3145736 | tf_op jit(solution)/shard_map/ppermute | solution.py:99
  131.8 12.6 %collective-permute-start.8 = (f32[2,2,32,896]{3,2,1,0:T(8,128)S(1)}, f32[2,2,32,896]{3,2,1,0:T(8,128)S(1)}, u32[]{:S(2)}, u32[]{:S(2)}) collective-permute-start(f32[2,2,32,896]{3,2,1,0:T(8,128)S(1)} %dynamic-slice_bitcast_fusion.1), channel_id=1, source_target_pairs={{0,8},{4,12},{8,0},{12,4},{1,9},{5,13},{9,1},{13,5},{2,10},{6,14},... | collective-permute-start | bytes 1376264 | tf_op jit(solution)/shard_map/ppermute | solution.py:71
  134.8 27.7 %collective-permute-start.19 = (f32[2]{0:T(128)S(1)}, f32[2]{0:T(128)S(1)}, u32[]{:S(2)}, u32[]{:S(2)}) collective-permute-start(f32[2]{0:T(128)S(1)} %pad_maximum_fusion.6), channel_id=1, source_target_pairs={{0,16},{16,0},{1,17},{17,1},{2,18},{18,2},{3,19},{19,3},{4,20},{20... | collective-permute-start | bytes 32 | tf_op jit(solution)/shard_map/ppermute | solution.py:45
  142.7 7.3 %collective-permute-start.12 = (f32[2,32,896]{2,1,0:T(8,128)S(1)}, f32[2,32,896]{2,1,0:T(8,128)S(1)}, u32[]{:S(2)}, u32[]{:S(2)}) collective-permute-start(f32[2,32,896]{2,1,0:T(8,128)S(1)} %dynamic-slice_bitcast_fusion.2), channel_id=1, source_target_pairs={{0,8},{4,12},{8,0},{12,4},{1,9},{5,13},{9,1},{13,5},{2,10},{6,14},... | collective-permute-start | bytes 688136 | tf_op jit(solution)/shard_map/ppermute | solution.py:71
  144.5 8.3 %collective-permute-start.9 = (f32[2,32,896]{2,1,0:T(8,128)S(1)}, f32[2,32,896]{2,1,0:T(8,128)S(1)}, u32[]{:S(2)}, u32[]{:S(2)}) collective-permute-start(f32[2,32,896]{2,1,0:T(8,128)S(1)} %dynamic-slice_bitcast_fusion.3), channel_id=1, source_target_pairs={{0,1},{1,0},{2,3},{3,2},{4,5},{5,4},{6,7},{7,6},{8,9},{9,8},{10,11... | collective-permute-start | bytes 688136 | tf_op jit(solution)/shard_map/ppermute | solution.py:71
  150.1 11.0 %collective-permute-start.13 = (f32[32,896]{1,0:T(8,128)S(1)}, f32[32,896]{1,0:T(8,128)S(1)}, u32[]{:S(2)}, u32[]{:S(2)}) collective-permute-start(f32[32,896]{1,0:T(8,128)S(1)} %dynamic-slice_bitcast_fusion.4), channel_id=1, source_target_pairs={{0,2},{1,3},{2,0},{3,1},{4,6},{5,7},{6,4},{7,5},{8,10},{9,11},{10,... | collective-permute-start | bytes 344072 | tf_op jit(solution)/shard_map/ppermute | solution.py:71
  152.8 9.5 %collective-permute-start.10 = (f32[32,896]{1,0:T(8,128)S(1)}, f32[32,896]{1,0:T(8,128)S(1)}, u32[]{:S(2)}, u32[]{:S(2)}) collective-permute-start(f32[32,896]{1,0:T(8,128)S(1)} %dynamic-slice_bitcast_fusion.5), channel_id=1, source_target_pairs={{0,2},{1,3},{2,0},{3,1},{4,6},{5,7},{6,4},{7,5},{8,10},{9,11},{10,... | collective-permute-start | bytes 344072 | tf_op jit(solution)/shard_map/ppermute | solution.py:71
  162.4 8.1 %collective-permute-start.14 = (bf16[64,896]{1,0:T(8,128)(2,1)S(1)}, bf16[64,896]{1,0:T(8,128)(2,1)S(1)}, u32[]{:S(2)}, u32[]{:S(2)}) collective-permute-start(bf16[64,896]{1,0:T(8,128)(2,1)S(1)} %pad_maximum_fusion.1), channel_id=1, source_target_pairs={{0,2},{1,3},{2,0},{3,1},{4,6},{5,7},{6,4},{7,5},{8,10},{9,11},{10,... | collective-permute-start | bytes 344072 | tf_op jit(solution)/shard_map/ppermute | solution.py:82
  170.5 6.1 %collective-permute-start.15 = (bf16[2,64,896]{2,1,0:T(8,128)(2,1)S(1)}, bf16[2,64,896]{2,1,0:T(8,128)(2,1)S(1)}, u32[]{:S(2)}, u32[]{:S(2)}) collective-permute-start(bf16[2,64,896]{2,1,0:T(8,128)(2,1)S(1)} %maximum_select_fusion.5), channel_id=1, source_target_pairs={{0,1},{1,0},{2,3},{3,2},{4,5},{5,4},{6,7},{7,6},{8,9},{9,8},{10,11... | collective-permute-start | bytes 688136 | tf_op jit(solution)/shard_map/ppermute | solution.py:82
  176.7 6.5 %collective-permute-start.18 = (bf16[128,896]{1,0:T(8,128)(2,1)S(1)}, bf16[128,896]{1,0:T(8,128)(2,1)S(1)}, u32[]{:S(2)}, u32[]{:S(2)}) collective-permute-start(bf16[128,896]{1,0:T(8,128)(2,1)S(1)} %bitcast.95), channel_id=1, source_target_pairs={{0,16},{16,0},{1,17},{17,1},{2,18},{18,2},{3,19},{19,3},{4,20},{20... | collective-permute-start | bytes 688136 | tf_op jit(solution)/shard_map/ppermute | solution.py:235
  178.3 7.1 %collective-permute-start.16 = (bf16[128,896]{1,0:T(8,128)(2,1)S(1)}, bf16[128,896]{1,0:T(8,128)(2,1)S(1)}, u32[]{:S(2)}, u32[]{:S(2)}) collective-permute-start(bf16[128,896]{1,0:T(8,128)(2,1)S(1)} %bitcast.93), channel_id=1, source_target_pairs={{0,16},{16,0},{1,17},{17,1},{2,18},{18,2},{3,19},{19,3},{4,20},{20... | collective-permute-start | bytes 688136 | tf_op jit(solution)/shard_map/ppermute | solution.py:235

commit v14 on v13

--- a/solution.py
+++ b/solution.py
@@ -36,6 +36,23 @@
     return stats
 
 
+def shift_gather(x, ax):
+    n = lax.axis_size(ax)
+    got = [x] + [lax.ppermute(x, ax, [(k, (k + sh) % n) for k in range(n)]) for sh in range(1, n)]
+    rev = jnp.stack([got[(-j) % n] for j in range(n)])
+    return jnp.roll(rev, lax.axis_index(ax), axis=0)
+
+
+def gather_combine(stats, axes):
+    for ax in axes:
+        g = shift_gather(stats, ax)
+        out = g[0]
+        for k in range(1, g.shape[0]):
+            out = combine(out, g[k])
+        stats = out
+    return stats
+
+
 def tree_sum(x, ax):
     n = lax.axis_size(ax)
     if n & (n - 1):
@@ -125,7 +142,7 @@
     weight = valid.astype(jnp.float32)
 
     stats = jnp.stack([peak_here, exp_here, picked_here])
-    stats = butterfly(stats, ("voc", "wid"))
+    stats = gather_combine(stats, ("voc", "wid"))
     log_total = stats[0] + jnp.log(stats[1])
     picked = stats[2]
     sums = jnp.stack([jnp.sum(weight * (log_total - picked)), jnp.sum(weight)])

time: 191 us -> 192 us (level)
  waiting for transfers between devices: 79 us -> 85.1 us
  starting transfers between devices: 26.6 us -> 21.4 us
    ppermute x6, starting transfers between devices: 10.9 us -> 5.35 us  [halving_steps(): x = keep + lax.ppermute(send, ax, [(k, k ^ b) for k in range(n)])]
    ppermute x6, waiting for transfers between devices: 18.2 us -> 23.4 us  [halving_steps(): x = keep + lax.ppermute(send, ax, [(k, k ^ b) for k in range(n)])]
    ppermute x4 -> x6, waiting for transfers between devices: 6.45 us -> 7.24 us  [shift_gather(): lax.ppermute(x, ax, [(k, (k + sh) % n) for k in range(n)])]
    ppermute x4 -> x6, starting transfers between devices: 6.69 us -> 7.02 us  [shift_gather(): lax.ppermute(x, ax, [(k, (k + sh) % n) for k in range(n)])]
  transfers between devices with their start and end apart: 20 -> 22, of which waited for: 14 -> 16; matrix products, arithmetic and copies ran while one was open for 14% -> 14% of each run, Pallas kernels for 0% -> 0%
where the time goes in v14:
time: 192 us
  waiting for transfers between devices  85.1 us (44%)
  blocking collectives  39.1 us (20%)
  matrix products  30.9 us (16%)
  starting transfers between devices  21.4 us (11%)
  other arithmetic  8.22 us (4%)
  between operations  3.54 us (2%)
  local copies, waits for them, and re-layouts  3.47 us (2%)
    psum x1, blocking collectives, on_device(): summed = lax.psum(partial_value, 'wid')  39.1 us
    ppermute x1, waiting for transfers between devices, tok_pieces(): pieces.append(lax.ppermute(x, 'tok', perm))  32.5 us
    ppermute x6, waiting for transfers between devices, halving_steps(): x = keep + lax.ppermute(send, ax, [(k, k ^ b) for k in range(n)])  23.4 us
    ppermute x4, waiting for transfers between devices, doubling_gather(): other = lax.ppermute(x, ax, [(k, k ^ b) for k in range(n)])  19 us
    dot_general x4, matrix products, quarter_dots(): jnp.dot(dlogits, lax.dynamic_slice_in_dim(piece, sel * q_cols, q_cols, ax...  9.96 us
    dot_general x4, matrix products, on_device(): lax.dot_general(rows[i], hid[i * half_rows:(i + 1) * half_rows], by_pos,...  9.77 us
    dot_general x2, matrix products, on_device(): lax.dot_general(cols, piece, (((1,), (1,)), ((), ())), preferred_element_...  7.57 us
    ppermute x6, waiting for transfers between devices, shift_gather(): lax.ppermute(x, ax, [(k, (k + sh) % n) for k in range(n)])  7.24 us
  transfers between devices with their start and end apart: 22, of which 16 were waited for; matrix products, arithmetic and copies ran while one was open for 14% of the time, Pallas kernels for 0%

profile of v14, /device:TPU:0, one launch (start us, length us, event | category | flops | bytes accessed | tf_op | source)
XLA Modules:
  0.0 191.8 jit_solution(765140626620460381)
XLA Ops:
  0.6 3.0 %collective-permute-start.2 = (bf16[1216,1792]{1,0:T(8,128)(2,1)}, bf16[1216,1792]{1,0:T(8,128)(2,1)}, u32[]{:S(2)}, u32[]{:S(2)}) collective-permute-start(bf16[1216,1792]{1,0:T(8,128)(2,1)} %param.9), channel_id=1, source_target_pairs={{0,16},{16,0},{1,17},{17,1},{2,18},{18,2},{3,19},{19,3},{4,20},{20... | collective-permute-start | bytes 13074440 | tf_op jit(solution)/shard_map/ppermute | solution.py:11
  3.6 3.6 %fusion.79 = f32[256,896]{1,0:T(8,128)S(1)} fusion(bf16[256,2048]{1,0:T(8,128)(2,1)} %param.7, bf16[896,2048]{1,0:T(8,128)(2,1)} %param.8), kind=kOutput, calls=%fused_computation.138 | convolution fusion | flops 939524096 | bytes 5636096 | tf_op jit(solution)/shard_map/dot_general | solution.py:118
  7.3 39.1 %all-reduce.1 = bf16[256,896]{1,0:T(8,128)(2,1)S(1)} all-reduce(f32[256,896]{1,0:T(8,128)S(1)} %fusion.79), channel_id=1, replica_groups=mesh['tok'=2,'voc'=4,'wid'=4] {'wid'}, use_global_device_ids=true, to_apply=%region_0.0 | all-reduce | flops 229376 | bytes 1376256 | tf_op jit(solution)/shard_map/psum | solution.py:121
  48.0 7.9 %collective-permute-done = bf16[256,896]{1,0:T(8,128)(2,1)S(1)} collective-permute-done((bf16[256,896]{1,0:T(8,128)(2,1)S(1)}, bf16[256,896]{1,0:T(8,128)(2,1)S(1)}, u32[]{:S(2)}, u32[]{:S(2)}) %collective-permute-start) | collective-permute-done | bytes 458784 | tf_op jit(solution)/shard_map/ppermute | solution.py:99
  56.4 2.2 %collective-permute-done.1 = bf16[2,256,896]{2,1,0:T(8,128)(2,1)S(1)} collective-permute-done((bf16[2,256,896]{2,1,0:T(8,128)(2,1)S(1)}, bf16[2,256,896]{2,1,0:T(8,128)(2,1)S(1)}, u32[]{:S(2)}, u32[]{:S(2)}) %collective-permute-start.1) | collective-permute-done | bytes 917536 | tf_op jit(solution)/shard_map/ppermute | solution.py:99
  59.1 2.4 %copy.8 = bf16[256,4,896]{0,2,1:T(8,128)(2,1)} copy(bf16[256,4,896]{2,0,1:T(8,128)(2,1)S(1)} %bitcast.166) | data formatting | bytes 3670016 | tf_op jit(solution)/shard_map/transpose | solution.py:124
  61.5 4.0 %fusion.21 = f32[256,1216]{0,1:T(8,128)S(1)} fusion(bf16[1216,1792]{1,0:T(8,128)(2,1)} %param.9, bf16[256,3584]{0,1:T(8,128)(2,1)} %bitcast.170, s32[]{:T(128)S(6)} %select_n.177), kind=kOutput, calls=%fused_computation.24 | convolution fusion | flops 1115684864 | bytes 6520836 | tf_op jit(solution)/shard_map/dot_general | solution.py:131
  65.5 32.5 %collective-permute-done.2 = bf16[1216,1792]{1,0:T(8,128)(2,1)} collective-permute-done((bf16[1216,1792]{1,0:T(8,128)(2,1)}, bf16[1216,1792]{1,0:T(8,128)(2,1)}, u32[]{:S(2)}, u32[]{:S(2)}) %collective-permute-start.2) | collective-permute-done | bytes 4358176 | tf_op jit(solution)/shard_map/ppermute | solution.py:11
  98.0 3.6 %fusion.78 = (f32[256]{0:T(256)S(1)}, f32[256,1216]{0,1:T(8,128)S(1)}) fusion(f32[256,1216]{0,1:T(8,128)S(1)} %fusion.21, bf16[1216,1792]{1,0:T(8,128)(2,1)} %collective-permute-done.2, bf16[256,3584]{0,1:T(8,128)(2,1)S(1)} %bitcast.171, s32[]{:T(128)S(6)} %select_n.179), kind=kOutput, calls=%fused_computation.137 | convolution fusion | flops 1116307200 | bytes 7767044 | tf_op jit(solution)/shard_map/dot_general | solution.py:131
  107.0 2.7 %collective-permute-start.7 = (f32[3,256]{1,0:T(4,128)S(1)}, f32[3,256]{1,0:T(4,128)S(1)}, u32[]{:S(2)}, u32[]{:S(2)}) collective-permute-start(f32[3,256]{1,0:T(4,128)S(1)} %get-tuple-element.23), channel_id=1, source_target_pairs={{0,2},{1,3},{2,0},{3,1},{4,6},{5,7},{6,4},{7,5},{8,10},{9,11},{10,... | collective-permute-start | bytes 9224 | tf_op jit(solution)/shard_map/ppermute | solution.py:41
  113.2 3.1 %collective-permute-done.8 = f32[3,256]{1,0:T(4,128)S(1)} collective-permute-done((f32[3,256]{1,0:T(4,128)S(1)}, f32[3,256]{1,0:T(4,128)S(1)}, u32[]{:S(2)}, u32[]{:S(2)}) %collective-permute-start.8) | collective-permute-done | bytes 3104 | tf_op jit(solution)/shard_map/ppermute | solution.py:41
  117.4 2.5 %fusion.14 = f32[1,256,896]{2,1,0:T(8,128)S(1)} fusion(bf16[256,1216]{0,1:T(8,128)(2,1)S(1)} %multiply_convert_fusion, bf16[1216,1792]{1,0:T(8,128)(2,1)} %param.9, s32[]{:T(128)S(6)} %select_n.182), kind=kOutput, calls=%fused_computation.15 | convolution fusion | flops 557842432 | bytes 3719172 | tf_op jit(solution)/shard_map/dot_general | solution.py:175
  119.9 2.5 %fusion.17 = f32[1,256,896]{2,1,0:T(8,128)S(1)} fusion(bf16[256,1216]{0,1:T(8,128)(2,1)S(1)} %multiply_convert_fusion, bf16[1216,1792]{1,0:T(8,128)(2,1)} %collective-permute-done.2, s32[]{:T(128)S(6)} %select_n.182), kind=kOutput, calls=%fused_computation.16 | convolution fusion | flops 557842432 | bytes 3719172 | tf_op jit(solution)/shard_map/dot_general | solution.py:175
  122.7 2.5 %fusion.8 = f32[1,256,896]{2,1,0:T(8,128)S(1)} fusion(bf16[256,1216]{0,1:T(8,128)(2,1)S(1)} %multiply_convert_fusion, bf16[1216,1792]{1,0:T(8,128)(2,1)} %param.9, s32[]{:T(128)S(6)} %select_n.181), kind=kOutput, calls=%fused_computation.13 | convolution fusion | flops 557842432 | bytes 3719172 | tf_op jit(solution)/shard_map/dot_general | solution.py:175
  125.2 2.5 %fusion.11 = f32[1,256,896]{2,1,0:T(8,128)S(1)} fusion(bf16[256,1216]{0,1:T(8,128)(2,1)S(1)} %multiply_convert_fusion, bf16[1216,1792]{1,0:T(8,128)(2,1)} %collective-permute-done.2, s32[]{:T(128)S(6)} %select_n.181), kind=kOutput, calls=%fused_computation.14 | convolution fusion | flops 557842432 | bytes 3719172 | tf_op jit(solution)/shard_map/dot_general | solution.py:175
  133.9 8.8 %collective-permute-done.13 = f32[2,2,32,896]{3,2,1,0:T(8,128)} collective-permute-done((f32[2,2,32,896]{3,2,1,0:T(8,128)S(1)}, f32[2,2,32,896]{3,2,1,0:T(8,128)}, u32[]{:S(2)}, u32[]{:S(2)}) %collective-permute-start.13) | collective-permute-done | bytes 458784 | tf_op jit(solution)/shard_map/ppermute | solution.py:88
  145.8 5.2 %collective-permute-done.14 = f32[2,32,896]{2,1,0:T(8,128)S(1)} collective-permute-done((f32[2,32,896]{2,1,0:T(8,128)S(1)}, f32[2,32,896]{2,1,0:T(8,128)S(1)}, u32[]{:S(2)}, u32[]{:S(2)}) %collective-permute-start.14) | collective-permute-done | bytes 229408 | tf_op jit(solution)/shard_map/ppermute | solution.py:88
  151.6 2.6 %collective-permute-start.12 = (f32[32,896]{1,0:T(8,128)S(1)}, f32[32,896]{1,0:T(8,128)S(1)}, u32[]{:S(2)}, u32[]{:S(2)}) collective-permute-start(f32[32,896]{1,0:T(8,128)S(1)} %dynamic-slice_bitcast_fusion.5), channel_id=1, source_target_pairs={{0,2},{1,3},{2,0},{3,1},{4,6},{5,7},{6,4},{7,5},{8,10},{9,11},{10,... | collective-permute-start | bytes 344072 | tf_op jit(solution)/shard_map/ppermute | solution.py:88
  154.2 6.9 %collective-permute-done.15 = f32[32,896]{1,0:T(8,128)S(1)} collective-permute-done((f32[32,896]{1,0:T(8,128)S(1)}, f32[32,896]{1,0:T(8,128)S(1)}, u32[]{:S(2)}, u32[]{:S(2)}) %collective-permute-start.15) | collective-permute-done | bytes 114720 | tf_op jit(solution)/shard_map/ppermute | solution.py:88
  166.7 2.5 %collective-permute-done.16 = bf16[64,896]{1,0:T(8,128)(2,1)S(1)} collective-permute-done((bf16[64,896]{1,0:T(8,128)(2,1)S(1)}, bf16[64,896]{1,0:T(8,128)(2,1)S(1)}, u32[]{:S(2)}, u32[]{:S(2)}) %collective-permute-start.16) | collective-permute-done | bytes 114720 | tf_op jit(solution)/shard_map/ppermute | solution.py:99
  169.4 6.4 %collective-permute-done.17 = bf16[2,64,896]{2,1,0:T(8,128)(2,1)S(1)} collective-permute-done((bf16[2,64,896]{2,1,0:T(8,128)(2,1)S(1)}, bf16[2,64,896]{2,1,0:T(8,128)(2,1)S(1)}, u32[]{:S(2)}, u32[]{:S(2)}) %collective-permute-start.17) | collective-permute-done | bytes 229408 | tf_op jit(solution)/shard_map/ppermute | solution.py:99
  178.0 2.2 %fusion.26 = f32[896,2048]{1,0:T(8,128)S(1)} fusion(bf16[128,896]{1,0:T(8,128)(2,1)S(1)} %bitcast.177, bf16[256,2048]{1,0:T(8,128)(2,1)} %param.7), kind=kOutput, calls=%fused_computation.29 | convolution fusion | flops 469762048 | bytes 8093696 | tf_op jit(solution)/shard_map/dot_general | solution.py:258
  180.2 2.2 %fusion.28 = f32[896,2048]{1,0:T(8,128)S(1)} fusion(bf16[128,896]{1,0:T(8,128)(2,1)S(1)} %bitcast.175, bf16[256,2048]{1,0:T(8,128)(2,1)} %param.7), kind=kOutput, calls=%fused_computation.31 | convolution fusion | flops 469762048 | bytes 8093696 | tf_op jit(solution)/shard_map/dot_general | solution.py:258
  186.4 4.3 %add_add_fusion = f32[896,2048]{1,0:T(8,128)} fusion(f32[896,2048]{1,0:T(8,128)S(1)} %fusion.23, f32[896,2048]{1,0:T(8,128)S(1)} %fusion.28, f32[896,2048]{1,0:T(8,128)S(1)} %fusion.26, bf16[128,896]{1,0:T(8,128)(2,1)S(1)} %collective-permute-done.18, bf16[256,2048]{1,0:T(8,128)(2,1)S(1)} %collective-permute-done.19), kind=kOutput, calls=%fused_computation | convolution fusion | flops 475267072 | bytes 30113792 | tf_op jit(solution)/shard_map/dot_general | solution.py:258
  (79 shorter events, 33.1 us)
Async XLA Ops:
  0.6 97.4 %collective-permute-start.2 = (bf16[1216,1792]{1,0:T(8,128)(2,1)}, bf16[1216,1792]{1,0:T(8,128)(2,1)}, u32[]{:S(2)}, u32[]{:S(2)}) collective-permute-start(bf16[1216,1792]{1,0:T(8,128)(2,1)} %param.9), channel_id=1, source_target_pairs={{0,16},{16,0},{1,17},{17,1},{2,18},{18,2},{3,19},{19,3},{4,20},{20... | collective-permute-start | bytes 13074440 | tf_op jit(solution)/shard_map/ppermute | solution.py:11
  7.3 48.9 %copy-start.2 = (s32[256]{0:T(256)S(1)}, s32[256]{0:T(256)}, u32[]{:S(2)}) copy-start(s32[256]{0:T(256)} %param.10) | copy-start | bytes 3076
  46.4 9.5 %collective-permute-start = (bf16[256,896]{1,0:T(8,128)(2,1)S(1)}, bf16[256,896]{1,0:T(8,128)(2,1)S(1)}, u32[]{:S(2)}, u32[]{:S(2)}) collective-permute-start(bf16[256,896]{1,0:T(8,128)(2,1)S(1)} %all-reduce.1), channel_id=1, source_target_pairs={{0,8},{4,12},{8,0},{12,4},{1,9},{5,13},{9,1},{13,5},{2,10},{6,14},... | collective-permute-start | bytes 1376264 | tf_op jit(solution)/shard_map/ppermute | solution.py:99
  56.1 2.5 %collective-permute-start.1 = (bf16[2,256,896]{2,1,0:T(8,128)(2,1)S(1)}, bf16[2,256,896]{2,1,0:T(8,128)(2,1)S(1)}, u32[]{:S(2)}, u32[]{:S(2)}) collective-permute-start(bf16[2,256,896]{2,1,0:T(8,128)(2,1)S(1)} %maximum_select_fusion.2), channel_id=1, source_target_pairs={{0,4},{4,0},{8,12},{12,8},{1,5},{5,1},{9,13},{13,9},{2,6},{6,2},{1... | collective-permute-start | bytes 2752520 | tf_op jit(solution)/shard_map/ppermute | solution.py:99
  65.5 46.1 %copy-start.1 = (s32[256]{0:T(256)S(1)}, s32[256]{0:T(256)}, u32[]{:S(2)}) copy-start(s32[256]{0:T(256)} %param.11) | copy-start | bytes 3076
  102.0 3.7 %collective-permute-start.4 = (f32[3,256]{1,0:T(4,128)S(1)}, f32[3,256]{1,0:T(4,128)S(1)}, u32[]{:S(2)}, u32[]{:S(2)}) collective-permute-start(f32[3,256]{1,0:T(4,128)S(1)} %get-tuple-element.25), channel_id=1, source_target_pairs={{0,8},{4,12},{8,0},{12,4},{1,9},{5,13},{9,1},{13,5},{2,10},{6,14},... | collective-permute-start | bytes 9224 | tf_op jit(solution)/shard_map/ppermute | solution.py:41
  103.8 1.8 collective-permute-start.3
  103.8 3.0 %collective-permute-start.5 = (f32[3,256]{1,0:T(4,128)S(1)}, f32[3,256]{1,0:T(4,128)S(1)}, u32[]{:S(2)}, u32[]{:S(2)}) collective-permute-start(f32[3,256]{1,0:T(4,128)S(1)} %get-tuple-element.25), channel_id=1, source_target_pairs={{0,4},{4,8},{8,12},{12,0},{1,5},{5,9},{9,13},{13,1},{2,6},{6,10},{... | collective-permute-start | bytes 9224 | tf_op jit(solution)/shard_map/ppermute | solution.py:41
  107.0 4.7 %collective-permute-start.7 = (f32[3,256]{1,0:T(4,128)S(1)}, f32[3,256]{1,0:T(4,128)S(1)}, u32[]{:S(2)}, u32[]{:S(2)}) collective-permute-start(f32[3,256]{1,0:T(4,128)S(1)} %get-tuple-element.23), channel_id=1, source_target_pairs={{0,2},{1,3},{2,0},{3,1},{4,6},{5,7},{6,4},{7,5},{8,10},{9,11},{10,... | collective-permute-start | bytes 9224 | tf_op jit(solution)/shard_map/ppermute | solution.py:41
  109.6 3.6 %collective-permute-start.6 = (f32[3,256]{1,0:T(4,128)S(1)}, f32[3,256]{1,0:T(4,128)S(1)}, u32[]{:S(2)}, u32[]{:S(2)}) collective-permute-start(f32[3,256]{1,0:T(4,128)S(1)} %get-tuple-element.23), channel_id=1, source_target_pairs={{0,3},{1,0},{2,1},{3,2},{4,7},{5,4},{6,5},{7,6},{8,11},{9,8},{10,9... | collective-permute-start | bytes 9224 | tf_op jit(solution)/shard_map/ppermute | solution.py:41
  111.0 5.4 %collective-permute-start.8 = (f32[3,256]{1,0:T(4,128)S(1)}, f32[3,256]{1,0:T(4,128)S(1)}, u32[]{:S(2)}, u32[]{:S(2)}) collective-permute-start(f32[3,256]{1,0:T(4,128)S(1)} %get-tuple-element.23), channel_id=1, source_target_pairs={{0,1},{1,2},{2,3},{3,0},{4,5},{5,6},{6,7},{7,4},{8,9},{9,10},{10,1... | collective-permute-start | bytes 9224 | tf_op jit(solution)/shard_map/ppermute | solution.py:41
  122.6 5.1 %collective-permute-start.9 = (f32[2,256,896]{2,1,0:T(8,128)S(1)}, f32[2,256,896]{2,1,0:T(8,128)}, u32[]{:S(2)}, u32[]{:S(2)}) collective-permute-start(f32[2,256,896]{2,1,0:T(8,128)S(1)} %pad_maximum_fusion), channel_id=1, source_target_pairs={{0,4},{4,0},{8,12},{12,8},{1,5},{5,1},{9,13},{13,9},{2,6},{6,2},{1... | collective-permute-start | bytes 5505032 | tf_op jit(solution)/shard_map/ppermute | solution.py:185
  129.6 13.1 %collective-permute-start.13 = (f32[2,2,32,896]{3,2,1,0:T(8,128)S(1)}, f32[2,2,32,896]{3,2,1,0:T(8,128)}, u32[]{:S(2)}, u32[]{:S(2)}) collective-permute-start(f32[2,2,32,896]{3,2,1,0:T(8,128)S(1)} %dynamic-slice_bitcast_fusion), channel_id=1, source_target_pairs={{0,1},{1,0},{2,3},{3,2},{4,5},{5,4},{6,7},{7,6},{8,9},{9,8},{10,11... | collective-permute-start | bytes 1376264 | tf_op jit(solution)/shard_map/ppermute | solution.py:88
  129.7 52.6 %collective-permute-start.19 = (bf16[256,2048]{1,0:T(8,128)(2,1)}, bf16[256,2048]{1,0:T(8,128)(2,1)S(1)}, u32[]{:S(2)}, u32[]{:S(2)}) collective-permute-start(bf16[256,2048]{1,0:T(8,128)(2,1)} %param.7), channel_id=1, source_target_pairs={{0,16},{16,0},{1,17},{17,1},{2,18},{18,2},{3,19},{19,3},{4,20},{20... | collective-permute-start | bytes 3145736 | tf_op jit(solution)/shard_map/ppermute | solution.py:116
  131.3 13.1 %collective-permute-start.10 = (f32[2,2,32,896]{3,2,1,0:T(8,128)S(1)}, f32[2,2,32,896]{3,2,1,0:T(8,128)S(1)}, u32[]{:S(2)}, u32[]{:S(2)}) collective-permute-start(f32[2,2,32,896]{3,2,1,0:T(8,128)S(1)} %dynamic-slice_bitcast_fusion.1), channel_id=1, source_target_pairs={{0,8},{4,12},{8,0},{12,4},{1,9},{5,13},{9,1},{13,5},{2,10},{6,14},... | collective-permute-start | bytes 1376264 | tf_op jit(solution)/shard_map/ppermute | solution.py:88
  133.3 30.1 %collective-permute-start.21 = (f32[2]{0:T(128)S(1)}, f32[2]{0:T(128)S(1)}, u32[]{:S(2)}, u32[]{:S(2)}) collective-permute-start(f32[2]{0:T(128)S(1)} %pad_maximum_fusion.4), channel_id=1, source_target_pairs={{0,16},{16,0},{1,17},{17,1},{2,18},{18,2},{3,19},{19,3},{4,20},{20... | collective-permute-start | bytes 32 | tf_op jit(solution)/shard_map/ppermute | solution.py:62
  143.8 7.3 %collective-permute-start.14 = (f32[2,32,896]{2,1,0:T(8,128)S(1)}, f32[2,32,896]{2,1,0:T(8,128)S(1)}, u32[]{:S(2)}, u32[]{:S(2)}) collective-permute-start(f32[2,32,896]{2,1,0:T(8,128)S(1)} %dynamic-slice_bitcast_fusion.2), channel_id=1, source_target_pairs={{0,8},{4,12},{8,0},{12,4},{1,9},{5,13},{9,1},{13,5},{2,10},{6,14},... | collective-permute-start | bytes 688136 | tf_op jit(solution)/shard_map/ppermute | solution.py:88
  144.5 7.0 %collective-permute-start.11 = (f32[2,32,896]{2,1,0:T(8,128)S(1)}, f32[2,32,896]{2,1,0:T(8,128)S(1)}, u32[]{:S(2)}, u32[]{:S(2)}) collective-permute-start(f32[2,32,896]{2,1,0:T(8,128)S(1)} %dynamic-slice_bitcast_fusion.3), channel_id=1, source_target_pairs={{0,1},{1,0},{2,3},{3,2},{4,5},{5,4},{6,7},{7,6},{8,9},{9,8},{10,11... | collective-permute-start | bytes 688136 | tf_op jit(solution)/shard_map/ppermute | solution.py:88
  151.1 10.0 %collective-permute-start.15 = (f32[32,896]{1,0:T(8,128)S(1)}, f32[32,896]{1,0:T(8,128)S(1)}, u32[]{:S(2)}, u32[]{:S(2)}) collective-permute-start(f32[32,896]{1,0:T(8,128)S(1)} %dynamic-slice_bitcast_fusion.4), channel_id=1, source_target_pairs={{0,2},{1,3},{2,0},{3,1},{4,6},{5,7},{6,4},{7,5},{8,10},{9,11},{10,... | collective-permute-start | bytes 344072 | tf_op jit(solution)/shard_map/ppermute | solution.py:88
  151.6 11.7 %collective-permute-start.12 = (f32[32,896]{1,0:T(8,128)S(1)}, f32[32,896]{1,0:T(8,128)S(1)}, u32[]{:S(2)}, u32[]{:S(2)}) collective-permute-start(f32[32,896]{1,0:T(8,128)S(1)} %dynamic-slice_bitcast_fusion.5), channel_id=1, source_target_pairs={{0,2},{1,3},{2,0},{3,1},{4,6},{5,7},{6,4},{7,5},{8,10},{9,11},{10,... | collective-permute-start | bytes 344072 | tf_op jit(solution)/shard_map/ppermute | solution.py:88
  163.3 5.9 %collective-permute-start.16 = (bf16[64,896]{1,0:T(8,128)(2,1)S(1)}, bf16[64,896]{1,0:T(8,128)(2,1)S(1)}, u32[]{:S(2)}, u32[]{:S(2)}) collective-permute-start(bf16[64,896]{1,0:T(8,128)(2,1)S(1)} %pad_maximum_fusion.1), channel_id=1, source_target_pairs={{0,2},{1,3},{2,0},{3,1},{4,6},{5,7},{6,4},{7,5},{8,10},{9,11},{10,... | collective-permute-start | bytes 344072 | tf_op jit(solution)/shard_map/ppermute | solution.py:99
  169.2 6.5 %collective-permute-start.17 = (bf16[2,64,896]{2,1,0:T(8,128)(2,1)S(1)}, bf16[2,64,896]{2,1,0:T(8,128)(2,1)S(1)}, u32[]{:S(2)}, u32[]{:S(2)}) collective-permute-start(bf16[2,64,896]{2,1,0:T(8,128)(2,1)S(1)} %maximum_select_fusion.5), channel_id=1, source_target_pairs={{0,1},{1,0},{2,3},{3,2},{4,5},{5,4},{6,7},{7,6},{8,9},{9,8},{10,11... | collective-permute-start | bytes 688136 | tf_op jit(solution)/shard_map/ppermute | solution.py:99
  175.9 8.1 %collective-permute-start.20 = (bf16[128,896]{1,0:T(8,128)(2,1)S(1)}, bf16[128,896]{1,0:T(8,128)(2,1)S(1)}, u32[]{:S(2)}, u32[]{:S(2)}) collective-permute-start(bf16[128,896]{1,0:T(8,128)(2,1)S(1)} %bitcast.176), channel_id=1, source_target_pairs={{0,16},{16,0},{1,17},{17,1},{2,18},{18,2},{3,19},{19,3},{4,20},{20... | collective-permute-start | bytes 688136 | tf_op jit(solution)/shard_map/ppermute | solution.py:252
  177.5 9.0 %collective-permute-start.18 = (bf16[128,896]{1,0:T(8,128)(2,1)S(1)}, bf16[128,896]{1,0:T(8,128)(2,1)S(1)}, u32[]{:S(2)}, u32[]{:S(2)}) collective-permute-start(bf16[128,896]{1,0:T(8,128)(2,1)S(1)} %bitcast.174), channel_id=1, source_target_pairs={{0,16},{16,0},{1,17},{17,1},{2,18},{18,2},{3,19},{19,3},{4,20},{20... | collective-permute-start | bytes 688136 | tf_op jit(solution)/shard_map/ppermute | solution.py:252
  (1 other events, 36.5 us)

commit v15 on v13

--- a/solution.py
+++ b/solution.py
@@ -112,16 +112,16 @@
     for k, piece in enumerate(table_pieces):
         cols = lax.dynamic_slice_in_dim(projected, ((t - k) % n_tok) * d_cols, d_cols, axis=1)
         part = lax.dot_general(
-            cols, piece, (((1,), (1,)), ((), ())), preferred_element_type=jnp.float32
+            piece, cols, (((1,), (1,)), ((), ())), preferred_element_type=jnp.float32
         )
         logits = part if logits is None else logits + part
 
     block_base = (lax.axis_index("voc") * lax.axis_size("wid") + lax.axis_index("wid")) * block_rows
     local_ids = targets - block_base
-    is_target = local_ids[:, None] == lax.broadcasted_iota(jnp.int32, (tok_rows, block_rows), 1)
-    picked_here = jnp.sum(jnp.where(is_target, logits, 0.0), axis=1)
-    peak_here = jnp.max(logits, axis=1)
-    exp_here = jnp.sum(jnp.exp(logits - peak_here[:, None]), axis=1)
+    is_target = local_ids[None, :] == lax.broadcasted_iota(jnp.int32, (block_rows, tok_rows), 0)
+    picked_here = jnp.sum(jnp.where(is_target, logits, 0.0), axis=0)
+    peak_here = jnp.max(logits, axis=0)
+    exp_here = jnp.sum(jnp.exp(logits - peak_here[None, :]), axis=0)
     weight = valid.astype(jnp.float32)
 
     stats = jnp.stack([peak_here, exp_here, picked_here])
@@ -132,8 +132,10 @@
     sums = tree_sum(sums, "tok")
 
     dlogits = (
-        weight[:, None] * (jnp.exp(logits - log_total[:, None]) - is_target.astype(jnp.float32))
-    ).astype(jnp.bfloat16)
+        (weight[None, :] * (jnp.exp(logits - log_total[None, :]) - is_target.astype(jnp.float32)))
+        .astype(jnp.bfloat16)
+        .T
+    )
 
     n_voc, n_wid = lax.axis_size("voc"), lax.axis_size("wid")
     grad_rows_pos = None

time: 191 us -> 191 us (level)
  transfers between devices with their start and end apart: 20 -> 20, of which waited for: 14 -> 15; matrix products, arithmetic and copies ran while one was open for 14% -> 14% of each run, Pallas kernels for 0% -> 0%
where the time goes in v15:
time: 191 us; the launch traced here: 190 us
  waiting for transfers between devices  78.7 us (41%)
  blocking collectives  39.1 us (20%)
  matrix products  30.8 us (16%)
  starting transfers between devices  26.3 us (14%)
  other arithmetic  8.16 us (4%)
  between operations  3.54 us (2%)
  local copies, waits for them, and re-layouts  3.47 us (2%)
    psum x1, blocking collectives, on_device(): summed = lax.psum(partial_value, 'wid')  39.1 us
    ppermute x1, waiting for transfers between devices, tok_pieces(): pieces.append(lax.ppermute(x, 'tok', perm))  32.6 us
    ppermute x4, waiting for transfers between devices, doubling_gather(): other = lax.ppermute(x, ax, [(k, k ^ b) for k in range(n)])  20.8 us
    ppermute x6, waiting for transfers between devices, halving_steps(): x = keep + lax.ppermute(send, ax, [(k, k ^ b) for k in range(n)])  17.9 us
    ppermute x6, starting transfers between devices, halving_steps(): x = keep + lax.ppermute(send, ax, [(k, k ^ b) for k in range(n)])  10.6 us
    dot_general x4, matrix products, quarter_dots(): jnp.dot(dlogits, lax.dynamic_slice_in_dim(piece, sel * q_cols, q_cols, ax...  9.96 us
    dot_general x4, matrix products, on_device(): lax.dot_general(rows[i], hid[i * half_rows:(i + 1) * half_rows], by_pos,...  9.78 us
    dot_general x2, matrix products, on_device(): lax.dot_general(piece, cols, (((1,), (1,)), ((), ())), preferred_element_...  7.46 us
  transfers between devices with their start and end apart: 20, of which 15 were waited for; matrix products, arithmetic and copies ran while one was open for 14% of the time, Pallas kernels for 0%

profile of v15, /device:TPU:0, one launch (start us, length us, event | category | flops | bytes accessed | tf_op | source)
XLA Modules:
  0.0 190.1 jit_solution(12973415312136311734)
XLA Ops:
  0.6 3.0 %collective-permute-start.2 = (bf16[1216,1792]{1,0:T(8,128)(2,1)}, bf16[1216,1792]{1,0:T(8,128)(2,1)}, u32[]{:S(2)}, u32[]{:S(2)}) collective-permute-start(bf16[1216,1792]{1,0:T(8,128)(2,1)} %param.7), channel_id=1, source_target_pairs={{0,16},{16,0},{1,17},{17,1},{2,18},{18,2},{3,19},{19,3},{4,20},{20... | collective-permute-start | bytes 13074440 | tf_op jit(solution)/shard_map/ppermute | solution.py:11
  3.6 3.6 %fusion.60 = f32[256,896]{1,0:T(8,128)S(1)} fusion(bf16[256,2048]{1,0:T(8,128)(2,1)} %param.5, bf16[896,2048]{1,0:T(8,128)(2,1)} %param.6), kind=kOutput, calls=%fused_computation.103 | convolution fusion | flops 939524096 | bytes 5636096 | tf_op jit(solution)/shard_map/dot_general | solution.py:101
  7.3 39.1 %all-reduce.1 = bf16[256,896]{1,0:T(8,128)(2,1)S(1)} all-reduce(f32[256,896]{1,0:T(8,128)S(1)} %fusion.60), channel_id=1, replica_groups=mesh['tok'=2,'voc'=4,'wid'=4] {'wid'}, use_global_device_ids=true, to_apply=%region_0.0 | all-reduce | flops 229376 | bytes 1376256 | tf_op jit(solution)/shard_map/psum | solution.py:104
  48.0 7.9 %collective-permute-done = bf16[256,896]{1,0:T(8,128)(2,1)S(1)} collective-permute-done((bf16[256,896]{1,0:T(8,128)(2,1)S(1)}, bf16[256,896]{1,0:T(8,128)(2,1)S(1)}, u32[]{:S(2)}, u32[]{:S(2)}) %collective-permute-start) | collective-permute-done | bytes 458784 | tf_op jit(solution)/shard_map/ppermute | solution.py:82
  56.4 2.2 %collective-permute-done.1 = bf16[2,256,896]{2,1,0:T(8,128)(2,1)S(1)} collective-permute-done((bf16[2,256,896]{2,1,0:T(8,128)(2,1)S(1)}, bf16[2,256,896]{2,1,0:T(8,128)(2,1)S(1)}, u32[]{:S(2)}, u32[]{:S(2)}) %collective-permute-start.1) | collective-permute-done | bytes 917536 | tf_op jit(solution)/shard_map/ppermute | solution.py:82
  59.1 2.4 %copy.8 = bf16[256,4,896]{0,2,1:T(8,128)(2,1)} copy(bf16[256,4,896]{2,0,1:T(8,128)(2,1)S(1)} %bitcast.104) | data formatting | bytes 3670016 | tf_op jit(solution)/shard_map/transpose | solution.py:107
  61.5 3.9 %fusion.28 = f32[256,1216]{0,1:T(8,128)S(1)} fusion(bf16[1216,1792]{1,0:T(8,128)(2,1)} %param.7, bf16[256,3584]{0,1:T(8,128)(2,1)} %bitcast.108, s32[]{:T(128)S(6)} %select_n.168), kind=kOutput, calls=%fused_computation.31 | convolution fusion | flops 1115684864 | bytes 6520836 | tf_op jit(solution)/shard_map/dot_general | solution.py:114
  65.5 32.6 %collective-permute-done.2 = bf16[1216,1792]{1,0:T(8,128)(2,1)} collective-permute-done((bf16[1216,1792]{1,0:T(8,128)(2,1)}, bf16[1216,1792]{1,0:T(8,128)(2,1)}, u32[]{:S(2)}, u32[]{:S(2)}) %collective-permute-start.2) | collective-permute-done | bytes 4358176 | tf_op jit(solution)/shard_map/ppermute | solution.py:11
  98.0 3.5 %fusion.59 = (f32[256]{0:T(256)S(1)}, f32[256,1216]{0,1:T(8,128)S(1)}) fusion(f32[256,1216]{0,1:T(8,128)S(1)} %fusion.28, bf16[1216,1792]{1,0:T(8,128)(2,1)} %collective-permute-done.2, bf16[256,3584]{0,1:T(8,128)(2,1)S(1)} %bitcast.109, s32[]{:T(128)S(6)} %select_n.170), kind=kOutput, calls=%fused_computation.102 | convolution fusion | flops 1116307200 | bytes 7767044 | tf_op jit(solution)/shard_map/dot_general | solution.py:114
  106.9 1.9 collective-permute-start.5
  110.6 2.9 %collective-permute-start.6 = (f32[3,256]{1,0:T(4,128)S(1)}, f32[3,256]{1,0:T(4,128)S(1)}, u32[]{:S(2)}, u32[]{:S(2)}) collective-permute-start(f32[3,256]{1,0:T(4,128)S(1)} %pad_maximum_fusion.5), channel_id=1, source_target_pairs={{0,2},{1,3},{2,0},{3,1},{4,6},{5,7},{6,4},{7,5},{8,10},{9,11},{10,... | collective-permute-start | bytes 9224 | tf_op jit(solution)/shard_map/ppermute | solution.py:33
  115.6 2.5 %fusion.14 = f32[1,256,896]{2,1,0:T(8,128)S(1)} fusion(bf16[1216,256]{1,0:T(8,128)(2,1)S(1)} %fusion.26, bf16[1216,1792]{1,0:T(8,128)(2,1)} %param.7, s32[]{:T(128)S(6)} %select_n.173), kind=kOutput, calls=%fused_computation.15 | convolution fusion | flops 557842432 | bytes 3719172 | tf_op jit(solution)/shard_map/dot_general | solution.py:160
  118.1 2.5 %fusion.17 = f32[1,256,896]{2,1,0:T(8,128)S(1)} fusion(bf16[1216,256]{1,0:T(8,128)(2,1)S(1)} %fusion.26, bf16[1216,1792]{1,0:T(8,128)(2,1)} %collective-permute-done.2, s32[]{:T(128)S(6)} %select_n.173), kind=kOutput, calls=%fused_computation.16 | convolution fusion | flops 557842432 | bytes 3719172 | tf_op jit(solution)/shard_map/dot_general | solution.py:160
  120.8 2.5 %fusion.8 = f32[1,256,896]{2,1,0:T(8,128)S(1)} fusion(bf16[1216,256]{1,0:T(8,128)(2,1)S(1)} %fusion.26, bf16[1216,1792]{1,0:T(8,128)(2,1)} %param.7, s32[]{:T(128)S(6)} %select_n.172), kind=kOutput, calls=%fused_computation.13 | convolution fusion | flops 557842432 | bytes 3719172 | tf_op jit(solution)/shard_map/dot_general | solution.py:160
  123.3 2.5 %fusion.11 = f32[1,256,896]{2,1,0:T(8,128)S(1)} fusion(bf16[1216,256]{1,0:T(8,128)(2,1)S(1)} %fusion.26, bf16[1216,1792]{1,0:T(8,128)(2,1)} %collective-permute-done.2, s32[]{:T(128)S(6)} %select_n.172), kind=kOutput, calls=%fused_computation.14 | convolution fusion | flops 557842432 | bytes 3719172 | tf_op jit(solution)/shard_map/dot_general | solution.py:160
  135.3 5.6 %collective-permute-done.11 = f32[2,2,32,896]{3,2,1,0:T(8,128)} collective-permute-done((f32[2,2,32,896]{3,2,1,0:T(8,128)S(1)}, f32[2,2,32,896]{3,2,1,0:T(8,128)}, u32[]{:S(2)}, u32[]{:S(2)}) %collective-permute-start.11) | collective-permute-done | bytes 458784 | tf_op jit(solution)/shard_map/ppermute | solution.py:71
  145.5 3.9 %collective-permute-done.12 = f32[2,32,896]{2,1,0:T(8,128)S(1)} collective-permute-done((f32[2,32,896]{2,1,0:T(8,128)S(1)}, f32[2,32,896]{2,1,0:T(8,128)S(1)}, u32[]{:S(2)}, u32[]{:S(2)}) %collective-permute-start.12) | collective-permute-done | bytes 229408 | tf_op jit(solution)/shard_map/ppermute | solution.py:71
  149.4 2.7 %collective-permute-start.13 = (f32[32,896]{1,0:T(8,128)S(1)}, f32[32,896]{1,0:T(8,128)S(1)}, u32[]{:S(2)}, u32[]{:S(2)}) collective-permute-start(f32[32,896]{1,0:T(8,128)S(1)} %dynamic-slice_bitcast_fusion.4), channel_id=1, source_target_pairs={{0,2},{1,3},{2,0},{3,1},{4,6},{5,7},{6,4},{7,5},{8,10},{9,11},{10,... | collective-permute-start | bytes 344072 | tf_op jit(solution)/shard_map/ppermute | solution.py:71
  153.6 6.8 %collective-permute-done.13 = f32[32,896]{1,0:T(8,128)S(1)} collective-permute-done((f32[32,896]{1,0:T(8,128)S(1)}, f32[32,896]{1,0:T(8,128)S(1)}, u32[]{:S(2)}, u32[]{:S(2)}) %collective-permute-start.13) | collective-permute-done | bytes 114720 | tf_op jit(solution)/shard_map/ppermute | solution.py:71
  165.1 4.7 %collective-permute-done.14 = bf16[64,896]{1,0:T(8,128)(2,1)S(1)} collective-permute-done((bf16[64,896]{1,0:T(8,128)(2,1)S(1)}, bf16[64,896]{1,0:T(8,128)(2,1)S(1)}, u32[]{:S(2)}, u32[]{:S(2)}) %collective-permute-start.14) | collective-permute-done | bytes 114720 | tf_op jit(solution)/shard_map/ppermute | solution.py:82
  170.0 5.9 %collective-permute-done.15 = bf16[2,64,896]{2,1,0:T(8,128)(2,1)S(1)} collective-permute-done((bf16[2,64,896]{2,1,0:T(8,128)(2,1)S(1)}, bf16[2,64,896]{2,1,0:T(8,128)(2,1)S(1)}, u32[]{:S(2)}, u32[]{:S(2)}) %collective-permute-start.15) | collective-permute-done | bytes 229408 | tf_op jit(solution)/shard_map/ppermute | solution.py:82
  178.1 2.2 %fusion.33 = f32[896,2048]{1,0:T(8,128)S(1)} fusion(bf16[128,896]{1,0:T(8,128)(2,1)S(1)} %bitcast.115, bf16[256,2048]{1,0:T(8,128)(2,1)} %param.5), kind=kOutput, calls=%fused_computation.36 | convolution fusion | flops 469762048 | bytes 8093696 | tf_op jit(solution)/shard_map/dot_general | solution.py:243
  180.3 2.2 %fusion.35 = f32[896,2048]{1,0:T(8,128)S(1)} fusion(bf16[128,896]{1,0:T(8,128)(2,1)S(1)} %bitcast.113, bf16[256,2048]{1,0:T(8,128)(2,1)} %param.5), kind=kOutput, calls=%fused_computation.38 | convolution fusion | flops 469762048 | bytes 8093696 | tf_op jit(solution)/shard_map/dot_general | solution.py:243
  184.7 4.3 %add_add_fusion = f32[896,2048]{1,0:T(8,128)} fusion(f32[896,2048]{1,0:T(8,128)S(1)} %fusion.30, f32[896,2048]{1,0:T(8,128)S(1)} %fusion.35, f32[896,2048]{1,0:T(8,128)S(1)} %fusion.33, bf16[128,896]{1,0:T(8,128)(2,1)S(1)} %collective-permute-done.16, bf16[256,2048]{1,0:T(8,128)(2,1)S(1)} %collective-permute-done.17), kind=kOutput, calls=%fused_computation | convolution fusion | flops 475267072 | bytes 30113792 | tf_op jit(solution)/shard_map/dot_general | solution.py:243
  (76 shorter events, 35.3 us)
Async XLA Ops:
  0.6 97.4 %collective-permute-start.2 = (bf16[1216,1792]{1,0:T(8,128)(2,1)}, bf16[1216,1792]{1,0:T(8,128)(2,1)}, u32[]{:S(2)}, u32[]{:S(2)}) collective-permute-start(bf16[1216,1792]{1,0:T(8,128)(2,1)} %param.7), channel_id=1, source_target_pairs={{0,16},{16,0},{1,17},{17,1},{2,18},{18,2},{3,19},{19,3},{4,20},{20... | collective-permute-start | bytes 13074440 | tf_op jit(solution)/shard_map/ppermute | solution.py:11
  7.3 48.9 %copy-start.2 = (s32[256]{0:T(256)S(1)}, s32[256]{0:T(256)}, u32[]{:S(2)}) copy-start(s32[256]{0:T(256)} %param.8) | copy-start | bytes 3076
  46.4 9.5 %collective-permute-start = (bf16[256,896]{1,0:T(8,128)(2,1)S(1)}, bf16[256,896]{1,0:T(8,128)(2,1)S(1)}, u32[]{:S(2)}, u32[]{:S(2)}) collective-permute-start(bf16[256,896]{1,0:T(8,128)(2,1)S(1)} %all-reduce.1), channel_id=1, source_target_pairs={{0,8},{4,12},{8,0},{12,4},{1,9},{5,13},{9,1},{13,5},{2,10},{6,14},... | collective-permute-start | bytes 1376264 | tf_op jit(solution)/shard_map/ppermute | solution.py:82
  56.1 2.5 %collective-permute-start.1 = (bf16[2,256,896]{2,1,0:T(8,128)(2,1)S(1)}, bf16[2,256,896]{2,1,0:T(8,128)(2,1)S(1)}, u32[]{:S(2)}, u32[]{:S(2)}) collective-permute-start(bf16[2,256,896]{2,1,0:T(8,128)(2,1)S(1)} %maximum_select_fusion.2), channel_id=1, source_target_pairs={{0,4},{4,0},{8,12},{12,8},{1,5},{5,1},{9,13},{13,9},{2,6},{6,2},{1... | collective-permute-start | bytes 2752520 | tf_op jit(solution)/shard_map/ppermute | solution.py:82
  61.5 36.5 %copy-start = (bf16[256,4,896]{0,2,1:T(8,128)(2,1)S(1)}, bf16[256,4,896]{0,2,1:T(8,128)(2,1)}, u32[]{:S(2)}) copy-start(bf16[256,4,896]{0,2,1:T(8,128)(2,1)} %copy.8) | copy-start | bytes 5505028
  65.5 48.1 %copy-start.1 = (s32[256]{0:T(256)S(1)}, s32[256]{0:T(256)}, u32[]{:S(2)}) copy-start(s32[256]{0:T(256)} %param.9) | copy-start | bytes 3076
  101.9 1.2 collective-permute-start.3
  103.2 3.7 %collective-permute-start.4 = (f32[3,256]{1,0:T(4,128)S(1)}, f32[3,256]{1,0:T(4,128)S(1)}, u32[]{:S(2)}, u32[]{:S(2)}) collective-permute-start(f32[3,256]{1,0:T(4,128)S(1)} %pad_maximum_fusion.3), channel_id=1, source_target_pairs={{0,8},{4,12},{8,0},{12,4},{1,9},{5,13},{9,1},{13,5},{2,10},{6,14},... | collective-permute-start | bytes 9224 | tf_op jit(solution)/shard_map/ppermute | solution.py:33
  106.9 3.7 %collective-permute-start.5 = (f32[3,256]{1,0:T(4,128)S(1)}, f32[3,256]{1,0:T(4,128)S(1)}, u32[]{:S(2)}, u32[]{:S(2)}) collective-permute-start(f32[3,256]{1,0:T(4,128)S(1)} %pad_maximum_fusion.4), channel_id=1, source_target_pairs={{0,1},{1,0},{2,3},{3,2},{4,5},{5,4},{6,7},{7,6},{8,9},{9,8},{10,11... | collective-permute-start | bytes 9224 | tf_op jit(solution)/shard_map/ppermute | solution.py:33
  110.6 4.6 %collective-permute-start.6 = (f32[3,256]{1,0:T(4,128)S(1)}, f32[3,256]{1,0:T(4,128)S(1)}, u32[]{:S(2)}, u32[]{:S(2)}) collective-permute-start(f32[3,256]{1,0:T(4,128)S(1)} %pad_maximum_fusion.5), channel_id=1, source_target_pairs={{0,2},{1,3},{2,0},{3,1},{4,6},{5,7},{6,4},{7,5},{8,10},{9,11},{10,... | collective-permute-start | bytes 9224 | tf_op jit(solution)/shard_map/ppermute | solution.py:33
  120.7 5.1 %collective-permute-start.7 = (f32[2,256,896]{2,1,0:T(8,128)S(1)}, f32[2,256,896]{2,1,0:T(8,128)}, u32[]{:S(2)}, u32[]{:S(2)}) collective-permute-start(f32[2,256,896]{2,1,0:T(8,128)S(1)} %pad_maximum_fusion), channel_id=1, source_target_pairs={{0,4},{4,0},{8,12},{12,8},{1,5},{5,1},{9,13},{13,9},{2,6},{6,2},{1... | collective-permute-start | bytes 5505032 | tf_op jit(solution)/shard_map/ppermute | solution.py:170
  127.8 13.1 %collective-permute-start.11 = (f32[2,2,32,896]{3,2,1,0:T(8,128)S(1)}, f32[2,2,32,896]{3,2,1,0:T(8,128)}, u32[]{:S(2)}, u32[]{:S(2)}) collective-permute-start(f32[2,2,32,896]{3,2,1,0:T(8,128)S(1)} %dynamic-slice_bitcast_fusion), channel_id=1, source_target_pairs={{0,1},{1,0},{2,3},{3,2},{4,5},{5,4},{6,7},{7,6},{8,9},{9,8},{10,11... | collective-permute-start | bytes 1376264 | tf_op jit(solution)/shard_map/ppermute | solution.py:71
  129.6 52.9 %collective-permute-start.17 = (bf16[256,2048]{1,0:T(8,128)(2,1)}, bf16[256,2048]{1,0:T(8,128)(2,1)S(1)}, u32[]{:S(2)}, u32[]{:S(2)}) collective-permute-start(bf16[256,2048]{1,0:T(8,128)(2,1)} %param.5), channel_id=1, source_target_pairs={{0,16},{16,0},{1,17},{17,1},{2,18},{18,2},{3,19},{19,3},{4,20},{20... | collective-permute-start | bytes 3145736 | tf_op jit(solution)/shard_map/ppermute | solution.py:99
  131.8 12.4 %collective-permute-start.8 = (f32[2,2,32,896]{3,2,1,0:T(8,128)S(1)}, f32[2,2,32,896]{3,2,1,0:T(8,128)S(1)}, u32[]{:S(2)}, u32[]{:S(2)}) collective-permute-start(f32[2,2,32,896]{3,2,1,0:T(8,128)S(1)} %dynamic-slice_bitcast_fusion.1), channel_id=1, source_target_pairs={{0,8},{4,12},{8,0},{12,4},{1,9},{5,13},{9,1},{13,5},{2,10},{6,14},... | collective-permute-start | bytes 1376264 | tf_op jit(solution)/shard_map/ppermute | solution.py:71
  134.8 27.0 %collective-permute-start.19 = (f32[2]{0:T(128)S(1)}, f32[2]{0:T(128)S(1)}, u32[]{:S(2)}, u32[]{:S(2)}) collective-permute-start(f32[2]{0:T(128)S(1)} %pad_maximum_fusion.6), channel_id=1, source_target_pairs={{0,16},{16,0},{1,17},{17,1},{2,18},{18,2},{3,19},{19,3},{4,20},{20... | collective-permute-start | bytes 32 | tf_op jit(solution)/shard_map/ppermute | solution.py:45
  142.0 7.3 %collective-permute-start.12 = (f32[2,32,896]{2,1,0:T(8,128)S(1)}, f32[2,32,896]{2,1,0:T(8,128)S(1)}, u32[]{:S(2)}, u32[]{:S(2)}) collective-permute-start(f32[2,32,896]{2,1,0:T(8,128)S(1)} %dynamic-slice_bitcast_fusion.2), channel_id=1, source_target_pairs={{0,8},{4,12},{8,0},{12,4},{1,9},{5,13},{9,1},{13,5},{2,10},{6,14},... | collective-permute-start | bytes 688136 | tf_op jit(solution)/shard_map/ppermute | solution.py:71
  144.3 7.8 %collective-permute-start.9 = (f32[2,32,896]{2,1,0:T(8,128)S(1)}, f32[2,32,896]{2,1,0:T(8,128)S(1)}, u32[]{:S(2)}, u32[]{:S(2)}) collective-permute-start(f32[2,32,896]{2,1,0:T(8,128)S(1)} %dynamic-slice_bitcast_fusion.3), channel_id=1, source_target_pairs={{0,1},{1,0},{2,3},{3,2},{4,5},{5,4},{6,7},{7,6},{8,9},{9,8},{10,11... | collective-permute-start | bytes 688136 | tf_op jit(solution)/shard_map/ppermute | solution.py:71
  149.4 11.0 %collective-permute-start.13 = (f32[32,896]{1,0:T(8,128)S(1)}, f32[32,896]{1,0:T(8,128)S(1)}, u32[]{:S(2)}, u32[]{:S(2)}) collective-permute-start(f32[32,896]{1,0:T(8,128)S(1)} %dynamic-slice_bitcast_fusion.4), channel_id=1, source_target_pairs={{0,2},{1,3},{2,0},{3,1},{4,6},{5,7},{6,4},{7,5},{8,10},{9,11},{10,... | collective-permute-start | bytes 344072 | tf_op jit(solution)/shard_map/ppermute | solution.py:71
  152.2 9.5 %collective-permute-start.10 = (f32[32,896]{1,0:T(8,128)S(1)}, f32[32,896]{1,0:T(8,128)S(1)}, u32[]{:S(2)}, u32[]{:S(2)}) collective-permute-start(f32[32,896]{1,0:T(8,128)S(1)} %dynamic-slice_bitcast_fusion.5), channel_id=1, source_target_pairs={{0,2},{1,3},{2,0},{3,1},{4,6},{5,7},{6,4},{7,5},{8,10},{9,11},{10,... | collective-permute-start | bytes 344072 | tf_op jit(solution)/shard_map/ppermute | solution.py:71
  161.7 8.1 %collective-permute-start.14 = (bf16[64,896]{1,0:T(8,128)(2,1)S(1)}, bf16[64,896]{1,0:T(8,128)(2,1)S(1)}, u32[]{:S(2)}, u32[]{:S(2)}) collective-permute-start(bf16[64,896]{1,0:T(8,128)(2,1)S(1)} %pad_maximum_fusion.1), channel_id=1, source_target_pairs={{0,2},{1,3},{2,0},{3,1},{4,6},{5,7},{6,4},{7,5},{8,10},{9,11},{10,... | collective-permute-start | bytes 344072 | tf_op jit(solution)/shard_map/ppermute | solution.py:82
  169.8 6.1 %collective-permute-start.15 = (bf16[2,64,896]{2,1,0:T(8,128)(2,1)S(1)}, bf16[2,64,896]{2,1,0:T(8,128)(2,1)S(1)}, u32[]{:S(2)}, u32[]{:S(2)}) collective-permute-start(bf16[2,64,896]{2,1,0:T(8,128)(2,1)S(1)} %maximum_select_fusion.5), channel_id=1, source_target_pairs={{0,1},{1,0},{2,3},{3,2},{4,5},{5,4},{6,7},{7,6},{8,9},{9,8},{10,11... | collective-permute-start | bytes 688136 | tf_op jit(solution)/shard_map/ppermute | solution.py:82
  176.1 6.5 %collective-permute-start.18 = (bf16[128,896]{1,0:T(8,128)(2,1)S(1)}, bf16[128,896]{1,0:T(8,128)(2,1)S(1)}, u32[]{:S(2)}, u32[]{:S(2)}) collective-permute-start(bf16[128,896]{1,0:T(8,128)(2,1)S(1)} %bitcast.114), channel_id=1, source_target_pairs={{0,16},{16,0},{1,17},{17,1},{2,18},{18,2},{3,19},{19,3},{4,20},{20... | collective-permute-start | bytes 688136 | tf_op jit(solution)/shard_map/ppermute | solution.py:237
  177.6 7.1 %collective-permute-start.16 = (bf16[128,896]{1,0:T(8,128)(2,1)S(1)}, bf16[128,896]{1,0:T(8,128)(2,1)S(1)}, u32[]{:S(2)}, u32[]{:S(2)}) collective-permute-start(bf16[128,896]{1,0:T(8,128)(2,1)S(1)} %bitcast.112), channel_id=1, source_target_pairs={{0,16},{16,0},{1,17},{17,1},{2,18},{18,2},{3,19},{19,3},{4,20},{20... | collective-permute-start | bytes 688136 | tf_op jit(solution)/shard_map/ppermute | solution.py:237

commit v16 on v15

--- a/solution.py
+++ b/solution.py
@@ -94,7 +94,22 @@
     t = lax.axis_index("tok")
     d_cols = table.shape[1]
 
-    table_pieces = tok_pieces(table, n_tok)
+    n_wid_early = lax.axis_size("wid")
+    chunked = (
+        n_tok == 2
+        and block_rows % 32 == 0
+        and lax.axis_size("voc") == 4
+        and is_pow2(n_wid_early)
+        and tok_rows % (2 * n_wid_early) == 0
+        and d_cols % 2 == 0
+    )
+    if chunked:
+        r1 = block_rows // 2
+        swap = [(0, 1), (1, 0)]
+        other_chunks = [lax.ppermute(table[:r1], "tok", swap), lax.ppermute(table[r1:], "tok", swap)]
+        table_pieces = [table]
+    else:
+        table_pieces = tok_pieces(table, n_tok)
     if n_tok == 2:
         hidden_other = lax.ppermute(hidden, "tok", [(0, 1), (1, 0)])
 
@@ -115,6 +130,15 @@
             piece, cols, (((1,), (1,)), ((), ())), preferred_element_type=jnp.float32
         )
         logits = part if logits is None else logits + part
+    if chunked:
+        cols = lax.dynamic_slice_in_dim(projected, (1 - t) * d_cols, d_cols, axis=1)
+        logits = logits + jnp.concatenate(
+            [
+                lax.dot_general(ch, cols, (((1,), (1,)), ((), ())), preferred_element_type=jnp.float32)
+                for ch in other_chunks
+            ],
+            axis=0,
+        )
 
     block_base = (lax.axis_index("voc") * lax.axis_size("wid") + lax.axis_index("wid")) * block_rows
     local_ids = targets - block_base
@@ -155,16 +179,18 @@
         c = lax.axis_index("voc") % 2
 
         def quarter_dots(sel):
-            return jnp.stack(
-                [
-                    jnp.dot(
-                        dlogits,
-                        lax.dynamic_slice_in_dim(piece, sel * q_cols, q_cols, axis=1),
-                        preferred_element_type=jnp.float32,
-                    )
-                    for piece in table_pieces
-                ]
-            )
+            def qdot(rows, piece):
+                return jnp.dot(
+                    rows,
+                    lax.dynamic_slice_in_dim(piece, sel * q_cols, q_cols, axis=1),
+                    preferred_element_type=jnp.float32,
+                )
+
+            if not chunked:
+                return jnp.stack([qdot(dlogits, piece) for piece in table_pieces])
+            own = qdot(dlogits, table)
+            other = qdot(dlogits[:, :r1], other_chunks[0]) + qdot(dlogits[:, r1:], other_chunks[1])
+            return jnp.stack([own, other])
 
         sent = quarter_dots(1 - c)
         received = lax.ppermute(sent, "voc", [(k, k ^ 1) for k in range(n_voc)])

time: 191 us -> 202 us (1.058)
  local copies, waits for them, and re-layouts: 3.47 us -> 8.32 us
  waiting for transfers between devices: 78.7 us -> 81.5 us
  matrix products: 30.8 us -> 33.3 us
    dot_general x4 -> x8, matrix products: 9.96 us -> 17.4 us  [the longest x6 12.3 us: qdot(): jnp.dot(rows, lax.dynamic_slice_in_dim(piece, sel * q_cols, q_cols, axis=...]
    slice x0 -> x1, local copies, waits for them, and re-layouts: none -> 4.82 us  [on_device(): table[:r1]]
    dot_general x2 -> x1, matrix products: 7.46 us -> 3.55 us  [on_device(): lax.dot_general(piece, cols, (((1,), (1,)), ((), ())), preferred_element_...]
    ppermute x1 -> x2, waiting for transfers between devices: 32.6 us -> 34.1 us  [the longest x1 34.1 us: on_device(): lax.ppermute(table[r1:], 'tok', swap)]
  transfers between devices with their start and end apart: 20 -> 21, of which waited for: 15 -> 15; matrix products, arithmetic and copies ran while one was open for 14% -> 13% of each run, Pallas kernels for 0% -> 0%
where the time goes in v16:
time: 202 us; the launch traced here: 201 us
  waiting for transfers between devices  81.5 us (40%)
  blocking collectives  38.8 us (19%)
  matrix products  33.3 us (16%)
  starting transfers between devices  26.2 us (13%)
  other arithmetic  9.39 us (5%)
  local copies, waits for them, and re-layouts  8.32 us (4%)
  between operations  3.52 us (2%)
    psum x1, blocking collectives, on_device(): summed = lax.psum(partial_value, 'wid')  38.8 us
    ppermute x1, waiting for transfers between devices, on_device(): lax.ppermute(table[r1:], 'tok', swap)  34.1 us
    ppermute x4, waiting for transfers between devices, doubling_gather(): other = lax.ppermute(x, ax, [(k, k ^ b) for k in range(n)])  21.8 us
    ppermute x6, waiting for transfers between devices, halving_steps(): x = keep + lax.ppermute(send, ax, [(k, k ^ b) for k in range(n)])  18.1 us
    dot_general x6, matrix products, qdot(): jnp.dot(rows, lax.dynamic_slice_in_dim(piece, sel * q_cols, q_cols, axis=...  12.3 us
    ppermute x6, starting transfers between devices, halving_steps(): x = keep + lax.ppermute(send, ax, [(k, k ^ b) for k in range(n)])  10.6 us
    dot_general x4, matrix products, on_device(): lax.dot_general(rows[i], hid[i * half_rows:(i + 1) * half_rows], by_pos,...  9.76 us
    ppermute x4, starting transfers between devices, butterfly(): other = lax.ppermute(stats, ax, [(i, i ^ b) for i in range(n)])  6.7 us
  transfers between devices with their start and end apart: 21, of which 15 were waited for; matrix products, arithmetic and copies ran while one was open for 13% of the time, Pallas kernels for 0%

profile of v16, /device:TPU:0, one launch (start us, length us, event | category | flops | bytes accessed | tf_op | source)
XLA Modules:
  0.0 200.9 jit_solution(6614656439272039792)
XLA Ops:
  0.6 4.8 %fusion.55 = (bf16[608,1792]{1,0:T(8,128)(2,1)}, bf16[608,1792]{1,0:T(8,128)(2,1)}) fusion(bf16[1216,1792]{1,0:T(8,128)(2,1)} %param.7), kind=kLoop, calls=%fused_computation.105 | loop fusion | bytes 8716288 | tf_op jit(solution)/shard_map/slice | solution.py:109
  5.5 2.9 %collective-permute-start.2 = (bf16[608,1792]{1,0:T(8,128)(2,1)}, bf16[608,1792]{1,0:T(8,128)(2,1)}, u32[]{:S(2)}, u32[]{:S(2)}) collective-permute-start(bf16[608,1792]{1,0:T(8,128)(2,1)} %get-tuple-element.12), channel_id=1, source_target_pairs={{0,16},{16,0},{1,17},{17,1},{2,18},{18,2},{3,19},{19,3},{4,20},{20... | collective-permute-start | bytes 6537224 | tf_op jit(solution)/shard_map/ppermute | solution.py:109
  8.4 2.6 %fusion.61 = f32[256,896]{1,0:T(8,128)S(1)} fusion(bf16[256,2048]{1,0:T(8,128)(2,1)} %param.5, bf16[896,2048]{1,0:T(8,128)(2,1)S(1)} %copy-done.3), kind=kOutput, calls=%fused_computation.111 | convolution fusion | flops 939524096 | bytes 5636096 | tf_op jit(solution)/shard_map/dot_general | solution.py:116
  11.0 38.8 %all-reduce.1 = bf16[256,896]{1,0:T(8,128)(2,1)S(1)} all-reduce(f32[256,896]{1,0:T(8,128)S(1)} %fusion.61), channel_id=1, replica_groups=mesh['tok'=2,'voc'=4,'wid'=4] {'wid'}, use_global_device_ids=true, to_apply=%region_0.0 | all-reduce | flops 229376 | bytes 1376256 | tf_op jit(solution)/shard_map/psum | solution.py:119
  51.4 9.0 %collective-permute-done = bf16[256,896]{1,0:T(8,128)(2,1)S(1)} collective-permute-done((bf16[256,896]{1,0:T(8,128)(2,1)S(1)}, bf16[256,896]{1,0:T(8,128)(2,1)S(1)}, u32[]{:S(2)}, u32[]{:S(2)}) %collective-permute-start) | collective-permute-done | bytes 458784 | tf_op jit(solution)/shard_map/ppermute | solution.py:82
  60.8 2.2 %collective-permute-done.1 = bf16[2,256,896]{2,1,0:T(8,128)(2,1)S(1)} collective-permute-done((bf16[2,256,896]{2,1,0:T(8,128)(2,1)S(1)}, bf16[2,256,896]{2,1,0:T(8,128)(2,1)S(1)}, u32[]{:S(2)}, u32[]{:S(2)}) %collective-permute-start.1) | collective-permute-done | bytes 917536 | tf_op jit(solution)/shard_map/ppermute | solution.py:82
  63.6 2.4 %copy.8 = bf16[256,4,896]{0,2,1:T(8,128)(2,1)} copy(bf16[256,4,896]{2,0,1:T(8,128)(2,1)S(1)} %bitcast.95) | data formatting | bytes 3670016 | tf_op jit(solution)/shard_map/transpose | solution.py:122
  66.0 2.7 %convolution_bitcast_fusion.2 = f32[608,256]{1,0:T(8,128)S(1)} fusion(bf16[608,1792]{1,0:T(8,128)(2,1)} %collective-permute-done.2, bf16[256,3584]{0,1:T(8,128)(2,1)} %bitcast.99, s32[]{:T(128)S(6)} %select_n.167), kind=kOutput, calls=%fused_computation.16 | convolution fusion | flops 557842432 | bytes 3719172 | tf_op jit(solution)/shard_map/dot_general | solution.py:137
  68.7 34.1 %collective-permute-done.3 = bf16[608,1792]{1,0:T(8,128)(2,1)} collective-permute-done((bf16[608,1792]{1,0:T(8,128)(2,1)}, bf16[608,1792]{1,0:T(8,128)(2,1)}, u32[]{:S(2)}, u32[]{:S(2)}) %collective-permute-start.3) | collective-permute-done | bytes 2179104 | tf_op jit(solution)/shard_map/ppermute | solution.py:109
  102.8 2.3 %convolution_bitcast_fusion.1 = f32[608,256]{1,0:T(8,128)S(1)} fusion(bf16[608,1792]{1,0:T(8,128)(2,1)} %collective-permute-done.3, bf16[256,3584]{0,1:T(8,128)(2,1)S(1)} %bitcast.100, s32[]{:T(128)S(6)} %select_n.167), kind=kOutput, calls=%fused_computation.15 | convolution fusion | flops 557842432 | bytes 3719172 | tf_op jit(solution)/shard_map/dot_general | solution.py:137
  105.2 3.6 %fusion.60 = (f32[256]{0:T(256)S(1)}, f32[1216,256]{1,0:T(8,128)S(1)}) fusion(f32[608,256]{1,0:T(8,128)S(1)} %convolution_bitcast_fusion.1, f32[608,256]{1,0:T(8,128)S(1)} %convolution_bitcast_fusion.2, bf16[1216,1792]{1,0:T(8,128)(2,1)} %param.7, bf16[256,3584]{0,1:T(8,128)(2,1)S(1)} %bitcast.101, s32[]{:T(128)S(6)} %select_n.166), kind=kOutput, calls=%fused_computation.110 | convolution fusion | flops 1116618496 | bytes 7767044 | tf_op jit(solution)/shard_map/dot_general | solution.py:129
  117.8 2.9 %collective-permute-start.7 = (f32[3,256]{1,0:T(4,128)S(1)}, f32[3,256]{1,0:T(4,128)S(1)}, u32[]{:S(2)}, u32[]{:S(2)}) collective-permute-start(f32[3,256]{1,0:T(4,128)S(1)} %pad_maximum_fusion.5), channel_id=1, source_target_pairs={{0,2},{1,3},{2,0},{3,1},{4,6},{5,7},{6,4},{7,5},{8,10},{9,11},{10,... | collective-permute-start | bytes 9224 | tf_op jit(solution)/shard_map/ppermute | solution.py:33
  122.7 2.5 %fusion.7 = f32[1,256,896]{2,1,0:T(8,128)S(1)} fusion(bf16[1216,1792]{1,0:T(8,128)(2,1)} %param.7, s32[]{:T(128)S(6)} %select_n.170, f32[1216,256]{1,0:T(8,128)S(1)} %get-tuple-element.37, f32[256]{0:T(256)S(1)} %bitcast.123, s32[256]{0:T(256)S(1)} %broadcast_subtract_fusion, f32[256]{0:T(256)S(1)} %convert_element_type.29), kind=kOutput, calls=%fused_computation.10 | convolution fusion | flops 559710208 | bytes 4344836 | tf_op jit(solution)/shard_map/dot_general | solution.py:183
  133.9 2.5 %fusion.4 = f32[1,256,896]{2,1,0:T(8,128)S(1)} fusion(bf16[1216,1792]{1,0:T(8,128)(2,1)} %param.7, s32[]{:T(128)S(6)} %select_n.169, f32[1216,256]{1,0:T(8,128)S(1)} %get-tuple-element.37, f32[256]{0:T(256)S(1)} %bitcast.124, s32[256]{0:T(256)S(1)} %broadcast_subtract_fusion, f32[256]{0:T(256)S(1)} %convert_element_type.29), kind=kOutput, calls=%fused_computation.9 | convolution fusion | flops 559710208 | bytes 4344836 | tf_op jit(solution)/shard_map/dot_general | solution.py:183
  138.4 1.9 collective-permute-start.12
  146.0 5.6 %collective-permute-done.12 = f32[2,2,32,896]{3,2,1,0:T(8,128)} collective-permute-done((f32[2,2,32,896]{3,2,1,0:T(8,128)S(1)}, f32[2,2,32,896]{3,2,1,0:T(8,128)}, u32[]{:S(2)}, u32[]{:S(2)}) %collective-permute-start.12) | collective-permute-done | bytes 458784 | tf_op jit(solution)/shard_map/ppermute | solution.py:71
  156.2 3.9 %collective-permute-done.13 = f32[2,32,896]{2,1,0:T(8,128)S(1)} collective-permute-done((f32[2,32,896]{2,1,0:T(8,128)S(1)}, f32[2,32,896]{2,1,0:T(8,128)S(1)}, u32[]{:S(2)}, u32[]{:S(2)}) %collective-permute-start.13) | collective-permute-done | bytes 229408 | tf_op jit(solution)/shard_map/ppermute | solution.py:71
  160.2 2.7 %collective-permute-start.14 = (f32[32,896]{1,0:T(8,128)S(1)}, f32[32,896]{1,0:T(8,128)S(1)}, u32[]{:S(2)}, u32[]{:S(2)}) collective-permute-start(f32[32,896]{1,0:T(8,128)S(1)} %dynamic-slice_bitcast_fusion.4), channel_id=1, source_target_pairs={{0,2},{1,3},{2,0},{3,1},{4,6},{5,7},{6,4},{7,5},{8,10},{9,11},{10,... | collective-permute-start | bytes 344072 | tf_op jit(solution)/shard_map/ppermute | solution.py:71
  164.4 6.9 %collective-permute-done.14 = f32[32,896]{1,0:T(8,128)S(1)} collective-permute-done((f32[32,896]{1,0:T(8,128)S(1)}, f32[32,896]{1,0:T(8,128)S(1)}, u32[]{:S(2)}, u32[]{:S(2)}) %collective-permute-start.14) | collective-permute-done | bytes 114720 | tf_op jit(solution)/shard_map/ppermute | solution.py:71
  175.9 4.7 %collective-permute-done.15 = bf16[64,896]{1,0:T(8,128)(2,1)S(1)} collective-permute-done((bf16[64,896]{1,0:T(8,128)(2,1)S(1)}, bf16[64,896]{1,0:T(8,128)(2,1)S(1)}, u32[]{:S(2)}, u32[]{:S(2)}) %collective-permute-start.15) | collective-permute-done | bytes 114720 | tf_op jit(solution)/shard_map/ppermute | solution.py:82
  180.8 5.9 %collective-permute-done.16 = bf16[2,64,896]{2,1,0:T(8,128)(2,1)S(1)} collective-permute-done((bf16[2,64,896]{2,1,0:T(8,128)(2,1)S(1)}, bf16[2,64,896]{2,1,0:T(8,128)(2,1)S(1)}, u32[]{:S(2)}, u32[]{:S(2)}) %collective-permute-start.16) | collective-permute-done | bytes 229408 | tf_op jit(solution)/shard_map/ppermute | solution.py:82
  188.9 2.2 %fusion.26 = f32[896,2048]{1,0:T(8,128)S(1)} fusion(bf16[128,896]{1,0:T(8,128)(2,1)S(1)} %bitcast.107, bf16[256,2048]{1,0:T(8,128)(2,1)} %param.5), kind=kOutput, calls=%fused_computation.36 | convolution fusion | flops 469762048 | bytes 8093696 | tf_op jit(solution)/shard_map/dot_general | solution.py:269
  191.1 2.2 %fusion.28 = f32[896,2048]{1,0:T(8,128)S(1)} fusion(bf16[128,896]{1,0:T(8,128)(2,1)S(1)} %bitcast.105, bf16[256,2048]{1,0:T(8,128)(2,1)} %param.5), kind=kOutput, calls=%fused_computation.38 | convolution fusion | flops 469762048 | bytes 8093696 | tf_op jit(solution)/shard_map/dot_general | solution.py:269
  195.5 4.3 %add_add_fusion = f32[896,2048]{1,0:T(8,128)} fusion(f32[896,2048]{1,0:T(8,128)S(1)} %fusion.23, f32[896,2048]{1,0:T(8,128)S(1)} %fusion.28, f32[896,2048]{1,0:T(8,128)S(1)} %fusion.26, bf16[128,896]{1,0:T(8,128)(2,1)S(1)} %collective-permute-done.17, bf16[256,2048]{1,0:T(8,128)(2,1)S(1)} %collective-permute-done.18), kind=kOutput, calls=%fused_computation | convolution fusion | flops 475267072 | bytes 30113792 | tf_op jit(solution)/shard_map/dot_general | solution.py:269
  (84 shorter events, 43.8 us)
Async XLA Ops:
  5.5 60.5 %collective-permute-start.2 = (bf16[608,1792]{1,0:T(8,128)(2,1)}, bf16[608,1792]{1,0:T(8,128)(2,1)}, u32[]{:S(2)}, u32[]{:S(2)}) collective-permute-start(bf16[608,1792]{1,0:T(8,128)(2,1)} %get-tuple-element.12), channel_id=1, source_target_pairs={{0,16},{16,0},{1,17},{17,1},{2,18},{18,2},{3,19},{19,3},{4,20},{20... | collective-permute-start | bytes 6537224 | tf_op jit(solution)/shard_map/ppermute | solution.py:109
  8.4 94.4 %collective-permute-start.3 = (bf16[608,1792]{1,0:T(8,128)(2,1)}, bf16[608,1792]{1,0:T(8,128)(2,1)}, u32[]{:S(2)}, u32[]{:S(2)}) collective-permute-start(bf16[608,1792]{1,0:T(8,128)(2,1)} %get-tuple-element.13), channel_id=1, source_target_pairs={{0,16},{16,0},{1,17},{17,1},{2,18},{18,2},{3,19},{19,3},{4,20},{20... | collective-permute-start | bytes 6537224 | tf_op jit(solution)/shard_map/ppermute | solution.py:109
  11.0 49.6 %copy-start.2 = (s32[256]{0:T(256)S(1)}, s32[256]{0:T(256)}, u32[]{:S(2)}) copy-start(s32[256]{0:T(256)} %param.8) | copy-start | bytes 3076
  49.8 10.5 %collective-permute-start = (bf16[256,896]{1,0:T(8,128)(2,1)S(1)}, bf16[256,896]{1,0:T(8,128)(2,1)S(1)}, u32[]{:S(2)}, u32[]{:S(2)}) collective-permute-start(bf16[256,896]{1,0:T(8,128)(2,1)S(1)} %all-reduce.1), channel_id=1, source_target_pairs={{0,8},{4,12},{8,0},{12,4},{1,9},{5,13},{9,1},{13,5},{2,10},{6,14},... | collective-permute-start | bytes 1376264 | tf_op jit(solution)/shard_map/ppermute | solution.py:82
  60.5 2.5 %collective-permute-start.1 = (bf16[2,256,896]{2,1,0:T(8,128)(2,1)S(1)}, bf16[2,256,896]{2,1,0:T(8,128)(2,1)S(1)}, u32[]{:S(2)}, u32[]{:S(2)}) collective-permute-start(bf16[2,256,896]{2,1,0:T(8,128)(2,1)S(1)} %maximum_select_fusion.2), channel_id=1, source_target_pairs={{0,4},{4,0},{8,12},{12,8},{1,5},{5,1},{9,13},{13,9},{2,6},{6,2},{1... | collective-permute-start | bytes 2752520 | tf_op jit(solution)/shard_map/ppermute | solution.py:82
  66.0 36.8 %copy-start = (bf16[256,4,896]{0,2,1:T(8,128)(2,1)S(1)}, bf16[256,4,896]{0,2,1:T(8,128)(2,1)}, u32[]{:S(2)}) copy-start(bf16[256,4,896]{0,2,1:T(8,128)(2,1)} %copy.8) | copy-start | bytes 5505028
  105.2 15.5 %copy-start.1 = (s32[256]{0:T(256)S(1)}, s32[256]{0:T(256)}, u32[]{:S(2)}) copy-start(s32[256]{0:T(256)} %param.9) | copy-start | bytes 3076
  109.1 1.2 collective-permute-start.4
  110.3 3.7 %collective-permute-start.5 = (f32[3,256]{1,0:T(4,128)S(1)}, f32[3,256]{1,0:T(4,128)S(1)}, u32[]{:S(2)}, u32[]{:S(2)}) collective-permute-start(f32[3,256]{1,0:T(4,128)S(1)} %pad_maximum_fusion.3), channel_id=1, source_target_pairs={{0,8},{4,12},{8,0},{12,4},{1,9},{5,13},{9,1},{13,5},{2,10},{6,14},... | collective-permute-start | bytes 9224 | tf_op jit(solution)/shard_map/ppermute | solution.py:33
  114.1 3.7 %collective-permute-start.6 = (f32[3,256]{1,0:T(4,128)S(1)}, f32[3,256]{1,0:T(4,128)S(1)}, u32[]{:S(2)}, u32[]{:S(2)}) collective-permute-start(f32[3,256]{1,0:T(4,128)S(1)} %pad_maximum_fusion.4), channel_id=1, source_target_pairs={{0,1},{1,0},{2,3},{3,2},{4,5},{5,4},{6,7},{7,6},{8,9},{9,8},{10,11... | collective-permute-start | bytes 9224 | tf_op jit(solution)/shard_map/ppermute | solution.py:33
  117.8 4.6 %collective-permute-start.7 = (f32[3,256]{1,0:T(4,128)S(1)}, f32[3,256]{1,0:T(4,128)S(1)}, u32[]{:S(2)}, u32[]{:S(2)}) collective-permute-start(f32[3,256]{1,0:T(4,128)S(1)} %pad_maximum_fusion.5), channel_id=1, source_target_pairs={{0,2},{1,3},{2,0},{3,1},{4,6},{5,7},{6,4},{7,5},{8,10},{9,11},{10,... | collective-permute-start | bytes 9224 | tf_op jit(solution)/shard_map/ppermute | solution.py:33
  130.3 6.2 %collective-permute-start.8 = (f32[2,256,896]{2,1,0:T(8,128)}, f32[2,256,896]{2,1,0:T(8,128)}, u32[]{:S(2)}, u32[]{:S(2)}) collective-permute-start(f32[2,256,896]{2,1,0:T(8,128)} %pad_maximum_fusion), channel_id=1, source_target_pairs={{0,4},{4,0},{8,12},{12,8},{1,5},{5,1},{9,13},{13,9},{2,6},{6,2},{1... | collective-permute-start | bytes 5505032 | tf_op jit(solution)/shard_map/ppermute | solution.py:196
  138.4 13.2 %collective-permute-start.12 = (f32[2,2,32,896]{3,2,1,0:T(8,128)S(1)}, f32[2,2,32,896]{3,2,1,0:T(8,128)}, u32[]{:S(2)}, u32[]{:S(2)}) collective-permute-start(f32[2,2,32,896]{3,2,1,0:T(8,128)S(1)} %dynamic-slice_bitcast_fusion), channel_id=1, source_target_pairs={{0,1},{1,0},{2,3},{3,2},{4,5},{5,4},{6,7},{7,6},{8,9},{9,8},{10,11... | collective-permute-start | bytes 1376264 | tf_op jit(solution)/shard_map/ppermute | solution.py:71
  140.3 53.0 %collective-permute-start.18 = (bf16[256,2048]{1,0:T(8,128)(2,1)}, bf16[256,2048]{1,0:T(8,128)(2,1)S(1)}, u32[]{:S(2)}, u32[]{:S(2)}) collective-permute-start(bf16[256,2048]{1,0:T(8,128)(2,1)} %param.5), channel_id=1, source_target_pairs={{0,16},{16,0},{1,17},{17,1},{2,18},{18,2},{3,19},{19,3},{4,20},{20... | collective-permute-start | bytes 3145736 | tf_op jit(solution)/shard_map/ppermute | solution.py:114
  142.5 12.4 %collective-permute-start.9 = (f32[2,2,32,896]{3,2,1,0:T(8,128)S(1)}, f32[2,2,32,896]{3,2,1,0:T(8,128)S(1)}, u32[]{:S(2)}, u32[]{:S(2)}) collective-permute-start(f32[2,2,32,896]{3,2,1,0:T(8,128)S(1)} %dynamic-slice_bitcast_fusion.1), channel_id=1, source_target_pairs={{0,8},{4,12},{8,0},{12,4},{1,9},{5,13},{9,1},{13,5},{2,10},{6,14},... | collective-permute-start | bytes 1376264 | tf_op jit(solution)/shard_map/ppermute | solution.py:71
  145.4 27.2 %collective-permute-start.20 = (f32[2]{0:T(128)S(1)}, f32[2]{0:T(128)S(1)}, u32[]{:S(2)}, u32[]{:S(2)}) collective-permute-start(f32[2]{0:T(128)S(1)} %pad_maximum_fusion.6), channel_id=1, source_target_pairs={{0,16},{16,0},{1,17},{17,1},{2,18},{18,2},{3,19},{19,3},{4,20},{20... | collective-permute-start | bytes 32 | tf_op jit(solution)/shard_map/ppermute | solution.py:45
  152.7 7.4 %collective-permute-start.13 = (f32[2,32,896]{2,1,0:T(8,128)S(1)}, f32[2,32,896]{2,1,0:T(8,128)S(1)}, u32[]{:S(2)}, u32[]{:S(2)}) collective-permute-start(f32[2,32,896]{2,1,0:T(8,128)S(1)} %dynamic-slice_bitcast_fusion.2), channel_id=1, source_target_pairs={{0,8},{4,12},{8,0},{12,4},{1,9},{5,13},{9,1},{13,5},{2,10},{6,14},... | collective-permute-start | bytes 688136 | tf_op jit(solution)/shard_map/ppermute | solution.py:71
  155.0 7.9 %collective-permute-start.10 = (f32[2,32,896]{2,1,0:T(8,128)S(1)}, f32[2,32,896]{2,1,0:T(8,128)S(1)}, u32[]{:S(2)}, u32[]{:S(2)}) collective-permute-start(f32[2,32,896]{2,1,0:T(8,128)S(1)} %dynamic-slice_bitcast_fusion.3), channel_id=1, source_target_pairs={{0,1},{1,0},{2,3},{3,2},{4,5},{5,4},{6,7},{7,6},{8,9},{9,8},{10,11... | collective-permute-start | bytes 688136 | tf_op jit(solution)/shard_map/ppermute | solution.py:71
  160.2 11.1 %collective-permute-start.14 = (f32[32,896]{1,0:T(8,128)S(1)}, f32[32,896]{1,0:T(8,128)S(1)}, u32[]{:S(2)}, u32[]{:S(2)}) collective-permute-start(f32[32,896]{1,0:T(8,128)S(1)} %dynamic-slice_bitcast_fusion.4), channel_id=1, source_target_pairs={{0,2},{1,3},{2,0},{3,1},{4,6},{5,7},{6,4},{7,5},{8,10},{9,11},{10,... | collective-permute-start | bytes 344072 | tf_op jit(solution)/shard_map/ppermute | solution.py:71
  162.9 9.6 %collective-permute-start.11 = (f32[32,896]{1,0:T(8,128)S(1)}, f32[32,896]{1,0:T(8,128)S(1)}, u32[]{:S(2)}, u32[]{:S(2)}) collective-permute-start(f32[32,896]{1,0:T(8,128)S(1)} %dynamic-slice_bitcast_fusion.5), channel_id=1, source_target_pairs={{0,2},{1,3},{2,0},{3,1},{4,6},{5,7},{6,4},{7,5},{8,10},{9,11},{10,... | collective-permute-start | bytes 344072 | tf_op jit(solution)/shard_map/ppermute | solution.py:71
  172.5 8.0 %collective-permute-start.15 = (bf16[64,896]{1,0:T(8,128)(2,1)S(1)}, bf16[64,896]{1,0:T(8,128)(2,1)S(1)}, u32[]{:S(2)}, u32[]{:S(2)}) collective-permute-start(bf16[64,896]{1,0:T(8,128)(2,1)S(1)} %pad_maximum_fusion.1), channel_id=1, source_target_pairs={{0,2},{1,3},{2,0},{3,1},{4,6},{5,7},{6,4},{7,5},{8,10},{9,11},{10,... | collective-permute-start | bytes 344072 | tf_op jit(solution)/shard_map/ppermute | solution.py:82
  180.6 6.1 %collective-permute-start.16 = (bf16[2,64,896]{2,1,0:T(8,128)(2,1)S(1)}, bf16[2,64,896]{2,1,0:T(8,128)(2,1)S(1)}, u32[]{:S(2)}, u32[]{:S(2)}) collective-permute-start(bf16[2,64,896]{2,1,0:T(8,128)(2,1)S(1)} %maximum_select_fusion.5), channel_id=1, source_target_pairs={{0,1},{1,0},{2,3},{3,2},{4,5},{5,4},{6,7},{7,6},{8,9},{9,8},{10,11... | collective-permute-start | bytes 688136 | tf_op jit(solution)/shard_map/ppermute | solution.py:82
  186.9 6.5 %collective-permute-start.19 = (bf16[128,896]{1,0:T(8,128)(2,1)S(1)}, bf16[128,896]{1,0:T(8,128)(2,1)S(1)}, u32[]{:S(2)}, u32[]{:S(2)}) collective-permute-start(bf16[128,896]{1,0:T(8,128)(2,1)S(1)} %bitcast.106), channel_id=1, source_target_pairs={{0,16},{16,0},{1,17},{17,1},{2,18},{18,2},{3,19},{19,3},{4,20},{20... | collective-permute-start | bytes 688136 | tf_op jit(solution)/shard_map/ppermute | solution.py:263
  188.4 7.1 %collective-permute-start.17 = (bf16[128,896]{1,0:T(8,128)(2,1)S(1)}, bf16[128,896]{1,0:T(8,128)(2,1)S(1)}, u32[]{:S(2)}, u32[]{:S(2)}) collective-permute-start(bf16[128,896]{1,0:T(8,128)(2,1)S(1)} %bitcast.104), channel_id=1, source_target_pairs={{0,16},{16,0},{1,17},{17,1},{2,18},{18,2},{3,19},{19,3},{4,20},{20... | collective-permute-start | bytes 688136 | tf_op jit(solution)/shard_map/ppermute | solution.py:263
  (1 other events, 7.8 us)

commit v17 on v15

--- a/solution.py
+++ b/solution.py
@@ -128,7 +128,11 @@
     stats = butterfly(stats, ("voc", "wid"))
     log_total = stats[0] + jnp.log(stats[1])
     picked = stats[2]
-    sums = jnp.stack([jnp.sum(weight * (log_total - picked)), jnp.sum(weight)])
+    sums = jnp.dot(
+        jnp.stack([weight * (log_total - picked), weight]),
+        jnp.ones((tok_rows,), jnp.float32),
+        precision=lax.Precision.HIGHEST,
+    )
     sums = tree_sum(sums, "tok")
 
     dlogits = (

time: 191 us -> 194 us (1.016)
  starting transfers between devices: 26.3 us -> 31.4 us
  other arithmetic: 8.16 us -> 5.81 us
    ppermute x2, waiting for transfers between devices: 1.06 us -> 5.4 us  [on_device(): lax.ppermute(grad_rows_pos[i * half_rows:(i + 1) * half_rows], 'tok', [(0...]
    ppermute x4, waiting for transfers between devices: 20.8 us -> 16.8 us  [doubling_gather(): other = lax.ppermute(x, ax, [(k, k ^ b) for k in range(n)])]
    ppermute x6, starting transfers between devices: 10.6 us -> 12.9 us  [halving_steps(): x = keep + lax.ppermute(send, ax, [(k, k ^ b) for k in range(n)])]
    dot_general x4, matrix products: 9.78 us -> 7.71 us  [on_device(): lax.dot_general(rows[i], hid[i * half_rows:(i + 1) * half_rows], by_pos,...]
    ppermute x1, waiting for transfers between devices: 0.01 us -> 2.01 us  [tree_sum(): x = x + lax.ppermute(x, ax, [(i, i ^ b) for i in range(n)])]
  transfers between devices with their start and end apart: 20 -> 20, of which waited for: 15 -> 16; matrix products, arithmetic and copies ran while one was open for 14% -> 12% of each run, Pallas kernels for 0% -> 0%
where the time goes in v17:
time: 194 us; the launch traced here: 193 us
  waiting for transfers between devices  80 us (41%)
  blocking collectives  39.1 us (20%)
  starting transfers between devices  31.4 us (16%)
  matrix products  29 us (15%)
  other arithmetic  5.81 us (3%)
  local copies, waits for them, and re-layouts  4.25 us (2%)
  between operations  3.52 us (2%)
    psum x1, blocking collectives, on_device(): summed = lax.psum(partial_value, 'wid')  39.1 us
    ppermute x1, waiting for transfers between devices, tok_pieces(): pieces.append(lax.ppermute(x, 'tok', perm))  32.5 us
    ppermute x4, waiting for transfers between devices, doubling_gather(): other = lax.ppermute(x, ax, [(k, k ^ b) for k in range(n)])  16.8 us
    ppermute x6, waiting for transfers between devices, halving_steps(): x = keep + lax.ppermute(send, ax, [(k, k ^ b) for k in range(n)])  16.7 us
    ppermute x6, starting transfers between devices, halving_steps(): x = keep + lax.ppermute(send, ax, [(k, k ^ b) for k in range(n)])  12.9 us
    dot_general x4, matrix products, quarter_dots(): jnp.dot(dlogits, lax.dynamic_slice_in_dim(piece, sel * q_cols, q_cols, ax...  9.99 us
    dot_general x4, matrix products, on_device(): lax.dot_general(rows[i], hid[i * half_rows:(i + 1) * half_rows], by_pos,...  7.71 us
    dot_general x2, matrix products, on_device(): lax.dot_general(piece, cols, (((1,), (1,)), ((), ())), preferred_element_...  7.57 us
  transfers between devices with their start and end apart: 20, of which 16 were waited for; matrix products, arithmetic and copies ran while one was open for 12% of the time, Pallas kernels for 0%

profile of v17, /device:TPU:0, one launch (start us, length us, event | category | flops | bytes accessed | tf_op | source)
XLA Modules:
  0.0 193.1 jit_solution(4095142906111010025)
XLA Ops:
  0.6 3.0 %collective-permute-start.2 = (bf16[1216,1792]{1,0:T(8,128)(2,1)}, bf16[1216,1792]{1,0:T(8,128)(2,1)}, u32[]{:S(2)}, u32[]{:S(2)}) collective-permute-start(bf16[1216,1792]{1,0:T(8,128)(2,1)} %param.7), channel_id=1, source_target_pairs={{0,16},{16,0},{1,17},{17,1},{2,18},{18,2},{3,19},{19,3},{4,20},{20... | collective-permute-start | bytes 13074440 | tf_op jit(solution)/shard_map/ppermute | solution.py:11
  3.6 3.6 %fusion.64 = f32[256,896]{1,0:T(8,128)S(1)} fusion(bf16[256,2048]{1,0:T(8,128)(2,1)} %param.5, bf16[896,2048]{1,0:T(8,128)(2,1)} %param.6), kind=kOutput, calls=%fused_computation.107 | convolution fusion | flops 939524096 | bytes 5636096 | tf_op jit(solution)/shard_map/dot_general | solution.py:101
  7.3 39.1 %all-reduce.1 = bf16[256,896]{1,0:T(8,128)(2,1)S(1)} all-reduce(f32[256,896]{1,0:T(8,128)S(1)} %fusion.64), channel_id=1, replica_groups=mesh['tok'=2,'voc'=4,'wid'=4] {'wid'}, use_global_device_ids=true, to_apply=%region_0.0 | all-reduce | flops 229376 | bytes 1376256 | tf_op jit(solution)/shard_map/psum | solution.py:104
  48.0 7.9 %collective-permute-done = bf16[256,896]{1,0:T(8,128)(2,1)S(1)} collective-permute-done((bf16[256,896]{1,0:T(8,128)(2,1)S(1)}, bf16[256,896]{1,0:T(8,128)(2,1)S(1)}, u32[]{:S(2)}, u32[]{:S(2)}) %collective-permute-start) | collective-permute-done | bytes 458784 | tf_op jit(solution)/shard_map/ppermute | solution.py:82
  56.4 2.2 %collective-permute-done.1 = bf16[2,256,896]{2,1,0:T(8,128)(2,1)S(1)} collective-permute-done((bf16[2,256,896]{2,1,0:T(8,128)(2,1)S(1)}, bf16[2,256,896]{2,1,0:T(8,128)(2,1)S(1)}, u32[]{:S(2)}, u32[]{:S(2)}) %collective-permute-start.1) | collective-permute-done | bytes 917536 | tf_op jit(solution)/shard_map/ppermute | solution.py:82
  59.1 2.4 %copy.8 = bf16[256,4,896]{0,2,1:T(8,128)(2,1)} copy(bf16[256,4,896]{2,0,1:T(8,128)(2,1)S(1)} %bitcast.106) | data formatting | bytes 3670016 | tf_op jit(solution)/shard_map/transpose | solution.py:107
  61.5 4.0 %fusion.28 = f32[256,1216]{0,1:T(8,128)S(1)} fusion(bf16[1216,1792]{1,0:T(8,128)(2,1)} %param.7, bf16[256,3584]{0,1:T(8,128)(2,1)} %bitcast.110, s32[]{:T(128)S(6)} %select_n.168), kind=kOutput, calls=%fused_computation.32 | convolution fusion | flops 1115684864 | bytes 6520836 | tf_op jit(solution)/shard_map/dot_general | solution.py:114
  65.5 32.5 %collective-permute-done.2 = bf16[1216,1792]{1,0:T(8,128)(2,1)} collective-permute-done((bf16[1216,1792]{1,0:T(8,128)(2,1)}, bf16[1216,1792]{1,0:T(8,128)(2,1)}, u32[]{:S(2)}, u32[]{:S(2)}) %collective-permute-start.2) | collective-permute-done | bytes 4358176 | tf_op jit(solution)/shard_map/ppermute | solution.py:11
  98.0 3.6 %fusion.63 = (f32[256]{0:T(256)S(1)}, f32[256,1216]{0,1:T(8,128)S(1)}) fusion(f32[256,1216]{0,1:T(8,128)S(1)} %fusion.28, bf16[1216,1792]{1,0:T(8,128)(2,1)} %collective-permute-done.2, bf16[256,3584]{0,1:T(8,128)(2,1)S(1)} %bitcast.111, s32[]{:T(128)S(6)} %select_n.170), kind=kOutput, calls=%fused_computation.106 | convolution fusion | flops 1116307200 | bytes 7767044 | tf_op jit(solution)/shard_map/dot_general | solution.py:114
  110.7 2.9 %collective-permute-start.6 = (f32[3,256]{1,0:T(4,128)S(1)}, f32[3,256]{1,0:T(4,128)S(1)}, u32[]{:S(2)}, u32[]{:S(2)}) collective-permute-start(f32[3,256]{1,0:T(4,128)S(1)} %pad_maximum_fusion.5), channel_id=1, source_target_pairs={{0,2},{1,3},{2,0},{3,1},{4,6},{5,7},{6,4},{7,5},{8,10},{9,11},{10,... | collective-permute-start | bytes 9224 | tf_op jit(solution)/shard_map/ppermute | solution.py:33
  115.6 2.5 %fusion.14 = f32[1,256,896]{2,1,0:T(8,128)S(1)} fusion(bf16[1216,256]{1,0:T(8,128)(2,1)S(1)} %fusion.26, bf16[1216,1792]{1,0:T(8,128)(2,1)} %param.7, s32[]{:T(128)S(6)} %select_n.173), kind=kOutput, calls=%fused_computation.15 | convolution fusion | flops 557842432 | bytes 3719172 | tf_op jit(solution)/shard_map/dot_general | solution.py:164
  118.1 2.5 %fusion.17 = f32[1,256,896]{2,1,0:T(8,128)S(1)} fusion(bf16[1216,256]{1,0:T(8,128)(2,1)S(1)} %fusion.26, bf16[1216,1792]{1,0:T(8,128)(2,1)} %collective-permute-done.2, s32[]{:T(128)S(6)} %select_n.173), kind=kOutput, calls=%fused_computation.16 | convolution fusion | flops 557842432 | bytes 3719172 | tf_op jit(solution)/shard_map/dot_general | solution.py:164
  120.9 2.5 %fusion.8 = f32[1,256,896]{2,1,0:T(8,128)S(1)} fusion(bf16[1216,256]{1,0:T(8,128)(2,1)S(1)} %fusion.26, bf16[1216,1792]{1,0:T(8,128)(2,1)} %param.7, s32[]{:T(128)S(6)} %select_n.172), kind=kOutput, calls=%fused_computation.13 | convolution fusion | flops 557842432 | bytes 3719172 | tf_op jit(solution)/shard_map/dot_general | solution.py:164
  123.4 2.5 %fusion.11 = f32[1,256,896]{2,1,0:T(8,128)S(1)} fusion(bf16[1216,256]{1,0:T(8,128)(2,1)S(1)} %fusion.26, bf16[1216,1792]{1,0:T(8,128)(2,1)} %collective-permute-done.2, s32[]{:T(128)S(6)} %select_n.172), kind=kOutput, calls=%fused_computation.14 | convolution fusion | flops 557842432 | bytes 3719172 | tf_op jit(solution)/shard_map/dot_general | solution.py:164
  133.6 7.4 %collective-permute-done.11 = f32[2,2,32,896]{3,2,1,0:T(8,128)} collective-permute-done((f32[2,2,32,896]{3,2,1,0:T(8,128)S(1)}, f32[2,2,32,896]{3,2,1,0:T(8,128)}, u32[]{:S(2)}, u32[]{:S(2)}) %collective-permute-start.11) | collective-permute-done | bytes 458784 | tf_op jit(solution)/shard_map/ppermute | solution.py:71
  146.6 2.8 %collective-permute-done.12 = f32[2,32,896]{2,1,0:T(8,128)S(1)} collective-permute-done((f32[2,32,896]{2,1,0:T(8,128)S(1)}, f32[2,32,896]{2,1,0:T(8,128)S(1)}, u32[]{:S(2)}, u32[]{:S(2)}) %collective-permute-start.12) | collective-permute-done | bytes 229408 | tf_op jit(solution)/shard_map/ppermute | solution.py:71
  149.5 2.7 %collective-permute-start.13 = (f32[32,896]{1,0:T(8,128)S(1)}, f32[32,896]{1,0:T(8,128)S(1)}, u32[]{:S(2)}, u32[]{:S(2)}) collective-permute-start(f32[32,896]{1,0:T(8,128)S(1)} %dynamic-slice_bitcast_fusion.4), channel_id=1, source_target_pairs={{0,2},{1,3},{2,0},{3,1},{4,6},{5,7},{6,4},{7,5},{8,10},{9,11},{10,... | collective-permute-start | bytes 344072 | tf_op jit(solution)/shard_map/ppermute | solution.py:71
  152.3 3.3 %collective-permute-start.10 = (f32[32,896]{1,0:T(8,128)S(1)}, f32[32,896]{1,0:T(8,128)S(1)}, u32[]{:S(2)}, u32[]{:S(2)}) collective-permute-start(f32[32,896]{1,0:T(8,128)S(1)} %dynamic-slice_bitcast_fusion.5), channel_id=1, source_target_pairs={{0,2},{1,3},{2,0},{3,1},{4,6},{5,7},{6,4},{7,5},{8,10},{9,11},{10,... | collective-permute-start | bytes 344072 | tf_op jit(solution)/shard_map/ppermute | solution.py:71
  155.6 5.1 %collective-permute-done.13 = f32[32,896]{1,0:T(8,128)S(1)} collective-permute-done((f32[32,896]{1,0:T(8,128)S(1)}, f32[32,896]{1,0:T(8,128)S(1)}, u32[]{:S(2)}, u32[]{:S(2)}) %collective-permute-start.13) | collective-permute-done | bytes 114720 | tf_op jit(solution)/shard_map/ppermute | solution.py:71
  164.0 2.0 %collective-permute-done.19 = f32[2]{0:T(128)S(1)} collective-permute-done((f32[2]{0:T(128)S(1)}, f32[2]{0:T(128)S(1)}, u32[]{:S(2)}, u32[]{:S(2)}) %collective-permute-start.19) | collective-permute-done | bytes 40 | tf_op jit(solution)/shard_map/ppermute | solution.py:45
  169.7 2.0 %collective-permute-start.15 = (bf16[2,64,896]{2,1,0:T(8,128)(2,1)S(1)}, bf16[2,64,896]{2,1,0:T(8,128)(2,1)S(1)}, u32[]{:S(2)}, u32[]{:S(2)}) collective-permute-start(bf16[2,64,896]{2,1,0:T(8,128)(2,1)S(1)} %maximum_select_fusion.5), channel_id=1, source_target_pairs={{0,1},{1,0},{2,3},{3,2},{4,5},{5,4},{6,7},{7,6},{8,9},{9,8},{10,11... | collective-permute-start | bytes 688136 | tf_op jit(solution)/shard_map/ppermute | solution.py:82
  171.7 4.9 %collective-permute-done.15 = bf16[2,64,896]{2,1,0:T(8,128)(2,1)S(1)} collective-permute-done((bf16[2,64,896]{2,1,0:T(8,128)(2,1)S(1)}, bf16[2,64,896]{2,1,0:T(8,128)(2,1)S(1)}, u32[]{:S(2)}, u32[]{:S(2)}) %collective-permute-start.15) | collective-permute-done | bytes 229408 | tf_op jit(solution)/shard_map/ppermute | solution.py:82
  181.1 4.1 %collective-permute-done.18 = bf16[128,896]{1,0:T(8,128)(2,1)S(1)} collective-permute-done((bf16[128,896]{1,0:T(8,128)(2,1)S(1)}, bf16[128,896]{1,0:T(8,128)(2,1)S(1)}, u32[]{:S(2)}, u32[]{:S(2)}) %collective-permute-start.18) | collective-permute-done | bytes 229408 | tf_op jit(solution)/shard_map/ppermute | solution.py:241
  187.7 4.3 %add_add_fusion = f32[896,2048]{1,0:T(8,128)} fusion(f32[896,2048]{1,0:T(8,128)S(1)} %fusion.30, f32[896,2048]{1,0:T(8,128)S(1)} %fusion.35, f32[896,2048]{1,0:T(8,128)S(1)} %fusion.33, bf16[128,896]{1,0:T(8,128)(2,1)S(1)} %collective-permute-done.16, bf16[256,2048]{1,0:T(8,128)(2,1)S(1)} %collective-permute-done.17), kind=kOutput, calls=%fused_computation | convolution fusion | flops 475267072 | bytes 30113792 | tf_op jit(solution)/shard_map/dot_general | solution.py:247
  (78 shorter events, 39.6 us)
Async XLA Ops:
  0.6 97.4 %collective-permute-start.2 = (bf16[1216,1792]{1,0:T(8,128)(2,1)}, bf16[1216,1792]{1,0:T(8,128)(2,1)}, u32[]{:S(2)}, u32[]{:S(2)}) collective-permute-start(bf16[1216,1792]{1,0:T(8,128)(2,1)} %param.7), channel_id=1, source_target_pairs={{0,16},{16,0},{1,17},{17,1},{2,18},{18,2},{3,19},{19,3},{4,20},{20... | collective-permute-start | bytes 13074440 | tf_op jit(solution)/shard_map/ppermute | solution.py:11
  7.3 48.9 %copy-start.3 = (s32[256]{0:T(256)S(1)}, s32[256]{0:T(256)}, u32[]{:S(2)}) copy-start(s32[256]{0:T(256)} %param.8) | copy-start | bytes 3076
  46.4 9.5 %collective-permute-start = (bf16[256,896]{1,0:T(8,128)(2,1)S(1)}, bf16[256,896]{1,0:T(8,128)(2,1)S(1)}, u32[]{:S(2)}, u32[]{:S(2)}) collective-permute-start(bf16[256,896]{1,0:T(8,128)(2,1)S(1)} %all-reduce.1), channel_id=1, source_target_pairs={{0,8},{4,12},{8,0},{12,4},{1,9},{5,13},{9,1},{13,5},{2,10},{6,14},... | collective-permute-start | bytes 1376264 | tf_op jit(solution)/shard_map/ppermute | solution.py:82
  56.1 2.5 %collective-permute-start.1 = (bf16[2,256,896]{2,1,0:T(8,128)(2,1)S(1)}, bf16[2,256,896]{2,1,0:T(8,128)(2,1)S(1)}, u32[]{:S(2)}, u32[]{:S(2)}) collective-permute-start(bf16[2,256,896]{2,1,0:T(8,128)(2,1)S(1)} %maximum_select_fusion.2), channel_id=1, source_target_pairs={{0,4},{4,0},{8,12},{12,8},{1,5},{5,1},{9,13},{13,9},{2,6},{6,2},{1... | collective-permute-start | bytes 2752520 | tf_op jit(solution)/shard_map/ppermute | solution.py:82
  61.5 36.5 %copy-start = (bf16[256,4,896]{0,2,1:T(8,128)(2,1)S(1)}, bf16[256,4,896]{0,2,1:T(8,128)(2,1)}, u32[]{:S(2)}) copy-start(bf16[256,4,896]{0,2,1:T(8,128)(2,1)} %copy.8) | copy-start | bytes 5505028
  65.5 48.1 %copy-start.2 = (s32[256]{0:T(256)S(1)}, s32[256]{0:T(256)}, u32[]{:S(2)}) copy-start(s32[256]{0:T(256)} %param.9) | copy-start | bytes 3076
  102.0 1.2 collective-permute-start.3
  103.3 3.7 %collective-permute-start.4 = (f32[3,256]{1,0:T(4,128)S(1)}, f32[3,256]{1,0:T(4,128)S(1)}, u32[]{:S(2)}, u32[]{:S(2)}) collective-permute-start(f32[3,256]{1,0:T(4,128)S(1)} %pad_maximum_fusion.3), channel_id=1, source_target_pairs={{0,8},{4,12},{8,0},{12,4},{1,9},{5,13},{9,1},{13,5},{2,10},{6,14},... | collective-permute-start | bytes 9224 | tf_op jit(solution)/shard_map/ppermute | solution.py:33
  107.0 3.7 %collective-permute-start.5 = (f32[3,256]{1,0:T(4,128)S(1)}, f32[3,256]{1,0:T(4,128)S(1)}, u32[]{:S(2)}, u32[]{:S(2)}) collective-permute-start(f32[3,256]{1,0:T(4,128)S(1)} %pad_maximum_fusion.4), channel_id=1, source_target_pairs={{0,1},{1,0},{2,3},{3,2},{4,5},{5,4},{6,7},{7,6},{8,9},{9,8},{10,11... | collective-permute-start | bytes 9224 | tf_op jit(solution)/shard_map/ppermute | solution.py:33
  110.7 4.6 %collective-permute-start.6 = (f32[3,256]{1,0:T(4,128)S(1)}, f32[3,256]{1,0:T(4,128)S(1)}, u32[]{:S(2)}, u32[]{:S(2)}) collective-permute-start(f32[3,256]{1,0:T(4,128)S(1)} %pad_maximum_fusion.5), channel_id=1, source_target_pairs={{0,2},{1,3},{2,0},{3,1},{4,6},{5,7},{6,4},{7,5},{8,10},{9,11},{10,... | collective-permute-start | bytes 9224 | tf_op jit(solution)/shard_map/ppermute | solution.py:33
  120.8 5.1 %collective-permute-start.7 = (f32[2,256,896]{2,1,0:T(8,128)S(1)}, f32[2,256,896]{2,1,0:T(8,128)}, u32[]{:S(2)}, u32[]{:S(2)}) collective-permute-start(f32[2,256,896]{2,1,0:T(8,128)S(1)} %pad_maximum_fusion), channel_id=1, source_target_pairs={{0,4},{4,0},{8,12},{12,8},{1,5},{5,1},{9,13},{13,9},{2,6},{6,2},{1... | collective-permute-start | bytes 5505032 | tf_op jit(solution)/shard_map/ppermute | solution.py:174
  127.9 13.1 %collective-permute-start.11 = (f32[2,2,32,896]{3,2,1,0:T(8,128)S(1)}, f32[2,2,32,896]{3,2,1,0:T(8,128)}, u32[]{:S(2)}, u32[]{:S(2)}) collective-permute-start(f32[2,2,32,896]{3,2,1,0:T(8,128)S(1)} %dynamic-slice_bitcast_fusion), channel_id=1, source_target_pairs={{0,1},{1,0},{2,3},{3,2},{4,5},{5,4},{6,7},{7,6},{8,9},{9,8},{10,11... | collective-permute-start | bytes 1376264 | tf_op jit(solution)/shard_map/ppermute | solution.py:71
  130.5 13.3 %collective-permute-start.8 = (f32[2,2,32,896]{3,2,1,0:T(8,128)}, f32[2,2,32,896]{3,2,1,0:T(8,128)}, u32[]{:S(2)}, u32[]{:S(2)}) collective-permute-start(f32[2,2,32,896]{3,2,1,0:T(8,128)} %dynamic-slice_bitcast_fusion.1), channel_id=1, source_target_pairs={{0,8},{4,12},{8,0},{12,4},{1,9},{5,13},{9,1},{13,5},{2,10},{6,14},... | collective-permute-start | bytes 1376264 | tf_op jit(solution)/shard_map/ppermute | solution.py:71
  132.1 49.1 %collective-permute-start.17 = (bf16[256,2048]{1,0:T(8,128)(2,1)}, bf16[256,2048]{1,0:T(8,128)(2,1)S(1)}, u32[]{:S(2)}, u32[]{:S(2)}) collective-permute-start(bf16[256,2048]{1,0:T(8,128)(2,1)} %param.5), channel_id=1, source_target_pairs={{0,16},{16,0},{1,17},{17,1},{2,18},{18,2},{3,19},{19,3},{4,20},{20... | collective-permute-start | bytes 3145736 | tf_op jit(solution)/shard_map/ppermute | solution.py:99
  142.1 7.3 %collective-permute-start.12 = (f32[2,32,896]{2,1,0:T(8,128)S(1)}, f32[2,32,896]{2,1,0:T(8,128)S(1)}, u32[]{:S(2)}, u32[]{:S(2)}) collective-permute-start(f32[2,32,896]{2,1,0:T(8,128)S(1)} %dynamic-slice_bitcast_fusion.2), channel_id=1, source_target_pairs={{0,8},{4,12},{8,0},{12,4},{1,9},{5,13},{9,1},{13,5},{2,10},{6,14},... | collective-permute-start | bytes 688136 | tf_op jit(solution)/shard_map/ppermute | solution.py:71
  145.0 7.3 %collective-permute-start.9 = (f32[2,32,896]{2,1,0:T(8,128)S(1)}, f32[2,32,896]{2,1,0:T(8,128)S(1)}, u32[]{:S(2)}, u32[]{:S(2)}) collective-permute-start(f32[2,32,896]{2,1,0:T(8,128)S(1)} %dynamic-slice_bitcast_fusion.3), channel_id=1, source_target_pairs={{0,1},{1,0},{2,3},{3,2},{4,5},{5,4},{6,7},{7,6},{8,9},{9,8},{10,11... | collective-permute-start | bytes 688136 | tf_op jit(solution)/shard_map/ppermute | solution.py:71
  149.5 11.2 %collective-permute-start.13 = (f32[32,896]{1,0:T(8,128)S(1)}, f32[32,896]{1,0:T(8,128)S(1)}, u32[]{:S(2)}, u32[]{:S(2)}) collective-permute-start(f32[32,896]{1,0:T(8,128)S(1)} %dynamic-slice_bitcast_fusion.4), channel_id=1, source_target_pairs={{0,2},{1,3},{2,0},{3,1},{4,6},{5,7},{6,4},{7,5},{8,10},{9,11},{10,... | collective-permute-start | bytes 344072 | tf_op jit(solution)/shard_map/ppermute | solution.py:71
  152.3 9.8 %collective-permute-start.10 = (f32[32,896]{1,0:T(8,128)S(1)}, f32[32,896]{1,0:T(8,128)S(1)}, u32[]{:S(2)}, u32[]{:S(2)}) collective-permute-start(f32[32,896]{1,0:T(8,128)S(1)} %dynamic-slice_bitcast_fusion.5), channel_id=1, source_target_pairs={{0,2},{1,3},{2,0},{3,1},{4,6},{5,7},{6,4},{7,5},{8,10},{9,11},{10,... | collective-permute-start | bytes 344072 | tf_op jit(solution)/shard_map/ppermute | solution.py:71
  160.8 18.1 %copy-start.1 = (bf16[256,2048]{1,0:T(8,128)(2,1)S(1)}, bf16[256,2048]{1,0:T(8,128)(2,1)}, u32[]{:S(2)}) copy-start(bf16[256,2048]{1,0:T(8,128)(2,1)} %param.5) | copy-start | bytes 3145732
  162.2 7.5 %collective-permute-start.14 = (bf16[64,896]{1,0:T(8,128)(2,1)S(1)}, bf16[64,896]{1,0:T(8,128)(2,1)S(1)}, u32[]{:S(2)}, u32[]{:S(2)}) collective-permute-start(bf16[64,896]{1,0:T(8,128)(2,1)S(1)} %pad_maximum_fusion.1), channel_id=1, source_target_pairs={{0,2},{1,3},{2,0},{3,1},{4,6},{5,7},{6,4},{7,5},{8,10},{9,11},{10,... | collective-permute-start | bytes 344072 | tf_op jit(solution)/shard_map/ppermute | solution.py:82
  162.4 3.6 %collective-permute-start.19 = (f32[2]{0:T(128)S(1)}, f32[2]{0:T(128)S(1)}, u32[]{:S(2)}, u32[]{:S(2)}) collective-permute-start(f32[2]{0:T(128)S(1)} %convolution_bitcast_fusion), channel_id=1, source_target_pairs={{0,16},{16,0},{1,17},{17,1},{2,18},{18,2},{3,19},{19,3},{4,20},{20... | collective-permute-start | bytes 32 | tf_op jit(solution)/shard_map/ppermute | solution.py:45
  169.7 6.9 %collective-permute-start.15 = (bf16[2,64,896]{2,1,0:T(8,128)(2,1)S(1)}, bf16[2,64,896]{2,1,0:T(8,128)(2,1)S(1)}, u32[]{:S(2)}, u32[]{:S(2)}) collective-permute-start(bf16[2,64,896]{2,1,0:T(8,128)(2,1)S(1)} %maximum_select_fusion.5), channel_id=1, source_target_pairs={{0,1},{1,0},{2,3},{3,2},{4,5},{5,4},{6,7},{7,6},{8,9},{9,8},{10,11... | collective-permute-start | bytes 688136 | tf_op jit(solution)/shard_map/ppermute | solution.py:82
  176.8 8.5 %collective-permute-start.18 = (bf16[128,896]{1,0:T(8,128)(2,1)S(1)}, bf16[128,896]{1,0:T(8,128)(2,1)S(1)}, u32[]{:S(2)}, u32[]{:S(2)}) collective-permute-start(bf16[128,896]{1,0:T(8,128)(2,1)S(1)} %bitcast.116), channel_id=1, source_target_pairs={{0,16},{16,0},{1,17},{17,1},{2,18},{18,2},{3,19},{19,3},{4,20},{20... | collective-permute-start | bytes 688136 | tf_op jit(solution)/shard_map/ppermute | solution.py:241
  178.3 9.4 %collective-permute-start.16 = (bf16[128,896]{1,0:T(8,128)(2,1)S(1)}, bf16[128,896]{1,0:T(8,128)(2,1)S(1)}, u32[]{:S(2)}, u32[]{:S(2)}) collective-permute-start(bf16[128,896]{1,0:T(8,128)(2,1)S(1)} %bitcast.114), channel_id=1, source_target_pairs={{0,16},{16,0},{1,17},{17,1},{2,18},{18,2},{3,19},{19,3},{4,20},{20... | collective-permute-start | bytes 688136 | tf_op jit(solution)/shard_map/ppermute | solution.py:241

commit v18 on v15

--- a/solution.py
+++ b/solution.py
@@ -66,8 +66,9 @@
         pos = dims.index((ax, b))
         n = lax.axis_size(ax)
         bit = (lax.axis_index(ax) // b) % 2 if bits is None else bits[(ax, b)]
-        keep = lax.dynamic_index_in_dim(x, bit, axis=pos, keepdims=False)
-        send = lax.dynamic_index_in_dim(x, 1 - bit, axis=pos, keepdims=False)
+        terms = x if isinstance(x, tuple) else (x,)
+        keep = sum(lax.dynamic_index_in_dim(y, bit, axis=pos, keepdims=False) for y in terms)
+        send = sum(lax.dynamic_index_in_dim(y, 1 - bit, axis=pos, keepdims=False) for y in terms)
         x = keep + lax.ppermute(send, ax, [(k, k ^ b) for k in range(n)])
         dims.pop(pos)
     return x
@@ -168,7 +169,7 @@
 
         sent = quarter_dots(1 - c)
         received = lax.ppermute(sent, "voc", [(k, k ^ 1) for k in range(n_voc)])
-        blocks = quarter_dots(c) + received
+        kept = quarter_dots(c)
         voc_bits = bit_list("voc", n_voc)
         wid_bits = bit_list("wid", n_wid)
         v = lax.axis_index("voc")
@@ -176,11 +177,17 @@
         for key in wid_bits:
             bits[key] = (lax.axis_index("wid") // key[1]) % 2
         dims = [voc_bits[-1]] + wid_bits[::-1]
-        blocks = blocks.reshape(tuple(2 for _ in dims) + (tok_rows // n_wid, q_cols))
+        shape = tuple(2 for _ in dims) + (tok_rows // n_wid, q_cols)
+        kept = kept.reshape(shape)
+        received = received.reshape(shape)
         half = tok_rows // n_wid // 2
         rest_voc = voc_bits[1:]
-        part_a = halving_steps(blocks[..., :half, :], dims, rest_voc + wid_bits, bits)
-        part_b = halving_steps(blocks[..., half:, :], dims, wid_bits[:1] + rest_voc + wid_bits[1:], bits)
+        part_a = halving_steps(
+            (kept[..., :half, :], received[..., :half, :]), dims, rest_voc + wid_bits, bits
+        )
+        part_b = halving_steps(
+            (kept[..., half:, :], received[..., half:, :]), dims, wid_bits[:1] + rest_voc + wid_bits[1:], bits
+        )
         mine = jnp.concatenate([part_a, part_b], axis=0).astype(jnp.bfloat16)
         grad_rows_pos = doubling_gather(mine, "wid").reshape((tok_rows, q_cols))
     elif grad_path:

time: 191 us -> 190 us (level)
  no operation moved by 1% of the time
where the time goes in v18:
time: 190 us
  waiting for transfers between devices  78.2 us (41%)
  blocking collectives  39.1 us (21%)
  matrix products  30.8 us (16%)
  starting transfers between devices  27 us (14%)
  other arithmetic  7.43 us (4%)
  between operations  3.53 us (2%)
  local copies, waits for them, and re-layouts  3.43 us (2%)
    psum x1, blocking collectives, on_device(): summed = lax.psum(partial_value, 'wid')  39.1 us
    ppermute x1, waiting for transfers between devices, tok_pieces(): pieces.append(lax.ppermute(x, 'tok', perm))  32.6 us
    ppermute x4, waiting for transfers between devices, doubling_gather(): other = lax.ppermute(x, ax, [(k, k ^ b) for k in range(n)])  20.1 us
    ppermute x6, waiting for transfers between devices, halving_steps(): x = keep + lax.ppermute(send, ax, [(k, k ^ b) for k in range(n)])  18.1 us
    ppermute x6, starting transfers between devices, halving_steps(): x = keep + lax.ppermute(send, ax, [(k, k ^ b) for k in range(n)])  11.1 us
    dot_general x4, matrix products, quarter_dots(): jnp.dot(dlogits, lax.dynamic_slice_in_dim(piece, sel * q_cols, q_cols, ax...  9.94 us
    dot_general x4, matrix products, on_device(): lax.dot_general(rows[i], hid[i * half_rows:(i + 1) * half_rows], by_pos,...  9.78 us
    dot_general x2, matrix products, on_device(): lax.dot_general(piece, cols, (((1,), (1,)), ((), ())), preferred_element_...  7.46 us
  transfers between devices with their start and end apart: 20, of which 15 were waited for; matrix products, arithmetic and copies ran while one was open for 14% of the time, Pallas kernels for 0%

profile of v18, /device:TPU:0, one launch (start us, length us, event | category | flops | bytes accessed | tf_op | source)
XLA Modules:
  0.0 189.5 jit_solution(8202139551139449954)
XLA Ops:
  0.6 3.0 %collective-permute-start.2 = (bf16[1216,1792]{1,0:T(8,128)(2,1)}, bf16[1216,1792]{1,0:T(8,128)(2,1)}, u32[]{:S(2)}, u32[]{:S(2)}) collective-permute-start(bf16[1216,1792]{1,0:T(8,128)(2,1)} %param.7), channel_id=1, source_target_pairs={{0,16},{16,0},{1,17},{17,1},{2,18},{18,2},{3,19},{19,3},{4,20},{20... | collective-permute-start | bytes 13074440 | tf_op jit(solution)/shard_map/ppermute | solution.py:11
  3.6 3.6 %fusion.63 = f32[256,896]{1,0:T(8,128)S(1)} fusion(bf16[256,2048]{1,0:T(8,128)(2,1)} %param.5, bf16[896,2048]{1,0:T(8,128)(2,1)} %param.6), kind=kOutput, calls=%fused_computation.113 | convolution fusion | flops 939524096 | bytes 5636096 | tf_op jit(solution)/shard_map/dot_general | solution.py:102
  7.3 39.1 %all-reduce.1 = bf16[256,896]{1,0:T(8,128)(2,1)S(1)} all-reduce(f32[256,896]{1,0:T(8,128)S(1)} %fusion.63), channel_id=1, replica_groups=mesh['tok'=2,'voc'=4,'wid'=4] {'wid'}, use_global_device_ids=true, to_apply=%region_0.0 | all-reduce | flops 229376 | bytes 1376256 | tf_op jit(solution)/shard_map/psum | solution.py:105
  48.0 7.9 %collective-permute-done = bf16[256,896]{1,0:T(8,128)(2,1)S(1)} collective-permute-done((bf16[256,896]{1,0:T(8,128)(2,1)S(1)}, bf16[256,896]{1,0:T(8,128)(2,1)S(1)}, u32[]{:S(2)}, u32[]{:S(2)}) %collective-permute-start) | collective-permute-done | bytes 458784 | tf_op jit(solution)/shard_map/ppermute | solution.py:83
  56.4 2.2 %collective-permute-done.1 = bf16[2,256,896]{2,1,0:T(8,128)(2,1)S(1)} collective-permute-done((bf16[2,256,896]{2,1,0:T(8,128)(2,1)S(1)}, bf16[2,256,896]{2,1,0:T(8,128)(2,1)S(1)}, u32[]{:S(2)}, u32[]{:S(2)}) %collective-permute-start.1) | collective-permute-done | bytes 917536 | tf_op jit(solution)/shard_map/ppermute | solution.py:83
  59.1 2.4 %copy.11 = bf16[256,4,896]{0,2,1:T(8,128)(2,1)} copy(bf16[256,4,896]{2,0,1:T(8,128)(2,1)S(1)} %bitcast.123) | data formatting | bytes 3670016 | tf_op jit(solution)/shard_map/transpose | solution.py:108
  61.5 3.9 %fusion.23 = f32[256,1216]{0,1:T(8,128)S(1)} fusion(bf16[1216,1792]{1,0:T(8,128)(2,1)} %param.7, bf16[256,3584]{0,1:T(8,128)(2,1)} %bitcast.127, s32[]{:T(128)S(6)} %select_n.172), kind=kOutput, calls=%fused_computation.31 | convolution fusion | flops 1115684864 | bytes 6520836 | tf_op jit(solution)/shard_map/dot_general | solution.py:115
  65.5 32.6 %collective-permute-done.2 = bf16[1216,1792]{1,0:T(8,128)(2,1)} collective-permute-done((bf16[1216,1792]{1,0:T(8,128)(2,1)}, bf16[1216,1792]{1,0:T(8,128)(2,1)}, u32[]{:S(2)}, u32[]{:S(2)}) %collective-permute-start.2) | collective-permute-done | bytes 4358176 | tf_op jit(solution)/shard_map/ppermute | solution.py:11
  98.0 3.5 %fusion.62 = (f32[256]{0:T(256)S(1)}, f32[256,1216]{0,1:T(8,128)S(1)}) fusion(f32[256,1216]{0,1:T(8,128)S(1)} %fusion.23, bf16[1216,1792]{1,0:T(8,128)(2,1)} %collective-permute-done.2, bf16[256,3584]{0,1:T(8,128)(2,1)S(1)} %bitcast.128, s32[]{:T(128)S(6)} %select_n.174), kind=kOutput, calls=%fused_computation.112 | convolution fusion | flops 1116307200 | bytes 7767044 | tf_op jit(solution)/shard_map/dot_general | solution.py:115
  110.6 2.9 %collective-permute-start.6 = (f32[3,256]{1,0:T(4,128)S(1)}, f32[3,256]{1,0:T(4,128)S(1)}, u32[]{:S(2)}, u32[]{:S(2)}) collective-permute-start(f32[3,256]{1,0:T(4,128)S(1)} %pad_maximum_fusion.5), channel_id=1, source_target_pairs={{0,2},{1,3},{2,0},{3,1},{4,6},{5,7},{6,4},{7,5},{8,10},{9,11},{10,... | collective-permute-start | bytes 9224 | tf_op jit(solution)/shard_map/ppermute | solution.py:33
  116.1 2.5 %fusion.8 = f32[1,256,896]{2,1,0:T(8,128)S(1)} fusion(bf16[1216,256]{1,0:T(8,128)(2,1)S(1)} %fusion.20, bf16[1216,1792]{1,0:T(8,128)(2,1)} %param.7, s32[]{:T(128)S(6)} %select_n.178), kind=kOutput, calls=%fused_computation.14 | convolution fusion | flops 557842432 | bytes 3719172 | tf_op jit(solution)/shard_map/dot_general | solution.py:161
  118.6 2.5 %fusion.11 = f32[1,256,896]{2,1,0:T(8,128)S(1)} fusion(bf16[1216,256]{1,0:T(8,128)(2,1)S(1)} %fusion.20, bf16[1216,1792]{1,0:T(8,128)(2,1)} %collective-permute-done.2, s32[]{:T(128)S(6)} %select_n.178), kind=kOutput, calls=%fused_computation.15 | convolution fusion | flops 557842432 | bytes 3719172 | tf_op jit(solution)/shard_map/dot_general | solution.py:161
  124.2 2.5 %fusion.6 = f32[256,896]{1,0:T(8,128)S(1)} fusion(bf16[1216,256]{1,0:T(8,128)(2,1)S(1)} %fusion.20, bf16[1216,1792]{1,0:T(8,128)(2,1)} %param.7, s32[]{:T(128)S(6)} %select_n.176), kind=kOutput, calls=%fused_computation.8 | convolution fusion | flops 557842432 | bytes 3719172 | tf_op jit(solution)/shard_map/dot_general | solution.py:161
  126.7 2.5 %fusion.4 = f32[256,896]{1,0:T(8,128)S(1)} fusion(bf16[1216,256]{1,0:T(8,128)(2,1)S(1)} %fusion.20, bf16[1216,1792]{1,0:T(8,128)(2,1)} %collective-permute-done.2, s32[]{:T(128)S(6)} %select_n.176), kind=kOutput, calls=%fused_computation.6 | convolution fusion | flops 557842432 | bytes 3719172 | tf_op jit(solution)/shard_map/dot_general | solution.py:161
  135.4 6.8 %collective-permute-done.11 = f32[2,2,32,896]{3,2,1,0:T(8,128)S(1)} collective-permute-done((f32[2,2,32,896]{3,2,1,0:T(8,128)S(1)}, f32[2,2,32,896]{3,2,1,0:T(8,128)S(1)}, u32[]{:S(2)}, u32[]{:S(2)}) %collective-permute-start.11) | collective-permute-done | bytes 458784 | tf_op jit(solution)/shard_map/ppermute | solution.py:72
  145.7 3.6 %collective-permute-done.12 = f32[2,32,896]{2,1,0:T(8,128)S(1)} collective-permute-done((f32[2,32,896]{2,1,0:T(8,128)S(1)}, f32[2,32,896]{2,1,0:T(8,128)S(1)}, u32[]{:S(2)}, u32[]{:S(2)}) %collective-permute-start.12) | collective-permute-done | bytes 229408 | tf_op jit(solution)/shard_map/ppermute | solution.py:72
  149.3 2.6 %collective-permute-start.13 = (f32[32,896]{1,0:T(8,128)S(1)}, f32[32,896]{1,0:T(8,128)S(1)}, u32[]{:S(2)}, u32[]{:S(2)}) collective-permute-start(f32[32,896]{1,0:T(8,128)S(1)} %dynamic-slice_bitcast_fusion.2), channel_id=1, source_target_pairs={{0,2},{1,3},{2,0},{3,1},{4,6},{5,7},{6,4},{7,5},{8,10},{9,11},{10,... | collective-permute-start | bytes 344072 | tf_op jit(solution)/shard_map/ppermute | solution.py:72
  152.0 2.5 %collective-permute-start.10 = (f32[32,896]{1,0:T(8,128)S(1)}, f32[32,896]{1,0:T(8,128)S(1)}, u32[]{:S(2)}, u32[]{:S(2)}) collective-permute-start(f32[32,896]{1,0:T(8,128)S(1)} %dynamic-slice_bitcast_fusion.3), channel_id=1, source_target_pairs={{0,2},{1,3},{2,0},{3,1},{4,6},{5,7},{6,4},{7,5},{8,10},{9,11},{10,... | collective-permute-start | bytes 344072 | tf_op jit(solution)/shard_map/ppermute | solution.py:72
  154.5 6.0 %collective-permute-done.13 = f32[32,896]{1,0:T(8,128)S(1)} collective-permute-done((f32[32,896]{1,0:T(8,128)S(1)}, f32[32,896]{1,0:T(8,128)S(1)}, u32[]{:S(2)}, u32[]{:S(2)}) %collective-permute-start.13) | collective-permute-done | bytes 114720 | tf_op jit(solution)/shard_map/ppermute | solution.py:72
  165.2 4.0 %collective-permute-done.14 = bf16[64,896]{1,0:T(8,128)(2,1)S(1)} collective-permute-done((bf16[64,896]{1,0:T(8,128)(2,1)S(1)}, bf16[64,896]{1,0:T(8,128)(2,1)S(1)}, u32[]{:S(2)}, u32[]{:S(2)}) %collective-permute-start.14) | collective-permute-done | bytes 114720 | tf_op jit(solution)/shard_map/ppermute | solution.py:83
  169.3 5.9 %collective-permute-done.15 = bf16[2,64,896]{2,1,0:T(8,128)(2,1)S(1)} collective-permute-done((bf16[2,64,896]{2,1,0:T(8,128)(2,1)S(1)}, bf16[2,64,896]{2,1,0:T(8,128)(2,1)S(1)}, u32[]{:S(2)}, u32[]{:S(2)}) %collective-permute-start.15) | collective-permute-done | bytes 229408 | tf_op jit(solution)/shard_map/ppermute | solution.py:83
  177.5 2.2 %fusion.28 = f32[896,2048]{1,0:T(8,128)S(1)} fusion(bf16[128,896]{1,0:T(8,128)(2,1)S(1)} %bitcast.134, bf16[256,2048]{1,0:T(8,128)(2,1)} %param.5), kind=kOutput, calls=%fused_computation.40 | convolution fusion | flops 469762048 | bytes 8093696 | tf_op jit(solution)/shard_map/dot_general | solution.py:250
  179.7 2.2 %fusion.30 = f32[896,2048]{1,0:T(8,128)S(1)} fusion(bf16[128,896]{1,0:T(8,128)(2,1)S(1)} %bitcast.132, bf16[256,2048]{1,0:T(8,128)(2,1)} %param.5), kind=kOutput, calls=%fused_computation.42 | convolution fusion | flops 469762048 | bytes 8093696 | tf_op jit(solution)/shard_map/dot_general | solution.py:250
  184.1 4.3 %add_add_fusion = f32[896,2048]{1,0:T(8,128)} fusion(f32[896,2048]{1,0:T(8,128)S(1)} %fusion.25, f32[896,2048]{1,0:T(8,128)S(1)} %fusion.30, f32[896,2048]{1,0:T(8,128)S(1)} %fusion.28, bf16[128,896]{1,0:T(8,128)(2,1)S(1)} %collective-permute-done.16, bf16[256,2048]{1,0:T(8,128)(2,1)S(1)} %collective-permute-done.17), kind=kOutput, calls=%fused_computation | convolution fusion | flops 475267072 | bytes 30113792 | tf_op jit(solution)/shard_map/dot_general | solution.py:250
  (84 shorter events, 34.7 us)
Async XLA Ops:
  0.6 97.4 %collective-permute-start.2 = (bf16[1216,1792]{1,0:T(8,128)(2,1)}, bf16[1216,1792]{1,0:T(8,128)(2,1)}, u32[]{:S(2)}, u32[]{:S(2)}) collective-permute-start(bf16[1216,1792]{1,0:T(8,128)(2,1)} %param.7), channel_id=1, source_target_pairs={{0,16},{16,0},{1,17},{17,1},{2,18},{18,2},{3,19},{19,3},{4,20},{20... | collective-permute-start | bytes 13074440 | tf_op jit(solution)/shard_map/ppermute | solution.py:11
  7.3 48.9 %copy-start.6 = (s32[256]{0:T(256)S(1)}, s32[256]{0:T(256)}, u32[]{:S(2)}) copy-start(s32[256]{0:T(256)} %param.8) | copy-start | bytes 3076
  46.4 9.5 %collective-permute-start = (bf16[256,896]{1,0:T(8,128)(2,1)S(1)}, bf16[256,896]{1,0:T(8,128)(2,1)S(1)}, u32[]{:S(2)}, u32[]{:S(2)}) collective-permute-start(bf16[256,896]{1,0:T(8,128)(2,1)S(1)} %all-reduce.1), channel_id=1, source_target_pairs={{0,8},{4,12},{8,0},{12,4},{1,9},{5,13},{9,1},{13,5},{2,10},{6,14},... | collective-permute-start | bytes 1376264 | tf_op jit(solution)/shard_map/ppermute | solution.py:83
  56.1 2.5 %collective-permute-start.1 = (bf16[2,256,896]{2,1,0:T(8,128)(2,1)S(1)}, bf16[2,256,896]{2,1,0:T(8,128)(2,1)S(1)}, u32[]{:S(2)}, u32[]{:S(2)}) collective-permute-start(bf16[2,256,896]{2,1,0:T(8,128)(2,1)S(1)} %maximum_select_fusion.2), channel_id=1, source_target_pairs={{0,4},{4,0},{8,12},{12,8},{1,5},{5,1},{9,13},{13,9},{2,6},{6,2},{1... | collective-permute-start | bytes 2752520 | tf_op jit(solution)/shard_map/ppermute | solution.py:83
  61.5 36.5 %copy-start = (bf16[256,4,896]{0,2,1:T(8,128)(2,1)S(1)}, bf16[256,4,896]{0,2,1:T(8,128)(2,1)}, u32[]{:S(2)}) copy-start(bf16[256,4,896]{0,2,1:T(8,128)(2,1)} %copy.11) | copy-start | bytes 5505028
  65.5 48.1 %copy-start.4 = (s32[256]{0:T(256)S(1)}, s32[256]{0:T(256)}, u32[]{:S(2)}) copy-start(s32[256]{0:T(256)} %param.9) | copy-start | bytes 3076
  101.9 1.2 collective-permute-start.3
  103.2 3.7 %collective-permute-start.4 = (f32[3,256]{1,0:T(4,128)S(1)}, f32[3,256]{1,0:T(4,128)S(1)}, u32[]{:S(2)}, u32[]{:S(2)}) collective-permute-start(f32[3,256]{1,0:T(4,128)S(1)} %pad_maximum_fusion.3), channel_id=1, source_target_pairs={{0,8},{4,12},{8,0},{12,4},{1,9},{5,13},{9,1},{13,5},{2,10},{6,14},... | collective-permute-start | bytes 9224 | tf_op jit(solution)/shard_map/ppermute | solution.py:33
  106.9 3.7 %collective-permute-start.5 = (f32[3,256]{1,0:T(4,128)S(1)}, f32[3,256]{1,0:T(4,128)S(1)}, u32[]{:S(2)}, u32[]{:S(2)}) collective-permute-start(f32[3,256]{1,0:T(4,128)S(1)} %pad_maximum_fusion.4), channel_id=1, source_target_pairs={{0,1},{1,0},{2,3},{3,2},{4,5},{5,4},{6,7},{7,6},{8,9},{9,8},{10,11... | collective-permute-start | bytes 9224 | tf_op jit(solution)/shard_map/ppermute | solution.py:33
  110.6 4.6 %collective-permute-start.6 = (f32[3,256]{1,0:T(4,128)S(1)}, f32[3,256]{1,0:T(4,128)S(1)}, u32[]{:S(2)}, u32[]{:S(2)}) collective-permute-start(f32[3,256]{1,0:T(4,128)S(1)} %pad_maximum_fusion.5), channel_id=1, source_target_pairs={{0,2},{1,3},{2,0},{3,1},{4,6},{5,7},{6,4},{7,5},{8,10},{9,11},{10,... | collective-permute-start | bytes 9224 | tf_op jit(solution)/shard_map/ppermute | solution.py:33
  122.5 6.7 %collective-permute-start.7 = (f32[2,256,896]{2,1,0:T(8,128)}, f32[2,256,896]{2,1,0:T(8,128)S(1)}, u32[]{:S(2)}, u32[]{:S(2)}) collective-permute-start(f32[2,256,896]{2,1,0:T(8,128)} %pad_maximum_fusion), channel_id=1, source_target_pairs={{0,4},{4,0},{8,12},{12,8},{1,5},{5,1},{9,13},{13,9},{2,6},{6,2},{1... | collective-permute-start | bytes 5505032 | tf_op jit(solution)/shard_map/ppermute | solution.py:171
  122.5 59.4 %collective-permute-start.17 = (bf16[256,2048]{1,0:T(8,128)(2,1)}, bf16[256,2048]{1,0:T(8,128)(2,1)S(1)}, u32[]{:S(2)}, u32[]{:S(2)}) collective-permute-start(bf16[256,2048]{1,0:T(8,128)(2,1)} %param.5), channel_id=1, source_target_pairs={{0,16},{16,0},{1,17},{17,1},{2,18},{18,2},{3,19},{19,3},{4,20},{20... | collective-permute-start | bytes 3145736 | tf_op jit(solution)/shard_map/ppermute | solution.py:100
  129.3 1.8 copy-start.1
  129.5 12.7 %collective-permute-start.11 = (f32[2,2,32,896]{3,2,1,0:T(8,128)S(1)}, f32[2,2,32,896]{3,2,1,0:T(8,128)S(1)}, u32[]{:S(2)}, u32[]{:S(2)}) collective-permute-start(f32[2,2,32,896]{3,2,1,0:T(8,128)S(1)} %fusion.34), channel_id=1, source_target_pairs={{0,1},{1,0},{2,3},{3,2},{4,5},{5,4},{6,7},{7,6},{8,9},{9,8},{10,11... | collective-permute-start | bytes 1376264 | tf_op jit(solution)/shard_map/ppermute | solution.py:72
  131.9 12.4 %collective-permute-start.8 = (f32[2,2,32,896]{3,2,1,0:T(8,128)S(1)}, f32[2,2,32,896]{3,2,1,0:T(8,128)S(1)}, u32[]{:S(2)}, u32[]{:S(2)}) collective-permute-start(f32[2,2,32,896]{3,2,1,0:T(8,128)S(1)} %add_bitcast_fusion), channel_id=1, source_target_pairs={{0,8},{4,12},{8,0},{12,4},{1,9},{5,13},{9,1},{13,5},{2,10},{6,14},... | collective-permute-start | bytes 1376264 | tf_op jit(solution)/shard_map/ppermute | solution.py:72
  134.8 27.0 %collective-permute-start.19 = (f32[2]{0:T(128)S(1)}, f32[2]{0:T(128)S(1)}, u32[]{:S(2)}, u32[]{:S(2)}) collective-permute-start(f32[2]{0:T(128)S(1)} %pad_maximum_fusion.6), channel_id=1, source_target_pairs={{0,16},{16,0},{1,17},{17,1},{2,18},{18,2},{3,19},{19,3},{4,20},{20... | collective-permute-start | bytes 32 | tf_op jit(solution)/shard_map/ppermute | solution.py:45
  142.3 7.0 %collective-permute-start.12 = (f32[2,32,896]{2,1,0:T(8,128)S(1)}, f32[2,32,896]{2,1,0:T(8,128)S(1)}, u32[]{:S(2)}, u32[]{:S(2)}) collective-permute-start(f32[2,32,896]{2,1,0:T(8,128)S(1)} %dynamic-slice_bitcast_fusion), channel_id=1, source_target_pairs={{0,8},{4,12},{8,0},{12,4},{1,9},{5,13},{9,1},{13,5},{2,10},{6,14},... | collective-permute-start | bytes 688136 | tf_op jit(solution)/shard_map/ppermute | solution.py:72
  144.5 7.5 %collective-permute-start.9 = (f32[2,32,896]{2,1,0:T(8,128)S(1)}, f32[2,32,896]{2,1,0:T(8,128)S(1)}, u32[]{:S(2)}, u32[]{:S(2)}) collective-permute-start(f32[2,32,896]{2,1,0:T(8,128)S(1)} %dynamic-slice_bitcast_fusion.1), channel_id=1, source_target_pairs={{0,1},{1,0},{2,3},{3,2},{4,5},{5,4},{6,7},{7,6},{8,9},{9,8},{10,11... | collective-permute-start | bytes 688136 | tf_op jit(solution)/shard_map/ppermute | solution.py:72
  149.3 11.2 %collective-permute-start.13 = (f32[32,896]{1,0:T(8,128)S(1)}, f32[32,896]{1,0:T(8,128)S(1)}, u32[]{:S(2)}, u32[]{:S(2)}) collective-permute-start(f32[32,896]{1,0:T(8,128)S(1)} %dynamic-slice_bitcast_fusion.2), channel_id=1, source_target_pairs={{0,2},{1,3},{2,0},{3,1},{4,6},{5,7},{6,4},{7,5},{8,10},{9,11},{10,... | collective-permute-start | bytes 344072 | tf_op jit(solution)/shard_map/ppermute | solution.py:72
  152.0 9.7 %collective-permute-start.10 = (f32[32,896]{1,0:T(8,128)S(1)}, f32[32,896]{1,0:T(8,128)S(1)}, u32[]{:S(2)}, u32[]{:S(2)}) collective-permute-start(f32[32,896]{1,0:T(8,128)S(1)} %dynamic-slice_bitcast_fusion.3), channel_id=1, source_target_pairs={{0,2},{1,3},{2,0},{3,1},{4,6},{5,7},{6,4},{7,5},{8,10},{9,11},{10,... | collective-permute-start | bytes 344072 | tf_op jit(solution)/shard_map/ppermute | solution.py:72
  161.8 7.4 %collective-permute-start.14 = (bf16[64,896]{1,0:T(8,128)(2,1)S(1)}, bf16[64,896]{1,0:T(8,128)(2,1)S(1)}, u32[]{:S(2)}, u32[]{:S(2)}) collective-permute-start(bf16[64,896]{1,0:T(8,128)(2,1)S(1)} %pad_maximum_fusion.1), channel_id=1, source_target_pairs={{0,2},{1,3},{2,0},{3,1},{4,6},{5,7},{6,4},{7,5},{8,10},{9,11},{10,... | collective-permute-start | bytes 344072 | tf_op jit(solution)/shard_map/ppermute | solution.py:83
  169.2 6.1 %collective-permute-start.15 = (bf16[2,64,896]{2,1,0:T(8,128)(2,1)S(1)}, bf16[2,64,896]{2,1,0:T(8,128)(2,1)S(1)}, u32[]{:S(2)}, u32[]{:S(2)}) collective-permute-start(bf16[2,64,896]{2,1,0:T(8,128)(2,1)S(1)} %maximum_select_fusion.5), channel_id=1, source_target_pairs={{0,1},{1,0},{2,3},{3,2},{4,5},{5,4},{6,7},{7,6},{8,9},{9,8},{10,11... | collective-permute-start | bytes 688136 | tf_op jit(solution)/shard_map/ppermute | solution.py:83
  175.4 6.5 %collective-permute-start.18 = (bf16[128,896]{1,0:T(8,128)(2,1)S(1)}, bf16[128,896]{1,0:T(8,128)(2,1)S(1)}, u32[]{:S(2)}, u32[]{:S(2)}) collective-permute-start(bf16[128,896]{1,0:T(8,128)(2,1)S(1)} %bitcast.133), channel_id=1, source_target_pairs={{0,16},{16,0},{1,17},{17,1},{2,18},{18,2},{3,19},{19,3},{4,20},{20... | collective-permute-start | bytes 688136 | tf_op jit(solution)/shard_map/ppermute | solution.py:244
  176.0 8.1 %collective-permute-start.16 = (bf16[128,896]{1,0:T(8,128)(2,1)S(1)}, bf16[128,896]{1,0:T(8,128)(2,1)S(1)}, u32[]{:S(2)}, u32[]{:S(2)}) collective-permute-start(bf16[128,896]{1,0:T(8,128)(2,1)S(1)} %bitcast.131), channel_id=1, source_target_pairs={{0,16},{16,0},{1,17},{17,1},{2,18},{18,2},{3,19},{19,3},{4,20},{20... | collective-permute-start | bytes 688136 | tf_op jit(solution)/shard_map/ppermute | solution.py:244
  (3 other events, 5.2 us)

commit v19 on v18

--- a/solution.py
+++ b/solution.py
@@ -250,7 +250,10 @@
                 lax.dot_general(rows[i], hid[i * half_rows : (i + 1) * half_rows], by_pos, preferred_element_type=jnp.float32)
                 for i in range(2)
             ]
-            sums_of.append(dots[0] + dots[1])
+            tok_sum = dots[0] + dots[1]
+            if not sums_of:
+                tok_sum = lax.optimization_barrier(tok_sum)
+            sums_of.append(tok_sum)
         grad_proj = sums_of[0] + sums_of[1]
     elif n_tok == 2:
         grad_other = lax.ppermute(grad_rows_t, "tok", [(0, 1), (1, 0)])

time: 190 us -> 196 us (1.032)
  local copies, waits for them, and re-layouts: 3.43 us -> 6.16 us
  matrix products: 30.8 us -> 33 us
    slice x1, local copies, waits for them, and re-layouts: 0.13 us -> 2.87 us  [on_device(): received[..., :half, :]]
    dot_general x4, matrix products: 9.78 us -> 11.8 us  [on_device(): lax.dot_general(rows[i], hid[i * half_rows:(i + 1) * half_rows], by_pos,...]
  transfers between devices with their start and end apart: 20 -> 20, of which waited for: 15 -> 15; matrix products, arithmetic and copies ran while one was open for 14% -> 15% of each run, Pallas kernels for 0% -> 0%
where the time goes in v19:
time: 196 us; the launch traced here: 195 us
  waiting for transfers between devices  78.7 us (40%)
  blocking collectives  39.1 us (20%)
  matrix products  33 us (17%)
  starting transfers between devices  25.6 us (13%)
  other arithmetic  8.99 us (5%)
  local copies, waits for them, and re-layouts  6.16 us (3%)
  between operations  3.52 us (2%)
    psum x1, blocking collectives, on_device(): summed = lax.psum(partial_value, 'wid')  39.1 us
    ppermute x1, waiting for transfers between devices, tok_pieces(): pieces.append(lax.ppermute(x, 'tok', perm))  32.5 us
    ppermute x4, waiting for transfers between devices, doubling_gather(): other = lax.ppermute(x, ax, [(k, k ^ b) for k in range(n)])  20.8 us
    ppermute x6, waiting for transfers between devices, halving_steps(): x = keep + lax.ppermute(send, ax, [(k, k ^ b) for k in range(n)])  18.9 us
    dot_general x4, matrix products, on_device(): lax.dot_general(rows[i], hid[i * half_rows:(i + 1) * half_rows], by_pos,...  11.8 us
    dot_general x4, matrix products, quarter_dots(): jnp.dot(dlogits, lax.dynamic_slice_in_dim(piece, sel * q_cols, q_cols, ax...  9.98 us
    ppermute x6, starting transfers between devices, halving_steps(): x = keep + lax.ppermute(send, ax, [(k, k ^ b) for k in range(n)])  9.97 us
    dot_general x2, matrix products, on_device(): lax.dot_general(piece, cols, (((1,), (1,)), ((), ())), preferred_element_...  7.57 us
  transfers between devices with their start and end apart: 20, of which 15 were waited for; matrix products, arithmetic and copies ran while one was open for 15% of the time, Pallas kernels for 0%

profile of v19, /device:TPU:0, one launch (start us, length us, event | category | flops | bytes accessed | tf_op | source)
XLA Modules:
  0.0 195.1 jit_solution(1544634481064101689)
XLA Ops:
  0.6 3.0 %collective-permute-start.2 = (bf16[1216,1792]{1,0:T(8,128)(2,1)}, bf16[1216,1792]{1,0:T(8,128)(2,1)}, u32[]{:S(2)}, u32[]{:S(2)}) collective-permute-start(bf16[1216,1792]{1,0:T(8,128)(2,1)} %param.7), channel_id=1, source_target_pairs={{0,16},{16,0},{1,17},{17,1},{2,18},{18,2},{3,19},{19,3},{4,20},{20... | collective-permute-start | bytes 13074440 | tf_op jit(solution)/shard_map/ppermute | solution.py:11
  3.6 3.6 %fusion.62 = f32[256,896]{1,0:T(8,128)S(1)} fusion(bf16[256,2048]{1,0:T(8,128)(2,1)} %param.5, bf16[896,2048]{1,0:T(8,128)(2,1)} %param.6), kind=kOutput, calls=%fused_computation.113 | convolution fusion | flops 939524096 | bytes 5636096 | tf_op jit(solution)/shard_map/dot_general | solution.py:102
  7.3 39.1 %all-reduce.1 = bf16[256,896]{1,0:T(8,128)(2,1)S(1)} all-reduce(f32[256,896]{1,0:T(8,128)S(1)} %fusion.62), channel_id=1, replica_groups=mesh['tok'=2,'voc'=4,'wid'=4] {'wid'}, use_global_device_ids=true, to_apply=%region_0.0 | all-reduce | flops 229376 | bytes 1376256 | tf_op jit(solution)/shard_map/psum | solution.py:105
  48.0 7.9 %collective-permute-done = bf16[256,896]{1,0:T(8,128)(2,1)S(1)} collective-permute-done((bf16[256,896]{1,0:T(8,128)(2,1)S(1)}, bf16[256,896]{1,0:T(8,128)(2,1)S(1)}, u32[]{:S(2)}, u32[]{:S(2)}) %collective-permute-start) | collective-permute-done | bytes 458784 | tf_op jit(solution)/shard_map/ppermute | solution.py:83
  56.4 2.2 %collective-permute-done.1 = bf16[2,256,896]{2,1,0:T(8,128)(2,1)S(1)} collective-permute-done((bf16[2,256,896]{2,1,0:T(8,128)(2,1)S(1)}, bf16[2,256,896]{2,1,0:T(8,128)(2,1)S(1)}, u32[]{:S(2)}, u32[]{:S(2)}) %collective-permute-start.1) | collective-permute-done | bytes 917536 | tf_op jit(solution)/shard_map/ppermute | solution.py:83
  59.1 2.4 %copy.11 = bf16[256,4,896]{0,2,1:T(8,128)(2,1)} copy(bf16[256,4,896]{2,0,1:T(8,128)(2,1)S(1)} %bitcast.123) | data formatting | bytes 3670016 | tf_op jit(solution)/shard_map/transpose | solution.py:108
  61.5 4.0 %fusion.23 = f32[256,1216]{0,1:T(8,128)S(1)} fusion(bf16[1216,1792]{1,0:T(8,128)(2,1)} %param.7, bf16[256,3584]{0,1:T(8,128)(2,1)} %bitcast.126, s32[]{:T(128)S(6)} %select_n.172), kind=kOutput, calls=%fused_computation.32 | convolution fusion | flops 1115684864 | bytes 6520836 | tf_op jit(solution)/shard_map/dot_general | solution.py:115
  65.5 32.5 %collective-permute-done.2 = bf16[1216,1792]{1,0:T(8,128)(2,1)} collective-permute-done((bf16[1216,1792]{1,0:T(8,128)(2,1)}, bf16[1216,1792]{1,0:T(8,128)(2,1)}, u32[]{:S(2)}, u32[]{:S(2)}) %collective-permute-start.2) | collective-permute-done | bytes 4358176 | tf_op jit(solution)/shard_map/ppermute | solution.py:11
  98.0 3.6 %fusion.61 = (f32[256]{0:T(256)S(1)}, f32[256,1216]{0,1:T(8,128)S(1)}) fusion(f32[256,1216]{0,1:T(8,128)S(1)} %fusion.23, bf16[1216,1792]{1,0:T(8,128)(2,1)} %collective-permute-done.2, bf16[256,3584]{0,1:T(8,128)(2,1)S(1)} %bitcast.127, s32[]{:T(128)S(6)} %select_n.174), kind=kOutput, calls=%fused_computation.112 | convolution fusion | flops 1116307200 | bytes 7767044 | tf_op jit(solution)/shard_map/dot_general | solution.py:115
  110.7 2.9 %collective-permute-start.6 = (f32[3,256]{1,0:T(4,128)S(1)}, f32[3,256]{1,0:T(4,128)S(1)}, u32[]{:S(2)}, u32[]{:S(2)}) collective-permute-start(f32[3,256]{1,0:T(4,128)S(1)} %pad_maximum_fusion.5), channel_id=1, source_target_pairs={{0,2},{1,3},{2,0},{3,1},{4,6},{5,7},{6,4},{7,5},{8,10},{9,11},{10,... | collective-permute-start | bytes 9224 | tf_op jit(solution)/shard_map/ppermute | solution.py:33
  115.6 2.5 %fusion.8 = f32[1,256,896]{2,1,0:T(8,128)S(1)} fusion(bf16[1216,256]{1,0:T(8,128)(2,1)S(1)} %fusion.20, bf16[1216,1792]{1,0:T(8,128)(2,1)} %param.7, s32[]{:T(128)S(6)} %select_n.178), kind=kOutput, calls=%fused_computation.15 | convolution fusion | flops 557842432 | bytes 3719172 | tf_op jit(solution)/shard_map/dot_general | solution.py:161
  118.1 2.5 %fusion.11 = f32[1,256,896]{2,1,0:T(8,128)S(1)} fusion(bf16[1216,256]{1,0:T(8,128)(2,1)S(1)} %fusion.20, bf16[1216,1792]{1,0:T(8,128)(2,1)} %collective-permute-done.2, s32[]{:T(128)S(6)} %select_n.178), kind=kOutput, calls=%fused_computation.16 | convolution fusion | flops 557842432 | bytes 3719172 | tf_op jit(solution)/shard_map/dot_general | solution.py:161
  122.0 2.5 %fusion.6 = f32[256,896]{1,0:T(8,128)S(1)} fusion(bf16[1216,256]{1,0:T(8,128)(2,1)S(1)} %fusion.20, bf16[1216,1792]{1,0:T(8,128)(2,1)} %param.7, s32[]{:T(128)S(6)} %select_n.176), kind=kOutput, calls=%fused_computation.9 | convolution fusion | flops 557842432 | bytes 3719172 | tf_op jit(solution)/shard_map/dot_general | solution.py:161
  124.5 2.5 %fusion.4 = f32[256,896]{1,0:T(8,128)S(1)} fusion(bf16[1216,256]{1,0:T(8,128)(2,1)S(1)} %fusion.20, bf16[1216,1792]{1,0:T(8,128)(2,1)} %collective-permute-done.2, s32[]{:T(128)S(6)} %select_n.176), kind=kOutput, calls=%fused_computation.7 | convolution fusion | flops 557842432 | bytes 3719172 | tf_op jit(solution)/shard_map/dot_general | solution.py:161
  127.1 2.9 %fusion.57 = (f32[2,2,2,32,896]{4,3,2,1,0:T(8,128)S(1)}, f32[2,2,2,32,896]{4,3,2,1,0:T(8,128)}) fusion(f32[2,2,2,64,896]{4,3,2,1,0:T(8,128)} %bitcast.17), kind=kLoop, calls=%fused_computation.108 | loop fusion | bytes 3670016 | tf_op jit(solution)/shard_map/slice | solution.py:186
  138.7 4.4 %collective-permute-done.8 = f32[2,2,32,896]{3,2,1,0:T(8,128)} collective-permute-done((f32[2,2,32,896]{3,2,1,0:T(8,128)S(1)}, f32[2,2,32,896]{3,2,1,0:T(8,128)}, u32[]{:S(2)}, u32[]{:S(2)}) %collective-permute-start.8) | collective-permute-done | bytes 458784 | tf_op jit(solution)/shard_map/ppermute | solution.py:72
  146.1 2.2 %collective-permute-done.11 = f32[2,2,32,896]{3,2,1,0:T(8,128)S(1)} collective-permute-done((f32[2,2,32,896]{3,2,1,0:T(8,128)S(1)}, f32[2,2,32,896]{3,2,1,0:T(8,128)S(1)}, u32[]{:S(2)}, u32[]{:S(2)}) %collective-permute-start.11) | collective-permute-done | bytes 458784 | tf_op jit(solution)/shard_map/ppermute | solution.py:72
  148.6 3.9 %collective-permute-done.9 = f32[2,32,896]{2,1,0:T(8,128)S(1)} collective-permute-done((f32[2,32,896]{2,1,0:T(8,128)S(1)}, f32[2,32,896]{2,1,0:T(8,128)S(1)}, u32[]{:S(2)}, u32[]{:S(2)}) %collective-permute-start.9) | collective-permute-done | bytes 229408 | tf_op jit(solution)/shard_map/ppermute | solution.py:72
  152.5 2.7 %collective-permute-start.10 = (f32[32,896]{1,0:T(8,128)S(1)}, f32[32,896]{1,0:T(8,128)S(1)}, u32[]{:S(2)}, u32[]{:S(2)}) collective-permute-start(f32[32,896]{1,0:T(8,128)S(1)} %dynamic-slice_bitcast_fusion.3), channel_id=1, source_target_pairs={{0,2},{1,3},{2,0},{3,1},{4,6},{5,7},{6,4},{7,5},{8,10},{9,11},{10,... | collective-permute-start | bytes 344072 | tf_op jit(solution)/shard_map/ppermute | solution.py:72
  157.2 7.0 %collective-permute-done.10 = f32[32,896]{1,0:T(8,128)S(1)} collective-permute-done((f32[32,896]{1,0:T(8,128)S(1)}, f32[32,896]{1,0:T(8,128)S(1)}, u32[]{:S(2)}, u32[]{:S(2)}) %collective-permute-start.10) | collective-permute-done | bytes 114720 | tf_op jit(solution)/shard_map/ppermute | solution.py:72
  168.9 4.7 %collective-permute-done.14 = bf16[64,896]{1,0:T(8,128)(2,1)S(1)} collective-permute-done((bf16[64,896]{1,0:T(8,128)(2,1)S(1)}, bf16[64,896]{1,0:T(8,128)(2,1)S(1)}, u32[]{:S(2)}, u32[]{:S(2)}) %collective-permute-start.14) | collective-permute-done | bytes 114720 | tf_op jit(solution)/shard_map/ppermute | solution.py:83
  173.9 5.9 %collective-permute-done.15 = bf16[2,64,896]{2,1,0:T(8,128)(2,1)S(1)} collective-permute-done((bf16[2,64,896]{2,1,0:T(8,128)(2,1)S(1)}, bf16[2,64,896]{2,1,0:T(8,128)(2,1)S(1)}, u32[]{:S(2)}, u32[]{:S(2)}) %collective-permute-start.15) | collective-permute-done | bytes 229408 | tf_op jit(solution)/shard_map/ppermute | solution.py:83
  184.2 2.2 %convolution_add_fusion = f32[896,2048]{1,0:T(8,128)S(1)} fusion(f32[896,2048]{1,0:T(8,128)S(1)} %fusion.29, bf16[128,896]{1,0:T(8,128)(2,1)S(1)} %bitcast.133, bf16[256,2048]{1,0:T(8,128)(2,1)} %param.5), kind=kOutput, calls=%fused_computation.1 | convolution fusion | flops 471597056 | bytes 15433728 | tf_op jit(solution)/shard_map/dot_general | solution.py:250
  188.7 5.3 %add_add_fusion = f32[896,2048]{1,0:T(8,128)} fusion(f32[896,2048]{1,0:T(8,128)S(1)} %convolution_add_fusion, f32[896,2048]{1,0:T(8,128)S(1)} %fusion.25, bf16[128,896]{1,0:T(8,128)(2,1)S(1)} %collective-permute-done.16, bf16[256,2048]{1,0:T(8,128)(2,1)} %collective-permute-done.17), kind=kOutput, calls=%fused_computation | convolution fusion | flops 473432064 | bytes 22773760 | tf_op jit(solution)/shard_map/dot_general | solution.py:250
  (82 shorter events, 39.0 us)
Async XLA Ops:
  0.6 97.4 %collective-permute-start.2 = (bf16[1216,1792]{1,0:T(8,128)(2,1)}, bf16[1216,1792]{1,0:T(8,128)(2,1)}, u32[]{:S(2)}, u32[]{:S(2)}) collective-permute-start(bf16[1216,1792]{1,0:T(8,128)(2,1)} %param.7), channel_id=1, source_target_pairs={{0,16},{16,0},{1,17},{17,1},{2,18},{18,2},{3,19},{19,3},{4,20},{20... | collective-permute-start | bytes 13074440 | tf_op jit(solution)/shard_map/ppermute | solution.py:11
  7.3 48.9 %copy-start.5 = (s32[256]{0:T(256)S(1)}, s32[256]{0:T(256)}, u32[]{:S(2)}) copy-start(s32[256]{0:T(256)} %param.8) | copy-start | bytes 3076
  46.4 9.5 %collective-permute-start = (bf16[256,896]{1,0:T(8,128)(2,1)S(1)}, bf16[256,896]{1,0:T(8,128)(2,1)S(1)}, u32[]{:S(2)}, u32[]{:S(2)}) collective-permute-start(bf16[256,896]{1,0:T(8,128)(2,1)S(1)} %all-reduce.1), channel_id=1, source_target_pairs={{0,8},{4,12},{8,0},{12,4},{1,9},{5,13},{9,1},{13,5},{2,10},{6,14},... | collective-permute-start | bytes 1376264 | tf_op jit(solution)/shard_map/ppermute | solution.py:83
  56.1 2.5 %collective-permute-start.1 = (bf16[2,256,896]{2,1,0:T(8,128)(2,1)S(1)}, bf16[2,256,896]{2,1,0:T(8,128)(2,1)S(1)}, u32[]{:S(2)}, u32[]{:S(2)}) collective-permute-start(bf16[2,256,896]{2,1,0:T(8,128)(2,1)S(1)} %maximum_select_fusion.2), channel_id=1, source_target_pairs={{0,4},{4,0},{8,12},{12,8},{1,5},{5,1},{9,13},{13,9},{2,6},{6,2},{1... | collective-permute-start | bytes 2752520 | tf_op jit(solution)/shard_map/ppermute | solution.py:83
  61.5 36.5 %copy-start.3 = (bf16[256,4,896]{0,2,1:T(8,128)(2,1)S(1)}, bf16[256,4,896]{0,2,1:T(8,128)(2,1)}, u32[]{:S(2)}) copy-start(bf16[256,4,896]{0,2,1:T(8,128)(2,1)} %copy.11) | copy-start | bytes 5505028
  65.5 48.1 %copy-start.4 = (s32[256]{0:T(256)S(1)}, s32[256]{0:T(256)}, u32[]{:S(2)}) copy-start(s32[256]{0:T(256)} %param.9) | copy-start | bytes 3076
  102.0 1.2 collective-permute-start.3
  103.3 3.7 %collective-permute-start.4 = (f32[3,256]{1,0:T(4,128)S(1)}, f32[3,256]{1,0:T(4,128)S(1)}, u32[]{:S(2)}, u32[]{:S(2)}) collective-permute-start(f32[3,256]{1,0:T(4,128)S(1)} %pad_maximum_fusion.3), channel_id=1, source_target_pairs={{0,8},{4,12},{8,0},{12,4},{1,9},{5,13},{9,1},{13,5},{2,10},{6,14},... | collective-permute-start | bytes 9224 | tf_op jit(solution)/shard_map/ppermute | solution.py:33
  107.0 3.7 %collective-permute-start.5 = (f32[3,256]{1,0:T(4,128)S(1)}, f32[3,256]{1,0:T(4,128)S(1)}, u32[]{:S(2)}, u32[]{:S(2)}) collective-permute-start(f32[3,256]{1,0:T(4,128)S(1)} %pad_maximum_fusion.4), channel_id=1, source_target_pairs={{0,1},{1,0},{2,3},{3,2},{4,5},{5,4},{6,7},{7,6},{8,9},{9,8},{10,11... | collective-permute-start | bytes 9224 | tf_op jit(solution)/shard_map/ppermute | solution.py:33
  110.7 4.6 %collective-permute-start.6 = (f32[3,256]{1,0:T(4,128)S(1)}, f32[3,256]{1,0:T(4,128)S(1)}, u32[]{:S(2)}, u32[]{:S(2)}) collective-permute-start(f32[3,256]{1,0:T(4,128)S(1)} %pad_maximum_fusion.5), channel_id=1, source_target_pairs={{0,2},{1,3},{2,0},{3,1},{4,6},{5,7},{6,4},{7,5},{8,10},{9,11},{10,... | collective-permute-start | bytes 9224 | tf_op jit(solution)/shard_map/ppermute | solution.py:33
  122.0 5.1 %collective-permute-start.7 = (f32[2,256,896]{2,1,0:T(8,128)}, f32[2,256,896]{2,1,0:T(8,128)}, u32[]{:S(2)}, u32[]{:S(2)}) collective-permute-start(f32[2,256,896]{2,1,0:T(8,128)} %pad_maximum_fusion), channel_id=1, source_target_pairs={{0,4},{4,0},{8,12},{12,8},{1,5},{5,1},{9,13},{13,9},{2,6},{6,2},{1... | collective-permute-start | bytes 5505032 | tf_op jit(solution)/shard_map/ppermute | solution.py:171
  130.0 13.1 %collective-permute-start.8 = (f32[2,2,32,896]{3,2,1,0:T(8,128)S(1)}, f32[2,2,32,896]{3,2,1,0:T(8,128)}, u32[]{:S(2)}, u32[]{:S(2)}) collective-permute-start(f32[2,2,32,896]{3,2,1,0:T(8,128)S(1)} %add_bitcast_fusion), channel_id=1, source_target_pairs={{0,8},{4,12},{8,0},{12,4},{1,9},{5,13},{9,1},{13,5},{2,10},{6,14},... | collective-permute-start | bytes 1376264 | tf_op jit(solution)/shard_map/ppermute | solution.py:72
  131.8 54.6 %collective-permute-start.17 = (bf16[256,2048]{1,0:T(8,128)(2,1)}, bf16[256,2048]{1,0:T(8,128)(2,1)}, u32[]{:S(2)}, u32[]{:S(2)}) collective-permute-start(bf16[256,2048]{1,0:T(8,128)(2,1)} %param.5), channel_id=1, source_target_pairs={{0,16},{16,0},{1,17},{17,1},{2,18},{18,2},{3,19},{19,3},{4,20},{20... | collective-permute-start | bytes 3145736 | tf_op jit(solution)/shard_map/ppermute | solution.py:100
  135.1 13.2 %copy-start = (f32[2,2,2,32,896]{4,3,2,1,0:T(8,128)S(1)}, f32[2,2,2,32,896]{4,3,2,1,0:T(8,128)}, u32[]{:S(2)}) copy-start(f32[2,2,2,32,896]{4,3,2,1,0:T(8,128)} %get-tuple-element.13) | copy-start | bytes 2752516
  135.1 13.2 %collective-permute-start.11 = (f32[2,2,32,896]{3,2,1,0:T(8,128)S(1)}, f32[2,2,32,896]{3,2,1,0:T(8,128)S(1)}, u32[]{:S(2)}, u32[]{:S(2)}) collective-permute-start(f32[2,2,32,896]{3,2,1,0:T(8,128)S(1)} %fusion.33), channel_id=1, source_target_pairs={{0,1},{1,0},{2,3},{3,2},{4,5},{5,4},{6,7},{7,6},{8,9},{9,8},{10,11... | collective-permute-start | bytes 1376264 | tf_op jit(solution)/shard_map/ppermute | solution.py:72
  138.2 27.4 %collective-permute-start.19 = (f32[2]{0:T(128)S(1)}, f32[2]{0:T(128)S(1)}, u32[]{:S(2)}, u32[]{:S(2)}) collective-permute-start(f32[2]{0:T(128)S(1)} %pad_maximum_fusion.6), channel_id=1, source_target_pairs={{0,16},{16,0},{1,17},{17,1},{2,18},{18,2},{3,19},{19,3},{4,20},{20... | collective-permute-start | bytes 32 | tf_op jit(solution)/shard_map/ppermute | solution.py:45
  144.3 8.2 %collective-permute-start.9 = (f32[2,32,896]{2,1,0:T(8,128)S(1)}, f32[2,32,896]{2,1,0:T(8,128)S(1)}, u32[]{:S(2)}, u32[]{:S(2)}) collective-permute-start(f32[2,32,896]{2,1,0:T(8,128)S(1)} %dynamic-slice_bitcast_fusion.1), channel_id=1, source_target_pairs={{0,1},{1,0},{2,3},{3,2},{4,5},{5,4},{6,7},{7,6},{8,9},{9,8},{10,11... | collective-permute-start | bytes 688136 | tf_op jit(solution)/shard_map/ppermute | solution.py:72
  148.5 6.7 %collective-permute-start.12 = (f32[2,32,896]{2,1,0:T(8,128)S(1)}, f32[2,32,896]{2,1,0:T(8,128)S(1)}, u32[]{:S(2)}, u32[]{:S(2)}) collective-permute-start(f32[2,32,896]{2,1,0:T(8,128)S(1)} %dynamic-slice_bitcast_fusion), channel_id=1, source_target_pairs={{0,8},{4,12},{8,0},{12,4},{1,9},{5,13},{9,1},{13,5},{2,10},{6,14},... | collective-permute-start | bytes 688136 | tf_op jit(solution)/shard_map/ppermute | solution.py:72
  152.5 11.7 %collective-permute-start.10 = (f32[32,896]{1,0:T(8,128)S(1)}, f32[32,896]{1,0:T(8,128)S(1)}, u32[]{:S(2)}, u32[]{:S(2)}) collective-permute-start(f32[32,896]{1,0:T(8,128)S(1)} %dynamic-slice_bitcast_fusion.3), channel_id=1, source_target_pairs={{0,2},{1,3},{2,0},{3,1},{4,6},{5,7},{6,4},{7,5},{8,10},{9,11},{10,... | collective-permute-start | bytes 344072 | tf_op jit(solution)/shard_map/ppermute | solution.py:72
  155.3 10.2 %collective-permute-start.13 = (f32[32,896]{1,0:T(8,128)S(1)}, f32[32,896]{1,0:T(8,128)S(1)}, u32[]{:S(2)}, u32[]{:S(2)}) collective-permute-start(f32[32,896]{1,0:T(8,128)S(1)} %dynamic-slice_bitcast_fusion.2), channel_id=1, source_target_pairs={{0,2},{1,3},{2,0},{3,1},{4,6},{5,7},{6,4},{7,5},{8,10},{9,11},{10,... | collective-permute-start | bytes 344072 | tf_op jit(solution)/shard_map/ppermute | solution.py:72
  165.5 8.2 %collective-permute-start.14 = (bf16[64,896]{1,0:T(8,128)(2,1)S(1)}, bf16[64,896]{1,0:T(8,128)(2,1)S(1)}, u32[]{:S(2)}, u32[]{:S(2)}) collective-permute-start(bf16[64,896]{1,0:T(8,128)(2,1)S(1)} %pad_maximum_fusion.1), channel_id=1, source_target_pairs={{0,2},{1,3},{2,0},{3,1},{4,6},{5,7},{6,4},{7,5},{8,10},{9,11},{10,... | collective-permute-start | bytes 344072 | tf_op jit(solution)/shard_map/ppermute | solution.py:83
  173.7 6.1 %collective-permute-start.15 = (bf16[2,64,896]{2,1,0:T(8,128)(2,1)S(1)}, bf16[2,64,896]{2,1,0:T(8,128)(2,1)S(1)}, u32[]{:S(2)}, u32[]{:S(2)}) collective-permute-start(bf16[2,64,896]{2,1,0:T(8,128)(2,1)S(1)} %maximum_select_fusion.5), channel_id=1, source_target_pairs={{0,1},{1,0},{2,3},{3,2},{4,5},{5,4},{6,7},{7,6},{8,9},{9,8},{10,11... | collective-permute-start | bytes 688136 | tf_op jit(solution)/shard_map/ppermute | solution.py:83
  179.9 6.5 %collective-permute-start.18 = (bf16[128,896]{1,0:T(8,128)(2,1)S(1)}, bf16[128,896]{1,0:T(8,128)(2,1)S(1)}, u32[]{:S(2)}, u32[]{:S(2)}) collective-permute-start(bf16[128,896]{1,0:T(8,128)(2,1)S(1)} %bitcast.132), channel_id=1, source_target_pairs={{0,16},{16,0},{1,17},{17,1},{2,18},{18,2},{3,19},{19,3},{4,20},{20... | collective-permute-start | bytes 688136 | tf_op jit(solution)/shard_map/ppermute | solution.py:244
  180.1 8.6 %collective-permute-start.16 = (bf16[128,896]{1,0:T(8,128)(2,1)S(1)}, bf16[128,896]{1,0:T(8,128)(2,1)S(1)}, u32[]{:S(2)}, u32[]{:S(2)}) collective-permute-start(bf16[128,896]{1,0:T(8,128)(2,1)S(1)} %bitcast.130), channel_id=1, source_target_pairs={{0,16},{16,0},{1,17},{17,1},{2,18},{18,2},{3,19},{19,3},{4,20},{20... | collective-permute-start | bytes 688136 | tf_op jit(solution)/shard_map/ppermute | solution.py:244
  (2 other events, 12.7 us)

commit v20 on v18

--- a/solution.py
+++ b/solution.py
@@ -96,7 +96,13 @@
     d_cols = table.shape[1]
 
     table_pieces = tok_pieces(table, n_tok)
-    if n_tok == 2:
+    early_hidden = n_tok == 2 and not (
+        lax.axis_size("voc") == 4
+        and is_pow2(lax.axis_size("wid"))
+        and tok_rows % (2 * lax.axis_size("wid")) == 0
+        and d_cols % 2 == 0
+    )
+    if early_hidden:
         hidden_other = lax.ppermute(hidden, "tok", [(0, 1), (1, 0)])
 
     partial_value = lax.dot_general(
@@ -170,6 +176,8 @@
         sent = quarter_dots(1 - c)
         received = lax.ppermute(sent, "voc", [(k, k ^ 1) for k in range(n_voc)])
         kept = quarter_dots(c)
+        hidden_send, kept = lax.optimization_barrier((hidden, kept))
+        hidden_other = lax.ppermute(hidden_send, "tok", [(0, 1), (1, 0)])
         voc_bits = bit_list("voc", n_voc)
         wid_bits = bit_list("wid", n_wid)
         v = lax.axis_index("voc")

time: 190 us -> 194 us (1.021)
  local copies, waits for them, and re-layouts: 3.43 us -> 5.93 us
  waiting for transfers between devices: 78.2 us -> 80.5 us
    ppermute x2, waiting for transfers between devices: 1.06 us -> 3.11 us  [on_device(): lax.ppermute(grad_rows_pos[i * half_rows:(i + 1) * half_rows], 'tok', [(0...]
  transfers between devices with their start and end apart: 20 -> 20, of which waited for: 15 -> 15; matrix products, arithmetic and copies ran while one was open for 14% -> 13% of each run, Pallas kernels for 0% -> 0%
where the time goes in v20:
time: 194 us; the launch traced here: 193 us
  waiting for transfers between devices  80.5 us (41%)
  blocking collectives  39.1 us (20%)
  matrix products  29.7 us (15%)
  starting transfers between devices  26.5 us (14%)
  other arithmetic  8.04 us (4%)
  local copies, waits for them, and re-layouts  5.93 us (3%)
  between operations  3.53 us (2%)
    psum x1, blocking collectives, on_device(): summed = lax.psum(partial_value, 'wid')  39.1 us
    ppermute x1, waiting for transfers between devices, tok_pieces(): pieces.append(lax.ppermute(x, 'tok', perm))  32.6 us
    ppermute x4, waiting for transfers between devices, doubling_gather(): other = lax.ppermute(x, ax, [(k, k ^ b) for k in range(n)])  20.8 us
    ppermute x6, waiting for transfers between devices, halving_steps(): x = keep + lax.ppermute(send, ax, [(k, k ^ b) for k in range(n)])  17.6 us
    ppermute x6, starting transfers between devices, halving_steps(): x = keep + lax.ppermute(send, ax, [(k, k ^ b) for k in range(n)])  10.9 us
    dot_general x4, matrix products, quarter_dots(): jnp.dot(dlogits, lax.dynamic_slice_in_dim(piece, sel * q_cols, q_cols, ax...  9.94 us
    dot_general x4, matrix products, on_device(): lax.dot_general(rows[i], hid[i * half_rows:(i + 1) * half_rows], by_pos,...  8.7 us
    dot_general x2, matrix products, on_device(): lax.dot_general(piece, cols, (((1,), (1,)), ((), ())), preferred_element_...  7.46 us
  transfers between devices with their start and end apart: 20, of which 15 were waited for; matrix products, arithmetic and copies ran while one was open for 13% of the time, Pallas kernels for 0%

profile of v20, /device:TPU:0, one launch (start us, length us, event | category | flops | bytes accessed | tf_op | source)
XLA Modules:
  0.0 193.4 jit_solution(7670949036394068696)
XLA Ops:
  0.6 3.0 %collective-permute-start.2 = (bf16[1216,1792]{1,0:T(8,128)(2,1)}, bf16[1216,1792]{1,0:T(8,128)(2,1)}, u32[]{:S(2)}, u32[]{:S(2)}) collective-permute-start(bf16[1216,1792]{1,0:T(8,128)(2,1)} %param.7), channel_id=1, source_target_pairs={{0,16},{16,0},{1,17},{17,1},{2,18},{18,2},{3,19},{19,3},{4,20},{20... | collective-permute-start | bytes 13074440 | tf_op jit(solution)/shard_map/ppermute | solution.py:11
  3.6 3.6 %fusion.63 = f32[256,896]{1,0:T(8,128)S(1)} fusion(bf16[256,2048]{1,0:T(8,128)(2,1)} %param.5, bf16[896,2048]{1,0:T(8,128)(2,1)} %param.6), kind=kOutput, calls=%fused_computation.106 | convolution fusion | flops 939524096 | bytes 5636096 | tf_op jit(solution)/shard_map/dot_general | solution.py:108
  7.3 39.1 %all-reduce.1 = bf16[256,896]{1,0:T(8,128)(2,1)S(1)} all-reduce(f32[256,896]{1,0:T(8,128)S(1)} %fusion.63), channel_id=1, replica_groups=mesh['tok'=2,'voc'=4,'wid'=4] {'wid'}, use_global_device_ids=true, to_apply=%region_0.0 | all-reduce | flops 229376 | bytes 1376256 | tf_op jit(solution)/shard_map/psum | solution.py:111
  48.0 7.9 %collective-permute-done = bf16[256,896]{1,0:T(8,128)(2,1)S(1)} collective-permute-done((bf16[256,896]{1,0:T(8,128)(2,1)S(1)}, bf16[256,896]{1,0:T(8,128)(2,1)S(1)}, u32[]{:S(2)}, u32[]{:S(2)}) %collective-permute-start) | collective-permute-done | bytes 458784 | tf_op jit(solution)/shard_map/ppermute | solution.py:83
  56.4 2.2 %collective-permute-done.1 = bf16[2,256,896]{2,1,0:T(8,128)(2,1)S(1)} collective-permute-done((bf16[2,256,896]{2,1,0:T(8,128)(2,1)S(1)}, bf16[2,256,896]{2,1,0:T(8,128)(2,1)S(1)}, u32[]{:S(2)}, u32[]{:S(2)}) %collective-permute-start.1) | collective-permute-done | bytes 917536 | tf_op jit(solution)/shard_map/ppermute | solution.py:83
  59.1 2.4 %copy.11 = bf16[256,4,896]{0,2,1:T(8,128)(2,1)} copy(bf16[256,4,896]{2,0,1:T(8,128)(2,1)S(1)} %bitcast.119) | data formatting | bytes 3670016 | tf_op jit(solution)/shard_map/transpose | solution.py:114
  61.5 3.9 %fusion.28 = f32[256,1216]{0,1:T(8,128)S(1)} fusion(bf16[1216,1792]{1,0:T(8,128)(2,1)} %param.7, bf16[256,3584]{0,1:T(8,128)(2,1)} %bitcast.122, s32[]{:T(128)S(6)} %select_n.172), kind=kOutput, calls=%fused_computation.31 | convolution fusion | flops 1115684864 | bytes 6520836 | tf_op jit(solution)/shard_map/dot_general | solution.py:121
  65.5 32.6 %collective-permute-done.2 = bf16[1216,1792]{1,0:T(8,128)(2,1)} collective-permute-done((bf16[1216,1792]{1,0:T(8,128)(2,1)}, bf16[1216,1792]{1,0:T(8,128)(2,1)}, u32[]{:S(2)}, u32[]{:S(2)}) %collective-permute-start.2) | collective-permute-done | bytes 4358176 | tf_op jit(solution)/shard_map/ppermute | solution.py:11
  98.0 3.5 %fusion.62 = (f32[256]{0:T(256)S(1)}, f32[256,1216]{0,1:T(8,128)S(1)}) fusion(f32[256,1216]{0,1:T(8,128)S(1)} %fusion.28, bf16[1216,1792]{1,0:T(8,128)(2,1)} %collective-permute-done.2, bf16[256,3584]{0,1:T(8,128)(2,1)S(1)} %bitcast.123, s32[]{:T(128)S(6)} %select_n.174), kind=kOutput, calls=%fused_computation.105 | convolution fusion | flops 1116307200 | bytes 7767044 | tf_op jit(solution)/shard_map/dot_general | solution.py:121
  105.0 1.8 collective-permute-done.4
  106.9 1.9 collective-permute-start.5
  110.6 2.9 %collective-permute-start.6 = (f32[3,256]{1,0:T(4,128)S(1)}, f32[3,256]{1,0:T(4,128)S(1)}, u32[]{:S(2)}, u32[]{:S(2)}) collective-permute-start(f32[3,256]{1,0:T(4,128)S(1)} %pad_maximum_fusion.6), channel_id=1, source_target_pairs={{0,2},{1,3},{2,0},{3,1},{4,6},{5,7},{6,4},{7,5},{8,10},{9,11},{10,... | collective-permute-start | bytes 9224 | tf_op jit(solution)/shard_map/ppermute | solution.py:33
  115.6 2.5 %fusion.14 = f32[1,256,896]{2,1,0:T(8,128)S(1)} fusion(bf16[1216,256]{1,0:T(8,128)(2,1)S(1)} %fusion.26, bf16[1216,1792]{1,0:T(8,128)(2,1)} %param.7, s32[]{:T(128)S(6)} %select_n.178), kind=kOutput, calls=%fused_computation.15 | convolution fusion | flops 557842432 | bytes 3719172 | tf_op jit(solution)/shard_map/dot_general | solution.py:167
  118.1 2.5 %fusion.17 = f32[1,256,896]{2,1,0:T(8,128)S(1)} fusion(bf16[1216,256]{1,0:T(8,128)(2,1)S(1)} %fusion.26, bf16[1216,1792]{1,0:T(8,128)(2,1)} %collective-permute-done.2, s32[]{:T(128)S(6)} %select_n.178), kind=kOutput, calls=%fused_computation.16 | convolution fusion | flops 557842432 | bytes 3719172 | tf_op jit(solution)/shard_map/dot_general | solution.py:167
  121.9 2.5 %fusion.8 = f32[1,256,896]{2,1,0:T(8,128)S(1)} fusion(bf16[1216,256]{1,0:T(8,128)(2,1)S(1)} %fusion.26, bf16[1216,1792]{1,0:T(8,128)(2,1)} %param.7, s32[]{:T(128)S(6)} %select_n.176), kind=kOutput, calls=%fused_computation.13 | convolution fusion | flops 557842432 | bytes 3719172 | tf_op jit(solution)/shard_map/dot_general | solution.py:167
  124.4 2.5 %fusion.11 = f32[1,256,896]{2,1,0:T(8,128)S(1)} fusion(bf16[1216,256]{1,0:T(8,128)(2,1)S(1)} %fusion.26, bf16[1216,1792]{1,0:T(8,128)(2,1)} %collective-permute-done.2, s32[]{:T(128)S(6)} %select_n.176), kind=kOutput, calls=%fused_computation.14 | convolution fusion | flops 557842432 | bytes 3719172 | tf_op jit(solution)/shard_map/dot_general | solution.py:167
  129.8 1.9 collective-permute-start.11
  137.4 5.6 %collective-permute-done.11 = f32[2,2,32,896]{3,2,1,0:T(8,128)} collective-permute-done((f32[2,2,32,896]{3,2,1,0:T(8,128)S(1)}, f32[2,2,32,896]{3,2,1,0:T(8,128)}, u32[]{:S(2)}, u32[]{:S(2)}) %collective-permute-start.11) | collective-permute-done | bytes 458784 | tf_op jit(solution)/shard_map/ppermute | solution.py:72
  147.7 3.9 %collective-permute-done.12 = f32[2,32,896]{2,1,0:T(8,128)S(1)} collective-permute-done((f32[2,32,896]{2,1,0:T(8,128)S(1)}, f32[2,32,896]{2,1,0:T(8,128)S(1)}, u32[]{:S(2)}, u32[]{:S(2)}) %collective-permute-start.12) | collective-permute-done | bytes 229408 | tf_op jit(solution)/shard_map/ppermute | solution.py:72
  151.7 2.7 %collective-permute-start.13 = (f32[32,896]{1,0:T(8,128)S(1)}, f32[32,896]{1,0:T(8,128)S(1)}, u32[]{:S(2)}, u32[]{:S(2)}) collective-permute-start(f32[32,896]{1,0:T(8,128)S(1)} %dynamic-slice_bitcast_fusion.2), channel_id=1, source_target_pairs={{0,2},{1,3},{2,0},{3,1},{4,6},{5,7},{6,4},{7,5},{8,10},{9,11},{10,... | collective-permute-start | bytes 344072 | tf_op jit(solution)/shard_map/ppermute | solution.py:72
  155.8 6.9 %collective-permute-done.13 = f32[32,896]{1,0:T(8,128)S(1)} collective-permute-done((f32[32,896]{1,0:T(8,128)S(1)}, f32[32,896]{1,0:T(8,128)S(1)}, u32[]{:S(2)}, u32[]{:S(2)}) %collective-permute-start.13) | collective-permute-done | bytes 114720 | tf_op jit(solution)/shard_map/ppermute | solution.py:72
  167.4 4.7 %collective-permute-done.14 = bf16[64,896]{1,0:T(8,128)(2,1)S(1)} collective-permute-done((bf16[64,896]{1,0:T(8,128)(2,1)S(1)}, bf16[64,896]{1,0:T(8,128)(2,1)S(1)}, u32[]{:S(2)}, u32[]{:S(2)}) %collective-permute-start.14) | collective-permute-done | bytes 114720 | tf_op jit(solution)/shard_map/ppermute | solution.py:83
  172.3 5.9 %collective-permute-done.15 = bf16[2,64,896]{2,1,0:T(8,128)(2,1)S(1)} collective-permute-done((bf16[2,64,896]{2,1,0:T(8,128)(2,1)S(1)}, bf16[2,64,896]{2,1,0:T(8,128)(2,1)S(1)}, u32[]{:S(2)}, u32[]{:S(2)}) %collective-permute-start.15) | collective-permute-done | bytes 229408 | tf_op jit(solution)/shard_map/ppermute | solution.py:83
  187.0 5.3 %add_add_fusion = f32[896,2048]{1,0:T(8,128)} fusion(f32[896,2048]{1,0:T(8,128)S(1)} %fusion.30, f32[896,2048]{1,0:T(8,128)S(1)} %fusion.35, f32[896,2048]{1,0:T(8,128)S(1)} %fusion.33, bf16[128,896]{1,0:T(8,128)(2,1)S(1)} %collective-permute-done.16, bf16[256,2048]{1,0:T(8,128)(2,1)} %copy-done.2), kind=kOutput, calls=%fused_computation | convolution fusion | flops 475267072 | bytes 30113792 | tf_op jit(solution)/shard_map/dot_general | solution.py:258
  (83 shorter events, 38.1 us)
Async XLA Ops:
  0.6 97.4 %collective-permute-start.2 = (bf16[1216,1792]{1,0:T(8,128)(2,1)}, bf16[1216,1792]{1,0:T(8,128)(2,1)}, u32[]{:S(2)}, u32[]{:S(2)}) collective-permute-start(bf16[1216,1792]{1,0:T(8,128)(2,1)} %param.7), channel_id=1, source_target_pairs={{0,16},{16,0},{1,17},{17,1},{2,18},{18,2},{3,19},{19,3},{4,20},{20... | collective-permute-start | bytes 13074440 | tf_op jit(solution)/shard_map/ppermute | solution.py:11
  7.3 48.9 %copy-start.5 = (s32[256]{0:T(256)S(1)}, s32[256]{0:T(256)}, u32[]{:S(2)}) copy-start(s32[256]{0:T(256)} %param.8) | copy-start | bytes 3076
  46.4 9.5 %collective-permute-start = (bf16[256,896]{1,0:T(8,128)(2,1)S(1)}, bf16[256,896]{1,0:T(8,128)(2,1)S(1)}, u32[]{:S(2)}, u32[]{:S(2)}) collective-permute-start(bf16[256,896]{1,0:T(8,128)(2,1)S(1)} %all-reduce.1), channel_id=1, source_target_pairs={{0,8},{4,12},{8,0},{12,4},{1,9},{5,13},{9,1},{13,5},{2,10},{6,14},... | collective-permute-start | bytes 1376264 | tf_op jit(solution)/shard_map/ppermute | solution.py:83
  56.1 2.5 %collective-permute-start.1 = (bf16[2,256,896]{2,1,0:T(8,128)(2,1)S(1)}, bf16[2,256,896]{2,1,0:T(8,128)(2,1)S(1)}, u32[]{:S(2)}, u32[]{:S(2)}) collective-permute-start(bf16[2,256,896]{2,1,0:T(8,128)(2,1)S(1)} %maximum_select_fusion.2), channel_id=1, source_target_pairs={{0,4},{4,0},{8,12},{12,8},{1,5},{5,1},{9,13},{13,9},{2,6},{6,2},{1... | collective-permute-start | bytes 2752520 | tf_op jit(solution)/shard_map/ppermute | solution.py:83
  61.5 36.5 %copy-start.1 = (bf16[256,4,896]{0,2,1:T(8,128)(2,1)S(1)}, bf16[256,4,896]{0,2,1:T(8,128)(2,1)}, u32[]{:S(2)}) copy-start(bf16[256,4,896]{0,2,1:T(8,128)(2,1)} %copy.11) | copy-start | bytes 5505028
  65.5 48.1 %copy-start.4 = (s32[256]{0:T(256)S(1)}, s32[256]{0:T(256)}, u32[]{:S(2)}) copy-start(s32[256]{0:T(256)} %param.9) | copy-start | bytes 3076
  101.9 1.2 collective-permute-start.3
  103.2 3.7 %collective-permute-start.4 = (f32[3,256]{1,0:T(4,128)S(1)}, f32[3,256]{1,0:T(4,128)S(1)}, u32[]{:S(2)}, u32[]{:S(2)}) collective-permute-start(f32[3,256]{1,0:T(4,128)S(1)} %pad_maximum_fusion.4), channel_id=1, source_target_pairs={{0,8},{4,12},{8,0},{12,4},{1,9},{5,13},{9,1},{13,5},{2,10},{6,14},... | collective-permute-start | bytes 9224 | tf_op jit(solution)/shard_map/ppermute | solution.py:33
  106.9 3.7 %collective-permute-start.5 = (f32[3,256]{1,0:T(4,128)S(1)}, f32[3,256]{1,0:T(4,128)S(1)}, u32[]{:S(2)}, u32[]{:S(2)}) collective-permute-start(f32[3,256]{1,0:T(4,128)S(1)} %pad_maximum_fusion.5), channel_id=1, source_target_pairs={{0,1},{1,0},{2,3},{3,2},{4,5},{5,4},{6,7},{7,6},{8,9},{9,8},{10,11... | collective-permute-start | bytes 9224 | tf_op jit(solution)/shard_map/ppermute | solution.py:33
  110.6 4.6 %collective-permute-start.6 = (f32[3,256]{1,0:T(4,128)S(1)}, f32[3,256]{1,0:T(4,128)S(1)}, u32[]{:S(2)}, u32[]{:S(2)}) collective-permute-start(f32[3,256]{1,0:T(4,128)S(1)} %pad_maximum_fusion.6), channel_id=1, source_target_pairs={{0,2},{1,3},{2,0},{3,1},{4,6},{5,7},{6,4},{7,5},{8,10},{9,11},{10,... | collective-permute-start | bytes 9224 | tf_op jit(solution)/shard_map/ppermute | solution.py:33
  121.9 5.2 %collective-permute-start.7 = (f32[2,256,896]{2,1,0:T(8,128)}, f32[2,256,896]{2,1,0:T(8,128)}, u32[]{:S(2)}, u32[]{:S(2)}) collective-permute-start(f32[2,256,896]{2,1,0:T(8,128)} %pad_maximum_fusion.1), channel_id=1, source_target_pairs={{0,4},{4,0},{8,12},{12,8},{1,5},{5,1},{9,13},{13,9},{2,6},{6,2},{1... | collective-permute-start | bytes 5505032 | tf_op jit(solution)/shard_map/ppermute | solution.py:177
  129.8 13.2 %collective-permute-start.11 = (f32[2,2,32,896]{3,2,1,0:T(8,128)S(1)}, f32[2,2,32,896]{3,2,1,0:T(8,128)}, u32[]{:S(2)}, u32[]{:S(2)}) collective-permute-start(f32[2,2,32,896]{3,2,1,0:T(8,128)S(1)} %add_bitcast_fusion), channel_id=1, source_target_pairs={{0,1},{1,0},{2,3},{3,2},{4,5},{5,4},{6,7},{7,6},{8,9},{9,8},{10,11... | collective-permute-start | bytes 1376264 | tf_op jit(solution)/shard_map/ppermute | solution.py:72
  132.4 13.6 %collective-permute-start.8 = (f32[2,2,32,896]{3,2,1,0:T(8,128)S(1)}, f32[2,2,32,896]{3,2,1,0:T(8,128)S(1)}, u32[]{:S(2)}, u32[]{:S(2)}) collective-permute-start(f32[2,2,32,896]{3,2,1,0:T(8,128)S(1)} %add_bitcast_fusion.1), channel_id=1, source_target_pairs={{0,8},{4,12},{8,0},{12,4},{1,9},{5,13},{9,1},{13,5},{2,10},{6,14},... | collective-permute-start | bytes 1376264 | tf_op jit(solution)/shard_map/ppermute | solution.py:72
  135.3 28.8 %collective-permute-start.19 = (f32[2]{0:T(128)S(1)}, f32[2]{0:T(128)S(1)}, u32[]{:S(2)}, u32[]{:S(2)}) collective-permute-start(f32[2]{0:T(128)S(1)} %pad_maximum_fusion.7), channel_id=1, source_target_pairs={{0,16},{16,0},{1,17},{17,1},{2,18},{18,2},{3,19},{19,3},{4,20},{20... | collective-permute-start | bytes 32 | tf_op jit(solution)/shard_map/ppermute | solution.py:45
  136.8 45.9 %collective-permute-start.17 = (bf16[256,2048]{1,0:T(8,128)(2,1)}, bf16[256,2048]{1,0:T(8,128)(2,1)S(1)}, u32[]{:S(2)}, u32[]{:S(2)}) collective-permute-start(bf16[256,2048]{1,0:T(8,128)(2,1)} %param.5), channel_id=1, source_target_pairs={{0,16},{16,0},{1,17},{17,1},{2,18},{18,2},{3,19},{19,3},{4,20},{20... | collective-permute-start | bytes 3145736 | tf_op jit(solution)/shard_map/ppermute | solution.py:180
  144.2 7.4 %collective-permute-start.12 = (f32[2,32,896]{2,1,0:T(8,128)S(1)}, f32[2,32,896]{2,1,0:T(8,128)S(1)}, u32[]{:S(2)}, u32[]{:S(2)}) collective-permute-start(f32[2,32,896]{2,1,0:T(8,128)S(1)} %dynamic-slice_bitcast_fusion), channel_id=1, source_target_pairs={{0,8},{4,12},{8,0},{12,4},{1,9},{5,13},{9,1},{13,5},{2,10},{6,14},... | collective-permute-start | bytes 688136 | tf_op jit(solution)/shard_map/ppermute | solution.py:72
  146.1 8.3 %collective-permute-start.9 = (f32[2,32,896]{2,1,0:T(8,128)S(1)}, f32[2,32,896]{2,1,0:T(8,128)S(1)}, u32[]{:S(2)}, u32[]{:S(2)}) collective-permute-start(f32[2,32,896]{2,1,0:T(8,128)S(1)} %dynamic-slice_bitcast_fusion.1), channel_id=1, source_target_pairs={{0,1},{1,0},{2,3},{3,2},{4,5},{5,4},{6,7},{7,6},{8,9},{9,8},{10,11... | collective-permute-start | bytes 688136 | tf_op jit(solution)/shard_map/ppermute | solution.py:72
  151.7 11.0 %collective-permute-start.13 = (f32[32,896]{1,0:T(8,128)S(1)}, f32[32,896]{1,0:T(8,128)S(1)}, u32[]{:S(2)}, u32[]{:S(2)}) collective-permute-start(f32[32,896]{1,0:T(8,128)S(1)} %dynamic-slice_bitcast_fusion.2), channel_id=1, source_target_pairs={{0,2},{1,3},{2,0},{3,1},{4,6},{5,7},{6,4},{7,5},{8,10},{9,11},{10,... | collective-permute-start | bytes 344072 | tf_op jit(solution)/shard_map/ppermute | solution.py:72
  154.4 9.6 %collective-permute-start.10 = (f32[32,896]{1,0:T(8,128)S(1)}, f32[32,896]{1,0:T(8,128)S(1)}, u32[]{:S(2)}, u32[]{:S(2)}) collective-permute-start(f32[32,896]{1,0:T(8,128)S(1)} %dynamic-slice_bitcast_fusion.3), channel_id=1, source_target_pairs={{0,2},{1,3},{2,0},{3,1},{4,6},{5,7},{6,4},{7,5},{8,10},{9,11},{10,... | collective-permute-start | bytes 344072 | tf_op jit(solution)/shard_map/ppermute | solution.py:72
  162.7 17.8 %copy-start.3 = (bf16[256,2048]{1,0:T(8,128)(2,1)S(1)}, bf16[256,2048]{1,0:T(8,128)(2,1)}, u32[]{:S(2)}) copy-start(bf16[256,2048]{1,0:T(8,128)(2,1)} %param.5) | copy-start | bytes 3145732
  164.0 8.1 %collective-permute-start.14 = (bf16[64,896]{1,0:T(8,128)(2,1)S(1)}, bf16[64,896]{1,0:T(8,128)(2,1)S(1)}, u32[]{:S(2)}, u32[]{:S(2)}) collective-permute-start(bf16[64,896]{1,0:T(8,128)(2,1)S(1)} %pad_maximum_fusion.2), channel_id=1, source_target_pairs={{0,2},{1,3},{2,0},{3,1},{4,6},{5,7},{6,4},{7,5},{8,10},{9,11},{10,... | collective-permute-start | bytes 344072 | tf_op jit(solution)/shard_map/ppermute | solution.py:83
  172.1 6.1 %collective-permute-start.15 = (bf16[2,64,896]{2,1,0:T(8,128)(2,1)S(1)}, bf16[2,64,896]{2,1,0:T(8,128)(2,1)S(1)}, u32[]{:S(2)}, u32[]{:S(2)}) collective-permute-start(bf16[2,64,896]{2,1,0:T(8,128)(2,1)S(1)} %maximum_select_fusion.5), channel_id=1, source_target_pairs={{0,1},{1,0},{2,3},{3,2},{4,5},{5,4},{6,7},{7,6},{8,9},{9,8},{10,11... | collective-permute-start | bytes 688136 | tf_op jit(solution)/shard_map/ppermute | solution.py:83
  178.4 6.2 %collective-permute-start.18 = (bf16[128,896]{1,0:T(8,128)(2,1)S(1)}, bf16[128,896]{1,0:T(8,128)(2,1)S(1)}, u32[]{:S(2)}, u32[]{:S(2)}) collective-permute-start(bf16[128,896]{1,0:T(8,128)(2,1)S(1)} %bitcast.128), channel_id=1, source_target_pairs={{0,16},{16,0},{1,17},{17,1},{2,18},{18,2},{3,19},{19,3},{4,20},{20... | collective-permute-start | bytes 688136 | tf_op jit(solution)/shard_map/ppermute | solution.py:252
  179.9 7.1 %collective-permute-start.16 = (bf16[128,896]{1,0:T(8,128)(2,1)S(1)}, bf16[128,896]{1,0:T(8,128)(2,1)S(1)}, u32[]{:S(2)}, u32[]{:S(2)}) collective-permute-start(bf16[128,896]{1,0:T(8,128)(2,1)S(1)} %bitcast.126), channel_id=1, source_target_pairs={{0,16},{16,0},{1,17},{17,1},{2,18},{18,2},{3,19},{19,3},{4,20},{20... | collective-permute-start | bytes 688136 | tf_op jit(solution)/shard_map/ppermute | solution.py:252
  (2 other events, 3.9 us)
